TPU v7x, 32 devices: a whole 2x2x4 slice. The times are simulated.
32 devices in a mesh: mix: 2 (over x), seq: 16 (over z, y, core).
Axes of the slice: x: 2, y: 2, z: 4, core: 2. Of those that a mesh axis runs over, the one named last changes fastest.
Arguments:
- frames: bfloat16 [4096, 1024], P(('mix', 'seq')), parts along dimension 0, may hold values from -18 to 18
- segment_ids: int32 [4096], P(('mix', 'seq')), parts along dimension 0, may hold values from 0 to 2, never falling along the last dimension, each value on 1 to 1500 neighbouring positions
- out_grad: bfloat16 [4096, 1024], P(('mix', 'seq')), parts along dimension 0, may hold values from -6 to 6
- ln_gain: float32 [2048], P(('mix', 'seq')), parts along dimension 0, may hold values from 0.5 to 2
- w_in: bfloat16 [2048, 2048], P(('mix', 'seq')), parts along dimension 0, may hold values from -0.1875 to 0.1875
- dw_kernel: float32 [62, 1024], P('mix', 'seq'), parts along dimension 0, may hold values from -1 to 1
- bn_gain: float32 [2048], P(('mix', 'seq')), parts along dimension 0, may hold values from 0.5 to 2
- bn_bias: float32 [2048], P(('mix', 'seq')), parts along dimension 0, may hold values from -3 to 3
- w_out: bfloat16 [2048, 1024], P(('mix', 'seq')), parts along dimension 0, may hold values from -0.1875 to 0.1875
Outputs:
- outputs: bfloat16 [4096, 1024], P(('mix', 'seq')), parts along dimension 0
- grad_frames: bfloat16 [4096, 1024], P(('mix', 'seq')), parts along dimension 0
- grad_w_in: float32 [2048, 2048], P(('mix', 'seq')), parts along dimension 0
- grad_w_out: float32 [2048, 1024], P(('mix', 'seq')), parts along dimension 0
- grad_kernel: float32 [62, 1024], P('mix', 'seq'), parts along dimension 0
- grad_ln_gain: float32 [2048], P(('mix', 'seq')), parts along dimension 0
- grad_bn_gain: float32 [2048], P(('mix', 'seq')), parts along dimension 0
- grad_bn_bias: float32 [2048], P(('mix', 'seq')), parts along dimension 0
There are 2 independent parts, one for each index of `mix`. A program takes and returns all parts, laid end to end along the dimension named above; each array names one. Nothing has to cross between parts.
Inputs may be any that keep to these rules, and one draw needn't show every extreme that they name: `segment_ids`: ids never fall along the stream; every utterance number is used, by 1 to 1500 consecutive frames, one utterance exactly 1500.
All inputs are finite; a program needn't handle non-finite values.
Results may differ from a plain program's by a relative error of at most 0.012.
The roundings to bfloat16 on the way count: a program that leaves them out, or rounds other values in their place, can miss the bound.
Values may be sent and summed in bfloat16 or wider, within the bound.
No kernel may reach another device: no remote copies, remote signals or barrier semaphores. Data moves between devices by JAX's collectives and lax.ppermute only.
A program may use at most 128 MiB of HBM per device.

v0:
```python
import math

import jax
import jax.numpy as jnp
from jax import lax
from jax.sharding import PartitionSpec as P

EPSILON = 1e-05


def with_halo(cells, sides, width):
    for axis, dim in sides:
        count = lax.axis_size(axis)
        ends = count - 1
        head = lax.slice_in_dim(cells, 0, width, axis=dim)
        tail = lax.slice_in_dim(cells, cells.shape[dim] - width, cells.shape[dim], axis=dim)
        cells = jnp.concatenate(
            [
                lax.ppermute(tail, axis, [(i, (i + 1) % count) for i in range(ends)]),
                cells,
                lax.ppermute(head, axis, [((i + 1) % count, i) for i in range(ends)]),
            ],
            axis=dim,
        )
    return cells


def local(frames, segment_ids, out_grad, ln_gain, w_in, dw_kernel, bn_gain, bn_bias, w_out):
    frame_count = frames.shape[0]
    width = frames.shape[1]
    taps = dw_kernel.shape[0]
    margin = taps // 2
    devices = lax.axis_size("seq")
    stream = frame_count * devices
    grad_scale = 1.0 / math.sqrt(stream)
    share = width // devices
    gains, kernel, bn_scale, bn_shift = (
        lax.all_gather(ln_gain, "seq", axis=0, tiled=True),
        lax.all_gather(dw_kernel, "seq", axis=1, tiled=True),
        lax.all_gather(bn_gain, "seq", axis=0, tiled=True),
        lax.all_gather(bn_bias, "seq", axis=0, tiled=True),
    )
    own_ids = segment_ids + 1
    padded_ids = with_halo(own_ids, (("seq", 0),), margin)
    masks = [
        (padded_ids[tap_index : tap_index + frame_count] == own_ids).astype(jnp.float32)[:, None]
        for tap_index in range(taps)
    ]
    frames_float = frames.astype(jnp.float32)
    mean_ln = jnp.mean(frames_float, axis=1, keepdims=True)
    centred = frames_float - mean_ln
    rstd_ln = lax.rsqrt(jnp.mean(centred * centred, axis=1, keepdims=True) + EPSILON)
    ln_hat = centred * rstd_ln
    ln_x = (ln_hat * gains).astype(jnp.bfloat16)
    columns = ln_x
    hidden = jnp.dot(
        columns, lax.all_gather(w_in, "seq", axis=0, tiled=True), preferred_element_type=jnp.float32
    )
    left_half = hidden[:, :width]
    right_gate = jax.nn.sigmoid(hidden[:, width:])
    glu = (left_half * right_gate).astype(jnp.bfloat16)
    padded_glu = with_halo(glu, (("seq", 0),), margin)
    conv_out = jnp.zeros((frame_count, width), jnp.float32)
    for tap_index in range(taps):
        conv_out = (
            conv_out
            + kernel[tap_index]
            * padded_glu[tap_index : tap_index + frame_count].astype(jnp.float32)
            * masks[tap_index]
        )
    plain_sums, square_sums = lax.psum(
        (jnp.sum(conv_out, axis=0), jnp.sum(conv_out * conv_out, axis=0)), "seq"
    )
    bn_mean = plain_sums / stream
    bn_var = square_sums / stream - bn_mean * bn_mean
    bn_rstd = lax.rsqrt(bn_var + EPSILON)
    bn_hat = (conv_out - bn_mean) * bn_rstd
    zed = bn_hat * bn_scale + bn_shift
    zed_gate = jax.nn.sigmoid(zed)
    activation = (zed * zed_gate).astype(jnp.bfloat16)
    columns = activation
    projected = jnp.dot(
        columns,
        lax.all_gather(w_out, "seq", axis=0, tiled=True),
        preferred_element_type=jnp.float32,
    )
    outputs = (frames_float + projected).astype(jnp.bfloat16)
    grad_w_out = lax.psum_scatter(
        jnp.einsum("fa,fb->ab", activation, out_grad, preferred_element_type=jnp.float32)
        * grad_scale,
        "seq",
        scatter_dimension=0,
        tiled=True,
    )
    grad_act = jnp.einsum(
        "fe,ne->fn",
        out_grad,
        lax.all_gather(w_out, "seq", axis=0, tiled=True),
        preferred_element_type=jnp.float32,
    )
    grad_zed = grad_act * zed_gate * (1.0 + zed * (1.0 - zed_gate))
    bias_total, gain_total = lax.psum(
        (jnp.sum(grad_zed, axis=0), jnp.sum(grad_zed * bn_hat, axis=0)), "seq"
    )
    grad_conv = bn_scale * bn_rstd * (grad_zed - bias_total / stream - bn_hat * gain_total / stream)
    first_channel = lax.axis_index("seq") * share
    grad_bn_bias = lax.dynamic_slice_in_dim(bias_total, first_channel, share, 0) * grad_scale
    grad_bn_gain = lax.dynamic_slice_in_dim(gain_total, first_channel, share, 0) * grad_scale
    kernel_rows = [
        jnp.sum(
            grad_conv
            * padded_glu[tap_index : tap_index + frame_count].astype(jnp.float32)
            * masks[tap_index],
            axis=0,
        )
        for tap_index in range(taps)
    ]
    kernel_term = jnp.stack(kernel_rows) * grad_scale
    padded_conv = with_halo(grad_conv, (("seq", 0),), margin)
    grad_glu = jnp.zeros((frame_count, width), jnp.float32)
    for tap_index in range(taps):
        mirror = 2 * margin - tap_index
        grad_glu = (
            grad_glu
            + kernel[tap_index] * padded_conv[mirror : mirror + frame_count] * masks[mirror]
        )
    grad_hidden = jnp.concatenate(
        [grad_glu * right_gate, grad_glu * left_half * right_gate * (1.0 - right_gate)], axis=1
    ).astype(jnp.bfloat16)
    grad_ln = jnp.einsum(
        "fe,ne->fn",
        grad_hidden,
        lax.all_gather(w_in, "seq", axis=0, tiled=True),
        preferred_element_type=jnp.float32,
    )
    in_term = (
        jnp.einsum("fa,fb->ab", ln_x, grad_hidden, preferred_element_type=jnp.float32) * grad_scale
    )
    gain_term = jnp.sum(grad_ln * ln_hat, axis=0) * grad_scale
    grad_w_in, grad_kernel, grad_ln_gain = (
        lax.psum_scatter(in_term, "seq", scatter_dimension=0, tiled=True),
        lax.psum_scatter(kernel_term, "seq", scatter_dimension=1, tiled=True),
        lax.psum_scatter(gain_term, "seq", scatter_dimension=0, tiled=True),
    )
    grad_hat = grad_ln * gains
    grad_input = rstd_ln * (
        grad_hat
        - jnp.mean(grad_hat, axis=1, keepdims=True)
        - ln_hat * jnp.mean(grad_hat * ln_hat, axis=1, keepdims=True)
    )
    grad_frames = (out_grad.astype(jnp.float32) + grad_input).astype(jnp.bfloat16)
    return (
        outputs,
        grad_frames,
        grad_w_in,
        grad_w_out,
        grad_kernel,
        grad_ln_gain,
        grad_bn_gain,
        grad_bn_bias,
    )


def solution(mesh):
    return jax.shard_map(
        local,
        mesh=mesh,
        in_specs=(
            P(("mix", "seq"), None),
            P(("mix", "seq")),
            P(("mix", "seq"), None),
            P(("mix", "seq")),
            P(("mix", "seq"), None),
            P("mix", "seq"),
            P(("mix", "seq")),
            P(("mix", "seq")),
            P(("mix", "seq"), None),
        ),
        out_specs=(
            P(("mix", "seq"), None),
            P(("mix", "seq"), None),
            P(("mix", "seq"), None),
            P(("mix", "seq"), None),
            P("mix", "seq"),
            P(("mix", "seq")),
            P(("mix", "seq")),
            P(("mix", "seq")),
        ),
        check_vma=False,
    )
```

profile of v0, /device:TPU:0, one launch (start us, length us, event | category | flops | bytes accessed | tf_op | source)
XLA Modules:
  0.0 432.6 jit_solution(1981038902537433708)
XLA Ops:
  7.2 0.7 all-gather.4.cloned.1.call-update
  7.9 0.7 all-gather.6.cloned.1.call-update
  8.7 0.7 broadcast_add_fusion
  9.4 2.3 collective-permute-start.1
  11.8 1.3 collective-permute-start.3
  13.1 26.5 %all-gather = f32[16,64,31]{1,2,0:T(8,128)S(1)} all-gather(f32[1,64,31]{1,2,0:T(8,128)} %bitcast.175), channel_id=1, replica_groups=mesh['mix'=2,'seq'=16] {'seq'}, dimensions={0}, use_global_device_ids=true | all-gather | bytes 134912 | tf_op jit(solution)/shard_map/all_gather | solution.py:39
  39.6 0.2 copy.18
  39.9 1.3 fusion.301
  41.9 0.9 dynamic-update-slice.2
  42.7 0.8 dynamic-update-slice
  43.6 30.2 %all-reduce = f32[1024]{0:T(1024)S(1)} all-reduce(f32[1024]{0:T(1024)S(1)} %dynamic-update-slice), channel_id=1, replica_groups=mesh['mix'=2,'seq'=16] {'seq'}, use_global_device_ids=true, to_apply=%add | all-reduce | flops 1024 | bytes 8192
  73.8 1.1 convert_reduce_fusion
  74.9 1.2 fusion.129
  76.2 0.9 dynamic-update-slice.1
  77.1 0.7 compare_convert_fusion.29
  77.9 3.1 fusion.291
  81.2 1.5 collective-permute-start
  82.7 1.3 collective-permute-start.2
  84.1 1.7 collective-permute-done.2
  85.8 4.7 %fusion.294 = (f32[1024]{0:T(1024)S(1)}, f32[1024]{0:T(1024)S(1)}, f32[128,1024]{1,0:T(8,128)S(1)}) fusion(f32[128]{0:T(128)S(1)} %get-tuple-element.110, bf16[15,1024]{1,0:T(8,128)(2,1)S(1)} %collective-permute-done.2, bf16[128,1024]{1,0:T(8,128)(2,1)S(1)} %multiply_convert_fusion.3, f32[1024]{0:T(1024)S(1)} %bitcast.107, f32[128]{0:T(128)S(1)} %get-tuple-element.111, ...), kind=kLoop, calls=%fused_computation.505 | loop fusion | flops 28178432 | bytes 998400 | tf_op jit(solution)/shard_map/reduce_sum | solution.py:72
  90.5 59.8 %all-reduce.5 = (f32[1024]{0:T(1024)S(1)}, f32[1024]{0:T(1024)S(1)}, f32[1024]{0:T(1024)S(1)}, f32[1024]{0:T(1024)S(1)}) all-reduce(f32[1024]{0:T(1024)S(1)} %dynamic-update-slice.2, f32[1024]{0:T(1024)S(1)} %dynamic-update-slice.1, f32[1024]{0:T(1024)S(1)} %get-tuple-element.45, ...), channel_id=1, replica_groups=mesh['mix'=2,'seq'=16] {'seq'}, use_global_device_ids=true, to_apply=%add.2 | all-reduce | flops 4096 | bytes 32768
  150.3 2.5 fusion.293
  152.8 30.0 %all-reduce.4 = (f32[1024]{0:T(1024)S(1)}, f32[1024]{0:T(1024)S(1)}) all-reduce(f32[1024]{0:T(1024)S(1)} %get-tuple-element.43, f32[1024]{0:T(1024)S(1)} %get-tuple-element.42), channel_id=1, replica_groups=mesh['mix'=2,'seq'=16] {'seq'}, use_global_device_ids=true, to_apply=%region_9.0 | all-reduce | flops 2048 | bytes 16384 | tf_op jit(solution)/shard_map/psum | solution.py:102
  182.8 0.9 fusion.250
  183.7 0.3 fusion.162
  184.0 0.4 fusion.208
  184.4 0.7 fusion.247
  185.1 0.7 fusion.180
  185.8 0.7 fusion.198
  186.5 0.2 stack.127
  186.7 1.0 copy.19
  187.8 2.7 convolution_multiply_fusion.1
  190.6 0.2 reduce-scatter.6.cloned.1.call-start
  190.8 1.3 collective-permute-start.4
  192.1 3.0 collective-permute-start.5
  195.2 0.9 collective-permute-done.5
  196.1 4.3 %multiply_convert_fusion.1 = (bf16[128,1024]{1,0:T(8,128)(2,1)S(1)}, f32[128,1024]{1,0:T(8,128)S(1)}) fusion(f32[128,2048]{1,0:T(8,128)S(1)} %fusion.291, f32[128]{0:T(128)S(1)} %get-tuple-element.94, f32[128,1024]{1,0:T(8,128)S(1)} %get-tuple-element.52, f32[15,1024]{1,0:T(8,128)S(1)} %collective-permute-done.5, f32[1024]{0:T(1024)S(1)} %bitcast.108, ...), kind=kLoop, calls=%fused_computation.415 | loop fusion | flops 16515072 | bytes 2100224 | tf_op jit(solution)/shard_map/convert
  200.4 0.2 multiply_convert_fusion
  200.6 4.6 %convolution_multiply_fusion = f32[1024,2048]{1,0:T(8,128)} fusion(bf16[128,1024]{1,0:T(8,128)(2,1)S(1)} %multiply_convert_fusion, bf16[128,1024]{1,0:T(8,128)(2,1)S(1)} %get-tuple-element.53, bf16[128,1024]{1,0:T(8,128)(2,1)S(1)} %copy-done, f32[1024]{0:T(1024)S(1)} %all-reduce, f32[128]{0:T(128)S(1)} %add_rsqrt_fusion.1, f32[128]{0:T(128)S(1)} %broadcast_multiply_fusion.6), kind=kOutput, calls=%fused_computation | convolution fusion | flops 540672000 | bytes 9180160 | tf_op jit(solution)/shard_map/fa,fb->ab/dot_general | solution.py:137
  205.9 0.6 dynamic-slice_multiply_fusion
  206.5 3.1 fusion.1
  209.6 1.6 fusion.128
  211.3 31.1 %all-reduce.3 = f32[1024]{0:T(1024)S(1)} all-reduce(f32[1024]{0:T(1024)S(1)} %broadcast_multiply_fusion.1), channel_id=5, replica_groups=mesh['mix'=2,'seq'=16] {'seq'}, use_global_device_ids=true, to_apply=%region_47.0.clone | all-reduce | flops 1024 | bytes 8192
  242.4 0.6 dynamic-slice.4
  243.0 1.0 fusion.127
  244.0 1.4 copy.20
  245.4 72.5 %reduce-scatter.8.cloned.1.call-done = f32[64,1024]{1,0:T(8,128)} async-done(((f32[1024,1024]{1,0:T(8,128)}), f32[64,1024]{1,0:T(8,128)}) %reduce-scatter.8.cloned.1.call-update) | async-done | bytes 262160 | tf_op jit(solution)/shard_map/reduce_scatter | solution.py:88
  317.9 108.2 %reduce-scatter.6.cloned.1.call-done = f32[64,2048]{1,0:T(8,128)} async-done(((f32[1024,2048]{1,0:T(8,128)}), f32[64,2048]{1,0:T(8,128)}) %reduce-scatter.6.cloned.1.call-update) | async-done | bytes 524304 | tf_op jit(solution)/shard_map/reduce_scatter | solution.py:141
  (41 shorter events, 0.9 us)
Async XLA Ops:
  7.2 70.7 %all-gather.4.cloned.1.call-start = ((), (), s32[]{:S(2)}) async-start(), calls=%async_computation.3 | async-start | bytes 4456448 | tf_op jit(solution)/shard_map/all_gather | solution.py:57
  7.9 142.4 %all-gather.6.cloned.1.call-start = ((), (), s32[]{:S(2)}) async-start(), calls=%async_computation.4 | async-start | bytes 2228224 | tf_op jit(solution)/shard_map/all_gather | solution.py:84
  8.6 235.3 %reduce-scatter.10.cloned.1.call-start = ((), (), s32[]{:S(2)}) async-start(), calls=%async_computation.7 | async-start | bytes 557056
  9.4 67.6 %collective-permute-start.1 = (s32[15]{0:T(128)S(1)}, s32[15]{0:T(128)S(1)}, u32[]{:S(2)}, u32[]{:S(2)}) collective-permute-start(s32[15]{0:T(128)S(1)} %get-tuple-element.128), channel_id=1, source_target_pairs={{0,1},{1,2},{2,3},{3,4},{4,5},{5,6},{6,7},{7,8},{8,9},{9,10},{10,1... | collective-permute-start | bytes 188 | tf_op jit(solution)/shard_map/ppermute | solution.py:19
  11.8 65.3 %collective-permute-start.3 = (s32[15]{0:T(128)S(1)}, s32[15]{0:T(128)S(1)}, u32[]{:S(2)}, u32[]{:S(2)}) collective-permute-start(s32[15]{0:T(128)S(1)} %get-tuple-element.129), channel_id=1, source_target_pairs={{1,0},{2,1},{3,2},{4,3},{5,4},{6,5},{7,6},{8,7},{9,8},{10,9},{11,1... | collective-permute-start | bytes 188 | tf_op jit(solution)/shard_map/ppermute | solution.py:21
  39.7 44.3 %copy-start.3 = (s32[128]{0:T(128)S(1)}, s32[128]{0:T(128)}, u32[]{:S(2)}) copy-start(s32[128]{0:T(128)} %param.10) | copy-start | bytes 1540
  76.1 74.2 %copy-start.2 = (bf16[128,1024]{1,0:T(8,128)(2,1)S(1)}, bf16[128,1024]{1,0:T(8,128)(2,1)}, u32[]{:S(2)}) copy-start(bf16[128,1024]{1,0:T(8,128)(2,1)} %param.11) | copy-start | bytes 786436
  81.2 2.9 collective-permute-start
  82.7 3.1 collective-permute-start.2
  187.8 130.1 %reduce-scatter.8.cloned.1.call-start = ((), (), s32[]{:S(2)}) async-start(), calls=%async_computation.6 | async-start | bytes 4456448 | tf_op jit(solution)/shard_map/reduce_scatter | solution.py:88
  190.6 10.0 %copy-start = (bf16[128,1024]{1,0:T(8,128)(2,1)S(1)}, bf16[128,1024]{1,0:T(8,128)(2,1)}, u32[]{:S(2)}) copy-start(bf16[128,1024]{1,0:T(8,128)(2,1)} %param.9) | copy-start | bytes 786436
  190.6 235.5 %reduce-scatter.6.cloned.1.call-start = ((), (), s32[]{:S(2)}) async-start(), calls=%async_computation.5 | async-start | bytes 8912896 | tf_op jit(solution)/shard_map/reduce_scatter | solution.py:141
  190.8 4.3 %collective-permute-start.4 = (f32[15,1024]{1,0:T(8,128)S(1)}, f32[15,1024]{1,0:T(8,128)S(1)}, u32[]{:S(2)}, u32[]{:S(2)}) collective-permute-start(f32[15,1024]{1,0:T(8,128)S(1)} %get-tuple-element.56), channel_id=1, source_target_pairs={{1,0},{2,1},{3,2},{4,3},{5,4},{6,5},{7,6},{8,7},{9,8},{10,9},{11,1... | collective-permute-start | bytes 184328 | tf_op jit(solution)/shard_map/ppermute | solution.py:21
  192.1 3.9 collective-permute-start.5
  205.9 3.7 copy-start.1
Sparse Core Ops, SparseCore 0:
  10.2 54.4 all-gather.3
  66.8 39.9 all-gather.5
  187.9 53.3 reduce-scatter.9
  246.1 71.7 reduce-scatter.7
  322.4 103.6 reduce-scatter.5
where the time goes:
time: 433 us
  waiting for transfers between devices  185 us (43%)
  blocking collectives  178 us (41%)
  other arithmetic  18.4 us (4%)
  matrix products  17.7 us (4%)
  between operations  15.4 us (4%)
  starting transfers between devices  11.1 us (3%)
  local copies, waits for them, and re-layouts  7.65 us (2%)
    unnamed x3, blocking collectives  121 us
    reduce_scatter x1, waiting for transfers between devices, local(): lax.psum_scatter(in_term, 'seq', scatter_dimension=0, tiled=True)  108 us
    reduce_scatter x1, waiting for transfers between devices, local(): lax.psum_scatter(jnp.einsum('fa,fb->ab', activation, out_grad, preferred_...  72.5 us
    psum x1, blocking collectives, local(): lax.psum((jnp.sum(grad_zed, axis=0), jnp.sum(grad_zed * bn_hat, axis=0)),...  30 us
    all_gather x1, blocking collectives, local(): lax.all_gather(dw_kernel, 'seq', axis=1, tiled=True)  26.5 us
  transfers between devices with their start and end apart: 11, of which 4 were waited for; matrix products, arithmetic and copies ran while one was open for 8% of the time, Pallas kernels for 0%

commit v1 on v0

--- a/solution.py
+++ b/solution.py
@@ -161,9 +161,158 @@
     )
 
 
+def channel_local(frames, segment_ids, out_grad, ln_gain, w_in, dw_kernel, bn_gain, bn_bias, w_out):
+    rows = frames.shape[0]
+    width = frames.shape[1]
+    taps = dw_kernel.shape[0]
+    margin = taps // 2
+    devices = lax.axis_size("seq")
+    stream = rows * devices
+    grad_scale = 1.0 / math.sqrt(stream)
+    share = width // devices
+
+    small = lax.all_gather(
+        jnp.concatenate([ln_gain, segment_ids.astype(jnp.float32)]), "seq", axis=0
+    )
+    gains = small[:, :share].reshape(width)
+    all_ids = small[:, share:].reshape(stream).astype(jnp.int32)
+
+    frames_all = lax.all_gather(frames, "seq", axis=0, tiled=True)
+    w_out_all = lax.all_gather(w_out, "seq", axis=0, tiled=True)
+    grad_all = lax.all_gather(out_grad, "seq", axis=0, tiled=True)
+    w_in_all = lax.all_gather(w_in, "seq", axis=0, tiled=True)
+
+    w_in_cols = lax.all_to_all(
+        w_in.reshape(share, 2, devices, share).transpose(2, 0, 1, 3),
+        "seq", 0, 0, tiled=True,
+    ).reshape(width, 2 * share)
+
+    def norm(block):
+        block_float = block.astype(jnp.float32)
+        mean = jnp.mean(block_float, axis=1, keepdims=True)
+        centred = block_float - mean
+        rstd = lax.rsqrt(jnp.mean(centred * centred, axis=1, keepdims=True) + EPSILON)
+        return centred * rstd, rstd
+
+    ln_all, _ = norm(frames_all)
+    ln_x_all = (ln_all * gains).astype(jnp.bfloat16)
+
+    hidden = jnp.dot(ln_x_all, w_in_cols, preferred_element_type=jnp.float32)
+    left_half = hidden[:, :share]
+    right_gate = jax.nn.sigmoid(hidden[:, share:])
+    glu = (left_half * right_gate).astype(jnp.bfloat16)
+
+    own_ids = all_ids + 1
+    padded_ids = jnp.pad(own_ids, margin)
+    masks = [
+        (padded_ids[tap_index : tap_index + stream] == own_ids).astype(jnp.float32)[:, None]
+        for tap_index in range(taps)
+    ]
+    padded_glu = jnp.pad(glu, ((margin, margin), (0, 0)))
+    conv_out = jnp.zeros((stream, share), jnp.float32)
+    for tap_index in range(taps):
+        conv_out = (
+            conv_out
+            + dw_kernel[tap_index]
+            * padded_glu[tap_index : tap_index + stream].astype(jnp.float32)
+            * masks[tap_index]
+        )
+    bn_mean = jnp.sum(conv_out, axis=0) / stream
+    bn_var = jnp.sum((conv_out - bn_mean) ** 2, axis=0) / stream
+    bn_rstd = lax.rsqrt(bn_var + EPSILON)
+    bn_hat = (conv_out - bn_mean) * bn_rstd
+    zed = bn_hat * bn_gain + bn_bias
+    zed_gate = jax.nn.sigmoid(zed)
+    activation = (zed * zed_gate).astype(jnp.bfloat16)
+
+    act_rows = (
+        lax.all_to_all(activation.reshape(devices, rows, share), "seq", 0, 0, tiled=True)
+        .transpose(1, 0, 2)
+        .reshape(rows, width)
+    )
+    projected = jnp.dot(act_rows, w_out_all, preferred_element_type=jnp.float32)
+    outputs = (frames.astype(jnp.float32) + projected).astype(jnp.bfloat16)
+
+    grad_w_out = (
+        jnp.einsum("fa,fb->ab", activation, grad_all, preferred_element_type=jnp.float32)
+        * grad_scale
+    )
+    grad_act = jnp.einsum("fe,ne->fn", grad_all, w_out, preferred_element_type=jnp.float32)
+    grad_zed = grad_act * zed_gate * (1.0 + zed * (1.0 - zed_gate))
+    bias_total = jnp.sum(grad_zed, axis=0)
+    gain_total = jnp.sum(grad_zed * bn_hat, axis=0)
+    grad_conv = bn_gain * bn_rstd * (grad_zed - bias_total / stream - bn_hat * gain_total / stream)
+    grad_kernel = (
+        jnp.stack(
+            [
+                jnp.sum(
+                    grad_conv
+                    * padded_glu[tap_index : tap_index + stream].astype(jnp.float32)
+                    * masks[tap_index],
+                    axis=0,
+                )
+                for tap_index in range(taps)
+            ]
+        )
+        * grad_scale
+    )
+    padded_conv = jnp.pad(grad_conv, ((margin, margin), (0, 0)))
+    grad_glu = jnp.zeros((stream, share), jnp.float32)
+    for tap_index in range(taps):
+        mirror = 2 * margin - tap_index
+        grad_glu = (
+            grad_glu
+            + dw_kernel[tap_index] * padded_conv[mirror : mirror + stream] * masks[mirror]
+        )
+    grad_hidden = jnp.concatenate(
+        [grad_glu * right_gate, grad_glu * left_half * right_gate * (1.0 - right_gate)], axis=1
+    ).astype(jnp.bfloat16)
+
+    in_cols = (
+        jnp.einsum("fa,fb->ab", ln_x_all, grad_hidden, preferred_element_type=jnp.float32)
+        * grad_scale
+    )
+    grad_w_in = (
+        lax.all_to_all(in_cols.reshape(devices, share, 2, share), "seq", 0, 0, tiled=True)
+        .transpose(1, 2, 0, 3)
+        .reshape(share, 2 * width)
+    )
+    hidden_rows = (
+        lax.all_to_all(grad_hidden.reshape(devices, rows, 2, share), "seq", 0, 0, tiled=True)
+        .transpose(1, 2, 0, 3)
+        .reshape(rows, 2 * width)
+    )
+    grad_ln = jnp.einsum(
+        "fe,ne->fn", hidden_rows, w_in_all, preferred_element_type=jnp.float32
+    )
+    ln_hat, rstd_ln = norm(frames)
+    grad_ln_gain = lax.psum_scatter(
+        jnp.sum(grad_ln * ln_hat, axis=0) * grad_scale, "seq", scatter_dimension=0, tiled=True
+    )
+    grad_hat = grad_ln * gains
+    grad_input = rstd_ln * (
+        grad_hat
+        - jnp.mean(grad_hat, axis=1, keepdims=True)
+        - ln_hat * jnp.mean(grad_hat * ln_hat, axis=1, keepdims=True)
+    )
+    grad_frames = (out_grad.astype(jnp.float32) + grad_input).astype(jnp.bfloat16)
+    return (
+        outputs,
+        grad_frames,
+        grad_w_in,
+        grad_w_out,
+        grad_kernel,
+        grad_ln_gain,
+        gain_total * grad_scale,
+        bias_total * grad_scale,
+    )
+
+
 def solution(mesh):
+    devices = mesh.shape["seq"]
+    body = channel_local if devices <= 16 else local
     return jax.shard_map(
-        local,
+        body,
         mesh=mesh,
         in_specs=(
             P(("mix", "seq"), None),

time: 433 us -> 270 us (0.62)
  waiting for transfers between devices: 185 us -> 72.4 us
  blocking collectives: 178 us -> 93.8 us
  starting transfers between devices: 11.1 us -> 22.1 us
  other arithmetic: 18.4 us -> 28.7 us
  local copies, waits for them, and re-layouts: 7.65 us -> 16.7 us
    reduce_scatter x2 -> x0, waiting for transfers between devices: 181 us -> none  [the longest x1 108 us: local(): lax.psum_scatter(in_term, 'seq', scatter_dimension=0, tiled=True)]
    all_gather x2 -> x4, waiting for transfers between devices: 0.02 us -> 48 us  [the longest x1 31.8 us: channel_local(): w_in_all = lax.all_gather(w_in, 'seq', axis=0, tiled=True)]
    psum x1 -> x0, blocking collectives: 30 us -> none  [local(): lax.psum((jnp.sum(grad_zed, axis=0), jnp.sum(grad_zed * bn_hat, axis=0)),...]
    unnamed x3 -> x2, blocking collectives: 121 us -> 93.8 us
    all_gather x1 -> x0, blocking collectives: 26.5 us -> none  [local(): lax.all_gather(dw_kernel, 'seq', axis=1, tiled=True)]
    all_to_all x0 -> x4, starting transfers between devices: none -> 22 us  [the longest x1 7.39 us: channel_local(): lax.all_to_all(w_in.reshape(share, 2, devices, share).transpose(2, 0, 1,...]
    all_to_all x0 -> x4, waiting for transfers between devices: none -> 21.8 us  [the longest x1 14.6 us: channel_local(): lax.all_to_all(in_cols.reshape(devices, share, 2, share), 'seq', 0, 0, ti...]
    ppermute x6 -> x0, starting transfers between devices: 10.8 us -> none  [the longest x3 6.9 us: with_halo(): lax.ppermute(tail, axis, [(i, (i + 1) % count) for i in range(ends)])]
  transfers between devices with their start and end apart: 11 -> 8, of which waited for: 4 -> 4; matrix products, arithmetic and copies ran while one was open for 8% -> 22% of each run, Pallas kernels for 0% -> 0%
where the time goes in v1:
time: 270 us; the launch traced here: 269 us
  blocking collectives  93.8 us (35%)
  waiting for transfers between devices  72.4 us (27%)
  other arithmetic  28.7 us (11%)
  starting transfers between devices  22.1 us (8%)
  matrix products  19.1 us (7%)
  local copies, waits for them, and re-layouts  16.7 us (6%)
  between operations  15.9 us (6%)
    unnamed x2, blocking collectives  93.8 us
    all_gather x1, waiting for transfers between devices, channel_local(): w_in_all = lax.all_gather(w_in, 'seq', axis=0, tiled=True)  31.8 us
    all_gather x1, waiting for transfers between devices, channel_local(): grad_all = lax.all_gather(out_grad, 'seq', axis=0, tiled=True)  16.2 us
    all_to_all x1, waiting for transfers between devices, channel_local(): lax.all_to_all(in_cols.reshape(devices, share, 2, share), 'seq', 0, 0, ti...  14.6 us
    all_to_all x1, starting transfers between devices, channel_local(): lax.all_to_all(w_in.reshape(share, 2, devices, share).transpose(2, 0, 1,...  7.39 us
    all_to_all x1, waiting for transfers between devices, channel_local(): lax.all_to_all(grad_hidden.reshape(devices, rows, 2, share), 'seq', 0, 0,...  7.11 us
    unnamed x88, local copies, waits for them, and re-layouts  6.06 us
    mul x1, other arithmetic, channel_local(): grad_glu * right_gate  5.98 us
  transfers between devices with their start and end apart: 8, of which 4 were waited for; matrix products, arithmetic and copies ran while one was open for 22% of the time, Pallas kernels for 0%

profile of v1, /device:TPU:0, one launch (start us, length us, event | category | flops | bytes accessed | tf_op | source)
XLA Modules:
  0.0 268.8 jit_solution(10674082711596979769)
XLA Ops:
  7.3 0.7 all-gather.6.cloned.1.call-update
  8.0 0.7 all-gather.10.cloned.1.call-update
  8.7 0.7 all-gather.8.cloned.1.call-update
  9.4 1.5 reshape.122
  10.9 0.6 copy.27
  11.5 1.1 reshape.136
  12.6 7.4 %all-to-all-start = ((bf16[16,2,4096]{2,1,0:T(2,128)(2,1)}), bf16[16,2,4096]{2,1,0:T(2,128)(2,1)S(1)}, u32[]{:S(2)}, u32[]{:S(2)}) async-start(bf16[16,2,4096]{2,1,0:T(2,128)(2,1)} %reshape.136), calls=%async_computation | async-start | bytes 524288 | tf_op jit(solution)/shard_map/all_to_all | solution.py:185
  20.6 1.0 slice_bitcast_fusion.30
  21.7 1.0 slice_bitcast_fusion.29
  23.0 0.6 fusion.253
  24.5 62.7 %all-reduce.3 = f32[3072]{0:T(1024)S(1)} all-reduce(f32[3072]{0:T(1024)S(1)} %maximum_dynamic-update-slice_fusion), channel_id=2, replica_groups=mesh['mix'=2,'seq'=16] {'seq'}, use_global_device_ids=true, to_apply=%add.3 | all-reduce | flops 3072 | bytes 24576
  87.5 0.5 add_rsqrt_fusion.1
  90.1 3.0 %convert_reduce_fusion = f32[2048]{0:T(1024)S(1)} fusion(bf16[2048,1024]{1,0:T(8,128)(2,1)} %all-gather.6.cloned.1.call-done), kind=kLoop, calls=%fused_computation.1 | loop fusion | flops 4192256 | bytes 4202496 | tf_op jit(solution)/shard_map/reduce_sum | solution.py:192
  93.5 1.4 fusion.2
  94.9 1.4 fusion.4
  96.4 1.5 fusion.254
  98.3 4.2 %fusion.251 = (f32[64]{0:T(128)S(1)}, f32[2048,64]{0,1:T(8,128)S(1)}) fusion(f32[2048]{0:T(1024)S(1)} %get-tuple-element.109, f32[64]{0:T(128)S(1)} %get-tuple-element.78, f32[2048]{0:T(1024)S(1)} %get-tuple-element.81, f32[64]{0:T(128)S(1)} %get-tuple-element.79, f32[2048]{0:T(1024)S(1)} %get-tuple-element.82, f32[64]{0:T(128)S(1)} %get-tuple-element.50, ...), kind=kLoop, calls=%fused_computation.425 | loop fusion | flops 16121792 | bytes 1040384 | tf_op jit(solution)/shard_map/reduce_sum | solution.py:220
  102.7 0.5 fusion.248
  103.3 16.2 %all-gather.10.cloned.1.call-done = bf16[2048,1024]{1,0:T(8,128)(2,1)} async-done(((bf16[128,1024]{1,0:T(8,128)(2,1)}), bf16[2048,1024]{1,0:T(8,128)(2,1)}) %all-gather.10.cloned.1.call-update) | async-done | bytes 4194320 | tf_op jit(solution)/shard_map/all_gather | solution.py:182
  119.4 5.0 %fusion.250 = (f32[64]{0:T(128)S(1)}, f32[64]{0:T(128)}, bf16[2048,64]{0,1:T(8,128)(2,1)S(1)}, f32[2048,64]{0,1:T(8,128)}) fusion(f32[64]{0:T(128)S(1)} %get-tuple-element.115, f32[2048,64]{0,1:T(8,128)S(1)} %get-tuple-element.47, f32[64]{0:T(128)S(1)} %broadcast_multiply_fusion.9, f32[64]{0:T(128)S(1)} %copy-done.39, f32[64]{0:T(128)S(1)} %copy-done.36, ...), kind=kOutput, calls=%fused_computation.424 | convolution fusion | flops 270663552 | bytes 5637632 | tf_op jit(solution)/shard_map/fe,ne->fn/dot_general | solution.py:240
  124.5 0.8 copy_bitcast_fusion
  125.2 3.8 %all-to-all-start.1 = ((bf16[16,128,64]{1,2,0:T(8,128)(2,1)}), bf16[16,128,64]{1,2,0:T(8,128)(2,1)S(1)}, u32[]{:S(2)}, u32[]{:S(2)}) async-start(bf16[16,128,64]{1,2,0:T(8,128)(2,1)} %copy_bitcast_fusion), calls=%async_computation.1 | async-start | bytes 524288 | tf_op jit(solution)/shard_map/all_to_all | solution.py:229
  129.5 2.4 fusion.139
  131.9 6.0 %fusion.249 = (bf16[2048,64]{0,1:T(8,128)(2,1)S(1)}, f32[2048,64]{0,1:T(8,128)S(1)}) fusion(f32[2048,128]{0,1:T(8,128)S(1)} %fusion.254, f32[2048]{0:T(1024)S(1)} %get-tuple-element.80, f32[64]{0:T(128)} %copy-done.29, f32[2048]{0:T(1024)S(1)} %get-tuple-element.98, f32[64]{0:T(128)} %copy-done.30, f32[2048]{0:T(1024)S(1)} %get-tuple-element.108, ...), kind=kLoop, calls=%fused_computation.423 | loop fusion | flops 12582912 | bytes 2088704 | tf_op jit(solution)/shard_map/mul | solution.py:268
  138.1 2.1 convolution_multiply_fusion.1
  140.2 1.6 reshape.127
  141.9 1.9 reshape.138
  143.9 1.0 copy.30
  144.9 5.8 %all-to-all-start.3 = ((f32[16,1,8192]{2,1,0:T(1,128)}), f32[16,1,8192]{2,1,0:T(1,128)S(1)}, u32[]{:S(2)}, u32[]{:S(2)}) async-start(f32[16,1,8192]{2,1,0:T(1,128)} %reshape.138), calls=%async_computation.3 | async-start | bytes 1048576 | tf_op jit(solution)/shard_map/all_to_all | solution.py:276
  150.9 0.8 fusion.115
  151.8 0.8 fusion.81
  152.6 0.8 fusion.63
  153.4 0.7 fusion.97
  154.3 14.6 %all-to-all-done.3 = f32[16,1,8192]{2,1,0:T(1,128)S(1)} async-done(((f32[16,1,8192]{2,1,0:T(1,128)}), f32[16,1,8192]{2,1,0:T(1,128)S(1)}, u32[]{:S(2)}, u32[]{:S(2)}) %all-to-all-start.3) | async-done | bytes 524320 | tf_op jit(solution)/shard_map/all_to_all | solution.py:276
  168.9 5.1 %all-to-all-start.2 = ((bf16[16,128,2,64]{1,3,2,0:T(8,128)(2,1)}), bf16[16,128,2,64]{1,3,2,0:T(8,128)(2,1)S(1)}, u32[]{:S(2)}, u32[]{:S(2)}) async-start(bf16[16,128,2,64]{1,3,2,0:T(8,128)(2,1)} %copy.30), calls=%async_computation.2 | async-start | bytes 1048576 | tf_op jit(solution)/shard_map/all_to_all | solution.py:281
  174.5 0.6 broadcast_multiply_fusion
  175.1 3.8 %convolution_multiply_fusion.2 = f32[64,1024]{1,0:T(8,128)} fusion(bf16[2048,64]{0,1:T(8,128)(2,1)S(1)} %get-tuple-element.48, bf16[2048,1024]{1,0:T(8,128)(2,1)} %all-gather.10.cloned.1.call-done), kind=kOutput, calls=%fused_computation.12 | convolution fusion | flops 268500992 | bytes 4718592 | tf_op jit(solution)/shard_map/fa,fb->ab/dot_general | solution.py:237
  178.9 2.8 %fusion.6 = bf16[128,1024]{1,0:T(8,128)(2,1)} fusion(bf16[128,1024]{0,1:T(8,128)(2,1)S(1)} %bitcast.141, bf16[1024,1024]{1,0:T(8,128)(2,1)} %all-gather.8.cloned.1.call-done, bf16[128,1024]{1,0:T(8,128)(2,1)S(1)} %copy-done.3), kind=kOutput, calls=%fused_computation.11 | convolution fusion | flops 268828672 | bytes 2883584 | tf_op jit(solution)/shard_map/dot_general | solution.py:233
  182.2 1.9 reduce
  184.1 0.8 reshape.139
  184.9 0.6 copy.32
  185.5 1.2 reshape.128
  186.7 7.1 %all-to-all-done.2 = bf16[16,128,2,64]{1,3,2,0:T(8,128)(2,1)S(1)} async-done(((bf16[16,128,2,64]{1,3,2,0:T(8,128)(2,1)}), bf16[16,128,2,64]{1,3,2,0:T(8,128)(2,1)S(1)}, u32[]{:S(2)}, u32[]{:S(2)}) %all-to-all-start.2) | async-done | bytes 524320 | tf_op jit(solution)/shard_map/all_to_all | solution.py:281
  193.8 31.8 %all-gather.12.cloned.1.call-done = bf16[1024,2048]{1,0:T(8,128)(2,1)} async-done(((bf16[64,2048]{1,0:T(8,128)(2,1)}), bf16[1024,2048]{1,0:T(8,128)(2,1)}) %all-gather.12.cloned.1.call-update) | async-done | bytes 4194320 | tf_op jit(solution)/shard_map/all_gather | solution.py:183
  225.7 3.8 %fusion.17 = (f32[1024]{0:T(1024)S(1)}, f32[128]{0:T(128)S(1)}, f32[128]{0:T(128)S(1)}, f32[128,1024]{1,0:T(8,128)S(1)}) fusion(bf16[128,1024]{1,0:T(8,128)(2,1)S(1)} %copy-done.3, f32[128]{0:T(128)S(1)} %copy-done.31, f32[128]{0:T(128)S(1)} %broadcast_multiply_fusion.7, f32[1024]{0:T(1024)S(1)} %mul.645, bf16[128,2048]{0,1:T(8,128)(2,1)S(1)} %bitcast.136, ...), kind=kOutput, calls=%fused_computation.88 | convolution fusion | flops 538049280 | bytes 5515264 | tf_op jit(solution)/shard_map/fe,ne->fn/dot_general | solution.py:285
  229.5 31.2 %all-reduce.4 = f32[1024]{0:T(1024)S(1)} all-reduce(f32[1024]{0:T(1024)S(1)} %broadcast_multiply_fusion.2), channel_id=3, replica_groups=mesh['mix'=2,'seq'=16] {'seq'}, use_global_device_ids=true, to_apply=%region_42.43.clone | all-reduce | flops 1024 | bytes 8192
  260.7 0.6 dynamic-slice.2
  261.3 1.0 fusion.16
  (120 shorter events, 6.0 us)
Async XLA Ops:
  7.2 15.8 %copy-start.32 = (u32[32]{0:T(128)S(1)}, u32[32]{0:T(128)}, u32[]{:S(2)}) copy-start(u32[32]{0:T(128)} %constant.48) | copy-start | bytes 388
  7.2 15.5 %copy-start.3 = (bf16[128,1024]{1,0:T(8,128)(2,1)S(1)}, bf16[128,1024]{1,0:T(8,128)(2,1)}, u32[]{:S(2)}) copy-start(bf16[128,1024]{1,0:T(8,128)(2,1)} %param.9) | copy-start | bytes 786436
  7.2 15.8 %copy-start.38 = (s32[128]{0:T(128)S(1)}, s32[128]{0:T(128)}, u32[]{:S(2)}) copy-start(s32[128]{0:T(128)} %param.10) | copy-start | bytes 1540
  7.2 17.1 %copy-start.35 = (f32[64]{0:T(128)S(1)}, f32[64]{0:T(128)}, u32[]{:S(2)}) copy-start(f32[64]{0:T(128)} %param.12) | copy-start | bytes 772
  7.2 82.9 %all-gather.6.cloned.1.call-start = ((), (), s32[]{:S(2)}) async-start(), calls=%async_computation.4 | async-start | bytes 4456448 | tf_op jit(solution)/shard_map/all_gather | solution.py:180
  7.9 111.5 %all-gather.10.cloned.1.call-start = ((), (), s32[]{:S(2)}) async-start(), calls=%async_computation.6 | async-start | bytes 4456448 | tf_op jit(solution)/shard_map/all_gather | solution.py:182
  8.7 170.3 %all-gather.8.cloned.1.call-start = ((), (), s32[]{:S(2)}) async-start(), calls=%async_computation.5 | async-start | bytes 2228224 | tf_op jit(solution)/shard_map/all_gather | solution.py:181
  12.6 76.4 %all-to-all-start = ((bf16[16,2,4096]{2,1,0:T(2,128)(2,1)}), bf16[16,2,4096]{2,1,0:T(2,128)(2,1)S(1)}, u32[]{:S(2)}, u32[]{:S(2)}) async-start(bf16[16,2,4096]{2,1,0:T(2,128)(2,1)} %reshape.136), calls=%async_computation | async-start | bytes 524288 | tf_op jit(solution)/shard_map/all_to_all | solution.py:185
  20.0 205.7 %all-gather.12.cloned.1.call-start = ((), (), s32[]{:S(2)}) async-start(), calls=%async_computation.7 | async-start | bytes 4456448 | tf_op jit(solution)/shard_map/all_gather | solution.py:183
  21.6 76.4 %copy-start.6 = (f32[64]{0:T(128)}, f32[64]{0:T(128)S(1)}, u32[]{:S(2)}) copy-start(f32[64]{0:T(128)S(1)} %get-tuple-element.55) | copy-start | bytes 772
  21.6 76.4 %copy-start.7 = (f32[64]{0:T(128)}, f32[64]{0:T(128)S(1)}, u32[]{:S(2)}) copy-start(f32[64]{0:T(128)S(1)} %get-tuple-element.56) | copy-start | bytes 772
  21.6 76.4 %copy-start.8 = (f32[64]{0:T(128)}, f32[64]{0:T(128)S(1)}, u32[]{:S(2)}) copy-start(f32[64]{0:T(128)S(1)} %get-tuple-element.57) | copy-start | bytes 772
  21.6 76.4 %copy-start.9 = (f32[64]{0:T(128)}, f32[64]{0:T(128)S(1)}, u32[]{:S(2)}) copy-start(f32[64]{0:T(128)S(1)} %get-tuple-element.58) | copy-start | bytes 772
  21.7 76.4 %copy-start.10 = (f32[64]{0:T(128)}, f32[64]{0:T(128)S(1)}, u32[]{:S(2)}) copy-start(f32[64]{0:T(128)S(1)} %get-tuple-element.59) | copy-start | bytes 772
  21.7 76.4 %copy-start.11 = (f32[64]{0:T(128)}, f32[64]{0:T(128)S(1)}, u32[]{:S(2)}) copy-start(f32[64]{0:T(128)S(1)} %get-tuple-element.60) | copy-start | bytes 772
  21.7 76.4 %copy-start.12 = (f32[64]{0:T(128)}, f32[64]{0:T(128)S(1)}, u32[]{:S(2)}) copy-start(f32[64]{0:T(128)S(1)} %get-tuple-element.61) | copy-start | bytes 772
  21.7 76.4 %copy-start.13 = (f32[64]{0:T(128)}, f32[64]{0:T(128)S(1)}, u32[]{:S(2)}) copy-start(f32[64]{0:T(128)S(1)} %get-tuple-element.62) | copy-start | bytes 772
  21.7 76.4 %copy-start.14 = (f32[64]{0:T(128)}, f32[64]{0:T(128)S(1)}, u32[]{:S(2)}) copy-start(f32[64]{0:T(128)S(1)} %get-tuple-element.63) | copy-start | bytes 772
  21.7 76.4 %copy-start.15 = (f32[64]{0:T(128)}, f32[64]{0:T(128)S(1)}, u32[]{:S(2)}) copy-start(f32[64]{0:T(128)S(1)} %get-tuple-element.64) | copy-start | bytes 772
  21.7 76.4 %copy-start.16 = (f32[64]{0:T(128)}, f32[64]{0:T(128)S(1)}, u32[]{:S(2)}) copy-start(f32[64]{0:T(128)S(1)} %get-tuple-element.65) | copy-start | bytes 772
  21.7 76.4 %copy-start.17 = (f32[64]{0:T(128)}, f32[64]{0:T(128)S(1)}, u32[]{:S(2)}) copy-start(f32[64]{0:T(128)S(1)} %get-tuple-element.66) | copy-start | bytes 772
  21.7 76.4 %copy-start.18 = (f32[64]{0:T(128)}, f32[64]{0:T(128)S(1)}, u32[]{:S(2)}) copy-start(f32[64]{0:T(128)S(1)} %get-tuple-element.67) | copy-start | bytes 772
  22.7 75.5 %copy-start.19 = (f32[64]{0:T(128)}, f32[64]{0:T(128)S(1)}, u32[]{:S(2)}) copy-start(f32[64]{0:T(128)S(1)} %get-tuple-element.68) | copy-start | bytes 772
  22.7 75.5 %copy-start.20 = (f32[64]{0:T(128)}, f32[64]{0:T(128)S(1)}, u32[]{:S(2)}) copy-start(f32[64]{0:T(128)S(1)} %get-tuple-element.69) | copy-start | bytes 772
  22.7 75.5 %copy-start.21 = (f32[64]{0:T(128)}, f32[64]{0:T(128)S(1)}, u32[]{:S(2)}) copy-start(f32[64]{0:T(128)S(1)} %get-tuple-element.70) | copy-start | bytes 772
  22.7 75.5 %copy-start.22 = (f32[64]{0:T(128)}, f32[64]{0:T(128)S(1)}, u32[]{:S(2)}) copy-start(f32[64]{0:T(128)S(1)} %get-tuple-element.71) | copy-start | bytes 772
  22.8 75.5 %copy-start.23 = (f32[64]{0:T(128)}, f32[64]{0:T(128)S(1)}, u32[]{:S(2)}) copy-start(f32[64]{0:T(128)S(1)} %get-tuple-element.72) | copy-start | bytes 772
  22.8 75.5 %copy-start.24 = (f32[64]{0:T(128)}, f32[64]{0:T(128)S(1)}, u32[]{:S(2)}) copy-start(f32[64]{0:T(128)S(1)} %get-tuple-element.73) | copy-start | bytes 772
  22.8 75.5 %copy-start.25 = (f32[64]{0:T(128)}, f32[64]{0:T(128)S(1)}, u32[]{:S(2)}) copy-start(f32[64]{0:T(128)S(1)} %get-tuple-element.74) | copy-start | bytes 772
  22.8 75.5 %copy-start.26 = (f32[64]{0:T(128)}, f32[64]{0:T(128)S(1)}, u32[]{:S(2)}) copy-start(f32[64]{0:T(128)S(1)} %get-tuple-element.75) | copy-start | bytes 772
  22.8 75.5 %copy-start.27 = (f32[64]{0:T(128)}, f32[64]{0:T(128)S(1)}, u32[]{:S(2)}) copy-start(f32[64]{0:T(128)S(1)} %get-tuple-element.76) | copy-start | bytes 772
  22.8 75.5 %copy-start.28 = (f32[64]{0:T(128)}, f32[64]{0:T(128)S(1)}, u32[]{:S(2)}) copy-start(f32[64]{0:T(128)S(1)} %get-tuple-element.77) | copy-start | bytes 772
  22.8 75.5 %copy-start.29 = (f32[64]{0:T(128)}, f32[64]{0:T(128)S(1)}, u32[]{:S(2)}) copy-start(f32[64]{0:T(128)S(1)} %get-tuple-element.78) | copy-start | bytes 772
  22.8 75.5 %copy-start.30 = (f32[64]{0:T(128)}, f32[64]{0:T(128)S(1)}, u32[]{:S(2)}) copy-start(f32[64]{0:T(128)S(1)} %get-tuple-element.79) | copy-start | bytes 772
  90.1 3.5 %copy-start = (bf16[2048,1024]{1,0:T(8,128)(2,1)S(1)}, bf16[2048,1024]{1,0:T(8,128)(2,1)}, u32[]{:S(2)}) copy-start(bf16[2048,1024]{1,0:T(8,128)(2,1)} %all-gather.6.cloned.1.call-done) | copy-start | bytes 12582916
  96.3 6.2 %copy-start.1 = (bf16[2048,1024]{1,0:T(8,128)(2,1)}, bf16[2048,1024]{1,0:T(8,128)(2,1)S(1)}, u32[]{:S(2)}) copy-start(bf16[2048,1024]{1,0:T(8,128)(2,1)S(1)} %fusion.4) | copy-start | bytes 12582916
  96.3 6.4 %copy-start.36 = (f32[64]{0:T(128)S(1)}, f32[64]{0:T(128)}, u32[]{:S(2)}) copy-start(f32[64]{0:T(128)} %param.15) | copy-start | bytes 772
  96.4 23.1 %copy-start.5 = (bf16[64,1024]{1,0:T(8,128)(2,1)S(1)}, bf16[64,1024]{1,0:T(8,128)(2,1)}, u32[]{:S(2)}) copy-start(bf16[64,1024]{1,0:T(8,128)(2,1)} %param.17) | copy-start | bytes 393220
  96.4 23.1 %copy-start.39 = (f32[64]{0:T(128)S(1)}, f32[64]{0:T(128)}, u32[]{:S(2)}) copy-start(f32[64]{0:T(128)} %param.16) | copy-start | bytes 772
  102.5 22.0 %copy-start.34 = (f32[64]{0:T(128)}, f32[64]{0:T(128)S(1)}, u32[]{:S(2)}) copy-start(f32[64]{0:T(128)S(1)} %broadcast_multiply_fusion.9) | copy-start | bytes 772
  103.3 21.2 %copy-start.33 = (f32[64]{0:T(128)}, f32[64]{0:T(128)S(1)}, u32[]{:S(2)}) copy-start(f32[64]{0:T(128)S(1)} %get-tuple-element.115) | copy-start | bytes 772
  125.2 19.7 %all-to-all-start.1 = ((bf16[16,128,64]{1,2,0:T(8,128)(2,1)}), bf16[16,128,64]{1,2,0:T(8,128)(2,1)S(1)}, u32[]{:S(2)}, u32[]{:S(2)}) async-start(bf16[16,128,64]{1,2,0:T(8,128)(2,1)} %copy_bitcast_fusion), calls=%async_computation.1 | async-start | bytes 524288 | tf_op jit(solution)/shard_map/all_to_all | solution.py:229
  129.0 9.1 %copy-start.2 = (bf16[2048,1024]{1,0:T(8,128)(2,1)S(1)}, bf16[2048,1024]{1,0:T(8,128)(2,1)}, u32[]{:S(2)}) copy-start(bf16[2048,1024]{1,0:T(8,128)(2,1)} %copy-done.1) | copy-start | bytes 12582916
  143.8 30.2 %copy-start.37 = (f32[64]{0:T(128)S(1)}, f32[64]{0:T(128)}, u32[]{:S(2)}) copy-start(f32[64]{0:T(128)} %get-tuple-element.42) | copy-start | bytes 772
  144.9 24.0 %all-to-all-start.3 = ((f32[16,1,8192]{2,1,0:T(1,128)}), f32[16,1,8192]{2,1,0:T(1,128)S(1)}, u32[]{:S(2)}, u32[]{:S(2)}) async-start(f32[16,1,8192]{2,1,0:T(1,128)} %reshape.138), calls=%async_computation.3 | async-start | bytes 1048576 | tf_op jit(solution)/shard_map/all_to_all | solution.py:276
  168.9 24.9 %all-to-all-start.2 = ((bf16[16,128,2,64]{1,3,2,0:T(8,128)(2,1)}), bf16[16,128,2,64]{1,3,2,0:T(8,128)(2,1)S(1)}, u32[]{:S(2)}, u32[]{:S(2)}) async-start(bf16[16,128,2,64]{1,3,2,0:T(8,128)(2,1)} %copy.30), calls=%async_computation.2 | async-start | bytes 1048576 | tf_op jit(solution)/shard_map/all_to_all | solution.py:281
  181.7 44.0 %copy-start.31 = (f32[128]{0:T(128)S(1)}, f32[128]{0:T(128)}, u32[]{:S(2)}) copy-start(f32[128]{0:T(128)} %add_rsqrt_fusion.1) | copy-start | bytes 1540
  185.5 75.8 %copy-start.4 = (bf16[128,1024]{1,0:T(8,128)(2,1)S(1)}, bf16[128,1024]{1,0:T(8,128)(2,1)}, u32[]{:S(2)}) copy-start(bf16[128,1024]{1,0:T(8,128)(2,1)} %param.11) | copy-start | bytes 786436
Sparse Core Ops, SparseCore 0:
  10.2 57.8 all-gather.5
  70.3 49.1 all-gather.9
  121.6 47.3 all-gather.7
  171.0 54.6 all-gather.11

commit v2 on v1

--- a/solution.py
+++ b/solution.py
@@ -171,21 +171,27 @@
     grad_scale = 1.0 / math.sqrt(stream)
     share = width // devices
 
-    small = lax.all_gather(
-        jnp.concatenate([ln_gain, segment_ids.astype(jnp.float32)]), "seq", axis=0
-    )
+    def spread(block):
+        copies = jnp.broadcast_to(block[None], (devices,) + block.shape)
+        return lax.all_to_all(copies, "seq", 0, 0, tiled=True)
+
+    small = spread(jnp.concatenate([ln_gain, segment_ids.astype(jnp.float32)]))
     gains = small[:, :share].reshape(width)
     all_ids = small[:, share:].reshape(stream).astype(jnp.int32)
 
     frames_all = lax.all_gather(frames, "seq", axis=0, tiled=True)
     w_out_all = lax.all_gather(w_out, "seq", axis=0, tiled=True)
     grad_all = lax.all_gather(out_grad, "seq", axis=0, tiled=True)
-    w_in_all = lax.all_gather(w_in, "seq", axis=0, tiled=True)
-
-    w_in_cols = lax.all_to_all(
-        w_in.reshape(share, 2, devices, share).transpose(2, 0, 1, 3),
-        "seq", 0, 0, tiled=True,
-    ).reshape(width, 2 * share)
+    w_in_all = spread(w_in).reshape(width, 2 * width)
+
+    first_channel = lax.axis_index("seq") * share
+    w_in_cols = jnp.concatenate(
+        [
+            lax.dynamic_slice_in_dim(w_in_all, first_channel, share, 1),
+            lax.dynamic_slice_in_dim(w_in_all, width + first_channel, share, 1),
+        ],
+        axis=1,
+    )
 
     def norm(block):
         block_float = block.astype(jnp.float32)
@@ -272,11 +278,6 @@
         jnp.einsum("fa,fb->ab", ln_x_all, grad_hidden, preferred_element_type=jnp.float32)
         * grad_scale
     )
-    grad_w_in = (
-        lax.all_to_all(in_cols.reshape(devices, share, 2, share), "seq", 0, 0, tiled=True)
-        .transpose(1, 2, 0, 3)
-        .reshape(share, 2 * width)
-    )
     hidden_rows = (
         lax.all_to_all(grad_hidden.reshape(devices, rows, 2, share), "seq", 0, 0, tiled=True)
         .transpose(1, 2, 0, 3)
@@ -286,9 +287,21 @@
         "fe,ne->fn", hidden_rows, w_in_all, preferred_element_type=jnp.float32
     )
     ln_hat, rstd_ln = norm(frames)
-    grad_ln_gain = lax.psum_scatter(
-        jnp.sum(grad_ln * ln_hat, axis=0) * grad_scale, "seq", scatter_dimension=0, tiled=True
-    )
+    gain_part = jnp.sum(grad_ln * ln_hat, axis=0) * grad_scale
+    packed = lax.all_to_all(
+        jnp.concatenate(
+            [in_cols.reshape(devices, share * 2 * share), gain_part.reshape(devices, share)],
+            axis=1,
+        ),
+        "seq", 0, 0, tiled=True,
+    )
+    grad_w_in = (
+        packed[:, : share * 2 * share]
+        .reshape(devices, share, 2, share)
+        .transpose(1, 2, 0, 3)
+        .reshape(share, 2 * width)
+    )
+    grad_ln_gain = jnp.sum(packed[:, share * 2 * share :], axis=0)
     grad_hat = grad_ln * gains
     grad_input = rstd_ln * (
         grad_hat

time: 270 us -> 258 us (0.956)
  blocking collectives: 93.8 us -> 13.7 us
  waiting for transfers between devices: 72.4 us -> 143 us
  starting transfers between devices: 22.1 us -> 27.9 us
  local copies, waits for them, and re-layouts: 16.7 us -> 11.5 us
    unnamed x2 -> x0, blocking collectives: 93.8 us -> none
    all_gather x1, waiting for transfers between devices: 0.02 us -> 53.9 us  [channel_local(): frames_all = lax.all_gather(frames, 'seq', axis=0, tiled=True)]
    all_to_all x2, waiting for transfers between devices: 14.6 us -> 52.6 us  [the longest x1 42.5 us: spread(): return lax.all_to_all(copies, 'seq', 0, 0, tiled=True)]
    all_gather x1 -> x0, waiting for transfers between devices: 31.8 us -> none  [channel_local(): w_in_all = lax.all_gather(w_in, 'seq', axis=0, tiled=True)]
    all_to_all x0 -> x1, blocking collectives: none -> 13.7 us  [spread(): return lax.all_to_all(copies, 'seq', 0, 0, tiled=True)]
    all_to_all x1, starting transfers between devices: 5.06 us -> 15.1 us  [channel_local(): lax.all_to_all(grad_hidden.reshape(devices, rows, 2, share), 'seq', 0, 0,...]
    unnamed x88 -> x19, local copies, waits for them, and re-layouts: 6.06 us -> 1 us
    all_to_all x1, waiting for transfers between devices: 0.01 us -> 4.86 us  [channel_local(): lax.all_to_all(activation.reshape(devices, rows, share), 'seq', 0, 0, til...]
  transfers between devices with their start and end apart: 8 -> 7, of which waited for: 4 -> 6; matrix products, arithmetic and copies ran while one was open for 22% -> 21% of each run, Pallas kernels for 0% -> 0%
where the time goes in v2:
time: 258 us; the launch traced here: 257 us
  waiting for transfers between devices  143 us (55%)
  starting transfers between devices  27.9 us (11%)
  other arithmetic  27.6 us (11%)
  matrix products  19.2 us (7%)
  between operations  14.1 us (5%)
  blocking collectives  13.7 us (5%)
  local copies, waits for them, and re-layouts  11.5 us (4%)
    all_gather x1, waiting for transfers between devices, channel_local(): frames_all = lax.all_gather(frames, 'seq', axis=0, tiled=True)  53.9 us
    all_to_all x1, waiting for transfers between devices, spread(): return lax.all_to_all(copies, 'seq', 0, 0, tiled=True)  42.5 us
    all_gather x1, waiting for transfers between devices, channel_local(): grad_all = lax.all_gather(out_grad, 'seq', axis=0, tiled=True)  20.9 us
    all_to_all x1, starting transfers between devices, channel_local(): lax.all_to_all(grad_hidden.reshape(devices, rows, 2, share), 'seq', 0, 0,...  15.1 us
    all_to_all x1, blocking collectives, spread(): return lax.all_to_all(copies, 'seq', 0, 0, tiled=True)  13.7 us
    all_to_all x1, waiting for transfers between devices, channel_local(): lax.all_to_all(jnp.concatenate([in_cols.reshape(devices, share * 2 * shar...  10.1 us
    all_to_all x1, waiting for transfers between devices, channel_local(): lax.all_to_all(grad_hidden.reshape(devices, rows, 2, share), 'seq', 0, 0,...  8.48 us
    mul x1, other arithmetic, channel_local(): grad_glu * right_gate  5.25 us
  transfers between devices with their start and end apart: 7, of which 6 were waited for; matrix products, arithmetic and copies ran while one was open for 21% of the time, Pallas kernels for 0%

profile of v2, /device:TPU:0, one launch (start us, length us, event | category | flops | bytes accessed | tf_op | source)
XLA Modules:
  0.0 256.8 jit_solution(2916747010213837527)
XLA Ops:
  7.2 0.7 all-gather.4.cloned.1.call-update
  7.9 0.7 all-gather.8.cloned.1.call-update
  8.7 0.7 convert_element_type.262
  9.3 0.7 pad_maximum_fusion.1
  10.1 13.7 %all_to_all.36 = f32[16,1,192]{2,1,0:T(1,128)S(1)} all-to-all(f32[16,1,192]{2,1,0:T(1,128)S(1)} %broadcast_in_dim.4), channel_id=1, replica_groups=mesh['mix'=2,'seq'=16] {'seq'}, dimensions={0} | all-to-all | bytes 24576 | tf_op jit(solution)/shard_map/all_to_all | solution.py:176
  23.8 3.4 %broadcast_in_dim.5 = bf16[16,64,2048]{2,1,0:T(8,128)(2,1)} broadcast(bf16[64,2048]{1,0:T(8,128)(2,1)} %param.13), dimensions={1,2} | broadcast | bytes 4456448 | tf_op jit(solution)/shard_map/broadcast_in_dim | solution.py:175
  27.2 4.7 %all-to-all-start.1 = ((bf16[16,64,2048]{2,1,0:T(8,128)(2,1)}), bf16[16,64,2048]{2,1,0:T(8,128)(2,1)}, u32[]{:S(2)}, u32[]{:S(2)}) async-start(bf16[16,64,2048]{2,1,0:T(8,128)(2,1)} %broadcast_in_dim.5), calls=%async_computation.1 | async-start | bytes 8388608 | tf_op jit(solution)/shard_map/all_to_all | solution.py:176
  31.9 0.7 all-gather.6.cloned.1.call-update
  33.4 53.9 %all-gather.4.cloned.1.call-done = bf16[2048,1024]{1,0:T(8,128)(2,1)} async-done(((bf16[128,1024]{1,0:T(8,128)(2,1)}), bf16[2048,1024]{1,0:T(8,128)(2,1)}) %all-gather.4.cloned.1.call-update) | async-done | bytes 4194320 | tf_op jit(solution)/shard_map/all_gather | solution.py:182
  87.4 3.0 %convert_reduce_fusion = f32[2048]{0:T(1024)S(1)} fusion(bf16[2048,1024]{1,0:T(8,128)(2,1)} %all-gather.4.cloned.1.call-done), kind=kLoop, calls=%fused_computation.1 | loop fusion | flops 4192256 | bytes 4202496 | tf_op jit(solution)/shard_map/reduce_sum | solution.py:198
  90.4 0.5 copy-done
  90.8 1.4 fusion.2
  92.2 42.5 %all-to-all-done.1 = bf16[16,64,2048]{2,1,0:T(8,128)(2,1)} async-done(((bf16[16,64,2048]{2,1,0:T(8,128)(2,1)}), bf16[16,64,2048]{2,1,0:T(8,128)(2,1)}, u32[]{:S(2)}, u32[]{:S(2)}) %all-to-all-start.1) | async-done | bytes 4194336 | tf_op jit(solution)/shard_map/all_to_all | solution.py:176
  134.8 1.2 constant_dynamic-slice_fusion.1
  136.0 3.5 %fusion.4 = bf16[2048,1024]{1,0:T(8,128)(2,1)S(1)} fusion(bf16[2048,1024]{1,0:T(8,128)(2,1)} %all-gather.4.cloned.1.call-done, f32[1024]{0:T(1024)S(1)} %mul.651, f32[2048]{0:T(1024)S(1)} %add_rsqrt_fusion, f32[2048]{0:T(1024)S(1)} %broadcast_multiply_fusion.1), kind=kLoop, calls=%fused_computation.6 | loop fusion | flops 10485760 | bytes 8409088 | tf_op jit(solution)/shard_map/convert_element_type | solution.py:204
  139.5 1.6 fusion.184
  141.1 0.3 copy-done.1
  141.6 4.2 %fusion.256 = (f32[64]{0:T(128)S(1)}, f32[2048,64]{0,1:T(8,128)S(1)}) fusion(f32[2048]{0:T(1024)S(1)} %get-tuple-element.111, f32[64]{0:T(128)S(1)} %get-tuple-element.80, f32[2048]{0:T(1024)S(1)} %get-tuple-element.83, f32[64]{0:T(128)S(1)} %get-tuple-element.81, f32[2048]{0:T(1024)S(1)} %get-tuple-element.84, f32[64]{0:T(128)S(1)} %get-tuple-element.52, ...), kind=kLoop, calls=%fused_computation.436 | loop fusion | flops 16121792 | bytes 1040384 | tf_op jit(solution)/shard_map/reduce_sum | solution.py:226
  146.1 20.9 %all-gather.8.cloned.1.call-done = bf16[2048,1024]{1,0:T(8,128)(2,1)} async-done(((bf16[128,1024]{1,0:T(8,128)(2,1)}), bf16[2048,1024]{1,0:T(8,128)(2,1)}) %all-gather.8.cloned.1.call-update) | async-done | bytes 4194320 | tf_op jit(solution)/shard_map/all_gather | solution.py:184
  166.9 3.7 %fusion.255 = (f32[64]{0:T(128)S(1)}, f32[64]{0:T(128)S(1)}, bf16[2048,64]{0,1:T(8,128)(2,1)S(1)}, f32[2048,64]{0,1:T(8,128)S(1)}) fusion(f32[64]{0:T(128)S(1)} %get-tuple-element.115, f32[2048,64]{0,1:T(8,128)S(1)} %get-tuple-element.47, f32[64]{0:T(128)S(1)} %broadcast_multiply_fusion.9, f32[64]{0:T(128)S(1)} %copy-done.7, f32[64]{0:T(128)S(1)} %copy-done.6, ...), kind=kOutput, calls=%fused_computation.435 | convolution fusion | flops 270663552 | bytes 5637632 | tf_op jit(solution)/shard_map/fe,ne->fn/dot_general | solution.py:246
  170.7 0.5 broadcast_multiply_fusion.3
  171.2 1.0 fusion.139
  172.2 0.8 fusion.115
  173.0 5.3 %fusion.254 = (bf16[2048,64]{0,1:T(8,128)(2,1)S(1)}, f32[2048,64]{0,1:T(8,128)S(1)}) fusion(f32[2048,128]{0,1:T(8,128)S(1)} %fusion.184, f32[2048]{0:T(1024)S(1)} %get-tuple-element.82, f32[64]{0:T(128)S(1)} %get-tuple-element.80, f32[2048]{0:T(1024)S(1)} %get-tuple-element.100, f32[64]{0:T(128)S(1)} %get-tuple-element.81, f32[2048]{0:T(1024)S(1)} %get-tuple-element.110, ...), kind=kLoop, calls=%fused_computation.434 | loop fusion | flops 12582912 | bytes 2088704 | tf_op jit(solution)/shard_map/mul | solution.py:274
  178.7 0.9 copy.22
  179.6 15.1 %all-to-all-start.3 = ((bf16[16,128,2,64]{1,3,2,0:T(8,128)(2,1)}), bf16[16,128,2,64]{1,3,2,0:T(8,128)(2,1)S(1)}, u32[]{:S(2)}, u32[]{:S(2)}) async-start(bf16[16,128,2,64]{1,3,2,0:T(8,128)(2,1)} %copy.22), calls=%async_computation.3 | async-start | bytes 1048576 | tf_op jit(solution)/shard_map/all_to_all | solution.py:282
  194.7 0.8 fusion.81
  195.5 0.7 fusion.97
  196.3 3.5 %convolution_multiply_fusion.1 = f32[1024,128]{1,0:T(8,128)S(1)} fusion(bf16[2048,1024]{1,0:T(8,128)(2,1)} %copy-done.1, bf16[2048,64]{0,1:T(8,128)(2,1)S(1)} %subtract_multiply_fusion, bf16[2048,64]{0,1:T(8,128)(2,1)S(1)} %get-tuple-element.44), kind=kOutput, calls=%fused_computation.9 | convolution fusion | flops 538050560 | bytes 5242880 | tf_op jit(solution)/shard_map/fa,fb->ab/dot_general | solution.py:278
  199.8 0.8 fusion.63
  200.7 0.2 fusion.45
  201.1 0.6 broadcast_multiply_fusion
  201.7 0.8 copy_bitcast_fusion.1
  202.4 3.8 %convolution_multiply_fusion.2 = f32[64,1024]{1,0:T(8,128)} fusion(bf16[2048,64]{0,1:T(8,128)(2,1)S(1)} %get-tuple-element.50, bf16[2048,1024]{1,0:T(8,128)(2,1)} %all-gather.8.cloned.1.call-done), kind=kOutput, calls=%fused_computation.12 | convolution fusion | flops 268500992 | bytes 4718592 | tf_op jit(solution)/shard_map/fa,fb->ab/dot_general | solution.py:243
  206.2 8.5 %all-to-all-done.3 = bf16[16,128,2,64]{1,3,2,0:T(8,128)(2,1)S(1)} async-done(((bf16[16,128,2,64]{1,3,2,0:T(8,128)(2,1)}), bf16[16,128,2,64]{1,3,2,0:T(8,128)(2,1)S(1)}, u32[]{:S(2)}, u32[]{:S(2)}) %all-to-all-start.3) | async-done | bytes 524320 | tf_op jit(solution)/shard_map/all_to_all | solution.py:282
  214.7 4.2 %all-to-all-start.2 = ((bf16[16,128,64]{1,2,0:T(8,128)(2,1)}), bf16[16,128,64]{1,2,0:T(8,128)(2,1)S(1)}, u32[]{:S(2)}, u32[]{:S(2)}) async-start(bf16[16,128,64]{1,2,0:T(8,128)(2,1)} %copy_bitcast_fusion.1), calls=%async_computation.2 | async-start | bytes 524288 | tf_op jit(solution)/shard_map/all_to_all | solution.py:235
  219.0 3.8 %fusion.17 = (f32[1024]{0:T(1024)S(1)}, f32[128]{0:T(128)S(1)}, f32[128]{0:T(128)S(1)}, f32[128,1024]{1,0:T(8,128)S(1)}) fusion(bf16[128,1024]{1,0:T(8,128)(2,1)S(1)} %copy-done.2, f32[128]{0:T(128)S(1)} %add_rsqrt_fusion.1, f32[128]{0:T(128)S(1)} %broadcast_multiply_fusion.7, f32[1024]{0:T(1024)S(1)} %mul.651, bf16[128,2048]{0,1:T(8,128)(2,1)S(1)} %bitcast.135, ...), kind=kOutput, calls=%fused_computation.90 | convolution fusion | flops 538049280 | bytes 5515264 | tf_op jit(solution)/shard_map/fe,ne->fn/dot_general | solution.py:286
  223.0 1.2 all_to_all.28
  224.1 4.9 %all-to-all-done.2 = bf16[16,128,64]{1,2,0:T(8,128)(2,1)S(1)} async-done(((bf16[16,128,64]{1,2,0:T(8,128)(2,1)}), bf16[16,128,64]{1,2,0:T(8,128)(2,1)S(1)}, u32[]{:S(2)}, u32[]{:S(2)}) %all-to-all-start.2) | async-done | bytes 262176 | tf_op jit(solution)/shard_map/all_to_all | solution.py:235
  229.0 3.8 %all-to-all-start.4 = ((f32[16,1,8256]{2,1,0:T(1,128)}), f32[16,1,8256]{2,1,0:T(1,128)S(1)}, u32[]{:S(2)}, u32[]{:S(2)}) async-start(f32[16,1,8256]{2,1,0:T(1,128)} %all_to_all.28), calls=%async_computation.4 | async-start | bytes 1064960 | tf_op jit(solution)/shard_map/all_to_all | solution.py:291
  232.8 0.5 broadcast_multiply_fusion.4
  233.3 2.8 %fusion.6 = bf16[128,1024]{1,0:T(8,128)(2,1)} fusion(bf16[128,1024]{0,1:T(8,128)(2,1)S(1)} %bitcast.137, bf16[1024,1024]{1,0:T(8,128)(2,1)} %all-gather.6.cloned.1.call-done, bf16[128,1024]{1,0:T(8,128)(2,1)S(1)} %copy-done.2), kind=kOutput, calls=%fused_computation.11 | convolution fusion | flops 268828672 | bytes 2883584 | tf_op jit(solution)/shard_map/dot_general | solution.py:239
  236.1 1.0 fusion.16
  237.1 10.1 %all-to-all-done.4 = f32[16,1,8256]{2,1,0:T(1,128)S(1)} async-done(((f32[16,1,8256]{2,1,0:T(1,128)}), f32[16,1,8256]{2,1,0:T(1,128)S(1)}, u32[]{:S(2)}, u32[]{:S(2)}) %all-to-all-start.4) | async-done | bytes 528416 | tf_op jit(solution)/shard_map/all_to_all | solution.py:291
  247.2 0.5 slice_reduce_fusion
  247.7 0.8 reshape.140
  248.5 0.6 copy.24
  249.1 1.2 reshape.141
  (49 shorter events, 2.0 us)
Async XLA Ops:
  7.2 80.2 %all-gather.4.cloned.1.call-start = ((), (), s32[]{:S(2)}) async-start(), calls=%async_computation.5 | async-start | bytes 4456448 | tf_op jit(solution)/shard_map/all_gather | solution.py:182
  7.9 159.0 %all-gather.8.cloned.1.call-start = ((), (), s32[]{:S(2)}) async-start(), calls=%async_computation.7 | async-start | bytes 4456448 | tf_op jit(solution)/shard_map/all_gather | solution.py:184
  27.2 5.4 %copy-start.2 = (bf16[128,1024]{1,0:T(8,128)(2,1)S(1)}, bf16[128,1024]{1,0:T(8,128)(2,1)}, u32[]{:S(2)}) copy-start(bf16[128,1024]{1,0:T(8,128)(2,1)} %param.9) | copy-start | bytes 786436
  27.2 5.8 %copy-start.5 = (f32[31,64]{1,0:T(8,128)S(1)}, f32[31,64]{1,0:T(8,128)}, u32[]{:S(2)}) copy-start(f32[31,64]{1,0:T(8,128)} %param.14) | copy-start | bytes 23812
  27.2 107.5 %all-to-all-start.1 = ((bf16[16,64,2048]{2,1,0:T(8,128)(2,1)}), bf16[16,64,2048]{2,1,0:T(8,128)(2,1)}, u32[]{:S(2)}, u32[]{:S(2)}) async-start(bf16[16,64,2048]{2,1,0:T(8,128)(2,1)} %broadcast_in_dim.5), calls=%async_computation.1 | async-start | bytes 8388608 | tf_op jit(solution)/shard_map/all_to_all | solution.py:176
  31.9 201.4 %all-gather.6.cloned.1.call-start = ((), (), s32[]{:S(2)}) async-start(), calls=%async_computation.6 | async-start | bytes 2228224 | tf_op jit(solution)/shard_map/all_gather | solution.py:183
  87.4 3.4 %copy-start = (bf16[2048,1024]{1,0:T(8,128)(2,1)S(1)}, bf16[2048,1024]{1,0:T(8,128)(2,1)}, u32[]{:S(2)}) copy-start(bf16[2048,1024]{1,0:T(8,128)(2,1)} %all-gather.4.cloned.1.call-done) | copy-start | bytes 12582916
  139.5 2.0 copy-start.1
  139.5 6.5 %copy-start.6 = (f32[64]{0:T(128)S(1)}, f32[64]{0:T(128)}, u32[]{:S(2)}) copy-start(f32[64]{0:T(128)} %param.15) | copy-start | bytes 772
  139.5 27.4 %copy-start.4 = (bf16[64,1024]{1,0:T(8,128)(2,1)S(1)}, bf16[64,1024]{1,0:T(8,128)(2,1)}, u32[]{:S(2)}) copy-start(bf16[64,1024]{1,0:T(8,128)(2,1)} %param.17) | copy-start | bytes 393220
  139.5 27.4 %copy-start.7 = (f32[64]{0:T(128)S(1)}, f32[64]{0:T(128)}, u32[]{:S(2)}) copy-start(f32[64]{0:T(128)} %param.16) | copy-start | bytes 772
  179.6 35.1 %all-to-all-start.3 = ((bf16[16,128,2,64]{1,3,2,0:T(8,128)(2,1)}), bf16[16,128,2,64]{1,3,2,0:T(8,128)(2,1)S(1)}, u32[]{:S(2)}, u32[]{:S(2)}) async-start(bf16[16,128,2,64]{1,3,2,0:T(8,128)(2,1)} %copy.22), calls=%async_computation.3 | async-start | bytes 1048576 | tf_op jit(solution)/shard_map/all_to_all | solution.py:282
  214.7 14.3 %all-to-all-start.2 = ((bf16[16,128,64]{1,2,0:T(8,128)(2,1)}), bf16[16,128,64]{1,2,0:T(8,128)(2,1)S(1)}, u32[]{:S(2)}, u32[]{:S(2)}) async-start(bf16[16,128,64]{1,2,0:T(8,128)(2,1)} %copy_bitcast_fusion.1), calls=%async_computation.2 | async-start | bytes 524288 | tf_op jit(solution)/shard_map/all_to_all | solution.py:235
  222.8 13.2 %copy-start.3 = (bf16[128,1024]{1,0:T(8,128)(2,1)S(1)}, bf16[128,1024]{1,0:T(8,128)(2,1)}, u32[]{:S(2)}) copy-start(bf16[128,1024]{1,0:T(8,128)(2,1)} %param.11) | copy-start | bytes 786436
  229.0 18.2 %all-to-all-start.4 = ((f32[16,1,8256]{2,1,0:T(1,128)}), f32[16,1,8256]{2,1,0:T(1,128)S(1)}, u32[]{:S(2)}, u32[]{:S(2)}) async-start(f32[16,1,8256]{2,1,0:T(1,128)} %all_to_all.28), calls=%async_computation.4 | async-start | bytes 1064960 | tf_op jit(solution)/shard_map/all_to_all | solution.py:291
Sparse Core Ops, SparseCore 0:
  10.2 77.1 all-gather.3
  89.5 77.3 all-gather.7
  169.1 46.4 all-gather.5

commit v3 on v2

--- a/solution.py
+++ b/solution.py
@@ -161,30 +161,39 @@
     )
 
 
+SEQ = ("chip", "core")
+
+
+def gather_rows(block):
+    chips = lax.all_gather(block, "chip", axis=0)
+    both = lax.all_gather(chips, "core", axis=0)
+    return both.transpose(1, 0, *range(2, both.ndim)).reshape(-1, *block.shape[1:])
+
+
 def channel_local(frames, segment_ids, out_grad, ln_gain, w_in, dw_kernel, bn_gain, bn_bias, w_out):
     rows = frames.shape[0]
     width = frames.shape[1]
     taps = dw_kernel.shape[0]
     margin = taps // 2
-    devices = lax.axis_size("seq")
+    devices = lax.axis_size("chip") * lax.axis_size("core")
     stream = rows * devices
     grad_scale = 1.0 / math.sqrt(stream)
     share = width // devices
 
     def spread(block):
         copies = jnp.broadcast_to(block[None], (devices,) + block.shape)
-        return lax.all_to_all(copies, "seq", 0, 0, tiled=True)
+        return lax.all_to_all(copies, SEQ, 0, 0, tiled=True)
 
     small = spread(jnp.concatenate([ln_gain, segment_ids.astype(jnp.float32)]))
     gains = small[:, :share].reshape(width)
     all_ids = small[:, share:].reshape(stream).astype(jnp.int32)
 
-    frames_all = lax.all_gather(frames, "seq", axis=0, tiled=True)
-    w_out_all = lax.all_gather(w_out, "seq", axis=0, tiled=True)
-    grad_all = lax.all_gather(out_grad, "seq", axis=0, tiled=True)
-    w_in_all = spread(w_in).reshape(width, 2 * width)
-
-    first_channel = lax.axis_index("seq") * share
+    frames_all = gather_rows(frames)
+    w_out_all = gather_rows(w_out)
+    grad_all = gather_rows(out_grad)
+    w_in_all = gather_rows(w_in)
+
+    first_channel = (lax.axis_index("chip") * lax.axis_size("core") + lax.axis_index("core")) * share
     w_in_cols = jnp.concatenate(
         [
             lax.dynamic_slice_in_dim(w_in_all, first_channel, share, 1),
@@ -232,7 +241,7 @@
     activation = (zed * zed_gate).astype(jnp.bfloat16)
 
     act_rows = (
-        lax.all_to_all(activation.reshape(devices, rows, share), "seq", 0, 0, tiled=True)
+        lax.all_to_all(activation.reshape(devices, rows, share), SEQ, 0, 0, tiled=True)
         .transpose(1, 0, 2)
         .reshape(rows, width)
     )
@@ -279,7 +288,7 @@
         * grad_scale
     )
     hidden_rows = (
-        lax.all_to_all(grad_hidden.reshape(devices, rows, 2, share), "seq", 0, 0, tiled=True)
+        lax.all_to_all(grad_hidden.reshape(devices, rows, 2, share), SEQ, 0, 0, tiled=True)
         .transpose(1, 2, 0, 3)
         .reshape(rows, 2 * width)
     )
@@ -293,7 +302,7 @@
             [in_cols.reshape(devices, share * 2 * share), gain_part.reshape(devices, share)],
             axis=1,
         ),
-        "seq", 0, 0, tiled=True,
+        SEQ, 0, 0, tiled=True,
     )
     grad_w_in = (
         packed[:, : share * 2 * share]
@@ -323,30 +332,40 @@
 
 def solution(mesh):
     devices = mesh.shape["seq"]
-    body = channel_local if devices <= 16 else local
+    if devices <= 16:
+        cores = 2
+        grid = mesh.devices.reshape(mesh.shape["mix"], devices // cores, cores)
+        mesh = jax.sharding.Mesh(grid, ("mix", "chip", "core"))
+        rows = ("mix", "chip", "core")
+        chans = ("chip", "core")
+        body = channel_local
+    else:
+        rows = ("mix", "seq")
+        chans = "seq"
+        body = local
     return jax.shard_map(
         body,
         mesh=mesh,
         in_specs=(
-            P(("mix", "seq"), None),
-            P(("mix", "seq")),
-            P(("mix", "seq"), None),
-            P(("mix", "seq")),
-            P(("mix", "seq"), None),
-            P("mix", "seq"),
-            P(("mix", "seq")),
-            P(("mix", "seq")),
-            P(("mix", "seq"), None),
+            P(rows, None),
+            P(rows),
+            P(rows, None),
+            P(rows),
+            P(rows, None),
+            P("mix", chans),
+            P(rows),
+            P(rows),
+            P(rows, None),
         ),
         out_specs=(
-            P(("mix", "seq"), None),
-            P(("mix", "seq"), None),
-            P(("mix", "seq"), None),
-            P(("mix", "seq"), None),
-            P("mix", "seq"),
-            P(("mix", "seq")),
-            P(("mix", "seq")),
-            P(("mix", "seq")),
+            P(rows, None),
+            P(rows, None),
+            P(rows, None),
+            P(rows, None),
+            P("mix", chans),
+            P(rows),
+            P(rows),
+            P(rows),
         ),
         check_vma=False,
     )

time: 258 us -> 345 us (1.34)
  waiting for transfers between devices: 143 us -> 243 us
  local copies, waits for them, and re-layouts: 11.5 us -> 25.9 us
  blocking collectives: 13.7 us -> 0 us
  starting transfers between devices: 27.9 us -> 17.7 us
  matrix products: 19.2 us -> 14.3 us
    all_gather x3 -> x8, waiting for transfers between devices: 74.8 us -> 214 us  [the longest x4 182 us: gather_rows(): chips = lax.all_gather(block, 'chip', axis=0)]
    all_to_all x3, waiting for transfers between devices: 55.9 us -> 16.1 us  [the longest x1 7.2 us: channel_local(): lax.all_to_all(grad_hidden.reshape(devices, rows, 2, share), SEQ, 0, 0, t...]
    all_to_all x1 -> x0, blocking collectives: 13.7 us -> none  [spread(): return lax.all_to_all(copies, 'seq', 0, 0, tiled=True)]
    all_to_all x3, starting transfers between devices: 24 us -> 13.6 us  [the longest x1 5.88 us: channel_local(): lax.all_to_all(grad_hidden.reshape(devices, rows, 2, share), SEQ, 0, 0, t...]
    transpose x0 -> x3, local copies, waits for them, and re-layouts: none -> 8.47 us  [gather_rows(): both.transpose(1, 0, *range(2, both.ndim)).reshape(-1, *block.shape[1:])]
    unnamed x19 -> x81, local copies, waits for them, and re-layouts: 1 us -> 5.88 us
    convert_element_type x0 -> x1, local copies, waits for them, and re-layouts: none -> 4.1 us  [norm(): block_float = block.astype(jnp.float32)]
  transfers between devices with their start and end apart: 7 -> 12, of which waited for: 6 -> 12; matrix products, arithmetic and copies ran while one was open for 21% -> 12% of each run, Pallas kernels for 0% -> 0%
where the time goes in v3:
time: 345 us; the launch traced here: 344 us
  waiting for transfers between devices  243 us (70%)
  other arithmetic  28.7 us (8%)
  local copies, waits for them, and re-layouts  25.9 us (8%)
  starting transfers between devices  17.7 us (5%)
  between operations  14.9 us (4%)
  matrix products  14.3 us (4%)
    all_gather x4, waiting for transfers between devices, gather_rows(): chips = lax.all_gather(block, 'chip', axis=0)  182 us
    all_gather x4, waiting for transfers between devices, gather_rows(): both = lax.all_gather(chips, 'core', axis=0)  32.5 us
    all_to_all x1, waiting for transfers between devices, channel_local(): lax.all_to_all(jnp.concatenate([in_cols.reshape(devices, share * 2 * shar...  9.71 us
    transpose x3, local copies, waits for them, and re-layouts, gather_rows(): both.transpose(1, 0, *range(2, both.ndim)).reshape(-1, *block.shape[1:])  8.47 us
    all_to_all x1, waiting for transfers between devices, channel_local(): lax.all_to_all(grad_hidden.reshape(devices, rows, 2, share), SEQ, 0, 0, t...  7.2 us
  transfers between devices with their start and end apart: 12, of which 12 were waited for; matrix products, arithmetic and copies ran while one was open for 12% of the time, Pallas kernels for 0%

profile of v3, /device:TPU:0, one launch (start us, length us, event | category | flops | bytes accessed | tf_op | source)
XLA Modules:
  0.0 344.2 jit_solution(3297179027154706061)
XLA Ops:
  7.3 0.7 all-gather.25.cloned.1.call-update
  8.0 0.7 all-gather.17.cloned.1.call-update
  10.0 43.0 %all-gather.25.cloned.1.call-done = bf16[512,1024]{1,0:T(8,128)(2,1)} async-done(((bf16[64,1024]{1,0:T(8,128)(2,1)}), bf16[512,1024]{1,0:T(8,128)(2,1)}) %all-gather.25.cloned.1.call-update) | async-done | bytes 1048592 | tf_op jit(solution)/shard_map/all_gather | solution.py:168
  53.1 50.1 %all-gather.17.cloned.1.call-done = bf16[1024,1024]{1,0:T(8,128)(2,1)} async-done(((bf16[128,1024]{1,0:T(8,128)(2,1)}), bf16[1024,1024]{1,0:T(8,128)(2,1)}) %all-gather.17.cloned.1.call-update) | async-done | bytes 2097168 | tf_op jit(solution)/shard_map/all_gather | solution.py:168
  103.3 49.9 %all-gather.21.cloned.1.call-done = bf16[512,2048]{1,0:T(8,128)(2,1)} async-done(((bf16[64,2048]{1,0:T(8,128)(2,1)}), bf16[512,2048]{1,0:T(8,128)(2,1)}) %all-gather.21.cloned.1.call-update) | async-done | bytes 2097168 | tf_op jit(solution)/shard_map/all_gather | solution.py:168
  153.9 3.5 %all-to-all-start = ((f32[16,1,192]{2,1,0:T(1,128)}), f32[16,1,192]{2,1,0:T(1,128)S(1)}, u32[]{:S(2)}, u32[]{:S(2)}) async-start(f32[16,1,192]{2,1,0:T(1,128)} %broadcast_in_dim.2), calls=%async_computation | async-start | bytes 32768 | tf_op jit(solution)/shard_map/all_to_all | solution.py:185
  158.7 5.2 %all-to-all-done = f32[16,1,192]{2,1,0:T(1,128)S(1)} async-done(((f32[16,1,192]{2,1,0:T(1,128)}), f32[16,1,192]{2,1,0:T(1,128)S(1)}, u32[]{:S(2)}, u32[]{:S(2)}) %all-to-all-start) | async-done | bytes 12320 | tf_op jit(solution)/shard_map/all_to_all | solution.py:185
  164.4 38.6 %all-gather.29.cloned.1.call-done = bf16[1024,1024]{1,0:T(8,128)(2,1)} async-done(((bf16[128,1024]{1,0:T(8,128)(2,1)}), bf16[1024,1024]{1,0:T(8,128)(2,1)}) %all-gather.29.cloned.1.call-update) | async-done | bytes 2097168 | tf_op jit(solution)/shard_map/all_gather | solution.py:168
  203.0 10.5 %all-gather.27.cloned.1.call-done = bf16[16,64,1024]{2,1,0:T(8,128)(2,1)} async-done(((bf16[8,64,1024]{2,1,0:T(8,128)(2,1)}), bf16[16,64,1024]{2,1,0:T(8,128)(2,1)}) %all-gather.27.cloned.1.call-update) | async-done | bytes 2097168 | tf_op jit(solution)/shard_map/all_gather | solution.py:169
  213.5 3.2 copy.34
  216.6 13.1 %all-gather.19.cloned.1.call-done = bf16[16,128,1024]{2,1,0:T(8,128)(2,1)} async-done(((bf16[8,128,1024]{2,1,0:T(8,128)(2,1)}), bf16[16,128,1024]{2,1,0:T(8,128)(2,1)}) %all-gather.19.cloned.1.call-update) | async-done | bytes 4194320 | tf_op jit(solution)/shard_map/all_gather | solution.py:169
  229.8 3.2 convert_bitcast_fusion
  233.0 4.1 %copy.29 = f32[8,2,128,1024]{3,2,1,0:T(8,128)} copy(f32[8,2,128,1024]{3,2,0,1:T(8,128)S(1)} %convert_bitcast_fusion) | data formatting | bytes 16777216 | tf_op jit(solution)/shard_map/convert_element_type | solution.py:206
  237.7 1.6 multiply_reduce_fusion
  239.4 6.8 %all-gather.23.cloned.1.call-done = bf16[16,64,2048]{2,1,0:T(8,128)(2,1)} async-done(((bf16[8,64,2048]{2,1,0:T(8,128)(2,1)}), bf16[16,64,2048]{2,1,0:T(8,128)(2,1)}) %all-gather.23.cloned.1.call-update) | async-done | bytes 4194320 | tf_op jit(solution)/shard_map/all_gather | solution.py:169
  246.2 2.7 copy.32
  249.1 3.2 copy-done.3
  252.3 1.7 fusion.2
  254.1 1.6 fusion.183
  256.2 4.2 %fusion.255 = (f32[64]{0:T(128)S(1)}, f32[2048,64]{0,1:T(8,128)S(1)}) fusion(f32[2048]{0:T(1024)S(1)} %get-tuple-element.111, f32[64]{0:T(128)S(1)} %get-tuple-element.80, f32[2048]{0:T(1024)S(1)} %get-tuple-element.83, f32[64]{0:T(128)S(1)} %get-tuple-element.81, f32[2048]{0:T(1024)S(1)} %get-tuple-element.84, f32[64]{0:T(128)S(1)} %get-tuple-element.52, ...), kind=kLoop, calls=%fused_computation.436 | loop fusion | flops 16121792 | bytes 1040384 | tf_op jit(solution)/shard_map/reduce_sum | solution.py:235
  260.4 2.1 all-gather.31.cloned.1.call-done
  262.6 2.7 copy.35
  265.5 1.7 copy-done.5
  267.2 1.6 fusion.254
  269.3 1.6 fusion.138
  270.9 5.3 %fusion.253 = (bf16[2048,64]{0,1:T(8,128)(2,1)S(1)}, f32[2048,64]{0,1:T(8,128)S(1)}) fusion(f32[2048,128]{0,1:T(8,128)S(1)} %fusion.183, f32[2048]{0:T(1024)S(1)} %get-tuple-element.82, f32[64]{0:T(128)S(1)} %get-tuple-element.80, f32[2048]{0:T(1024)S(1)} %get-tuple-element.100, f32[64]{0:T(128)S(1)} %get-tuple-element.81, f32[2048]{0:T(1024)S(1)} %get-tuple-element.110, ...), kind=kLoop, calls=%fused_computation.434 | loop fusion | flops 12582912 | bytes 2088704 | tf_op jit(solution)/shard_map/mul | solution.py:283
  276.5 1.3 convolution_multiply_fusion.1
  277.9 0.8 fusion.62
  278.8 0.8 fusion.80
  279.6 0.7 fusion.96
  280.5 0.9 copy.36
  281.4 5.9 %all-to-all-start.2 = ((bf16[16,128,2,64]{1,3,2,0:T(8,128)(2,1)}), bf16[16,128,2,64]{1,3,2,0:T(8,128)(2,1)S(1)}, u32[]{:S(2)}, u32[]{:S(2)}) async-start(bf16[16,128,2,64]{1,3,2,0:T(8,128)(2,1)} %copy.36), calls=%async_computation.2 | async-start | bytes 1048576 | tf_op jit(solution)/shard_map/all_to_all | solution.py:291
  287.3 0.8 fusion.114
  288.2 0.9 reshape.169
  290.1 0.8 copy_bitcast_fusion.1
  290.8 3.7 %convolution_multiply_fusion.2 = f32[64,1024]{1,0:T(8,128)} fusion(bf16[2048,64]{0,1:T(8,128)(2,1)S(1)} %get-tuple-element.50, bf16[2048,1024]{1,0:T(8,128)(2,1)} %bitcast.171), kind=kOutput, calls=%fused_computation.12 | convolution fusion | flops 268500992 | bytes 4718592 | tf_op jit(solution)/shard_map/fa,fb->ab/dot_general | solution.py:252
  294.6 7.2 %all-to-all-done.2 = bf16[16,128,2,64]{1,3,2,0:T(8,128)(2,1)S(1)} async-done(((bf16[16,128,2,64]{1,3,2,0:T(8,128)(2,1)}), bf16[16,128,2,64]{1,3,2,0:T(8,128)(2,1)S(1)}, u32[]{:S(2)}, u32[]{:S(2)}) %all-to-all-start.2) | async-done | bytes 524320 | tf_op jit(solution)/shard_map/all_to_all | solution.py:291
  301.8 4.2 %all-to-all-start.1 = ((bf16[16,128,64]{1,2,0:T(8,128)(2,1)}), bf16[16,128,64]{1,2,0:T(8,128)(2,1)}, u32[]{:S(2)}, u32[]{:S(2)}) async-start(bf16[16,128,64]{1,2,0:T(8,128)(2,1)} %copy_bitcast_fusion.1), calls=%async_computation.1 | async-start | bytes 524288 | tf_op jit(solution)/shard_map/all_to_all | solution.py:244
  306.1 4.0 %fusion.16 = (f32[1024]{0:T(1024)S(1)}, f32[128]{0:T(128)S(1)}, f32[128]{0:T(128)S(1)}, f32[128,1024]{1,0:T(8,128)S(1)}) fusion(bf16[128,1024]{1,0:T(8,128)(2,1)S(1)} %copy-done.6, f32[128]{0:T(128)S(1)} %copy-done.26, f32[128]{0:T(128)S(1)} %copy-done.25, f32[1024]{0:T(1024)S(1)} %copy-done.22, bf16[128,2048]{0,1:T(8,128)(2,1)S(1)} %bitcast.178, ...), kind=kOutput, calls=%fused_computation.90 | convolution fusion | flops 538049280 | bytes 5515264 | tf_op jit(solution)/shard_map/fe,ne->fn/dot_general | solution.py:295
  310.1 1.1 pad_maximum_fusion
  311.2 1.2 all_to_all.24
  312.4 3.7 %all-to-all-done.1 = bf16[16,128,64]{1,2,0:T(8,128)(2,1)} async-done(((bf16[16,128,64]{1,2,0:T(8,128)(2,1)}), bf16[16,128,64]{1,2,0:T(8,128)(2,1)}, u32[]{:S(2)}, u32[]{:S(2)}) %all-to-all-start.1) | async-done | bytes 262176 | tf_op jit(solution)/shard_map/all_to_all | solution.py:244
  316.0 3.8 %all-to-all-start.3 = ((f32[16,1,8256]{2,1,0:T(1,128)}), f32[16,1,8256]{2,1,0:T(1,128)S(1)}, u32[]{:S(2)}, u32[]{:S(2)}) async-start(f32[16,1,8256]{2,1,0:T(1,128)} %all_to_all.24), calls=%async_computation.3 | async-start | bytes 1064960 | tf_op jit(solution)/shard_map/all_to_all | solution.py:300
  320.4 2.1 fusion.5
  322.5 2.0 fusion.15
  324.5 9.7 %all-to-all-done.3 = f32[16,1,8256]{2,1,0:T(1,128)S(1)} async-done(((f32[16,1,8256]{2,1,0:T(1,128)}), f32[16,1,8256]{2,1,0:T(1,128)S(1)}, u32[]{:S(2)}, u32[]{:S(2)}) %all-to-all-start.3) | async-done | bytes 528416 | tf_op jit(solution)/shard_map/all_to_all | solution.py:300
  334.8 0.8 reshape.170
  336.2 1.2 reshape.171
  (131 shorter events, 9.2 us)
Async XLA Ops:
  7.2 150.3 %copy-start.6 = (bf16[128,1024]{1,0:T(8,128)(2,1)S(1)}, bf16[128,1024]{1,0:T(8,128)(2,1)}, u32[]{:S(2)}) copy-start(bf16[128,1024]{1,0:T(8,128)(2,1)} %param.9) | copy-start | bytes 786436
  7.2 146.0 %copy-start.37 = (s32[128]{0:T(128)S(1)}, s32[128]{0:T(128)}, u32[]{:S(2)}) copy-start(s32[128]{0:T(128)} %param.10) | copy-start | bytes 1540
  7.2 146.1 %copy-start.33 = (f32[64]{0:T(128)S(1)}, f32[64]{0:T(128)}, u32[]{:S(2)}) copy-start(f32[64]{0:T(128)} %param.12) | copy-start | bytes 772
  7.2 150.7 %copy-start.23 = (f32[31,64]{1,0:T(8,128)S(1)}, f32[31,64]{1,0:T(8,128)}, u32[]{:S(2)}) copy-start(f32[31,64]{1,0:T(8,128)} %param.14) | copy-start | bytes 23812
  7.2 45.8 %all-gather.25.cloned.1.call-start = ((), (), s32[]{:S(2)}) async-start(), calls=%async_computation.8 | async-start | bytes 1179648 | tf_op jit(solution)/shard_map/all_gather | solution.py:168
  7.9 95.3 %all-gather.17.cloned.1.call-start = ((), (), s32[]{:S(2)}) async-start(), calls=%async_computation.4 | async-start | bytes 2359296 | tf_op jit(solution)/shard_map/all_gather | solution.py:168
  8.7 144.5 %all-gather.21.cloned.1.call-start = ((), (), s32[]{:S(2)}) async-start(), calls=%async_computation.6 | async-start | bytes 2359296 | tf_op jit(solution)/shard_map/all_gather | solution.py:168
  9.4 193.6 %all-gather.29.cloned.1.call-start = ((), (), s32[]{:S(2)}) async-start(), calls=%async_computation.10 | async-start | bytes 2359296 | tf_op jit(solution)/shard_map/all_gather | solution.py:168
  10.0 203.5 %all-gather.27.cloned.1.call-start = ((), (), s32[]{:S(2)}) async-start(), calls=%async_computation.9 | async-start | bytes 3145728 | tf_op jit(solution)/shard_map/all_gather | solution.py:169
  53.1 176.7 %all-gather.19.cloned.1.call-start = ((), (), s32[]{:S(2)}) async-start(), calls=%async_computation.5 | async-start | bytes 6291456 | tf_op jit(solution)/shard_map/all_gather | solution.py:169
  103.3 142.9 %all-gather.23.cloned.1.call-start = ((), (), s32[]{:S(2)}) async-start(), calls=%async_computation.7 | async-start | bytes 6291456 | tf_op jit(solution)/shard_map/all_gather | solution.py:169
  153.9 10.0 %all-to-all-start = ((f32[16,1,192]{2,1,0:T(1,128)}), f32[16,1,192]{2,1,0:T(1,128)S(1)}, u32[]{:S(2)}, u32[]{:S(2)}) async-start(f32[16,1,192]{2,1,0:T(1,128)} %broadcast_in_dim.2), calls=%async_computation | async-start | bytes 32768 | tf_op jit(solution)/shard_map/all_to_all | solution.py:185
  157.5 105.1 %all-gather.31.cloned.1.call-start = ((), (), s32[]{:S(2)}) async-start(), calls=%async_computation.11 | async-start | bytes 6291456 | tf_op jit(solution)/shard_map/all_gather | solution.py:169
  164.0 85.1 %copy-start.21 = (f32[1024]{0:T(1024)}, f32[1024]{0:T(1024)S(1)}, u32[]{:S(2)}) copy-start(f32[1024]{0:T(1024)S(1)} %mul.654) | copy-start | bytes 12292
  164.2 106.7 %copy-start.8 = (f32[2048]{0:T(1024)}, f32[2048]{0:T(1024)S(1)}, u32[]{:S(2)}) copy-start(f32[2048]{0:T(1024)S(1)} %get-tuple-element.100) | copy-start | bytes 24580
  164.2 106.7 %copy-start.10 = (f32[2048]{0:T(1024)}, f32[2048]{0:T(1024)S(1)}, u32[]{:S(2)}) copy-start(f32[2048]{0:T(1024)S(1)} %get-tuple-element.106) | copy-start | bytes 24580
  164.2 106.7 %copy-start.12 = (f32[2048]{0:T(1024)}, f32[2048]{0:T(1024)S(1)}, u32[]{:S(2)}) copy-start(f32[2048]{0:T(1024)S(1)} %get-tuple-element.107) | copy-start | bytes 24580
  164.2 106.7 %copy-start.14 = (f32[2048]{0:T(1024)}, f32[2048]{0:T(1024)S(1)}, u32[]{:S(2)}) copy-start(f32[2048]{0:T(1024)S(1)} %get-tuple-element.108) | copy-start | bytes 24580
  164.2 106.7 %copy-start.16 = (f32[2048]{0:T(1024)}, f32[2048]{0:T(1024)S(1)}, u32[]{:S(2)}) copy-start(f32[2048]{0:T(1024)S(1)} %get-tuple-element.109) | copy-start | bytes 24580
  164.2 106.7 %copy-start.18 = (f32[2048]{0:T(1024)}, f32[2048]{0:T(1024)S(1)}, u32[]{:S(2)}) copy-start(f32[2048]{0:T(1024)S(1)} %get-tuple-element.110) | copy-start | bytes 24580
  233.0 4.1 %copy-start = (bf16[16,128,1024]{2,1,0:T(8,128)(2,1)S(1)}, bf16[16,128,1024]{2,1,0:T(8,128)(2,1)}, u32[]{:S(2)}) copy-start(bf16[16,128,1024]{2,1,0:T(8,128)(2,1)} %all-gather.19.cloned.1.call-done) | copy-start | bytes 12582916
  246.2 6.2 %copy-start.3 = (f32[8,2,128,1024]{3,2,1,0:T(8,128)S(1)}, f32[8,2,128,1024]{3,2,1,0:T(8,128)}, u32[]{:S(2)}) copy-start(f32[8,2,128,1024]{3,2,1,0:T(8,128)} %copy.29) | copy-start | bytes 25165828
  248.8 5.3 %copy-start.4 = (bf16[8,2,64,2048]{3,2,1,0:T(8,128)(2,1)}, bf16[8,2,64,2048]{3,2,1,0:T(8,128)(2,1)S(1)}, u32[]{:S(2)}) copy-start(bf16[8,2,64,2048]{3,2,1,0:T(8,128)(2,1)S(1)} %copy.32) | copy-start | bytes 12582916
  254.1 2.0 copy-start.1
  262.6 2.9 copy-start.34
  262.6 4.6 %copy-start.20 = (bf16[64,1024]{1,0:T(8,128)(2,1)S(1)}, bf16[64,1024]{1,0:T(8,128)(2,1)}, u32[]{:S(2)}) copy-start(bf16[64,1024]{1,0:T(8,128)(2,1)} %param.17) | copy-start | bytes 393220
  262.6 4.6 %copy-start.38 = (f32[64]{0:T(128)S(1)}, f32[64]{0:T(128)}, u32[]{:S(2)}) copy-start(f32[64]{0:T(128)} %param.16) | copy-start | bytes 772
  265.3 1.9 copy-start.5
  268.8 7.7 %copy-start.35 = (f32[64]{0:T(128)}, f32[64]{0:T(128)S(1)}, u32[]{:S(2)}) copy-start(f32[64]{0:T(128)S(1)} %get-tuple-element.42) | copy-start | bytes 772
  268.8 7.8 %copy-start.2 = (bf16[2048,1024]{1,0:T(8,128)(2,1)S(1)}, bf16[2048,1024]{1,0:T(8,128)(2,1)}, u32[]{:S(2)}) copy-start(bf16[2048,1024]{1,0:T(8,128)(2,1)} %copy-done.1) | copy-start | bytes 12582916
  276.2 1.6 copy-start.9
  276.2 1.6 copy-start.11
  276.2 1.6 copy-start.13
  276.2 1.6 copy-start.15
  277.9 11.4 %copy-start.27 = (f32[64]{0:T(128)S(1)}, f32[64]{0:T(128)}, u32[]{:S(2)}) copy-start(f32[64]{0:T(128)} %get-tuple-element.10) | copy-start | bytes 772
  277.9 11.4 %copy-start.28 = (f32[64]{0:T(128)S(1)}, f32[64]{0:T(128)}, u32[]{:S(2)}) copy-start(f32[64]{0:T(128)} %get-tuple-element.11) | copy-start | bytes 772
  277.9 11.4 %copy-start.29 = (f32[64]{0:T(128)S(1)}, f32[64]{0:T(128)}, u32[]{:S(2)}) copy-start(f32[64]{0:T(128)} %get-tuple-element.12) | copy-start | bytes 772
  277.9 11.4 %copy-start.30 = (f32[64]{0:T(128)S(1)}, f32[64]{0:T(128)}, u32[]{:S(2)}) copy-start(f32[64]{0:T(128)} %get-tuple-element.13) | copy-start | bytes 772
  277.9 11.4 %copy-start.31 = (f32[64]{0:T(128)S(1)}, f32[64]{0:T(128)}, u32[]{:S(2)}) copy-start(f32[64]{0:T(128)} %get-tuple-element.14) | copy-start | bytes 772
  277.9 11.4 %copy-start.32 = (f32[64]{0:T(128)S(1)}, f32[64]{0:T(128)}, u32[]{:S(2)}) copy-start(f32[64]{0:T(128)} %get-tuple-element.15) | copy-start | bytes 772
  281.4 20.4 %all-to-all-start.2 = ((bf16[16,128,2,64]{1,3,2,0:T(8,128)(2,1)}), bf16[16,128,2,64]{1,3,2,0:T(8,128)(2,1)S(1)}, u32[]{:S(2)}, u32[]{:S(2)}) async-start(bf16[16,128,2,64]{1,3,2,0:T(8,128)(2,1)} %copy.36), calls=%async_computation.2 | async-start | bytes 1048576 | tf_op jit(solution)/shard_map/all_to_all | solution.py:291
  288.1 17.9 %copy-start.22 = (f32[1024]{0:T(1024)S(1)}, f32[1024]{0:T(1024)}, u32[]{:S(2)}) copy-start(f32[1024]{0:T(1024)} %copy-done.21) | copy-start | bytes 12292
  288.1 17.9 %copy-start.25 = (f32[128]{0:T(128)S(1)}, f32[128]{0:T(128)}, u32[]{:S(2)}) copy-start(f32[128]{0:T(128)} %copy-done.24) | copy-start | bytes 1540
  288.2 17.9 %copy-start.26 = (f32[128]{0:T(128)S(1)}, f32[128]{0:T(128)}, u32[]{:S(2)}) copy-start(f32[128]{0:T(128)} %add_rsqrt_fusion.1) | copy-start | bytes 1540
  301.8 14.3 %all-to-all-start.1 = ((bf16[16,128,64]{1,2,0:T(8,128)(2,1)}), bf16[16,128,64]{1,2,0:T(8,128)(2,1)}, u32[]{:S(2)}, u32[]{:S(2)}) async-start(bf16[16,128,64]{1,2,0:T(8,128)(2,1)} %copy_bitcast_fusion.1), calls=%async_computation.1 | async-start | bytes 524288 | tf_op jit(solution)/shard_map/all_to_all | solution.py:244
  306.0 13.8 %copy-start.36 = (f32[64]{0:T(128)S(1)}, f32[64]{0:T(128)}, u32[]{:S(2)}) copy-start(f32[64]{0:T(128)} %copy-done.35) | copy-start | bytes 772
  306.1 14.3 %copy-start.7 = (bf16[8,2,64,1024]{3,2,1,0:T(8,128)(2,1)S(1)}, bf16[8,2,64,1024]{3,2,1,0:T(8,128)(2,1)}, u32[]{:S(2)}) copy-start(bf16[8,2,64,1024]{3,2,1,0:T(8,128)(2,1)} %copy.34) | copy-start | bytes 6291460
  316.0 18.2 %all-to-all-start.3 = ((f32[16,1,8256]{2,1,0:T(1,128)}), f32[16,1,8256]{2,1,0:T(1,128)S(1)}, u32[]{:S(2)}, u32[]{:S(2)}) async-start(f32[16,1,8256]{2,1,0:T(1,128)} %all_to_all.24), calls=%async_computation.3 | async-start | bytes 1064960 | tf_op jit(solution)/shard_map/all_to_all | solution.py:300
  (3 other events, 3.7 us)
Sparse Core Ops, SparseCore 0:
  10.2 42.8 all-gather.24
  55.2 48.0 all-gather.16
  105.4 47.7 all-gather.20
  155.2 47.7 all-gather.28
  204.4 9.0 all-gather.26
  214.9 14.8 all-gather.18
  231.3 14.8 all-gather.22
  247.7 14.8 all-gather.30

commit v4 on v2

--- a/solution.py
+++ b/solution.py
@@ -179,10 +179,17 @@
     gains = small[:, :share].reshape(width)
     all_ids = small[:, share:].reshape(stream).astype(jnp.int32)
 
-    frames_all = lax.all_gather(frames, "seq", axis=0, tiled=True)
-    w_out_all = lax.all_gather(w_out, "seq", axis=0, tiled=True)
-    grad_all = lax.all_gather(out_grad, "seq", axis=0, tiled=True)
-    w_in_all = spread(w_in).reshape(width, 2 * width)
+    in_rows = w_in.shape[0] * w_in.shape[1] // width
+    out_rows = w_out.shape[0]
+    pieces = lax.all_gather(
+        jnp.concatenate([frames, out_grad, w_out, w_in.reshape(in_rows, width)], axis=0),
+        "seq",
+        axis=0,
+    )
+    frames_all = pieces[:, :rows].reshape(stream, width)
+    grad_all = pieces[:, rows : 2 * rows].reshape(stream, width)
+    w_out_all = pieces[:, 2 * rows : 2 * rows + out_rows].reshape(width, width)
+    w_in_all = pieces[:, 2 * rows + out_rows :].reshape(width, 2 * width)
 
     first_channel = lax.axis_index("seq") * share
     w_in_cols = jnp.concatenate(

time: 258 us -> 237 us (0.919)
  waiting for transfers between devices: 143 us -> 126 us
  blocking collectives: 13.7 us -> 0 us
  other arithmetic: 27.6 us -> 41.3 us
  local copies, waits for them, and re-layouts: 11.5 us -> 21.2 us
  starting transfers between devices: 27.9 us -> 18.8 us
  matrix products: 19.2 us -> 14.8 us
    all_to_all x1, waiting for transfers between devices: 42.5 us -> 2.25 us  [spread(): return lax.all_to_all(copies, 'seq', 0, 0, tiled=True)]
    all_gather x3 -> x1, waiting for transfers between devices: 74.8 us -> 100 us  [channel_local(): lax.all_gather(jnp.concatenate([frames, out_grad, w_out, w_in.reshape(in_...]
    all_to_all x1 -> x0, blocking collectives: 13.7 us -> none  [spread(): return lax.all_to_all(copies, 'seq', 0, 0, tiled=True)]
    all_to_all x1, starting transfers between devices: 15.1 us -> 3.57 us  [channel_local(): lax.all_to_all(grad_hidden.reshape(devices, rows, 2, share), 'seq', 0, 0,...]
    slice x0 -> x1, other arithmetic: none -> 11.3 us  [channel_local(): grad_all = pieces[:, rows:2 * rows].reshape(stream, width)]
    reshape x0 -> x2, local copies, waits for them, and re-layouts: none -> 8.12 us  [the longest x1 7.08 us: channel_local(): w_in_all = pieces[:, 2 * rows + out_rows:].reshape(width, 2 * width)]
    broadcast_in_dim x2 -> x1, local copies, waits for them, and re-layouts: 3.44 us -> 0.62 us  [spread(): copies = jnp.broadcast_to(block[None], (devices,) + block.shape)]
    all_to_all x1, starting transfers between devices: 4.66 us -> 7.39 us  [spread(): return lax.all_to_all(copies, 'seq', 0, 0, tiled=True)]
  transfers between devices with their start and end apart: 7 -> 5, of which waited for: 6 -> 5; matrix products, arithmetic and copies ran while one was open for 21% -> 9% of each run, Pallas kernels for 0% -> 0%
where the time goes in v4:
time: 237 us; the launch traced here: 236 us
  waiting for transfers between devices  126 us (53%)
  other arithmetic  41.3 us (17%)
  local copies, waits for them, and re-layouts  21.2 us (9%)
  starting transfers between devices  18.8 us (8%)
  matrix products  14.8 us (6%)
  between operations  14.4 us (6%)
    all_gather x1, waiting for transfers between devices, channel_local(): lax.all_gather(jnp.concatenate([frames, out_grad, w_out, w_in.reshape(in_...  100 us
    slice x1, other arithmetic, channel_local(): grad_all = pieces[:, rows:2 * rows].reshape(stream, width)  11.3 us
    all_to_all x1, waiting for transfers between devices, channel_local(): lax.all_to_all(jnp.concatenate([in_cols.reshape(devices, share * 2 * shar...  10.1 us
    all_to_all x1, waiting for transfers between devices, channel_local(): lax.all_to_all(grad_hidden.reshape(devices, rows, 2, share), 'seq', 0, 0,...  8.01 us
    all_to_all x1, starting transfers between devices, spread(): return lax.all_to_all(copies, 'seq', 0, 0, tiled=True)  7.39 us
    reshape x1, local copies, waits for them, and re-layouts, channel_local(): w_in_all = pieces[:, 2 * rows + out_rows:].reshape(width, 2 * width)  7.08 us
    mul x1, other arithmetic, channel_local(): grad_glu * right_gate  5.27 us
    all_to_all x1, waiting for transfers between devices, channel_local(): lax.all_to_all(activation.reshape(devices, rows, share), 'seq', 0, 0, til...  4.82 us
  transfers between devices with their start and end apart: 5, of which 5 were waited for; matrix products, arithmetic and copies ran while one was open for 9% of the time, Pallas kernels for 0%

profile of v4, /device:TPU:0, one launch (start us, length us, event | category | flops | bytes accessed | tf_op | source)
XLA Modules:
  0.0 236.0 jit_solution(9545074175619735562)
XLA Ops:
  7.2 1.0 reshape.162
  8.3 2.1 pad_maximum_fusion
  10.4 0.7 convert_element_type.271
  11.0 0.7 pad_maximum_fusion.2
  11.8 0.6 broadcast_in_dim.2
  12.4 7.4 %all-to-all-start = ((f32[16,1,192]{2,1,0:T(1,128)}), f32[16,1,192]{2,1,0:T(1,128)S(1)}, u32[]{:S(2)}, u32[]{:S(2)}) async-start(f32[16,1,192]{2,1,0:T(1,128)} %broadcast_in_dim.2), calls=%async_computation | async-start | bytes 32768 | tf_op jit(solution)/shard_map/all_to_all | solution.py:176
  19.8 1.1 convert_reduce_fusion
  20.9 1.2 fusion.27
  22.1 1.0 slice_bitcast_fusion.29
  23.0 1.0 slice_bitcast_fusion.30
  24.1 2.2 all-to-all-done
  26.7 100.4 %all-gather.3.cloned.1.call-done = bf16[7168,1024]{1,0:T(8,128)(2,1)} async-done(((bf16[448,1024]{1,0:T(8,128)(2,1)}), bf16[7168,1024]{1,0:T(8,128)(2,1)}) %all-gather.3.cloned.1.call-update) | async-done | bytes 14680080 | tf_op jit(solution)/shard_map/all_gather | solution.py:184
  127.1 11.3 %fusion.269 = (bf16[16,128,1024]{2,1,0:T(8,128)(2,1)}, bf16[16,128,1024]{2,1,0:T(8,128)(2,1)}, f32[16,128,1024]{2,1,0:T(8,128)}) fusion(bf16[16,448,1024]{2,1,0:T(8,128)(2,1)} %bitcast.149), kind=kLoop, calls=%fused_computation.443 | loop fusion | flops 2097152 | bytes 29360128 | tf_op jit(solution)/shard_map/slice | solution.py:190
  138.4 3.2 %copy-done = bf16[7168,1024]{1,0:T(8,128)(2,1)S(1)} copy-done((bf16[7168,1024]{1,0:T(8,128)(2,1)S(1)}, bf16[7168,1024]{1,0:T(8,128)(2,1)}, u32[]{:S(2)}) %copy-start) | copy-done | bytes 14680088
  141.6 0.6 fusion.3
  142.2 1.4 multiply_reduce_fusion
  143.7 7.1 %reshape.163 = bf16[1024,2048]{1,0:T(8,128)(2,1)} reshape(bf16[16,128,1024]{2,1,0:T(8,128)(2,1)} %get-tuple-element.49) | data formatting | bytes 8388608 | tf_op jit(solution)/shard_map/reshape | solution.py:192
  150.7 1.2 constant_dynamic-slice_fusion.1
  152.0 4.1 %fusion.2 = bf16[2048,1024]{1,0:T(8,128)(2,1)S(1)} fusion(f32[16,128,1024]{2,1,0:T(8,128)} %get-tuple-element.50, f32[1024]{0:T(1024)S(1)} %mul.652, f32[2048]{0:T(1024)S(1)} %rsqrt_bitcast_fusion, f32[2048]{0:T(1024)S(1)} %get-tuple-element.115), kind=kLoop, calls=%fused_computation.3 | loop fusion | flops 8388608 | bytes 12603392 | tf_op jit(solution)/shard_map/convert_element_type | solution.py:211
  156.1 1.6 fusion.193
  157.9 4.2 %fusion.267 = (f32[64]{0:T(128)S(1)}, f32[2048,64]{0,1:T(8,128)S(1)}) fusion(f32[2048]{0:T(1024)S(1)} %get-tuple-element.114, f32[64]{0:T(128)S(1)} %get-tuple-element.83, f32[2048]{0:T(1024)S(1)} %get-tuple-element.86, f32[64]{0:T(128)S(1)} %get-tuple-element.84, f32[2048]{0:T(1024)S(1)} %get-tuple-element.87, f32[64]{0:T(128)S(1)} %get-tuple-element.55, ...), kind=kLoop, calls=%fused_computation.442 | loop fusion | flops 16121792 | bytes 1040384 | tf_op jit(solution)/shard_map/reduce_sum | solution.py:233
  162.3 1.6 fusion.266
  163.9 0.5 broadcast_multiply_fusion.3
  164.4 1.0 fusion.148
  165.5 5.3 %fusion.265 = (bf16[2048,64]{0,1:T(8,128)(2,1)S(1)}, f32[2048,64]{0,1:T(8,128)S(1)}) fusion(f32[2048,128]{0,1:T(8,128)S(1)} %fusion.193, f32[2048]{0:T(1024)S(1)} %get-tuple-element.85, f32[64]{0:T(128)S(1)} %get-tuple-element.83, f32[2048]{0:T(1024)S(1)} %get-tuple-element.103, f32[64]{0:T(128)S(1)} %get-tuple-element.84, f32[2048]{0:T(1024)S(1)} %get-tuple-element.113, ...), kind=kLoop, calls=%fused_computation.440 | loop fusion | flops 12582912 | bytes 2088704 | tf_op jit(solution)/shard_map/mul | solution.py:281
  171.0 1.3 convolution_multiply_fusion.1
  172.3 0.8 fusion.72
  173.1 0.8 fusion.90
  173.9 0.7 fusion.106
  174.8 0.9 copy.23
  175.7 3.6 %all-to-all-start.2 = ((bf16[16,128,2,64]{1,3,2,0:T(8,128)(2,1)}), bf16[16,128,2,64]{1,3,2,0:T(8,128)(2,1)S(1)}, u32[]{:S(2)}, u32[]{:S(2)}) async-start(bf16[16,128,2,64]{1,3,2,0:T(8,128)(2,1)} %copy.23), calls=%async_computation.2 | async-start | bytes 1048576 | tf_op jit(solution)/shard_map/all_to_all | solution.py:289
  179.3 0.8 fusion.124
  180.6 0.6 broadcast_multiply_fusion
  181.2 0.8 copy_bitcast_fusion.1
  182.0 3.7 %convolution_multiply_fusion.2 = f32[64,1024]{1,0:T(8,128)} fusion(bf16[2048,64]{0,1:T(8,128)(2,1)S(1)} %get-tuple-element.53, bf16[2048,1024]{1,0:T(8,128)(2,1)} %bitcast.153), kind=kOutput, calls=%fused_computation.15 | convolution fusion | flops 268500992 | bytes 4718592 | tf_op jit(solution)/shard_map/fa,fb->ab/dot_general | solution.py:250
  185.7 8.0 %all-to-all-done.2 = bf16[16,128,2,64]{1,3,2,0:T(8,128)(2,1)S(1)} async-done(((bf16[16,128,2,64]{1,3,2,0:T(8,128)(2,1)}), bf16[16,128,2,64]{1,3,2,0:T(8,128)(2,1)S(1)}, u32[]{:S(2)}, u32[]{:S(2)}) %all-to-all-start.2) | async-done | bytes 524320 | tf_op jit(solution)/shard_map/all_to_all | solution.py:289
  193.7 4.0 %all-to-all-start.1 = ((bf16[16,128,64]{1,2,0:T(8,128)(2,1)}), bf16[16,128,64]{1,2,0:T(8,128)(2,1)S(1)}, u32[]{:S(2)}, u32[]{:S(2)}) async-start(bf16[16,128,64]{1,2,0:T(8,128)(2,1)} %copy_bitcast_fusion.1), calls=%async_computation.1 | async-start | bytes 524288 | tf_op jit(solution)/shard_map/all_to_all | solution.py:242
  197.8 3.8 %fusion.26 = (f32[1024]{0:T(1024)S(1)}, f32[128]{0:T(128)S(1)}, f32[128]{0:T(128)S(1)}, f32[128,1024]{1,0:T(8,128)S(1)}) fusion(bf16[128,1024]{1,0:T(8,128)(2,1)S(1)} %copy-done.2, f32[128]{0:T(128)S(1)} %add_rsqrt_fusion, f32[128]{0:T(128)S(1)} %broadcast_multiply_fusion.7, f32[1024]{0:T(1024)S(1)} %mul.652, bf16[128,2048]{0,1:T(8,128)(2,1)S(1)} %bitcast.158, ...), kind=kOutput, calls=%fused_computation.94 | convolution fusion | flops 538049280 | bytes 5515264 | tf_op jit(solution)/shard_map/fe,ne->fn/dot_general | solution.py:293
  201.8 1.2 all_to_all.24
  203.0 4.8 %all-to-all-done.1 = bf16[16,128,64]{1,2,0:T(8,128)(2,1)S(1)} async-done(((bf16[16,128,64]{1,2,0:T(8,128)(2,1)}), bf16[16,128,64]{1,2,0:T(8,128)(2,1)S(1)}, u32[]{:S(2)}, u32[]{:S(2)}) %all-to-all-start.1) | async-done | bytes 262176 | tf_op jit(solution)/shard_map/all_to_all | solution.py:242
  207.8 3.8 %all-to-all-start.3 = ((f32[16,1,8256]{2,1,0:T(1,128)}), f32[16,1,8256]{2,1,0:T(1,128)S(1)}, u32[]{:S(2)}, u32[]{:S(2)}) async-start(f32[16,1,8256]{2,1,0:T(1,128)} %all_to_all.24), calls=%async_computation.3 | async-start | bytes 1064960 | tf_op jit(solution)/shard_map/all_to_all | solution.py:298
  212.1 2.8 %fusion.13 = bf16[128,1024]{1,0:T(8,128)(2,1)} fusion(bf16[16,448,1024]{2,1,0:T(8,128)(2,1)} %bitcast.150, bf16[128,1024]{1,0:T(8,128)(2,1)S(1)} %copy-done.2, bf16[16,128,64]{1,2,0:T(8,128)(2,1)S(1)} %all-to-all-done.1), kind=kOutput, calls=%fused_computation.14 | convolution fusion | flops 268828672 | bytes 2883584 | tf_op jit(solution)/shard_map/dot_general | solution.py:246
  214.9 1.0 fusion.25
  215.9 10.1 %all-to-all-done.3 = f32[16,1,8256]{2,1,0:T(1,128)S(1)} async-done(((f32[16,1,8256]{2,1,0:T(1,128)}), f32[16,1,8256]{2,1,0:T(1,128)S(1)}, u32[]{:S(2)}, u32[]{:S(2)}) %all-to-all-start.3) | async-done | bytes 528416 | tf_op jit(solution)/shard_map/all_to_all | solution.py:298
  226.1 0.5 slice_reduce_fusion
  226.6 0.8 reshape.168
  227.4 0.6 copy.25
  228.0 1.2 reshape.169
  (43 shorter events, 2.3 us)
Async XLA Ops:
  7.2 119.9 %all-gather.3.cloned.1.call-start = ((), (), s32[]{:S(2)}) async-start(), calls=%async_computation.4 | async-start | bytes 15597568 | tf_op jit(solution)/shard_map/all_gather | solution.py:184
  12.4 13.9 %all-to-all-start = ((f32[16,1,192]{2,1,0:T(1,128)}), f32[16,1,192]{2,1,0:T(1,128)S(1)}, u32[]{:S(2)}, u32[]{:S(2)}) async-start(f32[16,1,192]{2,1,0:T(1,128)} %broadcast_in_dim.2), calls=%async_computation | async-start | bytes 32768 | tf_op jit(solution)/shard_map/all_to_all | solution.py:176
  127.1 14.5 %copy-start = (bf16[7168,1024]{1,0:T(8,128)(2,1)S(1)}, bf16[7168,1024]{1,0:T(8,128)(2,1)}, u32[]{:S(2)}) copy-start(bf16[7168,1024]{1,0:T(8,128)(2,1)} %all-gather.3.cloned.1.call-done) | copy-start | bytes 44040196
  156.1 6.2 %copy-start.5 = (f32[64]{0:T(128)S(1)}, f32[64]{0:T(128)}, u32[]{:S(2)}) copy-start(f32[64]{0:T(128)} %param.15) | copy-start | bytes 772
  156.1 6.2 %copy-start.1 = (bf16[16,128,1024]{2,1,0:T(8,128)(2,1)S(1)}, bf16[16,128,1024]{2,1,0:T(8,128)(2,1)}, u32[]{:S(2)}) copy-start(bf16[16,128,1024]{2,1,0:T(8,128)(2,1)} %get-tuple-element.48) | copy-start | bytes 12582916
  156.1 6.2 %copy-start.4 = (bf16[64,1024]{1,0:T(8,128)(2,1)S(1)}, bf16[64,1024]{1,0:T(8,128)(2,1)}, u32[]{:S(2)}) copy-start(bf16[64,1024]{1,0:T(8,128)(2,1)} %param.17) | copy-start | bytes 393220
  156.1 6.2 %copy-start.6 = (f32[64]{0:T(128)S(1)}, f32[64]{0:T(128)}, u32[]{:S(2)}) copy-start(f32[64]{0:T(128)} %param.16) | copy-start | bytes 772
  175.7 18.0 %all-to-all-start.2 = ((bf16[16,128,2,64]{1,3,2,0:T(8,128)(2,1)}), bf16[16,128,2,64]{1,3,2,0:T(8,128)(2,1)S(1)}, u32[]{:S(2)}, u32[]{:S(2)}) async-start(bf16[16,128,2,64]{1,3,2,0:T(8,128)(2,1)} %copy.23), calls=%async_computation.2 | async-start | bytes 1048576 | tf_op jit(solution)/shard_map/all_to_all | solution.py:289
  180.1 17.7 %copy-start.2 = (bf16[128,1024]{1,0:T(8,128)(2,1)S(1)}, bf16[128,1024]{1,0:T(8,128)(2,1)}, u32[]{:S(2)}) copy-start(bf16[128,1024]{1,0:T(8,128)(2,1)} %param.9) | copy-start | bytes 786436
  193.7 14.1 %all-to-all-start.1 = ((bf16[16,128,64]{1,2,0:T(8,128)(2,1)}), bf16[16,128,64]{1,2,0:T(8,128)(2,1)S(1)}, u32[]{:S(2)}, u32[]{:S(2)}) async-start(bf16[16,128,64]{1,2,0:T(8,128)(2,1)} %copy_bitcast_fusion.1), calls=%async_computation.1 | async-start | bytes 524288 | tf_op jit(solution)/shard_map/all_to_all | solution.py:242
  201.7 13.2 %copy-start.3 = (bf16[128,1024]{1,0:T(8,128)(2,1)S(1)}, bf16[128,1024]{1,0:T(8,128)(2,1)}, u32[]{:S(2)}) copy-start(bf16[128,1024]{1,0:T(8,128)(2,1)} %param.11) | copy-start | bytes 786436
  207.8 18.2 %all-to-all-start.3 = ((f32[16,1,8256]{2,1,0:T(1,128)}), f32[16,1,8256]{2,1,0:T(1,128)S(1)}, u32[]{:S(2)}, u32[]{:S(2)}) async-start(f32[16,1,8256]{2,1,0:T(1,128)} %all_to_all.24), calls=%async_computation.3 | async-start | bytes 1064960 | tf_op jit(solution)/shard_map/all_to_all | solution.py:298
Sparse Core Ops, SparseCore 0:
  10.5 116.5 all-gather.2

commit v5 on v4

--- a/solution.py
+++ b/solution.py
@@ -179,23 +179,23 @@
     gains = small[:, :share].reshape(width)
     all_ids = small[:, share:].reshape(stream).astype(jnp.int32)
 
-    in_rows = w_in.shape[0] * w_in.shape[1] // width
     out_rows = w_out.shape[0]
     pieces = lax.all_gather(
-        jnp.concatenate([frames, out_grad, w_out, w_in.reshape(in_rows, width)], axis=0),
+        jnp.concatenate([frames, out_grad, w_out, w_in[:, :width], w_in[:, width:]], axis=0),
         "seq",
         axis=0,
     )
     frames_all = pieces[:, :rows].reshape(stream, width)
     grad_all = pieces[:, rows : 2 * rows].reshape(stream, width)
     w_out_all = pieces[:, 2 * rows : 2 * rows + out_rows].reshape(width, width)
-    w_in_all = pieces[:, 2 * rows + out_rows :].reshape(width, 2 * width)
+    w_in_left = pieces[:, 2 * rows + out_rows : 2 * rows + 2 * out_rows].reshape(width, width)
+    w_in_right = pieces[:, 2 * rows + 2 * out_rows :].reshape(width, width)
 
     first_channel = lax.axis_index("seq") * share
     w_in_cols = jnp.concatenate(
         [
-            lax.dynamic_slice_in_dim(w_in_all, first_channel, share, 1),
-            lax.dynamic_slice_in_dim(w_in_all, width + first_channel, share, 1),
+            lax.dynamic_slice_in_dim(w_in_left, first_channel, share, 1),
+            lax.dynamic_slice_in_dim(w_in_right, first_channel, share, 1),
         ],
         axis=1,
     )
@@ -238,13 +238,6 @@
     zed_gate = jax.nn.sigmoid(zed)
     activation = (zed * zed_gate).astype(jnp.bfloat16)
 
-    act_rows = (
-        lax.all_to_all(activation.reshape(devices, rows, share), "seq", 0, 0, tiled=True)
-        .transpose(1, 0, 2)
-        .reshape(rows, width)
-    )
-    projected = jnp.dot(act_rows, w_out_all, preferred_element_type=jnp.float32)
-    outputs = (frames.astype(jnp.float32) + projected).astype(jnp.bfloat16)
 
     grad_w_out = (
         jnp.einsum("fa,fb->ab", activation, grad_all, preferred_element_type=jnp.float32)
@@ -285,14 +278,20 @@
         jnp.einsum("fa,fb->ab", ln_x_all, grad_hidden, preferred_element_type=jnp.float32)
         * grad_scale
     )
+    back = lax.all_to_all(
+        jnp.concatenate([activation, grad_hidden], axis=1).reshape(devices, rows, 3 * share),
+        "seq", 0, 0, tiled=True,
+    )
+    act_rows = back[:, :, :share].transpose(1, 0, 2).reshape(rows, width)
     hidden_rows = (
-        lax.all_to_all(grad_hidden.reshape(devices, rows, 2, share), "seq", 0, 0, tiled=True)
-        .transpose(1, 2, 0, 3)
-        .reshape(rows, 2 * width)
-    )
+        back[:, :, share:].reshape(devices, rows, 2, share).transpose(1, 2, 0, 3)
+        .reshape(rows, 2, width)
+    )
+    projected = jnp.dot(act_rows, w_out_all, preferred_element_type=jnp.float32)
+    outputs = (frames.astype(jnp.float32) + projected).astype(jnp.bfloat16)
     grad_ln = jnp.einsum(
-        "fe,ne->fn", hidden_rows, w_in_all, preferred_element_type=jnp.float32
-    )
+        "fe,ne->fn", hidden_rows[:, 0], w_in_left, preferred_element_type=jnp.float32
+    ) + jnp.einsum("fe,ne->fn", hidden_rows[:, 1], w_in_right, preferred_element_type=jnp.float32)
     ln_hat, rstd_ln = norm(frames)
     gain_part = jnp.sum(grad_ln * ln_hat, axis=0) * grad_scale
     packed = lax.all_to_all(

time: 237 us -> 224 us (0.945)
  waiting for transfers between devices: 126 us -> 117 us
  other arithmetic: 41.3 us -> 37.7 us
    reshape x3 -> x1, local copies, waits for them, and re-layouts: 8.89 us -> 0.04 us  [channel_local(): back[:, :, share:].reshape(devices, rows, 2, share).transpose(1, 2, 0, 3)]
    all_to_all x2 -> x1, waiting for transfers between devices: 12.8 us -> 5.23 us  [channel_local(): lax.all_to_all(jnp.concatenate([activation, grad_hidden], axis=1).reshape...]
    slice x1, other arithmetic: 11.3 us -> 4.35 us  [channel_local(): grad_all = pieces[:, rows:2 * rows].reshape(stream, width)]
    mul x2 -> x0, other arithmetic: 5.44 us -> none  [the longest x1 5.27 us: channel_local(): grad_glu * right_gate]
    another operation x0 -> x2, other arithmetic: none -> 5.31 us
    unnamed x17 -> x28, local copies, waits for them, and re-layouts: 3.4 us -> 8.37 us
    all_to_all x2 -> x1, starting transfers between devices: 7.6 us -> 4.3 us  [channel_local(): lax.all_to_all(jnp.concatenate([activation, grad_hidden], axis=1).reshape...]
    another operation x1, local copies, waits for them, and re-layouts: 0.09 us -> 2.85 us  [channel_local(): jnp.stack([jnp.sum(grad_conv * padded_glu[tap_index:tap_index + stream].a...]
  transfers between devices with their start and end apart: 5 -> 4, of which waited for: 5 -> 4; matrix products, arithmetic and copies ran while one was open for 9% -> 11% of each run, Pallas kernels for 0% -> 0%
where the time goes in v5:
time: 224 us; the launch traced here: 223 us
  waiting for transfers between devices  117 us (52%)
  other arithmetic  37.7 us (17%)
  local copies, waits for them, and re-layouts  21.6 us (10%)
  starting transfers between devices  17.2 us (8%)
  matrix products  15.4 us (7%)
  between operations  14.4 us (6%)
    all_gather x1, waiting for transfers between devices, channel_local(): lax.all_gather(jnp.concatenate([frames, out_grad, w_out, w_in[:, :width],...  100 us
    all_to_all x1, waiting for transfers between devices, channel_local(): lax.all_to_all(jnp.concatenate([in_cols.reshape(devices, share * 2 * shar...  9.79 us
    unnamed x28, local copies, waits for them, and re-layouts  8.37 us
    all_to_all x1, starting transfers between devices, spread(): return lax.all_to_all(copies, 'seq', 0, 0, tiled=True)  7.39 us
    reduce_sum x6, other arithmetic, channel_local(): jnp.sum(grad_conv * padded_glu[tap_index:tap_index + stream].astype(jnp.f...  6.8 us
    all_to_all x1, starting transfers between devices, channel_local(): lax.all_to_all(jnp.concatenate([in_cols.reshape(devices, share * 2 * shar...  5.43 us
    another operation x2, other arithmetic  5.31 us
    all_to_all x1, waiting for transfers between devices, channel_local(): lax.all_to_all(jnp.concatenate([activation, grad_hidden], axis=1).reshape...  5.23 us
  transfers between devices with their start and end apart: 4, of which 4 were waited for; matrix products, arithmetic and copies ran while one was open for 11% of the time, Pallas kernels for 0%

profile of v5, /device:TPU:0, one launch (start us, length us, event | category | flops | bytes accessed | tf_op | source)
XLA Modules:
  0.0 223.5 jit_solution(16961837317428101071)
XLA Ops:
  7.2 1.0 constant_dynamic-update-slice_fusion.2
  8.2 1.0 constant_dynamic-update-slice_fusion.1
  9.2 0.9 constant_dynamic-update-slice_fusion
  10.1 0.9 slice_dynamic-update-slice_fusion.1
  11.0 0.9 slice_dynamic-update-slice_fusion
  11.9 0.9 copy-done.4
  12.9 0.7 convert_element_type.265
  13.5 0.7 pad_maximum_fusion.1
  14.9 7.4 %all-to-all-start = ((f32[16,1,192]{2,1,0:T(1,128)}), f32[16,1,192]{2,1,0:T(1,128)S(1)}, u32[]{:S(2)}, u32[]{:S(2)}) async-start(f32[16,1,192]{2,1,0:T(1,128)} %broadcast_in_dim.2), calls=%async_computation | async-start | bytes 32768 | tf_op jit(solution)/shard_map/all_to_all | solution.py:176
  22.3 1.1 convert_reduce_fusion
  23.4 1.2 fusion.27
  24.6 1.0 slice_bitcast_fusion.35
  25.5 1.0 slice_bitcast_fusion.36
  27.1 1.7 all-to-all-done
  29.2 100.4 %all-gather.3.cloned.1.call-done = bf16[7168,1024]{1,0:T(8,128)(2,1)} async-done(((bf16[448,1024]{1,0:T(8,128)(2,1)}), bf16[7168,1024]{1,0:T(8,128)(2,1)}) %all-gather.3.cloned.1.call-update) | async-done | bytes 14680080 | tf_op jit(solution)/shard_map/all_gather | solution.py:183
  129.6 2.8 %fusion.3 = f32[16,128]{1,0:T(8,128)S(1)} fusion(bf16[16,448,1024]{2,1,0:T(8,128)(2,1)} %bitcast.156), kind=kLoop, calls=%fused_computation.6 | loop fusion | flops 4192256 | bytes 4202496 | tf_op jit(solution)/shard_map/reduce_sum | solution.py:205
  132.4 4.3 %fusion.270 = (bf16[16,128,1024]{2,1,0:T(8,128)(2,1)S(1)}, f32[16,128,1024]{2,1,0:T(8,128)S(1)}) fusion(bf16[16,448,1024]{2,1,0:T(8,128)(2,1)} %bitcast.157), kind=kLoop, calls=%fused_computation.453 | loop fusion | flops 2097152 | bytes 20971520 | tf_op jit(solution)/shard_map/slice | solution.py:189
  136.7 3.3 %copy-done = bf16[7168,1024]{1,0:T(8,128)(2,1)S(1)} copy-done((bf16[7168,1024]{1,0:T(8,128)(2,1)S(1)}, bf16[7168,1024]{1,0:T(8,128)(2,1)}, u32[]{:S(2)}) %copy-start) | copy-done | bytes 14680088
  140.6 1.4 multiply_reduce_fusion
  142.6 1.9 fusion.2
  144.6 1.6 fusion.197
  146.3 4.2 %fusion.268 = (f32[64]{0:T(128)S(1)}, f32[2048,64]{0,1:T(8,128)S(1)}) fusion(f32[2048]{0:T(1024)S(1)} %get-tuple-element.102, f32[64]{0:T(128)S(1)} %get-tuple-element.82, f32[2048]{0:T(1024)S(1)} %get-tuple-element.85, f32[64]{0:T(128)S(1)} %get-tuple-element.83, f32[2048]{0:T(1024)S(1)} %get-tuple-element.86, f32[64]{0:T(128)S(1)} %get-tuple-element.54, ...), kind=kLoop, calls=%fused_computation.452 | loop fusion | flops 16121792 | bytes 1040384 | tf_op jit(solution)/shard_map/reduce_sum | solution.py:233
  150.8 1.6 fusion.267
  153.0 1.6 fusion.148
  154.5 1.4 fusion.124
  155.9 5.1 %multiply_convert_fusion.1 = (bf16[2048,64]{0,1:T(8,128)(2,1)S(1)}, f32[2048,64]{0,1:T(8,128)S(1)}) fusion(f32[2048,128]{0,1:T(8,128)S(1)} %fusion.197, f32[2048]{0:T(1024)S(1)} %get-tuple-element.113, f32[64]{0:T(128)S(1)} %get-tuple-element.82, f32[2048]{0:T(1024)S(1)} %get-tuple-element.112, f32[64]{0:T(128)S(1)} %get-tuple-element.83, ...), kind=kLoop, calls=%fused_computation.226 | loop fusion | flops 12582912 | bytes 2088704 | tf_op jit(solution)/shard_map/convert.1
  161.3 2.1 convolution_multiply_fusion.1
  163.4 1.1 copy_bitcast_fusion
  164.5 4.3 %all-to-all-start.1 = ((bf16[16,128,192]{1,2,0:T(8,128)(2,1)}), bf16[16,128,192]{1,2,0:T(8,128)(2,1)}, u32[]{:S(2)}, u32[]{:S(2)}) async-start(bf16[16,128,192]{1,2,0:T(8,128)(2,1)} %copy_bitcast_fusion), calls=%async_computation.1 | async-start | bytes 1572864 | tf_op jit(solution)/shard_map/all_to_all | solution.py:281
  168.8 0.8 fusion.54
  169.6 1.1 reshape.168
  170.8 1.4 fusion.90
  172.2 0.8 fusion.72
  173.0 0.7 fusion.106
  173.8 2.8 %stack.127 = f32[31,64]{1,0:T(8,128)S(1)} concatenate(f32[1,64]{1,0:T(1,128)} %bitcast.199, f32[1,64]{1,0:T(1,128)S(1)} %bitcast.192, f32[1,64]{1,0:T(1,128)S(1)} %bitcast.191, f32[1,64]{1,0:T(1,128)S(1)} %bitcast.190, f32[1,64]{1,0:T(1,128)S(1)} %bitcast.189, f32[1,64]{1,0:T(1,128)S(1)} %bitcast.188, f32[1,64]{1,0:T(1,128)S(1)} %bitcast.187, f32[1,64]{1,0:T(1,128)} %bitcast.186, ...), dimensions={0} | concatenate | bytes 15872 | tf_op jit(solution)/shard_map/stack | solution.py:252
  176.6 1.2 broadcast_multiply_fusion.4
  178.4 3.9 %convolution_multiply_fusion.2 = f32[64,1024]{1,0:T(8,128)} fusion(bf16[2048,64]{0,1:T(8,128)(2,1)} %copy-done.5, bf16[2048,1024]{1,0:T(8,128)(2,1)} %bitcast.162), kind=kOutput, calls=%fused_computation.16 | convolution fusion | flops 268500992 | bytes 4718592 | tf_op jit(solution)/shard_map/fa,fb->ab/dot_general | solution.py:243
  182.3 5.2 %all-to-all-done.1 = bf16[16,128,192]{1,2,0:T(8,128)(2,1)} async-done(((bf16[16,128,192]{1,2,0:T(8,128)(2,1)}), bf16[16,128,192]{1,2,0:T(8,128)(2,1)}, u32[]{:S(2)}, u32[]{:S(2)}) %all-to-all-start.1) | async-done | bytes 786464 | tf_op jit(solution)/shard_map/all_to_all | solution.py:281
  187.5 1.1 slice.627
  188.6 2.4 %fusion.196 = f32[128,1024]{1,0:T(8,128)S(1)} fusion(bf16[1024,1024]{1,0:T(8,128)(2,1)} %bitcast.166, bf16[128,2,1024]{0,2,1:T(8,128)(2,1)S(1)} %bitcast.171), kind=kOutput, calls=%fused_computation.294 | convolution fusion | flops 268435456 | bytes 2883584 | tf_op jit(solution)/shard_map/fe,ne->fn/dot_general | solution.py:292
  191.1 1.0 fusion.26
  192.2 1.2 all_to_all.20
  193.4 5.4 %all-to-all-start.2 = ((f32[16,1,8256]{2,1,0:T(1,128)}), f32[16,1,8256]{2,1,0:T(1,128)S(1)}, u32[]{:S(2)}, u32[]{:S(2)}) async-start(f32[16,1,8256]{2,1,0:T(1,128)} %all_to_all.20), calls=%async_computation.2 | async-start | bytes 1064960 | tf_op jit(solution)/shard_map/all_to_all | solution.py:297
  198.9 1.9 fusion.25
  200.8 2.9 %fusion.13 = bf16[128,1024]{1,0:T(8,128)(2,1)} fusion(bf16[16,448,1024]{2,1,0:T(8,128)(2,1)} %bitcast.158, bf16[128,1024]{1,0:T(8,128)(2,1)S(1)} %copy-done.3, bf16[16,128,192]{1,2,0:T(8,128)(2,1)} %all-to-all-done.1), kind=kOutput, calls=%fused_computation.15 | convolution fusion | flops 268828672 | bytes 2883584 | tf_op jit(solution)/shard_map/dot_general | solution.py:290
  203.7 9.8 %all-to-all-done.2 = f32[16,1,8256]{2,1,0:T(1,128)S(1)} async-done(((f32[16,1,8256]{2,1,0:T(1,128)}), f32[16,1,8256]{2,1,0:T(1,128)S(1)}, u32[]{:S(2)}, u32[]{:S(2)}) %all-to-all-start.2) | async-done | bytes 528416 | tf_op jit(solution)/shard_map/all_to_all | solution.py:297
  214.1 0.8 reshape.169
  215.5 1.2 reshape.170
  (52 shorter events, 5.8 us)
Async XLA Ops:
  7.2 122.4 %all-gather.3.cloned.1.call-start = ((), (), s32[]{:S(2)}) async-start(), calls=%async_computation.3 | async-start | bytes 15597568 | tf_op jit(solution)/shard_map/all_gather | solution.py:183
  11.9 0.9 copy-start.4
  14.9 13.9 %all-to-all-start = ((f32[16,1,192]{2,1,0:T(1,128)}), f32[16,1,192]{2,1,0:T(1,128)S(1)}, u32[]{:S(2)}, u32[]{:S(2)}) async-start(f32[16,1,192]{2,1,0:T(1,128)} %broadcast_in_dim.2), calls=%async_computation | async-start | bytes 32768 | tf_op jit(solution)/shard_map/all_to_all | solution.py:176
  132.4 7.6 %copy-start = (bf16[7168,1024]{1,0:T(8,128)(2,1)S(1)}, bf16[7168,1024]{1,0:T(8,128)(2,1)}, u32[]{:S(2)}) copy-start(bf16[7168,1024]{1,0:T(8,128)(2,1)} %all-gather.3.cloned.1.call-done) | copy-start | bytes 44040196
  140.0 10.8 %copy-start.1 = (bf16[16,128,1024]{2,1,0:T(8,128)(2,1)}, bf16[16,128,1024]{2,1,0:T(8,128)(2,1)S(1)}, u32[]{:S(2)}) copy-start(bf16[16,128,1024]{2,1,0:T(8,128)(2,1)S(1)} %get-tuple-element.48) | copy-start | bytes 12582916
  140.6 2.0 copy-start.2
  144.6 6.2 %copy-start.8 = (f32[64]{0:T(128)S(1)}, f32[64]{0:T(128)}, u32[]{:S(2)}) copy-start(f32[64]{0:T(128)} %param.15) | copy-start | bytes 772
  144.6 6.2 %copy-start.6 = (bf16[64,1024]{1,0:T(8,128)(2,1)S(1)}, bf16[64,1024]{1,0:T(8,128)(2,1)}, u32[]{:S(2)}) copy-start(bf16[64,1024]{1,0:T(8,128)(2,1)} %param.17) | copy-start | bytes 393220
  144.6 6.2 %copy-start.10 = (f32[64]{0:T(128)S(1)}, f32[64]{0:T(128)}, u32[]{:S(2)}) copy-start(f32[64]{0:T(128)} %param.16) | copy-start | bytes 772
  152.4 11.0 %copy-start.9 = (f32[64]{0:T(128)}, f32[64]{0:T(128)S(1)}, u32[]{:S(2)}) copy-start(f32[64]{0:T(128)S(1)} %get-tuple-element.42) | copy-start | bytes 772
  152.4 11.0 %copy-start.5 = (bf16[2048,64]{0,1:T(8,128)(2,1)}, bf16[2048,64]{0,1:T(8,128)(2,1)S(1)}, u32[]{:S(2)}) copy-start(bf16[2048,64]{0,1:T(8,128)(2,1)S(1)} %get-tuple-element.52) | copy-start | bytes 786436
  164.5 23.0 %all-to-all-start.1 = ((bf16[16,128,192]{1,2,0:T(8,128)(2,1)}), bf16[16,128,192]{1,2,0:T(8,128)(2,1)}, u32[]{:S(2)}, u32[]{:S(2)}) async-start(bf16[16,128,192]{1,2,0:T(8,128)(2,1)} %copy_bitcast_fusion), calls=%async_computation.1 | async-start | bytes 1572864 | tf_op jit(solution)/shard_map/all_to_all | solution.py:281
  178.4 12.7 %copy-start.3 = (bf16[128,1024]{1,0:T(8,128)(2,1)S(1)}, bf16[128,1024]{1,0:T(8,128)(2,1)}, u32[]{:S(2)}) copy-start(bf16[128,1024]{1,0:T(8,128)(2,1)} %param.9) | copy-start | bytes 786436
  178.4 12.7 %copy-start.7 = (f32[128]{0:T(128)S(1)}, f32[128]{0:T(128)}, u32[]{:S(2)}) copy-start(f32[128]{0:T(128)} %add_rsqrt_fusion) | copy-start | bytes 1540
  193.4 20.1 %all-to-all-start.2 = ((f32[16,1,8256]{2,1,0:T(1,128)}), f32[16,1,8256]{2,1,0:T(1,128)S(1)}, u32[]{:S(2)}, u32[]{:S(2)}) async-start(f32[16,1,8256]{2,1,0:T(1,128)} %all_to_all.20), calls=%async_computation.2 | async-start | bytes 1064960 | tf_op jit(solution)/shard_map/all_to_all | solution.py:297
Sparse Core Ops, SparseCore 0:
  13.0 116.5 all-gather.2

commit v6 on v5

--- a/solution.py
+++ b/solution.py
@@ -278,6 +278,28 @@
         jnp.einsum("fa,fb->ab", ln_x_all, grad_hidden, preferred_element_type=jnp.float32)
         * grad_scale
     )
+    moments = jnp.einsum(
+        "fa,fb->ab",
+        ln_all,
+        grad_hidden.astype(jnp.float32),
+        preferred_element_type=jnp.float32,
+        precision=lax.Precision.HIGHEST,
+    )
+    gain_part = jnp.sum(w_in_cols.astype(jnp.float32) * moments, axis=1) * grad_scale
+    packed = lax.all_to_all(
+        jnp.concatenate(
+            [in_cols.reshape(devices, share * 2 * share), gain_part.reshape(devices, share)],
+            axis=1,
+        ),
+        "seq", 0, 0, tiled=True,
+    )
+    grad_w_in = (
+        packed[:, : share * 2 * share]
+        .reshape(devices, share, 2, share)
+        .transpose(1, 2, 0, 3)
+        .reshape(share, 2 * width)
+    )
+    grad_ln_gain = jnp.sum(packed[:, share * 2 * share :], axis=0)
     back = lax.all_to_all(
         jnp.concatenate([activation, grad_hidden], axis=1).reshape(devices, rows, 3 * share),
         "seq", 0, 0, tiled=True,
@@ -293,21 +315,6 @@
         "fe,ne->fn", hidden_rows[:, 0], w_in_left, preferred_element_type=jnp.float32
     ) + jnp.einsum("fe,ne->fn", hidden_rows[:, 1], w_in_right, preferred_element_type=jnp.float32)
     ln_hat, rstd_ln = norm(frames)
-    gain_part = jnp.sum(grad_ln * ln_hat, axis=0) * grad_scale
-    packed = lax.all_to_all(
-        jnp.concatenate(
-            [in_cols.reshape(devices, share * 2 * share), gain_part.reshape(devices, share)],
-            axis=1,
-        ),
-        "seq", 0, 0, tiled=True,
-    )
-    grad_w_in = (
-        packed[:, : share * 2 * share]
-        .reshape(devices, share, 2, share)
-        .transpose(1, 2, 0, 3)
-        .reshape(share, 2 * width)
-    )
-    grad_ln_gain = jnp.sum(packed[:, share * 2 * share :], axis=0)
     grad_hat = grad_ln * gains
     grad_input = rstd_ln * (
         grad_hat

time: 224 us -> 242 us (1.080)
  other arithmetic: 37.7 us -> 50.1 us
  local copies, waits for them, and re-layouts: 21.6 us -> 29.5 us
  waiting for transfers between devices: 117 us -> 110 us
  matrix products: 15.4 us -> 19.5 us
    all_to_all x1, waiting for transfers between devices: 5.23 us -> 0.01 us  [channel_local(): lax.all_to_all(jnp.concatenate([activation, grad_hidden], axis=1).reshape...]
    slice x1, other arithmetic: 4.35 us -> 9.34 us  [channel_local(): grad_all = pieces[:, rows:2 * rows].reshape(stream, width)]
    mul x1 -> x2, other arithmetic: 0.01 us -> 4.14 us  [the longest x1 4.14 us: norm(): return (centred * rstd, rstd)]
    reshape x2, local copies, waits for them, and re-layouts: 1.91 us -> 5.16 us  [channel_local(): grad_w_in = packed[:, :share * 2 * share].reshape(devices, share, 2, shar...]
    dot_general x0 -> x1, matrix products: none -> 2.98 us  [channel_local(): jnp.einsum('fa,fb->ab', ln_all, grad_hidden.astype(jnp.float32), preferre...]
    unnamed x28 -> x228, local copies, waits for them, and re-layouts: 8.37 us -> 9.18 us
  transfers between devices with their start and end apart: 4 -> 4, of which waited for: 4 -> 3; matrix products, arithmetic and copies ran while one was open for 11% -> 15% of each run, Pallas kernels for 0% -> 0%
where the time goes in v6:
time: 242 us; the launch traced here: 241 us
  waiting for transfers between devices  110 us (45%)
  other arithmetic  50.1 us (21%)
  local copies, waits for them, and re-layouts  29.5 us (12%)
  matrix products  19.5 us (8%)
  starting transfers between devices  16.2 us (7%)
  between operations  15.8 us (7%)
    all_gather x1, waiting for transfers between devices, channel_local(): lax.all_gather(jnp.concatenate([frames, out_grad, w_out, w_in[:, :width],...  100 us
    slice x1, other arithmetic, channel_local(): grad_all = pieces[:, rows:2 * rows].reshape(stream, width)  9.34 us
    unnamed x228, local copies, waits for them, and re-layouts  9.18 us
    reduce_sum x6, other arithmetic, channel_local(): jnp.sum(grad_conv * padded_glu[tap_index:tap_index + stream].astype(jnp.f...  8.88 us
    all_to_all x1, waiting for transfers between devices, channel_local(): lax.all_to_all(jnp.concatenate([in_cols.reshape(devices, share * 2 * shar...  7.97 us
    all_to_all x1, starting transfers between devices, spread(): return lax.all_to_all(copies, 'seq', 0, 0, tiled=True)  7.39 us
    another operation x2, other arithmetic  6.46 us
    reshape x2, local copies, waits for them, and re-layouts, channel_local(): grad_w_in = packed[:, :share * 2 * share].reshape(devices, share, 2, shar...  5.16 us
  transfers between devices with their start and end apart: 4, of which 3 were waited for; matrix products, arithmetic and copies ran while one was open for 15% of the time, Pallas kernels for 0%

profile of v6, /device:TPU:0, one launch (start us, length us, event | category | flops | bytes accessed | tf_op | source)
XLA Modules:
  0.0 240.7 jit_solution(14975441684210303672)
XLA Ops:
  7.2 1.0 constant_dynamic-update-slice_fusion.2
  8.2 1.0 constant_dynamic-update-slice_fusion.1
  9.2 0.9 constant_dynamic-update-slice_fusion
  10.1 0.9 slice_dynamic-update-slice_fusion.1
  11.0 0.9 slice_dynamic-update-slice_fusion
  11.9 0.9 copy-done.5
  14.9 7.4 %all-to-all-start = ((f32[16,1,192]{2,1,0:T(1,128)}), f32[16,1,192]{2,1,0:T(1,128)S(1)}, u32[]{:S(2)}, u32[]{:S(2)}) async-start(f32[16,1,192]{2,1,0:T(1,128)} %broadcast_in_dim.2), calls=%async_computation | async-start | bytes 32768 | tf_op jit(solution)/shard_map/all_to_all | solution.py:176
  22.3 1.5 slice_bitcast_fusion.35
  23.9 1.7 slice_bitcast_fusion.36
  25.5 1.7 convert_reduce_fusion
  27.2 1.6 all-to-all-done
  29.5 100.1 %all-gather.3.cloned.1.call-done = bf16[7168,1024]{1,0:T(8,128)(2,1)} async-done(((bf16[448,1024]{1,0:T(8,128)(2,1)}), bf16[7168,1024]{1,0:T(8,128)(2,1)}) %all-gather.3.cloned.1.call-update) | async-done | bytes 14680080 | tf_op jit(solution)/shard_map/all_gather | solution.py:183
  129.6 2.8 %fusion.1 = f32[16,128]{1,0:T(8,128)S(1)} fusion(bf16[16,448,1024]{2,1,0:T(8,128)(2,1)} %bitcast.151), kind=kLoop, calls=%fused_computation.5 | loop fusion | flops 4192256 | bytes 4202496 | tf_op jit(solution)/shard_map/reduce_sum | solution.py:205
  132.4 9.3 %fusion.266 = (bf16[16,128,1024]{2,1,0:T(8,128)(2,1)}, f32[16,128,1024]{2,1,0:T(8,128)}) fusion(bf16[16,448,1024]{2,1,0:T(8,128)(2,1)} %bitcast.152), kind=kLoop, calls=%fused_computation.451 | loop fusion | flops 2097152 | bytes 20971520 | tf_op jit(solution)/shard_map/slice | solution.py:189
  141.8 2.7 %copy-done = bf16[7168,1024]{1,0:T(8,128)(2,1)S(1)} copy-done((bf16[7168,1024]{1,0:T(8,128)(2,1)S(1)}, bf16[7168,1024]{1,0:T(8,128)(2,1)}, u32[]{:S(2)}) %copy-start) | copy-done | bytes 14680088
  145.0 1.4 multiply_reduce_fusion
  147.0 4.1 %fusion = f32[2048,1024]{1,0:T(8,128)S(1)} fusion(f32[16,128,1024]{2,1,0:T(8,128)} %get-tuple-element.48, f32[2048]{0:T(1024)S(1)} %rsqrt_bitcast_fusion, f32[2048]{0:T(1024)S(1)} %get-tuple-element.113), kind=kLoop, calls=%fused_computation.1 | loop fusion | flops 4194304 | bytes 16793600 | tf_op jit(solution)/shard_map/mul | solution.py:208
  151.2 1.5 fusion.6
  153.2 4.9 %fusion.264 = (f32[64]{0:T(128)S(1)}, f32[2048,64]{0,1:T(8,128)S(1)}) fusion(f32[2048]{0:T(1024)S(1)} %get-tuple-element.101, f32[64]{0:T(128)} %get-tuple-element.81, f32[2048]{0:T(1024)S(1)} %get-tuple-element.84, f32[64]{0:T(128)} %get-tuple-element.82, f32[2048]{0:T(1024)S(1)} %get-tuple-element.85, f32[64]{0:T(128)} %get-tuple-element.53, ...), kind=kLoop, calls=%fused_computation.450 | loop fusion | flops 16121792 | bytes 1040384 | tf_op jit(solution)/shard_map/reduce_sum | solution.py:233
  158.8 2.8 %fusion.263 = (f32[64]{0:T(128)S(1)}, f32[64]{0:T(128)S(1)}, bf16[2048,64]{0,1:T(8,128)(2,1)}, f32[2048,64]{0,1:T(8,128)S(1)}) fusion(f32[64]{0:T(128)S(1)} %get-tuple-element.118, f32[2048,64]{0,1:T(8,128)S(1)} %get-tuple-element.46, f32[64]{0:T(128)S(1)} %broadcast_multiply_fusion.9, f32[64]{0:T(128)} %param.16, f32[64]{0:T(128)S(1)} %copy-done.108, ...), kind=kOutput, calls=%fused_computation.449 | convolution fusion | flops 270663552 | bytes 5637632 | tf_op jit(solution)/shard_map/fe,ne->fn/dot_general | solution.py:246
  162.2 1.6 fusion.149
  164.1 6.3 %multiply_convert_fusion.6 = (bf16[2048,64]{0,1:T(8,128)(2,1)S(1)}, f32[2048,64]{0,1:T(8,128)S(1)}) fusion(f32[2048,128]{0,1:T(8,128)S(1)} %fusion.6, f32[2048]{0:T(1024)S(1)} %copy-done.73, f32[64]{0:T(128)} %get-tuple-element.81, f32[2048]{0:T(1024)S(1)} %copy-done.71, f32[64]{0:T(128)} %get-tuple-element.82, f32[2048]{0:T(1024)S(1)} %copy-done.69, ...), kind=kLoop, calls=%fused_computation.226 | loop fusion | flops 12582912 | bytes 2088704 | tf_op jit(solution)/shard_map/convert.1
  170.6 2.1 fusion.7
  172.7 3.0 %fusion.18 = f32[1024]{0:T(1024)S(1)} fusion(f32[2048,1024]{1,0:T(8,128)S(1)} %fusion, bf16[2048,64]{0,1:T(8,128)(2,1)S(1)} %multiply_convert_fusion.5, bf16[2048,64]{0,1:T(8,128)(2,1)S(1)} %get-tuple-element.43, bf16[1024,64]{0,1:T(8,128)(2,1)S(1)} %copy-done.7, bf16[1024,64]{0,1:T(8,128)(2,1)S(1)} %copy.37), kind=kOutput, calls=%fused_computation.19 | convolution fusion | flops 3223059456 | bytes 9179136 | tf_op jit(solution)/shard_map/fa,fb->ab/dot_general | solution.py:281
  175.8 2.1 reshape.168
  177.9 1.1 pad_maximum_fusion
  179.1 1.2 all_to_all.20
  180.3 4.2 %all-to-all-start.2 = ((f32[16,1,8256]{2,1,0:T(1,128)}), f32[16,1,8256]{2,1,0:T(1,128)}, u32[]{:S(2)}, u32[]{:S(2)}) async-start(f32[16,1,8256]{2,1,0:T(1,128)} %all_to_all.20), calls=%async_computation.2 | async-start | bytes 1064960 | tf_op jit(solution)/shard_map/all_to_all | solution.py:289
  186.0 2.1 copy_bitcast_fusion
  188.1 1.4 fusion.125
  189.6 1.6 fusion.91
  191.2 8.0 %all-to-all-done.2 = f32[16,1,8256]{2,1,0:T(1,128)} async-done(((f32[16,1,8256]{2,1,0:T(1,128)}), f32[16,1,8256]{2,1,0:T(1,128)}, u32[]{:S(2)}, u32[]{:S(2)}) %all-to-all-start.2) | async-done | bytes 528416 | tf_op jit(solution)/shard_map/all_to_all | solution.py:289
  199.2 4.5 %all-to-all-start.1 = ((bf16[16,128,192]{1,2,0:T(8,128)(2,1)}), bf16[16,128,192]{1,2,0:T(8,128)(2,1)}, u32[]{:S(2)}, u32[]{:S(2)}) async-start(bf16[16,128,192]{1,2,0:T(8,128)(2,1)} %copy_bitcast_fusion), calls=%async_computation.1 | async-start | bytes 1572864 | tf_op jit(solution)/shard_map/all_to_all | solution.py:303
  203.7 1.5 fusion.55
  205.2 2.1 fusion.73
  208.1 1.4 stack.127
  209.5 1.1 broadcast_multiply_fusion.4
  211.3 3.7 %convolution_multiply_fusion.2 = f32[64,1024]{1,0:T(8,128)} fusion(bf16[2048,64]{0,1:T(8,128)(2,1)S(1)} %copy-done.9, bf16[2048,1024]{1,0:T(8,128)(2,1)} %bitcast.156), kind=kOutput, calls=%fused_computation.20 | convolution fusion | flops 268500992 | bytes 4718592 | tf_op jit(solution)/shard_map/fa,fb->ab/dot_general | solution.py:243
  215.0 1.1 copy.43
  216.1 0.8 slice.630
  216.9 2.8 %reshape.169 = f32[16,64,2,64]{3,2,1,0:T(2,128)} reshape(f32[16,8192]{1,0:T(8,128)} %slice.630) | data formatting | bytes 1048576 | tf_op jit(solution)/shard_map/reshape | solution.py:298
  219.7 2.8 %copy.34 = f32[64,2,16,64]{3,2,1,0:T(8,128)} copy(f32[64,2,16,64]{3,1,0,2:T(2,128)} %bitcast.162) | data formatting | bytes 1048576 | tf_op jit(solution)/shard_map/transpose | solution.py:299
  222.5 2.4 reshape.170
  225.4 1.1 slice.627
  226.6 2.4 %fusion.194 = f32[128,1024]{1,0:T(8,128)S(1)} fusion(bf16[1024,1024]{1,0:T(8,128)(2,1)} %bitcast.161, bf16[128,2,1024]{0,2,1:T(8,128)(2,1)S(1)} %bitcast.166), kind=kOutput, calls=%fused_computation.293 | convolution fusion | flops 268435456 | bytes 2883584 | tf_op jit(solution)/shard_map/fe,ne->fn/dot_general | solution.py:314
  229.0 1.0 fusion.262
  230.0 1.0 fusion.27
  231.0 2.9 %fusion.15 = bf16[128,1024]{1,0:T(8,128)(2,1)} fusion(bf16[16,448,1024]{2,1,0:T(8,128)(2,1)} %bitcast.153, bf16[128,1024]{1,0:T(8,128)(2,1)S(1)} %copy-done.3, bf16[16,128,192]{1,2,0:T(8,128)(2,1)} %all-to-all-done.1), kind=kOutput, calls=%fused_computation.18 | convolution fusion | flops 268828672 | bytes 2883584 | tf_op jit(solution)/shard_map/dot_general | solution.py:312
  (253 shorter events, 8.5 us)
Async XLA Ops:
  7.2 122.4 %all-gather.3.cloned.1.call-start = ((), (), s32[]{:S(2)}) async-start(), calls=%async_computation.3 | async-start | bytes 15597568 | tf_op jit(solution)/shard_map/all_gather | solution.py:183
  14.9 13.9 %all-to-all-start = ((f32[16,1,192]{2,1,0:T(1,128)}), f32[16,1,192]{2,1,0:T(1,128)S(1)}, u32[]{:S(2)}, u32[]{:S(2)}) async-start(f32[16,1,192]{2,1,0:T(1,128)} %broadcast_in_dim.2), calls=%async_computation | async-start | bytes 32768 | tf_op jit(solution)/shard_map/all_to_all | solution.py:176
  23.8 129.1 %copy-start.85 = (f32[64]{0:T(128)}, f32[64]{0:T(128)S(1)}, u32[]{:S(2)}) copy-start(f32[64]{0:T(128)S(1)} %get-tuple-element.72) | copy-start | bytes 772
  23.8 129.1 %copy-start.87 = (f32[64]{0:T(128)}, f32[64]{0:T(128)S(1)}, u32[]{:S(2)}) copy-start(f32[64]{0:T(128)S(1)} %get-tuple-element.73) | copy-start | bytes 772
  23.8 129.1 %copy-start.89 = (f32[64]{0:T(128)}, f32[64]{0:T(128)S(1)}, u32[]{:S(2)}) copy-start(f32[64]{0:T(128)S(1)} %get-tuple-element.74) | copy-start | bytes 772
  23.8 129.1 %copy-start.91 = (f32[64]{0:T(128)}, f32[64]{0:T(128)S(1)}, u32[]{:S(2)}) copy-start(f32[64]{0:T(128)S(1)} %get-tuple-element.75) | copy-start | bytes 772
  23.8 129.1 %copy-start.93 = (f32[64]{0:T(128)}, f32[64]{0:T(128)S(1)}, u32[]{:S(2)}) copy-start(f32[64]{0:T(128)S(1)} %get-tuple-element.76) | copy-start | bytes 772
  23.9 129.1 %copy-start.95 = (f32[64]{0:T(128)}, f32[64]{0:T(128)S(1)}, u32[]{:S(2)}) copy-start(f32[64]{0:T(128)S(1)} %get-tuple-element.77) | copy-start | bytes 772
  23.9 129.1 %copy-start.97 = (f32[64]{0:T(128)}, f32[64]{0:T(128)S(1)}, u32[]{:S(2)}) copy-start(f32[64]{0:T(128)S(1)} %get-tuple-element.78) | copy-start | bytes 772
  23.9 129.1 %copy-start.99 = (f32[64]{0:T(128)}, f32[64]{0:T(128)S(1)}, u32[]{:S(2)}) copy-start(f32[64]{0:T(128)S(1)} %get-tuple-element.79) | copy-start | bytes 772
  29.1 123.9 %copy-start.56 = (f32[2048]{0:T(1024)}, f32[2048]{0:T(1024)S(1)}, u32[]{:S(2)}) copy-start(f32[2048]{0:T(1024)S(1)} %get-tuple-element.106) | copy-start | bytes 24580
  29.1 123.9 %copy-start.59 = (f32[2048]{0:T(1024)}, f32[2048]{0:T(1024)S(1)}, u32[]{:S(2)}) copy-start(f32[2048]{0:T(1024)S(1)} %get-tuple-element.107) | copy-start | bytes 24580
  29.1 123.9 %copy-start.62 = (f32[2048]{0:T(1024)}, f32[2048]{0:T(1024)S(1)}, u32[]{:S(2)}) copy-start(f32[2048]{0:T(1024)S(1)} %get-tuple-element.108) | copy-start | bytes 24580
  29.1 123.9 %copy-start.65 = (f32[2048]{0:T(1024)}, f32[2048]{0:T(1024)S(1)}, u32[]{:S(2)}) copy-start(f32[2048]{0:T(1024)S(1)} %get-tuple-element.109) | copy-start | bytes 24580
  29.1 123.9 %copy-start.68 = (f32[2048]{0:T(1024)}, f32[2048]{0:T(1024)S(1)}, u32[]{:S(2)}) copy-start(f32[2048]{0:T(1024)S(1)} %get-tuple-element.110) | copy-start | bytes 24580
  29.1 123.9 %copy-start.70 = (f32[2048]{0:T(1024)}, f32[2048]{0:T(1024)S(1)}, u32[]{:S(2)}) copy-start(f32[2048]{0:T(1024)S(1)} %get-tuple-element.111) | copy-start | bytes 24580
  29.2 123.9 %copy-start.72 = (f32[2048]{0:T(1024)}, f32[2048]{0:T(1024)S(1)}, u32[]{:S(2)}) copy-start(f32[2048]{0:T(1024)S(1)} %get-tuple-element.112) | copy-start | bytes 24580
  29.2 123.9 %copy-start.74 = (f32[2048]{0:T(1024)}, f32[2048]{0:T(1024)S(1)}, u32[]{:S(2)}) copy-start(f32[2048]{0:T(1024)S(1)} %get-tuple-element.102) | copy-start | bytes 24580
  29.2 123.9 %copy-start.76 = (f32[2048]{0:T(1024)}, f32[2048]{0:T(1024)S(1)}, u32[]{:S(2)}) copy-start(f32[2048]{0:T(1024)S(1)} %get-tuple-element.103) | copy-start | bytes 24580
  29.2 123.9 %copy-start.78 = (f32[2048]{0:T(1024)}, f32[2048]{0:T(1024)S(1)}, u32[]{:S(2)}) copy-start(f32[2048]{0:T(1024)S(1)} %get-tuple-element.104) | copy-start | bytes 24580
  29.2 123.9 %copy-start.80 = (f32[2048]{0:T(1024)}, f32[2048]{0:T(1024)S(1)}, u32[]{:S(2)}) copy-start(f32[2048]{0:T(1024)S(1)} %get-tuple-element.105) | copy-start | bytes 24580
  29.2 123.9 %copy-start.82 = (f32[2048]{0:T(1024)}, f32[2048]{0:T(1024)S(1)}, u32[]{:S(2)}) copy-start(f32[2048]{0:T(1024)S(1)} %get-tuple-element.101) | copy-start | bytes 24580
  29.3 123.7 %copy-start.10 = (f32[2048]{0:T(1024)}, f32[2048]{0:T(1024)S(1)}, u32[]{:S(2)}) copy-start(f32[2048]{0:T(1024)S(1)} %get-tuple-element.95) | copy-start | bytes 24580
  29.3 123.7 %copy-start.13 = (f32[2048]{0:T(1024)}, f32[2048]{0:T(1024)S(1)}, u32[]{:S(2)}) copy-start(f32[2048]{0:T(1024)S(1)} %get-tuple-element.96) | copy-start | bytes 24580
  29.4 123.7 %copy-start.16 = (f32[2048]{0:T(1024)}, f32[2048]{0:T(1024)S(1)}, u32[]{:S(2)}) copy-start(f32[2048]{0:T(1024)S(1)} %get-tuple-element.97) | copy-start | bytes 24580
  29.4 123.7 %copy-start.19 = (f32[2048]{0:T(1024)}, f32[2048]{0:T(1024)S(1)}, u32[]{:S(2)}) copy-start(f32[2048]{0:T(1024)S(1)} %get-tuple-element.98) | copy-start | bytes 24580
  29.4 123.7 %copy-start.22 = (f32[2048]{0:T(1024)}, f32[2048]{0:T(1024)S(1)}, u32[]{:S(2)}) copy-start(f32[2048]{0:T(1024)S(1)} %get-tuple-element.99) | copy-start | bytes 24580
  29.4 123.7 %copy-start.25 = (f32[2048]{0:T(1024)}, f32[2048]{0:T(1024)S(1)}, u32[]{:S(2)}) copy-start(f32[2048]{0:T(1024)S(1)} %get-tuple-element.100) | copy-start | bytes 24580
  29.4 123.7 %copy-start.28 = (f32[2048]{0:T(1024)}, f32[2048]{0:T(1024)S(1)}, u32[]{:S(2)}) copy-start(f32[2048]{0:T(1024)S(1)} %get-tuple-element.89) | copy-start | bytes 24580
  29.4 123.7 %copy-start.31 = (f32[2048]{0:T(1024)}, f32[2048]{0:T(1024)S(1)}, u32[]{:S(2)}) copy-start(f32[2048]{0:T(1024)S(1)} %get-tuple-element.90) | copy-start | bytes 24580
  29.4 123.7 %copy-start.34 = (f32[2048]{0:T(1024)}, f32[2048]{0:T(1024)S(1)}, u32[]{:S(2)}) copy-start(f32[2048]{0:T(1024)S(1)} %get-tuple-element.91) | copy-start | bytes 24580
  29.4 123.7 %copy-start.37 = (f32[2048]{0:T(1024)}, f32[2048]{0:T(1024)S(1)}, u32[]{:S(2)}) copy-start(f32[2048]{0:T(1024)S(1)} %get-tuple-element.92) | copy-start | bytes 24580
  29.4 123.7 %copy-start.40 = (f32[2048]{0:T(1024)}, f32[2048]{0:T(1024)S(1)}, u32[]{:S(2)}) copy-start(f32[2048]{0:T(1024)S(1)} %get-tuple-element.93) | copy-start | bytes 24580
  29.4 123.7 %copy-start.43 = (f32[2048]{0:T(1024)}, f32[2048]{0:T(1024)S(1)}, u32[]{:S(2)}) copy-start(f32[2048]{0:T(1024)S(1)} %get-tuple-element.94) | copy-start | bytes 24580
  29.5 123.7 %copy-start.46 = (f32[2048]{0:T(1024)}, f32[2048]{0:T(1024)S(1)}, u32[]{:S(2)}) copy-start(f32[2048]{0:T(1024)S(1)} %get-tuple-element.84) | copy-start | bytes 24580
  29.5 123.7 %copy-start.48 = (f32[2048]{0:T(1024)}, f32[2048]{0:T(1024)S(1)}, u32[]{:S(2)}) copy-start(f32[2048]{0:T(1024)S(1)} %get-tuple-element.85) | copy-start | bytes 24580
  29.5 123.7 %copy-start.50 = (f32[2048]{0:T(1024)}, f32[2048]{0:T(1024)S(1)}, u32[]{:S(2)}) copy-start(f32[2048]{0:T(1024)S(1)} %get-tuple-element.86) | copy-start | bytes 24580
  29.5 123.7 %copy-start.52 = (f32[2048]{0:T(1024)}, f32[2048]{0:T(1024)S(1)}, u32[]{:S(2)}) copy-start(f32[2048]{0:T(1024)S(1)} %get-tuple-element.87) | copy-start | bytes 24580
  29.5 123.7 %copy-start.54 = (f32[2048]{0:T(1024)}, f32[2048]{0:T(1024)S(1)}, u32[]{:S(2)}) copy-start(f32[2048]{0:T(1024)S(1)} %get-tuple-element.88) | copy-start | bytes 24580
  179.0 26.2 %copy-start.58 = (f32[2048]{0:T(1024)S(1)}, f32[2048]{0:T(1024)}, u32[]{:S(2)}) copy-start(f32[2048]{0:T(1024)} %copy-done.56) | copy-start | bytes 24580
  179.0 26.1 %copy-start.61 = (f32[2048]{0:T(1024)S(1)}, f32[2048]{0:T(1024)}, u32[]{:S(2)}) copy-start(f32[2048]{0:T(1024)} %copy-done.59) | copy-start | bytes 24580
  179.0 26.1 %copy-start.64 = (f32[2048]{0:T(1024)S(1)}, f32[2048]{0:T(1024)}, u32[]{:S(2)}) copy-start(f32[2048]{0:T(1024)} %copy-done.62) | copy-start | bytes 24580
  179.1 28.2 %copy-start.12 = (f32[2048]{0:T(1024)S(1)}, f32[2048]{0:T(1024)}, u32[]{:S(2)}) copy-start(f32[2048]{0:T(1024)} %copy-done.10) | copy-start | bytes 24580
  179.1 28.2 %copy-start.15 = (f32[2048]{0:T(1024)S(1)}, f32[2048]{0:T(1024)}, u32[]{:S(2)}) copy-start(f32[2048]{0:T(1024)} %copy-done.13) | copy-start | bytes 24580
  179.1 28.2 %copy-start.18 = (f32[2048]{0:T(1024)S(1)}, f32[2048]{0:T(1024)}, u32[]{:S(2)}) copy-start(f32[2048]{0:T(1024)} %copy-done.16) | copy-start | bytes 24580
  179.1 28.2 %copy-start.21 = (f32[2048]{0:T(1024)S(1)}, f32[2048]{0:T(1024)}, u32[]{:S(2)}) copy-start(f32[2048]{0:T(1024)} %copy-done.19) | copy-start | bytes 24580
  180.3 18.9 %all-to-all-start.2 = ((f32[16,1,8256]{2,1,0:T(1,128)}), f32[16,1,8256]{2,1,0:T(1,128)}, u32[]{:S(2)}, u32[]{:S(2)}) async-start(f32[16,1,8256]{2,1,0:T(1,128)} %all_to_all.20), calls=%async_computation.2 | async-start | bytes 1064960 | tf_op jit(solution)/shard_map/all_to_all | solution.py:289
  199.2 26.3 %all-to-all-start.1 = ((bf16[16,128,192]{1,2,0:T(8,128)(2,1)}), bf16[16,128,192]{1,2,0:T(8,128)(2,1)}, u32[]{:S(2)}, u32[]{:S(2)}) async-start(bf16[16,128,192]{1,2,0:T(8,128)(2,1)} %copy_bitcast_fusion), calls=%async_computation.1 | async-start | bytes 1572864 | tf_op jit(solution)/shard_map/all_to_all | solution.py:303
  (66 other events, 518.1 us)
Sparse Core Ops, SparseCore 0:
  13.0 116.5 all-gather.2

commit v7 on v5

--- a/solution.py
+++ b/solution.py
@@ -278,10 +278,34 @@
         jnp.einsum("fa,fb->ab", ln_x_all, grad_hidden, preferred_element_type=jnp.float32)
         * grad_scale
     )
+    head = lax.reduce_precision(in_cols, exponent_bits=8, mantissa_bits=7)
+    tail = in_cols - head
+    w_rows = width // devices
+    weight_part = jnp.concatenate(
+        [
+            head.astype(jnp.bfloat16).reshape(devices, w_rows, 2 * share),
+            tail.astype(jnp.bfloat16).reshape(devices, w_rows, 2 * share),
+        ],
+        axis=1,
+    )
     back = lax.all_to_all(
-        jnp.concatenate([activation, grad_hidden], axis=1).reshape(devices, rows, 3 * share),
+        jnp.concatenate(
+            [
+                jnp.concatenate([activation, grad_hidden], axis=1).reshape(devices, rows, 3 * share),
+                weight_part,
+            ],
+            axis=2,
+        ),
         "seq", 0, 0, tiled=True,
     )
+    weight_back = back[:, : 2 * w_rows, 3 * share :].astype(jnp.float32)
+    grad_w_in = (
+        (weight_back[:, :w_rows] + weight_back[:, w_rows:])
+        .reshape(devices, w_rows, 2, share)
+        .transpose(1, 2, 0, 3)
+        .reshape(w_rows, 2 * width)
+    )
+    back = back[:, :, : 3 * share]
     act_rows = back[:, :, :share].transpose(1, 0, 2).reshape(rows, width)
     hidden_rows = (
         back[:, :, share:].reshape(devices, rows, 2, share).transpose(1, 2, 0, 3)
@@ -294,20 +318,9 @@
     ) + jnp.einsum("fe,ne->fn", hidden_rows[:, 1], w_in_right, preferred_element_type=jnp.float32)
     ln_hat, rstd_ln = norm(frames)
     gain_part = jnp.sum(grad_ln * ln_hat, axis=0) * grad_scale
-    packed = lax.all_to_all(
-        jnp.concatenate(
-            [in_cols.reshape(devices, share * 2 * share), gain_part.reshape(devices, share)],
-            axis=1,
-        ),
-        "seq", 0, 0, tiled=True,
-    )
-    grad_w_in = (
-        packed[:, : share * 2 * share]
-        .reshape(devices, share, 2, share)
-        .transpose(1, 2, 0, 3)
-        .reshape(share, 2 * width)
-    )
-    grad_ln_gain = jnp.sum(packed[:, share * 2 * share :], axis=0)
+    grad_ln_gain = jnp.sum(
+        lax.all_to_all(gain_part.reshape(devices, share), "seq", 0, 0, tiled=True), axis=0
+    )
     grad_hat = grad_ln * gains
     grad_input = rstd_ln * (
         grad_hat

time: 224 us -> 231 us (1.031)
  other arithmetic: 37.7 us -> 42.1 us
  starting transfers between devices: 17.2 us -> 19.8 us
    all_to_all x2, waiting for transfers between devices: 15 us -> 11.7 us  [the longest x1 11.7 us: channel_local(): lax.all_to_all(jnp.concatenate([jnp.concatenate([activation, grad_hidden]...]
    concatenate x1, other arithmetic: 0.04 us -> 2.91 us  [channel_local(): jnp.concatenate([jnp.concatenate([activation, grad_hidden], axis=1).resha...]
    all_to_all x2, starting transfers between devices: 9.73 us -> 12.4 us  [the longest x1 7.99 us: channel_local(): lax.all_to_all(gain_part.reshape(devices, share), 'seq', 0, 0, tiled=True)]
    all_to_all x1, waiting for transfers between devices: 1.75 us -> 4.33 us  [spread(): return lax.all_to_all(copies, 'seq', 0, 0, tiled=True)]
    unnamed x28 -> x139, local copies, waits for them, and re-layouts: 8.37 us -> 9.12 us
  transfers between devices with their start and end apart: 4 -> 4, of which waited for: 4 -> 3; matrix products, arithmetic and copies ran while one was open for 11% -> 12% of each run, Pallas kernels for 0% -> 0%
where the time goes in v7:
time: 231 us; the launch traced here: 230 us
  waiting for transfers between devices  116 us (50%)
  other arithmetic  42.1 us (18%)
  local copies, waits for them, and re-layouts  22.3 us (10%)
  starting transfers between devices  19.8 us (9%)
  between operations  15.2 us (7%)
  matrix products  14.4 us (6%)
    all_gather x1, waiting for transfers between devices, channel_local(): lax.all_gather(jnp.concatenate([frames, out_grad, w_out, w_in[:, :width],...  100 us
    all_to_all x1, waiting for transfers between devices, channel_local(): lax.all_to_all(jnp.concatenate([jnp.concatenate([activation, grad_hidden]...  11.7 us
    unnamed x139, local copies, waits for them, and re-layouts  9.12 us
    reduce_sum x6, other arithmetic, channel_local(): jnp.sum(grad_conv * padded_glu[tap_index:tap_index + stream].astype(jnp.f...  8.36 us
    all_to_all x1, starting transfers between devices, channel_local(): lax.all_to_all(gain_part.reshape(devices, share), 'seq', 0, 0, tiled=True)  7.99 us
    all_to_all x1, starting transfers between devices, spread(): return lax.all_to_all(copies, 'seq', 0, 0, tiled=True)  7.39 us
    another operation x2, other arithmetic  5.46 us
  transfers between devices with their start and end apart: 4, of which 3 were waited for; matrix products, arithmetic and copies ran while one was open for 12% of the time, Pallas kernels for 0%

profile of v7, /device:TPU:0, one launch (start us, length us, event | category | flops | bytes accessed | tf_op | source)
XLA Modules:
  0.0 230.2 jit_solution(14216532977970291570)
XLA Ops:
  7.2 1.0 constant_dynamic-update-slice_fusion.2
  8.2 1.0 constant_dynamic-update-slice_fusion.1
  9.2 0.9 constant_dynamic-update-slice_fusion
  10.1 0.9 slice_dynamic-update-slice_fusion.1
  11.0 0.9 slice_dynamic-update-slice_fusion
  11.9 0.9 copy-done.5
  12.9 0.7 convert_element_type.274
  13.5 0.7 pad_maximum_fusion
  14.3 0.6 broadcast_in_dim.2
  14.9 7.4 %all-to-all-start = ((f32[16,1,192]{2,1,0:T(1,128)}), f32[16,1,192]{2,1,0:T(1,128)S(1)}, u32[]{:S(2)}, u32[]{:S(2)}) async-start(f32[16,1,192]{2,1,0:T(1,128)} %broadcast_in_dim.2), calls=%async_computation | async-start | bytes 32768 | tf_op jit(solution)/shard_map/all_to_all | solution.py:176
  22.3 1.0 slice_bitcast_fusion.36
  23.4 1.0 slice_bitcast_fusion.35
  24.5 4.3 %all-to-all-done = f32[16,1,192]{2,1,0:T(1,128)S(1)} async-done(((f32[16,1,192]{2,1,0:T(1,128)}), f32[16,1,192]{2,1,0:T(1,128)S(1)}, u32[]{:S(2)}, u32[]{:S(2)}) %all-to-all-start) | async-done | bytes 12320 | tf_op jit(solution)/shard_map/all_to_all | solution.py:176
  29.3 100.3 %all-gather.3.cloned.1.call-done = bf16[7168,1024]{1,0:T(8,128)(2,1)} async-done(((bf16[448,1024]{1,0:T(8,128)(2,1)}), bf16[7168,1024]{1,0:T(8,128)(2,1)}) %all-gather.3.cloned.1.call-update) | async-done | bytes 14680080 | tf_op jit(solution)/shard_map/all_gather | solution.py:183
  129.6 2.8 %fusion.3 = f32[16,128]{1,0:T(8,128)S(1)} fusion(bf16[16,448,1024]{2,1,0:T(8,128)(2,1)} %bitcast.158), kind=kLoop, calls=%fused_computation.6 | loop fusion | flops 4192256 | bytes 4202496 | tf_op jit(solution)/shard_map/reduce_sum | solution.py:205
  132.4 4.3 %fusion.271 = (bf16[16,128,1024]{2,1,0:T(8,128)(2,1)S(1)}, f32[16,128,1024]{2,1,0:T(8,128)S(1)}) fusion(bf16[16,448,1024]{2,1,0:T(8,128)(2,1)} %bitcast.159), kind=kLoop, calls=%fused_computation.456 | loop fusion | flops 2097152 | bytes 20971520 | tf_op jit(solution)/shard_map/slice | solution.py:189
  136.7 3.3 %copy-done = bf16[7168,1024]{1,0:T(8,128)(2,1)S(1)} copy-done((bf16[7168,1024]{1,0:T(8,128)(2,1)S(1)}, bf16[7168,1024]{1,0:T(8,128)(2,1)}, u32[]{:S(2)}) %copy-start) | copy-done | bytes 14680088
  140.6 1.4 multiply_reduce_fusion
  142.6 1.9 fusion.2
  144.6 1.6 fusion.198
  146.6 4.2 %fusion.269 = (f32[64]{0:T(128)S(1)}, f32[2048,64]{0,1:T(8,128)S(1)}) fusion(f32[2048]{0:T(1024)S(1)} %get-tuple-element.106, f32[64]{0:T(128)S(1)} %get-tuple-element.86, f32[2048]{0:T(1024)S(1)} %get-tuple-element.89, f32[64]{0:T(128)S(1)} %get-tuple-element.87, f32[2048]{0:T(1024)S(1)} %get-tuple-element.90, f32[64]{0:T(128)S(1)} %get-tuple-element.58, ...), kind=kLoop, calls=%fused_computation.455 | loop fusion | flops 16121792 | bytes 1040384 | tf_op jit(solution)/shard_map/reduce_sum | solution.py:233
  151.3 1.6 fusion.268
  153.4 1.6 fusion.148
  155.3 5.3 %multiply_convert_fusion.1 = (bf16[2048,64]{0,1:T(8,128)(2,1)S(1)}, f32[2048,64]{0,1:T(8,128)S(1)}) fusion(f32[2048,128]{0,1:T(8,128)S(1)} %fusion.198, f32[2048]{0:T(1024)S(1)} %get-tuple-element.117, f32[64]{0:T(128)S(1)} %copy-done.60, f32[2048]{0:T(1024)S(1)} %get-tuple-element.116, f32[64]{0:T(128)S(1)} %copy-done.62, f32[2048]{0:T(1024)S(1)} %get-tuple-element.115, ...), kind=kLoop, calls=%fused_computation.230 | loop fusion | flops 12582912 | bytes 2088704 | tf_op jit(solution)/shard_map/convert.1
  160.7 2.1 reduce-precision_convert_fusion
  162.9 1.1 copy_bitcast_fusion
  163.9 2.0 copy.35
  165.9 2.0 copy.36
  167.9 2.9 %maximum_maximum_fusion = bf16[16,128,320]{1,2,0:T(8,128)(2,1)} fusion(bf16[16,64,128]{1,2,0:T(8,128)(2,1)} %copy.36, bf16[16,64,128]{1,2,0:T(8,128)(2,1)} %copy.35, bf16[16,128,192]{1,2,0:T(8,128)(2,1)} %copy_bitcast_fusion), kind=kLoop, calls=%fused_computation.11 | loop fusion | flops 3932160 | bytes 2621440 | tf_op jit(solution)/shard_map/concatenate | solution.py:292
  170.8 4.4 %all-to-all-start.1 = ((bf16[16,128,320]{1,2,0:T(8,128)(2,1)}), bf16[16,128,320]{1,2,0:T(8,128)(2,1)}, u32[]{:S(2)}, u32[]{:S(2)}) async-start(bf16[16,128,320]{1,2,0:T(8,128)(2,1)} %maximum_maximum_fusion), calls=%async_computation.1 | async-start | bytes 2621440 | tf_op jit(solution)/shard_map/all_to_all | solution.py:291
  176.6 1.5 fusion.54
  178.0 1.4 fusion.124
  179.4 1.6 fusion.90
  181.0 1.5 fusion.72
  182.6 0.7 fusion.106
  183.3 2.1 stack.127
  185.4 1.1 broadcast_multiply_fusion.4
  187.2 3.7 %convolution_multiply_fusion.2 = f32[64,1024]{1,0:T(8,128)} fusion(bf16[2048,64]{0,1:T(8,128)(2,1)S(1)} %get-tuple-element.54, bf16[2048,1024]{1,0:T(8,128)(2,1)} %bitcast.164), kind=kOutput, calls=%fused_computation.17 | convolution fusion | flops 268500992 | bytes 4718592 | tf_op jit(solution)/shard_map/fa,fb->ab/dot_general | solution.py:243
  190.9 11.7 %all-to-all-done.1 = bf16[16,128,320]{1,2,0:T(8,128)(2,1)} async-done(((bf16[16,128,320]{1,2,0:T(8,128)(2,1)}), bf16[16,128,320]{1,2,0:T(8,128)(2,1)}, u32[]{:S(2)}, u32[]{:S(2)}) %all-to-all-start.1) | async-done | bytes 1310752 | tf_op jit(solution)/shard_map/all_to_all | solution.py:291
  202.6 1.5 slice_convert_fusion.1
  204.5 0.8 fusion.197
  205.3 1.7 fusion.26
  207.1 0.7 mul.1690
  207.7 8.0 %all-to-all-start.2 = ((f32[16,1,64]{2,1,0:T(1,128)}), f32[16,1,64]{2,1,0:T(1,128)S(1)}, u32[]{:S(2)}, u32[]{:S(2)}) async-start(f32[16,1,64]{2,1,0:T(1,128)} %mul.1690), calls=%async_computation.2 | async-start | bytes 16384 | tf_op jit(solution)/shard_map/all_to_all | solution.py:322
  215.7 2.9 %fusion.13 = bf16[128,1024]{1,0:T(8,128)(2,1)} fusion(bf16[16,448,1024]{2,1,0:T(8,128)(2,1)} %bitcast.160, bf16[128,1024]{1,0:T(8,128)(2,1)S(1)} %copy-done.4, bf16[16,128,320]{1,2,0:T(8,128)(2,1)} %all-to-all-done.1), kind=kOutput, calls=%fused_computation.16 | convolution fusion | flops 268828672 | bytes 2883584 | tf_op jit(solution)/shard_map/dot_general | solution.py:314
  218.6 2.1 fusion.25
  220.7 0.9 copy.41
  221.6 1.2 reshape.184
  (162 shorter events, 5.8 us)
Async XLA Ops:
  7.2 122.4 %all-gather.3.cloned.1.call-start = ((), (), s32[]{:S(2)}) async-start(), calls=%async_computation.3 | async-start | bytes 15597568 | tf_op jit(solution)/shard_map/all_gather | solution.py:183
  14.9 13.9 %all-to-all-start = ((f32[16,1,192]{2,1,0:T(1,128)}), f32[16,1,192]{2,1,0:T(1,128)S(1)}, u32[]{:S(2)}, u32[]{:S(2)}) async-start(f32[16,1,192]{2,1,0:T(1,128)} %broadcast_in_dim.2), calls=%async_computation | async-start | bytes 32768 | tf_op jit(solution)/shard_map/all_to_all | solution.py:176
  23.3 123.1 %copy-start.17 = (f32[64]{0:T(128)}, f32[64]{0:T(128)S(1)}, u32[]{:S(2)}) copy-start(f32[64]{0:T(128)S(1)} %get-tuple-element.65) | copy-start | bytes 772
  23.3 123.1 %copy-start.19 = (f32[64]{0:T(128)}, f32[64]{0:T(128)S(1)}, u32[]{:S(2)}) copy-start(f32[64]{0:T(128)S(1)} %get-tuple-element.66) | copy-start | bytes 772
  23.3 123.1 %copy-start.21 = (f32[64]{0:T(128)}, f32[64]{0:T(128)S(1)}, u32[]{:S(2)}) copy-start(f32[64]{0:T(128)S(1)} %get-tuple-element.67) | copy-start | bytes 772
  23.3 123.1 %copy-start.23 = (f32[64]{0:T(128)}, f32[64]{0:T(128)S(1)}, u32[]{:S(2)}) copy-start(f32[64]{0:T(128)S(1)} %get-tuple-element.68) | copy-start | bytes 772
  23.3 123.1 %copy-start.25 = (f32[64]{0:T(128)}, f32[64]{0:T(128)S(1)}, u32[]{:S(2)}) copy-start(f32[64]{0:T(128)S(1)} %get-tuple-element.69) | copy-start | bytes 772
  23.3 123.1 %copy-start.27 = (f32[64]{0:T(128)}, f32[64]{0:T(128)S(1)}, u32[]{:S(2)}) copy-start(f32[64]{0:T(128)S(1)} %get-tuple-element.70) | copy-start | bytes 772
  23.3 123.1 %copy-start.29 = (f32[64]{0:T(128)}, f32[64]{0:T(128)S(1)}, u32[]{:S(2)}) copy-start(f32[64]{0:T(128)S(1)} %get-tuple-element.71) | copy-start | bytes 772
  23.3 123.1 %copy-start.31 = (f32[64]{0:T(128)}, f32[64]{0:T(128)S(1)}, u32[]{:S(2)}) copy-start(f32[64]{0:T(128)S(1)} %get-tuple-element.72) | copy-start | bytes 772
  23.4 123.1 %copy-start.33 = (f32[64]{0:T(128)}, f32[64]{0:T(128)S(1)}, u32[]{:S(2)}) copy-start(f32[64]{0:T(128)S(1)} %get-tuple-element.73) | copy-start | bytes 772
  23.4 123.1 %copy-start.35 = (f32[64]{0:T(128)}, f32[64]{0:T(128)S(1)}, u32[]{:S(2)}) copy-start(f32[64]{0:T(128)S(1)} %get-tuple-element.74) | copy-start | bytes 772
  23.4 123.1 %copy-start.37 = (f32[64]{0:T(128)}, f32[64]{0:T(128)S(1)}, u32[]{:S(2)}) copy-start(f32[64]{0:T(128)S(1)} %get-tuple-element.75) | copy-start | bytes 772
  24.4 122.1 %copy-start.39 = (f32[64]{0:T(128)}, f32[64]{0:T(128)S(1)}, u32[]{:S(2)}) copy-start(f32[64]{0:T(128)S(1)} %get-tuple-element.76) | copy-start | bytes 772
  24.4 122.1 %copy-start.41 = (f32[64]{0:T(128)}, f32[64]{0:T(128)S(1)}, u32[]{:S(2)}) copy-start(f32[64]{0:T(128)S(1)} %get-tuple-element.77) | copy-start | bytes 772
  24.4 122.1 %copy-start.43 = (f32[64]{0:T(128)}, f32[64]{0:T(128)S(1)}, u32[]{:S(2)}) copy-start(f32[64]{0:T(128)S(1)} %get-tuple-element.78) | copy-start | bytes 772
  24.4 122.1 %copy-start.45 = (f32[64]{0:T(128)}, f32[64]{0:T(128)S(1)}, u32[]{:S(2)}) copy-start(f32[64]{0:T(128)S(1)} %get-tuple-element.79) | copy-start | bytes 772
  24.4 122.1 %copy-start.47 = (f32[64]{0:T(128)}, f32[64]{0:T(128)S(1)}, u32[]{:S(2)}) copy-start(f32[64]{0:T(128)S(1)} %get-tuple-element.80) | copy-start | bytes 772
  24.4 122.1 %copy-start.49 = (f32[64]{0:T(128)}, f32[64]{0:T(128)S(1)}, u32[]{:S(2)}) copy-start(f32[64]{0:T(128)S(1)} %get-tuple-element.81) | copy-start | bytes 772
  24.4 122.1 %copy-start.51 = (f32[64]{0:T(128)}, f32[64]{0:T(128)S(1)}, u32[]{:S(2)}) copy-start(f32[64]{0:T(128)S(1)} %get-tuple-element.82) | copy-start | bytes 772
  24.4 122.1 %copy-start.53 = (f32[64]{0:T(128)}, f32[64]{0:T(128)S(1)}, u32[]{:S(2)}) copy-start(f32[64]{0:T(128)S(1)} %get-tuple-element.83) | copy-start | bytes 772
  24.4 122.1 %copy-start.55 = (f32[64]{0:T(128)}, f32[64]{0:T(128)S(1)}, u32[]{:S(2)}) copy-start(f32[64]{0:T(128)S(1)} %get-tuple-element.84) | copy-start | bytes 772
  24.4 122.1 %copy-start.57 = (f32[64]{0:T(128)}, f32[64]{0:T(128)S(1)}, u32[]{:S(2)}) copy-start(f32[64]{0:T(128)S(1)} %get-tuple-element.85) | copy-start | bytes 772
  24.5 122.1 %copy-start.59 = (f32[64]{0:T(128)}, f32[64]{0:T(128)S(1)}, u32[]{:S(2)}) copy-start(f32[64]{0:T(128)S(1)} %get-tuple-element.86) | copy-start | bytes 772
  24.5 122.1 %copy-start.61 = (f32[64]{0:T(128)}, f32[64]{0:T(128)S(1)}, u32[]{:S(2)}) copy-start(f32[64]{0:T(128)S(1)} %get-tuple-element.87) | copy-start | bytes 772
  28.9 113.7 %copy-start.13 = (f32[1024]{0:T(1024)}, f32[1024]{0:T(1024)S(1)}, u32[]{:S(2)}) copy-start(f32[1024]{0:T(1024)S(1)} %mul.659) | copy-start | bytes 12292
  29.1 125.9 %copy-start.6 = (f32[2048]{0:T(1024)}, f32[2048]{0:T(1024)S(1)}, u32[]{:S(2)}) copy-start(f32[2048]{0:T(1024)S(1)} %get-tuple-element.116) | copy-start | bytes 24580
  29.1 125.9 %copy-start.7 = (f32[2048]{0:T(1024)}, f32[2048]{0:T(1024)S(1)}, u32[]{:S(2)}) copy-start(f32[2048]{0:T(1024)S(1)} %get-tuple-element.107) | copy-start | bytes 24580
  29.1 125.9 %copy-start.8 = (f32[2048]{0:T(1024)}, f32[2048]{0:T(1024)S(1)}, u32[]{:S(2)}) copy-start(f32[2048]{0:T(1024)S(1)} %get-tuple-element.108) | copy-start | bytes 24580
  29.1 125.9 %copy-start.9 = (f32[2048]{0:T(1024)}, f32[2048]{0:T(1024)S(1)}, u32[]{:S(2)}) copy-start(f32[2048]{0:T(1024)S(1)} %get-tuple-element.109) | copy-start | bytes 24580
  29.1 125.9 %copy-start.10 = (f32[2048]{0:T(1024)}, f32[2048]{0:T(1024)S(1)}, u32[]{:S(2)}) copy-start(f32[2048]{0:T(1024)S(1)} %get-tuple-element.110) | copy-start | bytes 24580
  29.1 125.9 %copy-start.11 = (f32[2048]{0:T(1024)}, f32[2048]{0:T(1024)S(1)}, u32[]{:S(2)}) copy-start(f32[2048]{0:T(1024)S(1)} %get-tuple-element.117) | copy-start | bytes 24580
  132.4 7.6 %copy-start = (bf16[7168,1024]{1,0:T(8,128)(2,1)S(1)}, bf16[7168,1024]{1,0:T(8,128)(2,1)}, u32[]{:S(2)}) copy-start(bf16[7168,1024]{1,0:T(8,128)(2,1)} %all-gather.3.cloned.1.call-done) | copy-start | bytes 44040196
  140.0 11.0 %copy-start.1 = (bf16[16,128,1024]{2,1,0:T(8,128)(2,1)}, bf16[16,128,1024]{2,1,0:T(8,128)(2,1)S(1)}, u32[]{:S(2)}) copy-start(bf16[16,128,1024]{2,1,0:T(8,128)(2,1)S(1)} %get-tuple-element.48) | copy-start | bytes 12582916
  144.6 6.5 %copy-start.64 = (f32[64]{0:T(128)S(1)}, f32[64]{0:T(128)}, u32[]{:S(2)}) copy-start(f32[64]{0:T(128)} %param.15) | copy-start | bytes 772
  144.6 6.5 %copy-start.12 = (bf16[64,1024]{1,0:T(8,128)(2,1)S(1)}, bf16[64,1024]{1,0:T(8,128)(2,1)}, u32[]{:S(2)}) copy-start(bf16[64,1024]{1,0:T(8,128)(2,1)} %param.17) | copy-start | bytes 393220
  144.6 6.5 %copy-start.66 = (f32[64]{0:T(128)S(1)}, f32[64]{0:T(128)}, u32[]{:S(2)}) copy-start(f32[64]{0:T(128)} %param.16) | copy-start | bytes 772
  151.1 4.0 %copy-start.18 = (f32[64]{0:T(128)S(1)}, f32[64]{0:T(128)}, u32[]{:S(2)}) copy-start(f32[64]{0:T(128)} %copy-done.17) | copy-start | bytes 772
  151.1 4.0 %copy-start.20 = (f32[64]{0:T(128)S(1)}, f32[64]{0:T(128)}, u32[]{:S(2)}) copy-start(f32[64]{0:T(128)} %copy-done.19) | copy-start | bytes 772
  151.1 4.0 %copy-start.22 = (f32[64]{0:T(128)S(1)}, f32[64]{0:T(128)}, u32[]{:S(2)}) copy-start(f32[64]{0:T(128)} %copy-done.21) | copy-start | bytes 772
  151.1 4.0 %copy-start.24 = (f32[64]{0:T(128)S(1)}, f32[64]{0:T(128)}, u32[]{:S(2)}) copy-start(f32[64]{0:T(128)} %copy-done.23) | copy-start | bytes 772
  151.1 4.0 %copy-start.26 = (f32[64]{0:T(128)S(1)}, f32[64]{0:T(128)}, u32[]{:S(2)}) copy-start(f32[64]{0:T(128)} %copy-done.25) | copy-start | bytes 772
  151.1 4.0 %copy-start.28 = (f32[64]{0:T(128)S(1)}, f32[64]{0:T(128)}, u32[]{:S(2)}) copy-start(f32[64]{0:T(128)} %copy-done.27) | copy-start | bytes 772
  151.1 4.0 %copy-start.30 = (f32[64]{0:T(128)S(1)}, f32[64]{0:T(128)}, u32[]{:S(2)}) copy-start(f32[64]{0:T(128)} %copy-done.29) | copy-start | bytes 772
  151.1 4.0 %copy-start.32 = (f32[64]{0:T(128)S(1)}, f32[64]{0:T(128)}, u32[]{:S(2)}) copy-start(f32[64]{0:T(128)} %copy-done.31) | copy-start | bytes 772
  162.9 12.3 %copy-start.4 = (bf16[128,1024]{1,0:T(8,128)(2,1)S(1)}, bf16[128,1024]{1,0:T(8,128)(2,1)}, u32[]{:S(2)}) copy-start(bf16[128,1024]{1,0:T(8,128)(2,1)} %param.9) | copy-start | bytes 786436
  170.8 31.8 %all-to-all-start.1 = ((bf16[16,128,320]{1,2,0:T(8,128)(2,1)}), bf16[16,128,320]{1,2,0:T(8,128)(2,1)}, u32[]{:S(2)}, u32[]{:S(2)}) async-start(bf16[16,128,320]{1,2,0:T(8,128)(2,1)} %maximum_maximum_fusion), calls=%async_computation.1 | async-start | bytes 2621440 | tf_op jit(solution)/shard_map/all_to_all | solution.py:291
  207.7 15.1 %all-to-all-start.2 = ((f32[16,1,64]{2,1,0:T(1,128)}), f32[16,1,64]{2,1,0:T(1,128)S(1)}, u32[]{:S(2)}, u32[]{:S(2)}) async-start(f32[16,1,64]{2,1,0:T(1,128)} %mul.1690), calls=%async_computation.2 | async-start | bytes 16384 | tf_op jit(solution)/shard_map/all_to_all | solution.py:322
  (23 other events, 70.9 us)
Sparse Core Ops, SparseCore 0:
  13.0 116.5 all-gather.2

commit v8 on v5

--- a/solution.py
+++ b/solution.py
@@ -181,24 +181,22 @@
 
     out_rows = w_out.shape[0]
     pieces = lax.all_gather(
-        jnp.concatenate([frames, out_grad, w_out, w_in[:, :width], w_in[:, width:]], axis=0),
-        "seq",
-        axis=0,
+        jnp.concatenate([frames, out_grad, w_out], axis=0), "seq", axis=0
     )
     frames_all = pieces[:, :rows].reshape(stream, width)
     grad_all = pieces[:, rows : 2 * rows].reshape(stream, width)
-    w_out_all = pieces[:, 2 * rows : 2 * rows + out_rows].reshape(width, width)
-    w_in_left = pieces[:, 2 * rows + out_rows : 2 * rows + 2 * out_rows].reshape(width, width)
-    w_in_right = pieces[:, 2 * rows + 2 * out_rows :].reshape(width, width)
+    w_out_all = pieces[:, 2 * rows :].reshape(width, width)
+    w_in_late, _ = lax.optimization_barrier((w_in, pieces))
+    w_in_halves = lax.all_gather(
+        jnp.concatenate([w_in_late[:, :width], w_in_late[:, width:]], axis=0), "seq", axis=0
+    )
+    w_in_left = w_in_halves[:, :out_rows].reshape(width, width)
+    w_in_right = w_in_halves[:, out_rows:].reshape(width, width)
 
     first_channel = lax.axis_index("seq") * share
-    w_in_cols = jnp.concatenate(
-        [
-            lax.dynamic_slice_in_dim(w_in_left, first_channel, share, 1),
-            lax.dynamic_slice_in_dim(w_in_right, first_channel, share, 1),
-        ],
-        axis=1,
-    )
+    w_in_cols = lax.all_to_all(
+        w_in.reshape(share, 2, devices, share).transpose(2, 0, 1, 3), "seq", 0, 0, tiled=True
+    ).reshape(width, 2 * share)
 
     def norm(block):
         block_float = block.astype(jnp.float32)

time: 224 us -> 213 us (0.951)
  waiting for transfers between devices: 117 us -> 108 us
  starting transfers between devices: 17.2 us -> 20.9 us
  local copies, waits for them, and re-layouts: 21.6 us -> 18.6 us
  matrix products: 15.4 us -> 12.7 us
    all_gather x1 -> x2, waiting for transfers between devices: 100 us -> 64.3 us  [the longest x1 58.7 us: channel_local(): lax.all_gather(jnp.concatenate([frames, out_grad, w_out], axis=0), 'seq',...]
    all_to_all x0 -> x1, waiting for transfers between devices: none -> 14.2 us  [channel_local(): lax.all_to_all(w_in.reshape(share, 2, devices, share).transpose(2, 0, 1,...]
    all_to_all x1, waiting for transfers between devices: 5.23 us -> 19 us  [channel_local(): lax.all_to_all(jnp.concatenate([activation, grad_hidden], axis=1).reshape...]
    slice x1 -> x3, local copies, waits for them, and re-layouts: 0.56 us -> 7.6 us  [the longest x1 4.82 us: channel_local(): grad_all = pieces[:, rows:2 * rows].reshape(stream, width)]
    unnamed x28 -> x18, local copies, waits for them, and re-layouts: 8.37 us -> 1.53 us
    all_to_all x0 -> x1, starting transfers between devices: none -> 6.01 us  [channel_local(): lax.all_to_all(w_in.reshape(share, 2, devices, share).transpose(2, 0, 1,...]
    slice x1 -> x0, other arithmetic: 4.35 us -> none  [channel_local(): grad_all = pieces[:, rows:2 * rows].reshape(stream, width)]
    convert_element_type x1 -> x2, other arithmetic: 1.93 us -> 6.02 us  [channel_local(): ln_x_all = (ln_all * gains).astype(jnp.bfloat16)]
  transfers between devices with their start and end apart: 4 -> 6, of which waited for: 4 -> 5; matrix products, arithmetic and copies ran while one was open for 11% -> 23% of each run, Pallas kernels for 0% -> 0%
where the time goes in v8:
time: 213 us; the launch traced here: 212 us
  waiting for transfers between devices  108 us (51%)
  other arithmetic  37.5 us (18%)
  starting transfers between devices  20.9 us (10%)
  local copies, waits for them, and re-layouts  18.6 us (9%)
  between operations  14.4 us (7%)
  matrix products  12.7 us (6%)
    all_gather x1, waiting for transfers between devices, channel_local(): lax.all_gather(jnp.concatenate([frames, out_grad, w_out], axis=0), 'seq',...  58.7 us
    all_to_all x1, waiting for transfers between devices, channel_local(): lax.all_to_all(jnp.concatenate([activation, grad_hidden], axis=1).reshape...  19 us
    all_to_all x1, waiting for transfers between devices, channel_local(): lax.all_to_all(w_in.reshape(share, 2, devices, share).transpose(2, 0, 1,...  14.2 us
    all_to_all x1, waiting for transfers between devices, channel_local(): lax.all_to_all(jnp.concatenate([in_cols.reshape(devices, share * 2 * shar...  10.4 us
    all_to_all x1, starting transfers between devices, spread(): return lax.all_to_all(copies, 'seq', 0, 0, tiled=True)  7.39 us
    convert_element_type x2, other arithmetic, channel_local(): ln_x_all = (ln_all * gains).astype(jnp.bfloat16)  6.02 us
    all_to_all x1, starting transfers between devices, channel_local(): lax.all_to_all(w_in.reshape(share, 2, devices, share).transpose(2, 0, 1,...  6.01 us
    all_gather x1, waiting for transfers between devices, channel_local(): lax.all_gather(jnp.concatenate([w_in_late[:, :width], w_in_late[:, width:...  5.56 us
  transfers between devices with their start and end apart: 6, of which 5 were waited for; matrix products, arithmetic and copies ran while one was open for 23% of the time, Pallas kernels for 0%

profile of v8, /device:TPU:0, one launch (start us, length us, event | category | flops | bytes accessed | tf_op | source)
XLA Modules:
  0.0 212.1 jit_solution(14624082987364925782)
XLA Ops:
  7.2 2.0 pad_maximum_fusion
  9.2 0.7 convert_element_type.269
  9.9 0.7 pad_maximum_fusion.3
  10.6 0.6 broadcast_in_dim.2
  11.3 7.4 %all-to-all-start = ((f32[16,1,192]{2,1,0:T(1,128)}), f32[16,1,192]{2,1,0:T(1,128)S(1)}, u32[]{:S(2)}, u32[]{:S(2)}) async-start(f32[16,1,192]{2,1,0:T(1,128)} %broadcast_in_dim.2), calls=%async_computation | async-start | bytes 32768 | tf_op jit(solution)/shard_map/all_to_all | solution.py:176
  18.6 1.1 convert_reduce_fusion.1
  19.7 1.2 fusion.26
  20.9 1.0 slice_bitcast_fusion.35
  21.9 1.0 slice_bitcast_fusion.36
  22.9 1.5 reshape.184
  24.4 0.6 copy.31
  25.0 1.1 reshape.199
  26.1 6.0 %all-to-all-start.1 = ((bf16[16,2,4096]{2,1,0:T(2,128)(2,1)}), bf16[16,2,4096]{2,1,0:T(2,128)(2,1)S(1)}, u32[]{:S(2)}, u32[]{:S(2)}) async-start(bf16[16,2,4096]{2,1,0:T(2,128)(2,1)} %reshape.199), calls=%async_computation.1 | async-start | bytes 524288 | tf_op jit(solution)/shard_map/all_to_all | solution.py:197
  32.5 14.2 %all-to-all-done.1 = bf16[16,2,4096]{2,1,0:T(2,128)(2,1)S(1)} async-done(((bf16[16,2,4096]{2,1,0:T(2,128)(2,1)}), bf16[16,2,4096]{2,1,0:T(2,128)(2,1)S(1)}, u32[]{:S(2)}, u32[]{:S(2)}) %all-to-all-start.1) | async-done | bytes 262176 | tf_op jit(solution)/shard_map/all_to_all | solution.py:197
  47.8 58.7 %all-gather.5.cloned.1.call-done = bf16[5120,1024]{1,0:T(8,128)(2,1)} async-done(((bf16[320,1024]{1,0:T(8,128)(2,1)}), bf16[5120,1024]{1,0:T(8,128)(2,1)}) %all-gather.5.cloned.1.call-update) | async-done | bytes 10485776 | tf_op jit(solution)/shard_map/all_gather | solution.py:183
  106.4 2.8 %convert_reduce_fusion = f32[16,128]{1,0:T(8,128)S(1)} fusion(bf16[16,320,1024]{2,1,0:T(8,128)(2,1)} %bitcast.166), kind=kLoop, calls=%fused_computation.6 | loop fusion | flops 4192256 | bytes 4202496 | tf_op jit(solution)/shard_map/reduce_sum | solution.py:203
  109.3 4.8 %slice.622 = bf16[16,128,1024]{2,1,0:T(8,128)(2,1)} slice(bf16[16,320,1024]{2,1,0:T(8,128)(2,1)} %bitcast.167), slice={[0:16], [128:256], [0:1024]} | slice | bytes 8388608 | tf_op jit(solution)/shard_map/slice | solution.py:187
  114.1 0.7 pad_maximum_fusion.2
  114.9 3.2 %multiply_reduce_fusion = f32[16,128]{1,0:T(8,128)S(1)} fusion(f32[16,128]{1,0:T(8,128)S(1)} %get-tuple-element.87, bf16[16,320,1024]{2,1,0:T(8,128)(2,1)} %bitcast.168), kind=kLoop, calls=%fused_computation.5 | loop fusion | flops 8386560 | bytes 4210688 | tf_op jit(solution)/shard_map/reduce_sum | solution.py:205
  118.1 3.0 %multiply_convert_fusion = bf16[16,128,1024]{2,1,0:T(8,128)(2,1)S(1)} fusion(f32[1024]{0:T(1024)S(1)} %mul.660, f32[16,128]{1,0:T(8,128)S(1)} %get-tuple-element.89, f32[16,128]{1,0:T(8,128)S(1)} %get-tuple-element.87, bf16[16,320,1024]{2,1,0:T(8,128)(2,1)} %bitcast.169), kind=kLoop, calls=%fused_computation.4 | loop fusion | flops 10485760 | bytes 8409088 | tf_op jit(solution)/shard_map/convert_element_type | solution.py:209
  121.1 1.5 fusion.267
  122.8 4.2 %fusion.263 = (f32[64]{0:T(128)S(1)}, f32[2048,64]{0,1:T(8,128)S(1)}) fusion(f32[2048]{0:T(1024)S(1)} %get-tuple-element.108, f32[64]{0:T(128)S(1)} %get-tuple-element.84, f32[2048]{0:T(1024)S(1)} %get-tuple-element.91, f32[64]{0:T(128)S(1)} %get-tuple-element.85, f32[2048]{0:T(1024)S(1)} %get-tuple-element.92, f32[64]{0:T(128)S(1)} %get-tuple-element.56, ...), kind=kLoop, calls=%fused_computation.443 | loop fusion | flops 16121792 | bytes 1040384 | tf_op jit(solution)/shard_map/reduce_sum | solution.py:231
  127.3 1.6 fusion.262
  129.4 1.0 fusion.147
  130.4 5.3 %multiply_convert_fusion.2 = (bf16[2048,64]{0,1:T(8,128)(2,1)S(1)}, f32[2048,64]{0,1:T(8,128)S(1)}) fusion(f32[2048,128]{0,1:T(8,128)S(1)} %fusion.267, f32[2048]{0:T(1024)S(1)} %get-tuple-element.119, f32[64]{0:T(128)S(1)} %get-tuple-element.84, f32[2048]{0:T(1024)S(1)} %get-tuple-element.118, f32[64]{0:T(128)S(1)} %get-tuple-element.85, ...), kind=kLoop, calls=%fused_computation.227 | loop fusion | flops 12582912 | bytes 2088704 | tf_op jit(solution)/shard_map/convert.1
  135.9 1.1 copy_bitcast_fusion
  137.0 3.6 %all-to-all-start.2 = ((bf16[16,128,192]{1,2,0:T(8,128)(2,1)}), bf16[16,128,192]{1,2,0:T(8,128)(2,1)S(1)}, u32[]{:S(2)}, u32[]{:S(2)}) async-start(bf16[16,128,192]{1,2,0:T(8,128)(2,1)} %copy_bitcast_fusion), calls=%async_computation.2 | async-start | bytes 1572864 | tf_op jit(solution)/shard_map/all_to_all | solution.py:279
  140.6 3.0 %fusion.2 = bf16[2048,1024]{1,0:T(8,128)(2,1)S(1)} fusion(f32[1024]{0:T(1024)S(1)} %mul.660, f32[2048]{0:T(1024)S(1)} %get-tuple-element.88, f32[2048]{0:T(1024)S(1)} %get-tuple-element.86, bf16[16,320,1024]{2,1,0:T(8,128)(2,1)} %bitcast.170), kind=kLoop, calls=%fused_computation.3 | loop fusion | flops 10485760 | bytes 8409088 | tf_op jit(solution)/shard_map/convert_element_type | solution.py:209
  143.6 1.3 convolution_multiply_fusion.1
  145.3 0.8 fusion.123
  146.1 0.8 fusion.89
  146.9 0.8 fusion.71
  147.8 0.7 fusion.105
  148.6 0.6 broadcast_multiply_fusion
  149.2 3.7 %convolution_multiply_fusion.2 = f32[64,1024]{1,0:T(8,128)} fusion(bf16[2048,64]{0,1:T(8,128)(2,1)S(1)} %get-tuple-element.52, bf16[2048,1024]{1,0:T(8,128)(2,1)} %bitcast.173), kind=kOutput, calls=%fused_computation.16 | convolution fusion | flops 268500992 | bytes 4718592 | tf_op jit(solution)/shard_map/fa,fb->ab/dot_general | solution.py:241
  153.0 19.0 %all-to-all-done.2 = bf16[16,128,192]{1,2,0:T(8,128)(2,1)S(1)} async-done(((bf16[16,128,192]{1,2,0:T(8,128)(2,1)}), bf16[16,128,192]{1,2,0:T(8,128)(2,1)S(1)}, u32[]{:S(2)}, u32[]{:S(2)}) %all-to-all-start.2) | async-done | bytes 786464 | tf_op jit(solution)/shard_map/all_to_all | solution.py:279
  172.1 5.6 %all-gather.7.cloned.1.call-done = bf16[2048,1024]{1,0:T(8,128)(2,1)} async-done(((bf16[128,1024]{1,0:T(8,128)(2,1)}), bf16[2048,1024]{1,0:T(8,128)(2,1)}) %all-gather.7.cloned.1.call-update) | async-done | bytes 4194320 | tf_op jit(solution)/shard_map/all_gather | solution.py:190
  177.6 2.8 %fusion.265 = (bf16[16,64,1024]{2,1,0:T(8,128)(2,1)S(1)}, bf16[16,64,1024]{2,1,0:T(8,128)(2,1)S(1)}) fusion(bf16[16,128,1024]{2,1,0:T(8,128)(2,1)} %bitcast.177), kind=kLoop, calls=%fused_computation.444 | loop fusion | bytes 8388608 | tf_op jit(solution)/shard_map/slice | solution.py:194
  180.4 0.8 fusion.195
  181.3 1.0 fusion.25
  182.4 1.2 all_to_all.24
  183.6 3.8 %all-to-all-start.3 = ((f32[16,1,8256]{2,1,0:T(1,128)}), f32[16,1,8256]{2,1,0:T(1,128)S(1)}, u32[]{:S(2)}, u32[]{:S(2)}) async-start(f32[16,1,8256]{2,1,0:T(1,128)} %all_to_all.24), calls=%async_computation.3 | async-start | bytes 1064960 | tf_op jit(solution)/shard_map/all_to_all | solution.py:295
  188.0 2.8 %fusion.12 = bf16[128,1024]{1,0:T(8,128)(2,1)} fusion(bf16[16,320,1024]{2,1,0:T(8,128)(2,1)} %bitcast.171, bf16[128,1024]{1,0:T(8,128)(2,1)S(1)} %copy-done.1, bf16[16,128,192]{1,2,0:T(8,128)(2,1)S(1)} %all-to-all-done.2), kind=kOutput, calls=%fused_computation.15 | convolution fusion | flops 268828672 | bytes 2883584 | tf_op jit(solution)/shard_map/dot_general | solution.py:288
  190.7 1.0 fusion.24
  191.7 10.4 %all-to-all-done.3 = f32[16,1,8256]{2,1,0:T(1,128)S(1)} async-done(((f32[16,1,8256]{2,1,0:T(1,128)}), f32[16,1,8256]{2,1,0:T(1,128)S(1)}, u32[]{:S(2)}, u32[]{:S(2)}) %all-to-all-start.3) | async-done | bytes 528416 | tf_op jit(solution)/shard_map/all_to_all | solution.py:295
  202.7 0.8 reshape.193
  203.5 0.6 copy.37
  204.1 1.2 reshape.194
  (52 shorter events, 4.4 us)
Async XLA Ops:
  7.2 99.3 %all-gather.5.cloned.1.call-start = ((), (), s32[]{:S(2)}) async-start(), calls=%async_computation.4 | async-start | bytes 11141120 | tf_op jit(solution)/shard_map/all_gather | solution.py:183
  11.3 14.8 %all-to-all-start = ((f32[16,1,192]{2,1,0:T(1,128)}), f32[16,1,192]{2,1,0:T(1,128)S(1)}, u32[]{:S(2)}, u32[]{:S(2)}) async-start(f32[16,1,192]{2,1,0:T(1,128)} %broadcast_in_dim.2), calls=%async_computation | async-start | bytes 32768 | tf_op jit(solution)/shard_map/all_to_all | solution.py:176
  26.1 20.6 %all-to-all-start.1 = ((bf16[16,2,4096]{2,1,0:T(2,128)(2,1)}), bf16[16,2,4096]{2,1,0:T(2,128)(2,1)S(1)}, u32[]{:S(2)}, u32[]{:S(2)}) async-start(bf16[16,2,4096]{2,1,0:T(2,128)(2,1)} %reshape.199), calls=%async_computation.1 | async-start | bytes 524288 | tf_op jit(solution)/shard_map/all_to_all | solution.py:197
  32.1 145.5 %all-gather.7.cloned.1.call-start = ((), (), s32[]{:S(2)}) async-start(), calls=%async_computation.5 | async-start | bytes 4456448 | tf_op jit(solution)/shard_map/all_gather | solution.py:190
  109.3 4.8 %copy-start.3 = (bf16[64,2048]{1,0:T(8,128)(2,1)S(1)}, bf16[64,2048]{1,0:T(8,128)(2,1)}, u32[]{:S(2)}) copy-start(bf16[64,2048]{1,0:T(8,128)(2,1)} %param.13) | copy-start | bytes 786436
  121.1 6.2 %copy-start.5 = (f32[64]{0:T(128)S(1)}, f32[64]{0:T(128)}, u32[]{:S(2)}) copy-start(f32[64]{0:T(128)} %param.15) | copy-start | bytes 772
  121.1 6.2 %copy-start = (bf16[16,128,1024]{2,1,0:T(8,128)(2,1)S(1)}, bf16[16,128,1024]{2,1,0:T(8,128)(2,1)}, u32[]{:S(2)}) copy-start(bf16[16,128,1024]{2,1,0:T(8,128)(2,1)} %slice.622) | copy-start | bytes 12582916
  121.1 6.2 %copy-start.4 = (bf16[64,1024]{1,0:T(8,128)(2,1)S(1)}, bf16[64,1024]{1,0:T(8,128)(2,1)}, u32[]{:S(2)}) copy-start(bf16[64,1024]{1,0:T(8,128)(2,1)} %param.17) | copy-start | bytes 393220
  121.1 6.2 %copy-start.6 = (f32[64]{0:T(128)S(1)}, f32[64]{0:T(128)}, u32[]{:S(2)}) copy-start(f32[64]{0:T(128)} %param.16) | copy-start | bytes 772
  137.0 35.0 %all-to-all-start.2 = ((bf16[16,128,192]{1,2,0:T(8,128)(2,1)}), bf16[16,128,192]{1,2,0:T(8,128)(2,1)S(1)}, u32[]{:S(2)}, u32[]{:S(2)}) async-start(bf16[16,128,192]{1,2,0:T(8,128)(2,1)} %copy_bitcast_fusion), calls=%async_computation.2 | async-start | bytes 1572864 | tf_op jit(solution)/shard_map/all_to_all | solution.py:279
  177.6 3.6 %copy-start.1 = (bf16[128,1024]{1,0:T(8,128)(2,1)S(1)}, bf16[128,1024]{1,0:T(8,128)(2,1)}, u32[]{:S(2)}) copy-start(bf16[128,1024]{1,0:T(8,128)(2,1)} %param.9) | copy-start | bytes 786436
  181.3 9.5 %copy-start.2 = (bf16[128,1024]{1,0:T(8,128)(2,1)S(1)}, bf16[128,1024]{1,0:T(8,128)(2,1)}, u32[]{:S(2)}) copy-start(bf16[128,1024]{1,0:T(8,128)(2,1)} %param.11) | copy-start | bytes 786436
  183.6 18.5 %all-to-all-start.3 = ((f32[16,1,8256]{2,1,0:T(1,128)}), f32[16,1,8256]{2,1,0:T(1,128)S(1)}, u32[]{:S(2)}, u32[]{:S(2)}) async-start(f32[16,1,8256]{2,1,0:T(1,128)} %all_to_all.24), calls=%async_computation.3 | async-start | bytes 1064960 | tf_op jit(solution)/shard_map/all_to_all | solution.py:295
Sparse Core Ops, SparseCore 0:
  10.3 96.1 all-gather.4
  115.0 62.5 all-gather.6

commit v9 on v8

--- a/solution.py
+++ b/solution.py
@@ -180,23 +180,25 @@
     all_ids = small[:, share:].reshape(stream).astype(jnp.int32)
 
     out_rows = w_out.shape[0]
-    pieces = lax.all_gather(
-        jnp.concatenate([frames, out_grad, w_out], axis=0), "seq", axis=0
-    )
+    pieces = lax.all_gather(jnp.concatenate([frames, out_grad], axis=0), "seq", axis=0)
     frames_all = pieces[:, :rows].reshape(stream, width)
-    grad_all = pieces[:, rows : 2 * rows].reshape(stream, width)
-    w_out_all = pieces[:, 2 * rows :].reshape(width, width)
-    w_in_late, _ = lax.optimization_barrier((w_in, pieces))
-    w_in_halves = lax.all_gather(
-        jnp.concatenate([w_in_late[:, :width], w_in_late[:, width:]], axis=0), "seq", axis=0
-    )
-    w_in_left = w_in_halves[:, :out_rows].reshape(width, width)
-    w_in_right = w_in_halves[:, out_rows:].reshape(width, width)
-
-    first_channel = lax.axis_index("seq") * share
+    grad_all = pieces[:, rows:].reshape(stream, width)
     w_in_cols = lax.all_to_all(
         w_in.reshape(share, 2, devices, share).transpose(2, 0, 1, 3), "seq", 0, 0, tiled=True
     ).reshape(width, 2 * share)
+    w_in_late, w_out_late, _, _, _ = lax.optimization_barrier(
+        (w_in, w_out, pieces, w_in_cols, small)
+    )
+    weights = lax.all_gather(
+        jnp.concatenate([w_out_late, w_in_late[:, :width], w_in_late[:, width:]], axis=0),
+        "seq",
+        axis=0,
+    )
+    w_out_all = weights[:, :out_rows].reshape(width, width)
+    w_in_left = weights[:, out_rows : 2 * out_rows].reshape(width, width)
+    w_in_right = weights[:, 2 * out_rows :].reshape(width, width)
+
+    first_channel = lax.axis_index("seq") * share
 
     def norm(block):
         block_float = block.astype(jnp.float32)

time: 213 us -> 206 us (0.967)
  other arithmetic: 37.5 us -> 31 us
  waiting for transfers between devices: 108 us -> 113 us
  starting transfers between devices: 20.9 us -> 18.4 us
  local copies, waits for them, and re-layouts: 18.6 us -> 16.4 us
    all_to_all x1, waiting for transfers between devices: 0.01 us -> 3.31 us  [spread(): return lax.all_to_all(copies, 'seq', 0, 0, tiled=True)]
    reduce_sum x2, other arithmetic: 3.87 us -> 0.73 us  [norm(): mean = jnp.mean(block_float, axis=1, keepdims=True)]
    reduce_sum x2, other arithmetic: 4.38 us -> 1.82 us  [norm(): jnp.mean(centred * centred, axis=1, keepdims=True) + EPSILON]
    all_to_all x1, starting transfers between devices: 6.01 us -> 3.53 us  [channel_local(): lax.all_to_all(w_in.reshape(share, 2, devices, share).transpose(2, 0, 1,...]
  transfers between devices with their start and end apart: 6 -> 6, of which waited for: 5 -> 6; matrix products, arithmetic and copies ran while one was open for 23% -> 23% of each run, Pallas kernels for 0% -> 0%
where the time goes in v9:
time: 206 us
  waiting for transfers between devices  113 us (55%)
  other arithmetic  31 us (15%)
  starting transfers between devices  18.4 us (9%)
  local copies, waits for them, and re-layouts  16.4 us (8%)
  between operations  14.4 us (7%)
  matrix products  12.8 us (6%)
    all_gather x1, waiting for transfers between devices, channel_local(): lax.all_gather(jnp.concatenate([frames, out_grad], axis=0), 'seq', axis=0)  49.7 us
    all_to_all x1, waiting for transfers between devices, channel_local(): lax.all_to_all(jnp.concatenate([activation, grad_hidden], axis=1).reshape...  18.1 us
    all_gather x1, waiting for transfers between devices, channel_local(): lax.all_gather(jnp.concatenate([w_out_late, w_in_late[:, :width], w_in_la...  16.7 us
    all_to_all x1, waiting for transfers between devices, channel_local(): lax.all_to_all(w_in.reshape(share, 2, devices, share).transpose(2, 0, 1,...  14.5 us
    all_to_all x1, waiting for transfers between devices, channel_local(): lax.all_to_all(jnp.concatenate([in_cols.reshape(devices, share * 2 * shar...  10.4 us
    all_to_all x1, starting transfers between devices, spread(): return lax.all_to_all(copies, 'seq', 0, 0, tiled=True)  7.41 us
    another operation x2, other arithmetic  5.48 us
    convert_element_type x2, other arithmetic, channel_local(): ln_x_all = (ln_all * gains).astype(jnp.bfloat16)  5.14 us
  transfers between devices with their start and end apart: 6, of which 6 were waited for; matrix products, arithmetic and copies ran while one was open for 23% of the time, Pallas kernels for 0%

profile of v9, /device:TPU:0, one launch (start us, length us, event | category | flops | bytes accessed | tf_op | source)
XLA Modules:
  0.0 205.6 jit_solution(8749860038082689612)
XLA Ops:
  7.2 1.9 pad_maximum_fusion.1
  9.2 0.7 convert_element_type.269
  9.9 0.7 pad_maximum_fusion.3
  10.6 0.6 broadcast_in_dim.2
  11.2 7.4 %all-to-all-start = ((f32[16,1,192]{2,1,0:T(1,128)}), f32[16,1,192]{2,1,0:T(1,128)S(1)}, u32[]{:S(2)}, u32[]{:S(2)}) async-start(f32[16,1,192]{2,1,0:T(1,128)} %broadcast_in_dim.2), calls=%async_computation | async-start | bytes 32768 | tf_op jit(solution)/shard_map/all_to_all | solution.py:176
  18.6 1.5 reshape.184
  20.1 0.6 copy.31
  20.7 1.1 reshape.199
  21.8 3.3 %all-to-all-done = f32[16,1,192]{2,1,0:T(1,128)S(1)} async-done(((f32[16,1,192]{2,1,0:T(1,128)}), f32[16,1,192]{2,1,0:T(1,128)S(1)}, u32[]{:S(2)}, u32[]{:S(2)}) %all-to-all-start) | async-done | bytes 12320 | tf_op jit(solution)/shard_map/all_to_all | solution.py:176
  25.1 3.5 %all-to-all-start.1 = ((bf16[16,2,4096]{2,1,0:T(2,128)(2,1)}), bf16[16,2,4096]{2,1,0:T(2,128)(2,1)S(1)}, u32[]{:S(2)}, u32[]{:S(2)}) async-start(bf16[16,2,4096]{2,1,0:T(2,128)(2,1)} %reshape.199), calls=%async_computation.1 | async-start | bytes 524288 | tf_op jit(solution)/shard_map/all_to_all | solution.py:186
  28.7 14.5 %all-to-all-done.1 = bf16[16,2,4096]{2,1,0:T(2,128)(2,1)S(1)} async-done(((bf16[16,2,4096]{2,1,0:T(2,128)(2,1)}), bf16[16,2,4096]{2,1,0:T(2,128)(2,1)S(1)}, u32[]{:S(2)}, u32[]{:S(2)}) %all-to-all-start.1) | async-done | bytes 262176 | tf_op jit(solution)/shard_map/all_to_all | solution.py:186
  44.3 49.7 %all-gather.5.cloned.1.call-done = bf16[4096,1024]{1,0:T(8,128)(2,1)} async-done(((bf16[256,1024]{1,0:T(8,128)(2,1)}), bf16[4096,1024]{1,0:T(8,128)(2,1)}) %all-gather.5.cloned.1.call-update) | async-done | bytes 8388624 | tf_op jit(solution)/shard_map/all_gather | solution.py:183
  94.0 0.8 pad_maximum_fusion.2
  95.6 2.8 %slice.622 = bf16[16,128,1024]{2,1,0:T(8,128)(2,1)S(1)} slice(bf16[16,256,1024]{2,1,0:T(8,128)(2,1)} %bitcast.166), slice={[0:16], [128:256], [0:1024]} | slice | bytes 8388608 | tf_op jit(solution)/shard_map/slice | solution.py:185
  98.4 1.8 copy-done
  100.2 0.6 convert_reduce_fusion
  100.8 1.6 multiply_reduce_fusion
  102.5 1.4 multiply_convert_fusion
  103.9 1.5 fusion.267
  105.6 4.2 %fusion.263 = (f32[64]{0:T(128)S(1)}, f32[2048,64]{0,1:T(8,128)S(1)}) fusion(f32[2048]{0:T(1024)S(1)} %get-tuple-element.110, f32[64]{0:T(128)S(1)} %get-tuple-element.86, f32[2048]{0:T(1024)S(1)} %get-tuple-element.93, f32[64]{0:T(128)S(1)} %get-tuple-element.87, f32[2048]{0:T(1024)S(1)} %get-tuple-element.94, f32[64]{0:T(128)S(1)} %get-tuple-element.58, ...), kind=kLoop, calls=%fused_computation.443 | loop fusion | flops 16121792 | bytes 1040384 | tf_op jit(solution)/shard_map/reduce_sum | solution.py:233
  110.0 1.6 fusion.262
  111.6 0.5 broadcast_multiply_fusion.3
  112.1 1.0 fusion.147
  113.2 5.3 %multiply_convert_fusion.2 = (bf16[2048,64]{0,1:T(8,128)(2,1)S(1)}, f32[2048,64]{0,1:T(8,128)S(1)}) fusion(f32[2048,128]{0,1:T(8,128)S(1)} %fusion.267, f32[2048]{0:T(1024)S(1)} %get-tuple-element.121, f32[64]{0:T(128)S(1)} %get-tuple-element.86, f32[2048]{0:T(1024)S(1)} %get-tuple-element.120, f32[64]{0:T(128)S(1)} %get-tuple-element.87, ...), kind=kLoop, calls=%fused_computation.227 | loop fusion | flops 12582912 | bytes 2088704 | tf_op jit(solution)/shard_map/convert.1
  118.6 1.1 copy_bitcast_fusion
  119.8 3.6 %all-to-all-start.2 = ((bf16[16,128,192]{1,2,0:T(8,128)(2,1)}), bf16[16,128,192]{1,2,0:T(8,128)(2,1)S(1)}, u32[]{:S(2)}, u32[]{:S(2)}) async-start(bf16[16,128,192]{1,2,0:T(8,128)(2,1)} %copy_bitcast_fusion), calls=%async_computation.2 | async-start | bytes 1572864 | tf_op jit(solution)/shard_map/all_to_all | solution.py:281
  123.4 3.7 %fusion.2 = bf16[2048,1024]{1,0:T(8,128)(2,1)S(1)} fusion(f32[1024]{0:T(1024)S(1)} %mul.660, f32[2048]{0:T(1024)S(1)} %get-tuple-element.90, f32[2048]{0:T(1024)S(1)} %get-tuple-element.88, bf16[16,256,1024]{2,1,0:T(8,128)(2,1)} %bitcast.167), kind=kLoop, calls=%fused_computation.3 | loop fusion | flops 10485760 | bytes 8409088 | tf_op jit(solution)/shard_map/convert_element_type | solution.py:211
  127.1 1.3 convolution_multiply_fusion.1
  128.8 0.8 fusion.123
  129.6 0.8 fusion.89
  130.4 0.8 fusion.71
  131.3 0.7 fusion.105
  132.1 0.6 broadcast_multiply_fusion
  132.7 3.8 %convolution_multiply_fusion.2 = f32[64,1024]{1,0:T(8,128)} fusion(bf16[2048,64]{0,1:T(8,128)(2,1)S(1)} %get-tuple-element.54, bf16[2048,1024]{1,0:T(8,128)(2,1)} %bitcast.173), kind=kOutput, calls=%fused_computation.16 | convolution fusion | flops 268500992 | bytes 4718592 | tf_op jit(solution)/shard_map/fa,fb->ab/dot_general | solution.py:243
  136.5 18.1 %all-to-all-done.2 = bf16[16,128,192]{1,2,0:T(8,128)(2,1)S(1)} async-done(((bf16[16,128,192]{1,2,0:T(8,128)(2,1)}), bf16[16,128,192]{1,2,0:T(8,128)(2,1)S(1)}, u32[]{:S(2)}, u32[]{:S(2)}) %all-to-all-start.2) | async-done | bytes 786464 | tf_op jit(solution)/shard_map/all_to_all | solution.py:281
  154.7 16.7 %all-gather.7.cloned.1.call-done = bf16[3072,1024]{1,0:T(8,128)(2,1)} async-done(((bf16[192,1024]{1,0:T(8,128)(2,1)}), bf16[3072,1024]{1,0:T(8,128)(2,1)}) %all-gather.7.cloned.1.call-update) | async-done | bytes 6291472 | tf_op jit(solution)/shard_map/all_gather | solution.py:192
  171.4 2.7 %fusion.265 = (bf16[16,64,1024]{2,1,0:T(8,128)(2,1)S(1)}, bf16[16,64,1024]{2,1,0:T(8,128)(2,1)S(1)}) fusion(bf16[16,192,1024]{2,1,0:T(8,128)(2,1)} %bitcast.177), kind=kLoop, calls=%fused_computation.444 | loop fusion | bytes 8388608 | tf_op jit(solution)/shard_map/slice | solution.py:199
  174.1 0.8 fusion.195
  175.0 1.0 fusion.25
  176.1 1.2 all_to_all.24
  177.2 3.7 %all-to-all-start.3 = ((f32[16,1,8256]{2,1,0:T(1,128)}), f32[16,1,8256]{2,1,0:T(1,128)S(1)}, u32[]{:S(2)}, u32[]{:S(2)}) async-start(f32[16,1,8256]{2,1,0:T(1,128)} %all_to_all.24), calls=%async_computation.3 | async-start | bytes 1064960 | tf_op jit(solution)/shard_map/all_to_all | solution.py:297
  181.5 1.0 fusion.24
  182.5 2.8 %fusion.12 = bf16[128,1024]{1,0:T(8,128)(2,1)} fusion(bf16[16,192,1024]{2,1,0:T(8,128)(2,1)} %bitcast.178, bf16[128,1024]{1,0:T(8,128)(2,1)S(1)} %copy-done.2, bf16[16,128,192]{1,2,0:T(8,128)(2,1)S(1)} %all-to-all-done.2), kind=kOutput, calls=%fused_computation.15 | convolution fusion | flops 268828672 | bytes 2883584 | tf_op jit(solution)/shard_map/dot_general | solution.py:290
  185.3 10.4 %all-to-all-done.3 = f32[16,1,8256]{2,1,0:T(1,128)S(1)} async-done(((f32[16,1,8256]{2,1,0:T(1,128)}), f32[16,1,8256]{2,1,0:T(1,128)S(1)}, u32[]{:S(2)}, u32[]{:S(2)}) %all-to-all-start.3) | async-done | bytes 528416 | tf_op jit(solution)/shard_map/all_to_all | solution.py:297
  195.7 0.5 slice_reduce_fusion
  196.2 0.8 reshape.193
  197.0 0.6 copy.37
  197.6 1.2 reshape.194
  (56 shorter events, 3.7 us)
Async XLA Ops:
  7.2 86.8 %copy-start.3 = (bf16[64,2048]{1,0:T(8,128)(2,1)S(1)}, bf16[64,2048]{1,0:T(8,128)(2,1)}, u32[]{:S(2)}) copy-start(bf16[64,2048]{1,0:T(8,128)(2,1)} %param.13) | copy-start | bytes 786436
  7.2 86.8 %copy-start.5 = (bf16[64,1024]{1,0:T(8,128)(2,1)S(1)}, bf16[64,1024]{1,0:T(8,128)(2,1)}, u32[]{:S(2)}) copy-start(bf16[64,1024]{1,0:T(8,128)(2,1)} %param.17) | copy-start | bytes 393220
  7.2 86.8 %all-gather.5.cloned.1.call-start = ((), (), s32[]{:S(2)}) async-start(), calls=%async_computation.4 | async-start | bytes 8912896 | tf_op jit(solution)/shard_map/all_gather | solution.py:183
  9.1 85.6 %copy-start.2 = (bf16[128,1024]{1,0:T(8,128)(2,1)S(1)}, bf16[128,1024]{1,0:T(8,128)(2,1)}, u32[]{:S(2)}) copy-start(bf16[128,1024]{1,0:T(8,128)(2,1)} %param.9) | copy-start | bytes 786436
  9.1 86.0 %copy-start.6 = (f32[31,64]{1,0:T(8,128)S(1)}, f32[31,64]{1,0:T(8,128)}, u32[]{:S(2)}) copy-start(f32[31,64]{1,0:T(8,128)} %param.14) | copy-start | bytes 23812
  11.2 13.9 %all-to-all-start = ((f32[16,1,192]{2,1,0:T(1,128)}), f32[16,1,192]{2,1,0:T(1,128)S(1)}, u32[]{:S(2)}, u32[]{:S(2)}) async-start(f32[16,1,192]{2,1,0:T(1,128)} %broadcast_in_dim.2), calls=%async_computation | async-start | bytes 32768 | tf_op jit(solution)/shard_map/all_to_all | solution.py:176
  25.1 18.1 %all-to-all-start.1 = ((bf16[16,2,4096]{2,1,0:T(2,128)(2,1)}), bf16[16,2,4096]{2,1,0:T(2,128)(2,1)S(1)}, u32[]{:S(2)}, u32[]{:S(2)}) async-start(bf16[16,2,4096]{2,1,0:T(2,128)(2,1)} %reshape.199), calls=%async_computation.1 | async-start | bytes 524288 | tf_op jit(solution)/shard_map/all_to_all | solution.py:186
  28.7 142.7 %all-gather.7.cloned.1.call-start = ((), (), s32[]{:S(2)}) async-start(), calls=%async_computation.5 | async-start | bytes 6684672 | tf_op jit(solution)/shard_map/all_gather | solution.py:192
  95.6 4.6 %copy-start = (bf16[4096,1024]{1,0:T(8,128)(2,1)S(1)}, bf16[4096,1024]{1,0:T(8,128)(2,1)}, u32[]{:S(2)}) copy-start(bf16[4096,1024]{1,0:T(8,128)(2,1)} %all-gather.5.cloned.1.call-done) | copy-start | bytes 25165828
  100.2 9.8 %copy-start.1 = (bf16[16,128,1024]{2,1,0:T(8,128)(2,1)}, bf16[16,128,1024]{2,1,0:T(8,128)(2,1)S(1)}, u32[]{:S(2)}) copy-start(bf16[16,128,1024]{2,1,0:T(8,128)(2,1)S(1)} %slice.622) | copy-start | bytes 12582916
  103.9 6.1 %copy-start.7 = (f32[64]{0:T(128)S(1)}, f32[64]{0:T(128)}, u32[]{:S(2)}) copy-start(f32[64]{0:T(128)} %param.15) | copy-start | bytes 772
  103.9 6.1 %copy-start.8 = (f32[64]{0:T(128)S(1)}, f32[64]{0:T(128)}, u32[]{:S(2)}) copy-start(f32[64]{0:T(128)} %param.16) | copy-start | bytes 772
  119.8 34.8 %all-to-all-start.2 = ((bf16[16,128,192]{1,2,0:T(8,128)(2,1)}), bf16[16,128,192]{1,2,0:T(8,128)(2,1)S(1)}, u32[]{:S(2)}, u32[]{:S(2)}) async-start(bf16[16,128,192]{1,2,0:T(8,128)(2,1)} %copy_bitcast_fusion), calls=%async_computation.2 | async-start | bytes 1572864 | tf_op jit(solution)/shard_map/all_to_all | solution.py:281
  174.1 7.4 %copy-start.4 = (bf16[128,1024]{1,0:T(8,128)(2,1)S(1)}, bf16[128,1024]{1,0:T(8,128)(2,1)}, u32[]{:S(2)}) copy-start(bf16[128,1024]{1,0:T(8,128)(2,1)} %param.11) | copy-start | bytes 786436
  177.2 18.4 %all-to-all-start.3 = ((f32[16,1,8256]{2,1,0:T(1,128)}), f32[16,1,8256]{2,1,0:T(1,128)S(1)}, u32[]{:S(2)}, u32[]{:S(2)}) async-start(f32[16,1,8256]{2,1,0:T(1,128)} %all_to_all.24), calls=%async_computation.3 | async-start | bytes 1064960 | tf_op jit(solution)/shard_map/all_to_all | solution.py:297
Sparse Core Ops, SparseCore 0:
  10.8 83.1 all-gather.4
  96.8 74.5 all-gather.6

commit v10 on v9

--- a/solution.py
+++ b/solution.py
@@ -278,6 +278,11 @@
         jnp.einsum("fa,fb->ab", ln_x_all, grad_hidden, preferred_element_type=jnp.float32)
         * grad_scale
     )
+    grad_w_in = (
+        lax.all_to_all(in_cols.reshape(devices, share, 2, share), "seq", 0, 0, tiled=True)
+        .transpose(1, 2, 0, 3)
+        .reshape(share, 2 * width)
+    )
     back = lax.all_to_all(
         jnp.concatenate([activation, grad_hidden], axis=1).reshape(devices, rows, 3 * share),
         "seq", 0, 0, tiled=True,
@@ -294,20 +299,9 @@
     ) + jnp.einsum("fe,ne->fn", hidden_rows[:, 1], w_in_right, preferred_element_type=jnp.float32)
     ln_hat, rstd_ln = norm(frames)
     gain_part = jnp.sum(grad_ln * ln_hat, axis=0) * grad_scale
-    packed = lax.all_to_all(
-        jnp.concatenate(
-            [in_cols.reshape(devices, share * 2 * share), gain_part.reshape(devices, share)],
-            axis=1,
-        ),
-        "seq", 0, 0, tiled=True,
-    )
-    grad_w_in = (
-        packed[:, : share * 2 * share]
-        .reshape(devices, share, 2, share)
-        .transpose(1, 2, 0, 3)
-        .reshape(share, 2 * width)
-    )
-    grad_ln_gain = jnp.sum(packed[:, share * 2 * share :], axis=0)
+    grad_ln_gain = jnp.sum(
+        lax.all_to_all(gain_part.reshape(devices, share), "seq", 0, 0, tiled=True), axis=0
+    )
     grad_hat = grad_ln * gains
     grad_input = rstd_ln * (
         grad_hat

time: 206 us -> 207 us (level)
  waiting for transfers between devices: 113 us -> 96.4 us
  starting transfers between devices: 18.4 us -> 30.5 us
  local copies, waits for them, and re-layouts: 16.4 us -> 19.8 us
    all_gather x1, waiting for transfers between devices: 16.7 us -> 0.02 us  [channel_local(): lax.all_gather(jnp.concatenate([w_out_late, w_in_late[:, :width], w_in_la...]
    all_to_all x1 -> x2, waiting for transfers between devices: 10.4 us -> 22.7 us  [the longest x1 20.1 us: channel_local(): lax.all_to_all(in_cols.reshape(devices, share, 2, share), 'seq', 0, 0, ti...]
    all_to_all x1, waiting for transfers between devices: 18.1 us -> 6.1 us  [channel_local(): lax.all_to_all(jnp.concatenate([activation, grad_hidden], axis=1).reshape...]
    all_to_all x1, starting transfers between devices: 3.61 us -> 10.5 us  [channel_local(): lax.all_to_all(jnp.concatenate([activation, grad_hidden], axis=1).reshape...]
    all_to_all x1 -> x2, starting transfers between devices: 3.74 us -> 9.04 us  [the longest x1 5.47 us: channel_local(): lax.all_to_all(gain_part.reshape(devices, share), 'seq', 0, 0, tiled=True)]
    unnamed x22 -> x49, local copies, waits for them, and re-layouts: 3.36 us -> 6.05 us
    convert_element_type x2, other arithmetic: 5.14 us -> 3.05 us  [channel_local(): ln_x_all = (ln_all * gains).astype(jnp.bfloat16)]
  transfers between devices with their start and end apart: 6 -> 7, of which waited for: 6 -> 6; matrix products, arithmetic and copies ran while one was open for 23% -> 26% of each run, Pallas kernels for 0% -> 0%
where the time goes in v10:
time: 207 us; the launch traced here: 206 us
  waiting for transfers between devices  96.4 us (47%)
  other arithmetic  31.4 us (15%)
  starting transfers between devices  30.5 us (15%)
  local copies, waits for them, and re-layouts  19.8 us (10%)
  between operations  14.6 us (7%)
  matrix products  13.5 us (7%)
    all_gather x1, waiting for transfers between devices, channel_local(): lax.all_gather(jnp.concatenate([frames, out_grad], axis=0), 'seq', axis=0)  49.7 us
    all_to_all x1, waiting for transfers between devices, channel_local(): lax.all_to_all(in_cols.reshape(devices, share, 2, share), 'seq', 0, 0, ti...  20.1 us
    all_to_all x1, waiting for transfers between devices, channel_local(): lax.all_to_all(w_in.reshape(share, 2, devices, share).transpose(2, 0, 1,...  14.5 us
    all_to_all x1, starting transfers between devices, channel_local(): lax.all_to_all(jnp.concatenate([activation, grad_hidden], axis=1).reshape...  10.5 us
    all_to_all x1, starting transfers between devices, spread(): return lax.all_to_all(copies, 'seq', 0, 0, tiled=True)  7.39 us
    all_to_all x1, waiting for transfers between devices, channel_local(): lax.all_to_all(jnp.concatenate([activation, grad_hidden], axis=1).reshape...  6.1 us
    unnamed x49, local copies, waits for them, and re-layouts  6.05 us
    all_to_all x1, starting transfers between devices, channel_local(): lax.all_to_all(gain_part.reshape(devices, share), 'seq', 0, 0, tiled=True)  5.47 us
  transfers between devices with their start and end apart: 7, of which 6 were waited for; matrix products, arithmetic and copies ran while one was open for 26% of the time, Pallas kernels for 0%

profile of v10, /device:TPU:0, one launch (start us, length us, event | category | flops | bytes accessed | tf_op | source)
XLA Modules:
  0.0 206.3 jit_solution(16778406925119192009)
XLA Ops:
  7.2 1.9 pad_maximum_fusion
  9.2 0.7 convert_element_type.269
  9.8 0.7 pad_maximum_fusion.2
  10.6 0.6 broadcast_in_dim.2
  11.2 7.4 %all-to-all-start = ((f32[16,1,192]{2,1,0:T(1,128)}), f32[16,1,192]{2,1,0:T(1,128)S(1)}, u32[]{:S(2)}, u32[]{:S(2)}) async-start(f32[16,1,192]{2,1,0:T(1,128)} %broadcast_in_dim.2), calls=%async_computation | async-start | bytes 32768 | tf_op jit(solution)/shard_map/all_to_all | solution.py:176
  18.6 1.5 reshape.191
  20.6 1.1 reshape.205
  21.8 3.3 %all-to-all-done = f32[16,1,192]{2,1,0:T(1,128)S(1)} async-done(((f32[16,1,192]{2,1,0:T(1,128)}), f32[16,1,192]{2,1,0:T(1,128)S(1)}, u32[]{:S(2)}, u32[]{:S(2)}) %all-to-all-start) | async-done | bytes 12320 | tf_op jit(solution)/shard_map/all_to_all | solution.py:176
  25.1 3.5 %all-to-all-start.1 = ((bf16[16,2,4096]{2,1,0:T(2,128)(2,1)}), bf16[16,2,4096]{2,1,0:T(2,128)(2,1)S(1)}, u32[]{:S(2)}, u32[]{:S(2)}) async-start(bf16[16,2,4096]{2,1,0:T(2,128)(2,1)} %reshape.205), calls=%async_computation.1 | async-start | bytes 524288 | tf_op jit(solution)/shard_map/all_to_all | solution.py:186
  28.7 14.5 %all-to-all-done.1 = bf16[16,2,4096]{2,1,0:T(2,128)(2,1)S(1)} async-done(((bf16[16,2,4096]{2,1,0:T(2,128)(2,1)}), bf16[16,2,4096]{2,1,0:T(2,128)(2,1)S(1)}, u32[]{:S(2)}, u32[]{:S(2)}) %all-to-all-start.1) | async-done | bytes 262176 | tf_op jit(solution)/shard_map/all_to_all | solution.py:186
  44.2 49.7 %all-gather.5.cloned.1.call-done = bf16[4096,1024]{1,0:T(8,128)(2,1)} async-done(((bf16[256,1024]{1,0:T(8,128)(2,1)}), bf16[4096,1024]{1,0:T(8,128)(2,1)}) %all-gather.5.cloned.1.call-update) | async-done | bytes 8388624 | tf_op jit(solution)/shard_map/all_gather | solution.py:183
  94.0 0.8 pad_maximum_fusion.1
  95.2 2.8 %slice.614 = bf16[16,128,1024]{2,1,0:T(8,128)(2,1)S(1)} slice(bf16[16,256,1024]{2,1,0:T(8,128)(2,1)} %bitcast.164), slice={[0:16], [128:256], [0:1024]} | slice | bytes 8388608 | tf_op jit(solution)/shard_map/slice | solution.py:185
  98.1 1.8 copy-done
  99.9 0.6 convert_reduce_fusion
  100.5 1.6 multiply_reduce_fusion
  102.1 1.4 multiply_convert_fusion
  103.6 1.5 fusion.267
  105.2 4.2 %fusion.263 = (f32[64]{0:T(128)S(1)}, f32[2048,64]{0,1:T(8,128)S(1)}) fusion(f32[2048]{0:T(1024)S(1)} %get-tuple-element.110, f32[64]{0:T(128)S(1)} %get-tuple-element.86, f32[2048]{0:T(1024)S(1)} %get-tuple-element.93, f32[64]{0:T(128)S(1)} %get-tuple-element.87, f32[2048]{0:T(1024)S(1)} %get-tuple-element.94, f32[64]{0:T(128)S(1)} %get-tuple-element.58, ...), kind=kLoop, calls=%fused_computation.440 | loop fusion | flops 16121792 | bytes 1040384 | tf_op jit(solution)/shard_map/reduce_sum | solution.py:233
  109.7 1.6 fusion.262
  111.8 1.6 fusion.147
  113.4 4.9 %multiply_convert_fusion.2 = (bf16[2048,64]{0,1:T(8,128)(2,1)S(1)}, f32[2048,64]{0,1:T(8,128)S(1)}) fusion(f32[2048,128]{0,1:T(8,128)S(1)} %fusion.267, f32[2048]{0:T(1024)S(1)} %get-tuple-element.121, f32[64]{0:T(128)S(1)} %get-tuple-element.86, f32[2048]{0:T(1024)S(1)} %get-tuple-element.120, f32[64]{0:T(128)S(1)} %get-tuple-element.87, ...), kind=kLoop, calls=%fused_computation.225 | loop fusion | flops 12582912 | bytes 2088704 | tf_op jit(solution)/shard_map/convert.1
  118.5 1.6 fusion.2
  120.2 2.1 %convolution_multiply_fusion.1 = f32[1024,128]{1,0:T(8,128)} fusion(bf16[2048,1024]{1,0:T(8,128)(2,1)S(1)} %fusion.2, bf16[2048,64]{0,1:T(8,128)(2,1)S(1)} %multiply_convert_fusion.1, bf16[2048,64]{0,1:T(8,128)(2,1)S(1)} %get-tuple-element.48), kind=kOutput, calls=%fused_computation.11 | convolution fusion | flops 538050560 | bytes 5242880 | tf_op jit(solution)/shard_map/fa,fb->ab/dot_general | solution.py:278
  122.3 1.6 reshape.199
  123.9 1.9 reshape.207
  125.8 3.6 %all-to-all-start.3 = ((f32[16,1,8192]{2,1,0:T(1,128)}), f32[16,1,8192]{2,1,0:T(1,128)S(1)}, u32[]{:S(2)}, u32[]{:S(2)}) async-start(f32[16,1,8192]{2,1,0:T(1,128)} %reshape.207), calls=%async_computation.3 | async-start | bytes 1048576 | tf_op jit(solution)/shard_map/all_to_all | solution.py:282
  130.4 1.1 copy_bitcast_fusion
  131.5 0.8 fusion.123
  132.3 20.1 %all-to-all-done.3 = f32[16,1,8192]{2,1,0:T(1,128)S(1)} async-done(((f32[16,1,8192]{2,1,0:T(1,128)}), f32[16,1,8192]{2,1,0:T(1,128)S(1)}, u32[]{:S(2)}, u32[]{:S(2)}) %all-to-all-start.3) | async-done | bytes 524320 | tf_op jit(solution)/shard_map/all_to_all | solution.py:282
  152.4 10.5 %all-to-all-start.2 = ((bf16[16,128,192]{1,2,0:T(8,128)(2,1)}), bf16[16,128,192]{1,2,0:T(8,128)(2,1)S(1)}, u32[]{:S(2)}, u32[]{:S(2)}) async-start(bf16[16,128,192]{1,2,0:T(8,128)(2,1)} %copy_bitcast_fusion), calls=%async_computation.2 | async-start | bytes 1572864 | tf_op jit(solution)/shard_map/all_to_all | solution.py:286
  163.1 0.8 fusion.89
  163.9 0.8 fusion.71
  164.8 0.7 fusion.105
  166.8 3.7 %convolution_multiply_fusion.2 = f32[64,1024]{1,0:T(8,128)} fusion(bf16[2048,64]{0,1:T(8,128)(2,1)S(1)} %get-tuple-element.54, bf16[2048,1024]{1,0:T(8,128)(2,1)} %bitcast.171), kind=kOutput, calls=%fused_computation.16 | convolution fusion | flops 268500992 | bytes 4718592 | tf_op jit(solution)/shard_map/fa,fb->ab/dot_general | solution.py:243
  171.0 1.9 reduce.3
  172.9 0.8 reshape.208
  173.7 0.6 copy.51
  174.3 1.2 reshape.200
  175.5 6.1 %all-to-all-done.2 = bf16[16,128,192]{1,2,0:T(8,128)(2,1)S(1)} async-done(((bf16[16,128,192]{1,2,0:T(8,128)(2,1)}), bf16[16,128,192]{1,2,0:T(8,128)(2,1)S(1)}, u32[]{:S(2)}, u32[]{:S(2)}) %all-to-all-start.2) | async-done | bytes 786464 | tf_op jit(solution)/shard_map/all_to_all | solution.py:286
  181.7 2.7 %fusion.265 = (bf16[16,64,1024]{2,1,0:T(8,128)(2,1)S(1)}, bf16[16,64,1024]{2,1,0:T(8,128)(2,1)S(1)}) fusion(bf16[16,192,1024]{2,1,0:T(8,128)(2,1)} %bitcast.175), kind=kLoop, calls=%fused_computation.441 | loop fusion | bytes 8388608 | tf_op jit(solution)/shard_map/slice | solution.py:199
  184.5 0.8 fusion.195
  185.3 1.0 fusion.25
  186.4 0.7 mul.1700
  187.0 5.5 %all-to-all-start.4 = ((f32[16,1,64]{2,1,0:T(1,128)}), f32[16,1,64]{2,1,0:T(1,128)S(1)}, u32[]{:S(2)}, u32[]{:S(2)}) async-start(f32[16,1,64]{2,1,0:T(1,128)} %mul.1700), calls=%async_computation.4 | async-start | bytes 16384 | tf_op jit(solution)/shard_map/all_to_all | solution.py:303
  192.5 2.8 %fusion.12 = bf16[128,1024]{1,0:T(8,128)(2,1)} fusion(bf16[16,192,1024]{2,1,0:T(8,128)(2,1)} %bitcast.176, bf16[128,1024]{1,0:T(8,128)(2,1)S(1)} %copy-done.2, bf16[16,128,192]{1,2,0:T(8,128)(2,1)S(1)} %all-to-all-done.2), kind=kOutput, calls=%fused_computation.15 | convolution fusion | flops 268828672 | bytes 2883584 | tf_op jit(solution)/shard_map/dot_general | solution.py:295
  195.3 1.0 fusion.24
  196.3 2.6 %all-to-all-done.4 = f32[16,1,64]{2,1,0:T(1,128)S(1)} async-done(((f32[16,1,64]{2,1,0:T(1,128)}), f32[16,1,64]{2,1,0:T(1,128)S(1)}, u32[]{:S(2)}, u32[]{:S(2)}) %all-to-all-start.4) | async-done | bytes 4128 | tf_op jit(solution)/shard_map/all_to_all | solution.py:303
  (83 shorter events, 6.8 us)
Async XLA Ops:
  7.2 86.8 %copy-start.3 = (bf16[64,2048]{1,0:T(8,128)(2,1)S(1)}, bf16[64,2048]{1,0:T(8,128)(2,1)}, u32[]{:S(2)}) copy-start(bf16[64,2048]{1,0:T(8,128)(2,1)} %param.13) | copy-start | bytes 786436
  7.2 86.8 %copy-start.5 = (bf16[64,1024]{1,0:T(8,128)(2,1)S(1)}, bf16[64,1024]{1,0:T(8,128)(2,1)}, u32[]{:S(2)}) copy-start(bf16[64,1024]{1,0:T(8,128)(2,1)} %param.17) | copy-start | bytes 393220
  7.2 86.8 %all-gather.5.cloned.1.call-start = ((), (), s32[]{:S(2)}) async-start(), calls=%async_computation.5 | async-start | bytes 8912896 | tf_op jit(solution)/shard_map/all_gather | solution.py:183
  9.1 85.7 %copy-start.8 = (f32[31,64]{1,0:T(8,128)S(1)}, f32[31,64]{1,0:T(8,128)}, u32[]{:S(2)}) copy-start(f32[31,64]{1,0:T(8,128)} %param.14) | copy-start | bytes 23812
  11.2 13.9 %all-to-all-start = ((f32[16,1,192]{2,1,0:T(1,128)}), f32[16,1,192]{2,1,0:T(1,128)S(1)}, u32[]{:S(2)}, u32[]{:S(2)}) async-start(f32[16,1,192]{2,1,0:T(1,128)} %broadcast_in_dim.2), calls=%async_computation | async-start | bytes 32768 | tf_op jit(solution)/shard_map/all_to_all | solution.py:176
  25.1 18.1 %all-to-all-start.1 = ((bf16[16,2,4096]{2,1,0:T(2,128)(2,1)}), bf16[16,2,4096]{2,1,0:T(2,128)(2,1)S(1)}, u32[]{:S(2)}, u32[]{:S(2)}) async-start(bf16[16,2,4096]{2,1,0:T(2,128)(2,1)} %reshape.205), calls=%async_computation.1 | async-start | bytes 524288 | tf_op jit(solution)/shard_map/all_to_all | solution.py:186
  28.6 153.1 %all-gather.7.cloned.1.call-start = ((), (), s32[]{:S(2)}) async-start(), calls=%async_computation.6 | async-start | bytes 6684672 | tf_op jit(solution)/shard_map/all_gather | solution.py:192
  94.9 23.5 %copy-start.6 = (f32[1024]{0:T(1024)}, f32[1024]{0:T(1024)S(1)}, u32[]{:S(2)}) copy-start(f32[1024]{0:T(1024)S(1)} %mul.667) | copy-start | bytes 12292
  95.2 4.6 %copy-start = (bf16[4096,1024]{1,0:T(8,128)(2,1)S(1)}, bf16[4096,1024]{1,0:T(8,128)(2,1)}, u32[]{:S(2)}) copy-start(bf16[4096,1024]{1,0:T(8,128)(2,1)} %all-gather.5.cloned.1.call-done) | copy-start | bytes 25165828
  99.9 9.8 %copy-start.1 = (bf16[16,128,1024]{2,1,0:T(8,128)(2,1)}, bf16[16,128,1024]{2,1,0:T(8,128)(2,1)S(1)}, u32[]{:S(2)}) copy-start(bf16[16,128,1024]{2,1,0:T(8,128)(2,1)S(1)} %slice.614) | copy-start | bytes 12582916
  103.6 6.1 %copy-start.18 = (f32[64]{0:T(128)S(1)}, f32[64]{0:T(128)}, u32[]{:S(2)}) copy-start(f32[64]{0:T(128)} %param.15) | copy-start | bytes 772
  103.6 6.1 %copy-start.21 = (f32[64]{0:T(128)S(1)}, f32[64]{0:T(128)}, u32[]{:S(2)}) copy-start(f32[64]{0:T(128)} %param.16) | copy-start | bytes 772
  111.3 8.9 %copy-start.19 = (f32[64]{0:T(128)}, f32[64]{0:T(128)S(1)}, u32[]{:S(2)}) copy-start(f32[64]{0:T(128)S(1)} %get-tuple-element.46) | copy-start | bytes 772
  120.1 9.3 %copy-start.2 = (bf16[128,1024]{1,0:T(8,128)(2,1)S(1)}, bf16[128,1024]{1,0:T(8,128)(2,1)}, u32[]{:S(2)}) copy-start(bf16[128,1024]{1,0:T(8,128)(2,1)} %param.9) | copy-start | bytes 786436
  125.8 26.6 %all-to-all-start.3 = ((f32[16,1,8192]{2,1,0:T(1,128)}), f32[16,1,8192]{2,1,0:T(1,128)S(1)}, u32[]{:S(2)}, u32[]{:S(2)}) async-start(f32[16,1,8192]{2,1,0:T(1,128)} %reshape.207), calls=%async_computation.3 | async-start | bytes 1048576 | tf_op jit(solution)/shard_map/all_to_all | solution.py:282
  129.4 36.1 %copy-start.12 = (f32[64]{0:T(128)S(1)}, f32[64]{0:T(128)}, u32[]{:S(2)}) copy-start(f32[64]{0:T(128)} %get-tuple-element.14) | copy-start | bytes 772
  129.4 36.1 %copy-start.13 = (f32[64]{0:T(128)S(1)}, f32[64]{0:T(128)}, u32[]{:S(2)}) copy-start(f32[64]{0:T(128)} %get-tuple-element.15) | copy-start | bytes 772
  129.4 36.1 %copy-start.14 = (f32[64]{0:T(128)S(1)}, f32[64]{0:T(128)}, u32[]{:S(2)}) copy-start(f32[64]{0:T(128)} %get-tuple-element.16) | copy-start | bytes 772
  129.4 36.1 %copy-start.15 = (f32[64]{0:T(128)S(1)}, f32[64]{0:T(128)}, u32[]{:S(2)}) copy-start(f32[64]{0:T(128)} %get-tuple-element.17) | copy-start | bytes 772
  129.5 36.1 %copy-start.16 = (f32[64]{0:T(128)S(1)}, f32[64]{0:T(128)}, u32[]{:S(2)}) copy-start(f32[64]{0:T(128)} %get-tuple-element.18) | copy-start | bytes 772
  129.5 36.1 %copy-start.17 = (f32[64]{0:T(128)S(1)}, f32[64]{0:T(128)}, u32[]{:S(2)}) copy-start(f32[64]{0:T(128)} %get-tuple-element.19) | copy-start | bytes 772
  129.5 36.2 %copy-start.20 = (f32[64]{0:T(128)S(1)}, f32[64]{0:T(128)}, u32[]{:S(2)}) copy-start(f32[64]{0:T(128)} %copy-done.19) | copy-start | bytes 772
  129.6 22.8 %copy-start.9 = (f32[128]{0:T(128)}, f32[128]{0:T(128)S(1)}, u32[]{:S(2)}) copy-start(f32[128]{0:T(128)S(1)} %broadcast_multiply_fusion.7) | copy-start | bytes 1540
  152.4 29.2 %all-to-all-start.2 = ((bf16[16,128,192]{1,2,0:T(8,128)(2,1)}), bf16[16,128,192]{1,2,0:T(8,128)(2,1)S(1)}, u32[]{:S(2)}, u32[]{:S(2)}) async-start(bf16[16,128,192]{1,2,0:T(8,128)(2,1)} %copy_bitcast_fusion), calls=%async_computation.2 | async-start | bytes 1572864 | tf_op jit(solution)/shard_map/all_to_all | solution.py:286
  181.7 3.6 %copy-start.7 = (f32[1024]{0:T(1024)S(1)}, f32[1024]{0:T(1024)}, u32[]{:S(2)}) copy-start(f32[1024]{0:T(1024)} %copy-done.6) | copy-start | bytes 12292
  181.7 3.6 %copy-start.10 = (f32[128]{0:T(128)S(1)}, f32[128]{0:T(128)}, u32[]{:S(2)}) copy-start(f32[128]{0:T(128)} %copy-done.9) | copy-start | bytes 1540
  181.7 3.6 %copy-start.11 = (f32[128]{0:T(128)S(1)}, f32[128]{0:T(128)}, u32[]{:S(2)}) copy-start(f32[128]{0:T(128)} %add_rsqrt_fusion.1) | copy-start | bytes 1540
  184.4 10.9 %copy-start.4 = (bf16[128,1024]{1,0:T(8,128)(2,1)S(1)}, bf16[128,1024]{1,0:T(8,128)(2,1)}, u32[]{:S(2)}) copy-start(bf16[128,1024]{1,0:T(8,128)(2,1)} %param.11) | copy-start | bytes 786436
  187.0 11.9 %all-to-all-start.4 = ((f32[16,1,64]{2,1,0:T(1,128)}), f32[16,1,64]{2,1,0:T(1,128)S(1)}, u32[]{:S(2)}, u32[]{:S(2)}) async-start(f32[16,1,64]{2,1,0:T(1,128)} %mul.1700), calls=%async_computation.4 | async-start | bytes 16384 | tf_op jit(solution)/shard_map/all_to_all | solution.py:303
Sparse Core Ops, SparseCore 0:
  10.8 83.1 all-gather.4
  96.2 69.1 all-gather.6

commit v11 on v10

--- a/solution.py
+++ b/solution.py
@@ -278,11 +278,28 @@
         jnp.einsum("fa,fb->ab", ln_x_all, grad_hidden, preferred_element_type=jnp.float32)
         * grad_scale
     )
+    moments = jnp.einsum(
+        "fa,fb->ab",
+        ln_all,
+        grad_hidden.astype(jnp.float32),
+        preferred_element_type=jnp.float32,
+        precision=lax.Precision.HIGHEST,
+    )
+    gain_part = jnp.sum(w_in_cols.astype(jnp.float32) * moments, axis=1) * grad_scale
+    packed = lax.all_to_all(
+        jnp.concatenate(
+            [in_cols.reshape(devices, share * 2 * share), gain_part.reshape(devices, share)],
+            axis=1,
+        ),
+        "seq", 0, 0, tiled=True,
+    )
     grad_w_in = (
-        lax.all_to_all(in_cols.reshape(devices, share, 2, share), "seq", 0, 0, tiled=True)
+        packed[:, : share * 2 * share]
+        .reshape(devices, share, 2, share)
         .transpose(1, 2, 0, 3)
         .reshape(share, 2 * width)
     )
+    grad_ln_gain = jnp.sum(packed[:, share * 2 * share :], axis=0)
     back = lax.all_to_all(
         jnp.concatenate([activation, grad_hidden], axis=1).reshape(devices, rows, 3 * share),
         "seq", 0, 0, tiled=True,
@@ -298,10 +315,6 @@
         "fe,ne->fn", hidden_rows[:, 0], w_in_left, preferred_element_type=jnp.float32
     ) + jnp.einsum("fe,ne->fn", hidden_rows[:, 1], w_in_right, preferred_element_type=jnp.float32)
     ln_hat, rstd_ln = norm(frames)
-    gain_part = jnp.sum(grad_ln * ln_hat, axis=0) * grad_scale
-    grad_ln_gain = jnp.sum(
-        lax.all_to_all(gain_part.reshape(devices, share), "seq", 0, 0, tiled=True), axis=0
-    )
     grad_hat = grad_ln * gains
     grad_input = rstd_ln * (
         grad_hat

time: 207 us -> 202 us (0.976)
  starting transfers between devices: 30.5 us -> 22.2 us
  matrix products: 13.5 us -> 19.1 us
  other arithmetic: 31.4 us -> 29 us
    dot_general x0 -> x1, matrix products: none -> 6.38 us  [channel_local(): jnp.einsum('fa,fb->ab', ln_all, grad_hidden.astype(jnp.float32), preferre...]
    all_to_all x2 -> x1, starting transfers between devices: 9.04 us -> 3.64 us  [channel_local(): lax.all_to_all(jnp.concatenate([in_cols.reshape(devices, share * 2 * shar...]
    all_to_all x1, starting transfers between devices: 10.5 us -> 7.6 us  [channel_local(): lax.all_to_all(jnp.concatenate([activation, grad_hidden], axis=1).reshape...]
    all_to_all x2 -> x1, waiting for transfers between devices: 22.7 us -> 20.2 us  [channel_local(): lax.all_to_all(jnp.concatenate([in_cols.reshape(devices, share * 2 * shar...]
    unnamed x49 -> x30, local copies, waits for them, and re-layouts: 6.05 us -> 8.18 us
  transfers between devices with their start and end apart: 7 -> 6, of which waited for: 6 -> 5; matrix products, arithmetic and copies ran while one was open for 26% -> 25% of each run, Pallas kernels for 0% -> 0%
where the time goes in v11:
time: 202 us; the launch traced here: 201 us
  waiting for transfers between devices  94.8 us (47%)
  other arithmetic  29 us (14%)
  starting transfers between devices  22.2 us (11%)
  local copies, waits for them, and re-layouts  21.3 us (11%)
  matrix products  19.1 us (9%)
  between operations  14.5 us (7%)
    all_gather x1, waiting for transfers between devices, channel_local(): lax.all_gather(jnp.concatenate([frames, out_grad], axis=0), 'seq', axis=0)  49.7 us
    all_to_all x1, waiting for transfers between devices, channel_local(): lax.all_to_all(jnp.concatenate([in_cols.reshape(devices, share * 2 * shar...  20.2 us
    all_to_all x1, waiting for transfers between devices, channel_local(): lax.all_to_all(w_in.reshape(share, 2, devices, share).transpose(2, 0, 1,...  14.3 us
    unnamed x30, local copies, waits for them, and re-layouts  8.18 us
    all_to_all x1, starting transfers between devices, channel_local(): lax.all_to_all(jnp.concatenate([activation, grad_hidden], axis=1).reshape...  7.6 us
    all_to_all x1, starting transfers between devices, spread(): return lax.all_to_all(copies, 'seq', 0, 0, tiled=True)  7.39 us
    all_to_all x1, waiting for transfers between devices, channel_local(): lax.all_to_all(jnp.concatenate([activation, grad_hidden], axis=1).reshape...  7.26 us
    dot_general x1, matrix products, channel_local(): jnp.einsum('fa,fb->ab', ln_all, grad_hidden.astype(jnp.float32), preferre...  6.38 us
  transfers between devices with their start and end apart: 6, of which 5 were waited for; matrix products, arithmetic and copies ran while one was open for 25% of the time, Pallas kernels for 0%

profile of v11, /device:TPU:0, one launch (start us, length us, event | category | flops | bytes accessed | tf_op | source)
XLA Modules:
  0.0 200.9 jit_solution(1097234933509478596)
XLA Ops:
  7.3 1.9 pad_maximum_fusion.1
  9.2 0.7 convert_element_type.273
  9.9 0.7 pad_maximum_fusion.6
  10.6 0.6 broadcast_in_dim.2
  11.2 7.4 %all-to-all-start = ((f32[16,1,192]{2,1,0:T(1,128)}), f32[16,1,192]{2,1,0:T(1,128)S(1)}, u32[]{:S(2)}, u32[]{:S(2)}) async-start(f32[16,1,192]{2,1,0:T(1,128)} %broadcast_in_dim.2), calls=%async_computation | async-start | bytes 32768 | tf_op jit(solution)/shard_map/all_to_all | solution.py:176
  18.6 1.5 reshape.184
  20.7 1.1 reshape.199
  21.8 3.3 %all-to-all-done = f32[16,1,192]{2,1,0:T(1,128)S(1)} async-done(((f32[16,1,192]{2,1,0:T(1,128)}), f32[16,1,192]{2,1,0:T(1,128)S(1)}, u32[]{:S(2)}, u32[]{:S(2)}) %all-to-all-start) | async-done | bytes 12320 | tf_op jit(solution)/shard_map/all_to_all | solution.py:176
  25.1 3.5 %all-to-all-start.1 = ((bf16[16,2,4096]{2,1,0:T(2,128)(2,1)}), bf16[16,2,4096]{2,1,0:T(2,128)(2,1)S(1)}, u32[]{:S(2)}, u32[]{:S(2)}) async-start(bf16[16,2,4096]{2,1,0:T(2,128)(2,1)} %reshape.199), calls=%async_computation.1 | async-start | bytes 524288 | tf_op jit(solution)/shard_map/all_to_all | solution.py:186
  28.9 14.3 %all-to-all-done.1 = bf16[16,2,4096]{2,1,0:T(2,128)(2,1)S(1)} async-done(((bf16[16,2,4096]{2,1,0:T(2,128)(2,1)}), bf16[16,2,4096]{2,1,0:T(2,128)(2,1)S(1)}, u32[]{:S(2)}, u32[]{:S(2)}) %all-to-all-start.1) | async-done | bytes 262176 | tf_op jit(solution)/shard_map/all_to_all | solution.py:186
  44.2 49.7 %all-gather.5.cloned.1.call-done = bf16[4096,1024]{1,0:T(8,128)(2,1)} async-done(((bf16[256,1024]{1,0:T(8,128)(2,1)}), bf16[4096,1024]{1,0:T(8,128)(2,1)}) %all-gather.5.cloned.1.call-update) | async-done | bytes 8388624 | tf_op jit(solution)/shard_map/all_gather | solution.py:183
  94.0 0.8 pad_maximum_fusion.3
  95.2 2.8 %slice.622 = bf16[16,128,1024]{2,1,0:T(8,128)(2,1)S(1)} slice(bf16[16,256,1024]{2,1,0:T(8,128)(2,1)} %bitcast.162), slice={[0:16], [128:256], [0:1024]} | slice | bytes 8388608 | tf_op jit(solution)/shard_map/slice | solution.py:185
  98.0 1.8 copy-done.1
  99.8 0.6 convert_reduce_fusion
  100.4 1.6 multiply_reduce_fusion
  102.1 1.4 multiply_convert_fusion.1
  103.5 1.5 fusion.267
  105.2 4.2 %fusion.263 = (f32[64]{0:T(128)S(1)}, f32[2048,64]{0,1:T(8,128)S(1)}) fusion(f32[2048]{0:T(1024)S(1)} %get-tuple-element.109, f32[64]{0:T(128)S(1)} %get-tuple-element.85, f32[2048]{0:T(1024)S(1)} %get-tuple-element.92, f32[64]{0:T(128)S(1)} %get-tuple-element.86, f32[2048]{0:T(1024)S(1)} %get-tuple-element.93, f32[64]{0:T(128)S(1)} %get-tuple-element.57, ...), kind=kLoop, calls=%fused_computation.444 | loop fusion | flops 16121792 | bytes 1040384 | tf_op jit(solution)/shard_map/reduce_sum | solution.py:233
  109.7 1.6 fusion.262
  111.7 1.0 fusion.148
  112.8 5.1 %multiply_convert_fusion.6 = (bf16[2048,64]{0,1:T(8,128)(2,1)S(1)}, f32[2048,64]{0,1:T(8,128)S(1)}) fusion(f32[2048,128]{0,1:T(8,128)S(1)} %fusion.267, f32[2048]{0:T(1024)S(1)} %get-tuple-element.120, f32[64]{0:T(128)S(1)} %get-tuple-element.85, f32[2048]{0:T(1024)S(1)} %get-tuple-element.119, f32[64]{0:T(128)S(1)} %get-tuple-element.86, ...), kind=kLoop, calls=%fused_computation.227 | loop fusion | flops 12582912 | bytes 2088704 | tf_op jit(solution)/shard_map/convert.1
  118.1 1.3 fusion
  119.3 3.2 %copy-done = f32[2048,1024]{1,0:T(8,128)} copy-done((f32[2048,1024]{1,0:T(8,128)}, f32[2048,1024]{1,0:T(8,128)S(1)}, u32[]{:S(2)}) %copy-start) | copy-done | bytes 8388632
  122.6 1.3 fusion.6
  124.0 6.4 %fusion.17 = f32[1024]{0:T(1024)S(1)} fusion(f32[2048,1024]{1,0:T(8,128)} %copy-done, bf16[1024,128]{0,1:T(8,128)(2,1)S(1)} %reshape.185, bf16[2048,64]{0,1:T(8,128)(2,1)S(1)} %multiply_convert_fusion.5, bf16[2048,64]{0,1:T(8,128)(2,1)S(1)} %get-tuple-element.47), kind=kOutput, calls=%fused_computation.19 | convolution fusion | flops 3222666240 | bytes 9179136 | tf_op jit(solution)/shard_map/fa,fb->ab/dot_general | solution.py:281
  130.5 1.2 all_to_all.24
  131.6 3.6 %all-to-all-start.3 = ((f32[16,1,8256]{2,1,0:T(1,128)}), f32[16,1,8256]{2,1,0:T(1,128)S(1)}, u32[]{:S(2)}, u32[]{:S(2)}) async-start(f32[16,1,8256]{2,1,0:T(1,128)} %all_to_all.24), calls=%async_computation.3 | async-start | bytes 1064960 | tf_op jit(solution)/shard_map/all_to_all | solution.py:289
  135.5 1.1 copy_bitcast_fusion
  136.6 0.8 fusion.124
  137.5 0.8 fusion.90
  138.3 20.2 %all-to-all-done.3 = f32[16,1,8256]{2,1,0:T(1,128)S(1)} async-done(((f32[16,1,8256]{2,1,0:T(1,128)}), f32[16,1,8256]{2,1,0:T(1,128)S(1)}, u32[]{:S(2)}, u32[]{:S(2)}) %all-to-all-start.3) | async-done | bytes 528416 | tf_op jit(solution)/shard_map/all_to_all | solution.py:289
  158.5 0.8 copy-done.4
  159.3 7.6 %all-to-all-start.2 = ((bf16[16,128,192]{1,2,0:T(8,128)(2,1)}), bf16[16,128,192]{1,2,0:T(8,128)(2,1)S(1)}, u32[]{:S(2)}, u32[]{:S(2)}) async-start(bf16[16,128,192]{1,2,0:T(8,128)(2,1)} %copy_bitcast_fusion), calls=%async_computation.2 | async-start | bytes 1572864 | tf_op jit(solution)/shard_map/all_to_all | solution.py:303
  167.1 0.8 fusion.72
  168.0 0.7 fusion.106
  169.9 3.7 %convolution_multiply_fusion.2 = f32[64,1024]{1,0:T(8,128)} fusion(bf16[2048,64]{0,1:T(8,128)(2,1)S(1)} %get-tuple-element.53, bf16[2048,1024]{1,0:T(8,128)(2,1)} %bitcast.169), kind=kOutput, calls=%fused_computation.20 | convolution fusion | flops 268500992 | bytes 4718592 | tf_op jit(solution)/shard_map/fa,fb->ab/dot_general | solution.py:243
  173.7 0.8 copy-done.6
  174.6 0.8 reshape.193
  175.3 0.6 copy.38
  175.9 1.2 reshape.194
  177.1 1.2 slice_reduce_fusion
  178.3 7.3 %all-to-all-done.2 = bf16[16,128,192]{1,2,0:T(8,128)(2,1)S(1)} async-done(((bf16[16,128,192]{1,2,0:T(8,128)(2,1)}), bf16[16,128,192]{1,2,0:T(8,128)(2,1)S(1)}, u32[]{:S(2)}, u32[]{:S(2)}) %all-to-all-start.2) | async-done | bytes 786464 | tf_op jit(solution)/shard_map/all_to_all | solution.py:303
  185.7 2.7 %fusion.265 = (bf16[16,64,1024]{2,1,0:T(8,128)(2,1)S(1)}, bf16[16,64,1024]{2,1,0:T(8,128)(2,1)S(1)}) fusion(bf16[16,192,1024]{2,1,0:T(8,128)(2,1)} %bitcast.173), kind=kLoop, calls=%fused_computation.445 | loop fusion | bytes 8388608 | tf_op jit(solution)/shard_map/slice | solution.py:199
  188.4 0.8 fusion.193
  189.3 1.0 fusion.261
  190.3 1.0 fusion.26
  191.3 2.8 %fusion.14 = bf16[128,1024]{1,0:T(8,128)(2,1)} fusion(bf16[16,192,1024]{2,1,0:T(8,128)(2,1)} %bitcast.174, bf16[128,1024]{1,0:T(8,128)(2,1)S(1)} %copy-done.3, bf16[16,128,192]{1,2,0:T(8,128)(2,1)S(1)} %all-to-all-done.2), kind=kOutput, calls=%fused_computation.18 | convolution fusion | flops 268828672 | bytes 2883584 | tf_op jit(solution)/shard_map/dot_general | solution.py:312
  (65 shorter events, 5.5 us)
Async XLA Ops:
  7.2 21.5 %copy-start.3 = (bf16[128,1024]{1,0:T(8,128)(2,1)S(1)}, bf16[128,1024]{1,0:T(8,128)(2,1)}, u32[]{:S(2)}) copy-start(bf16[128,1024]{1,0:T(8,128)(2,1)} %param.9) | copy-start | bytes 786436
  7.2 86.8 %copy-start.7 = (bf16[64,2048]{1,0:T(8,128)(2,1)S(1)}, bf16[64,2048]{1,0:T(8,128)(2,1)}, u32[]{:S(2)}) copy-start(bf16[64,2048]{1,0:T(8,128)(2,1)} %param.13) | copy-start | bytes 786436
  7.2 21.6 %copy-start.10 = (f32[31,64]{1,0:T(8,128)S(1)}, f32[31,64]{1,0:T(8,128)}, u32[]{:S(2)}) copy-start(f32[31,64]{1,0:T(8,128)} %param.14) | copy-start | bytes 23812
  7.2 86.8 %copy-start.9 = (bf16[64,1024]{1,0:T(8,128)(2,1)S(1)}, bf16[64,1024]{1,0:T(8,128)(2,1)}, u32[]{:S(2)}) copy-start(bf16[64,1024]{1,0:T(8,128)(2,1)} %param.17) | copy-start | bytes 393220
  7.2 86.8 %all-gather.5.cloned.1.call-start = ((), (), s32[]{:S(2)}) async-start(), calls=%async_computation.4 | async-start | bytes 8912896 | tf_op jit(solution)/shard_map/all_gather | solution.py:183
  11.2 13.9 %all-to-all-start = ((f32[16,1,192]{2,1,0:T(1,128)}), f32[16,1,192]{2,1,0:T(1,128)S(1)}, u32[]{:S(2)}, u32[]{:S(2)}) async-start(f32[16,1,192]{2,1,0:T(1,128)} %broadcast_in_dim.2), calls=%async_computation | async-start | bytes 32768 | tf_op jit(solution)/shard_map/all_to_all | solution.py:176
  25.1 18.1 %all-to-all-start.1 = ((bf16[16,2,4096]{2,1,0:T(2,128)(2,1)}), bf16[16,2,4096]{2,1,0:T(2,128)(2,1)S(1)}, u32[]{:S(2)}, u32[]{:S(2)}) async-start(bf16[16,2,4096]{2,1,0:T(2,128)(2,1)} %reshape.199), calls=%async_computation.1 | async-start | bytes 524288 | tf_op jit(solution)/shard_map/all_to_all | solution.py:186
  28.6 157.1 %all-gather.7.cloned.1.call-start = ((), (), s32[]{:S(2)}) async-start(), calls=%async_computation.5 | async-start | bytes 6684672 | tf_op jit(solution)/shard_map/all_gather | solution.py:192
  95.2 4.6 %copy-start.1 = (bf16[4096,1024]{1,0:T(8,128)(2,1)S(1)}, bf16[4096,1024]{1,0:T(8,128)(2,1)}, u32[]{:S(2)}) copy-start(bf16[4096,1024]{1,0:T(8,128)(2,1)} %all-gather.5.cloned.1.call-done) | copy-start | bytes 25165828
  99.8 9.8 %copy-start.2 = (bf16[16,128,1024]{2,1,0:T(8,128)(2,1)}, bf16[16,128,1024]{2,1,0:T(8,128)(2,1)S(1)}, u32[]{:S(2)}) copy-start(bf16[16,128,1024]{2,1,0:T(8,128)(2,1)S(1)} %slice.622) | copy-start | bytes 12582916
  103.5 6.1 %copy-start.11 = (f32[64]{0:T(128)S(1)}, f32[64]{0:T(128)}, u32[]{:S(2)}) copy-start(f32[64]{0:T(128)} %param.15) | copy-start | bytes 772
  103.5 6.2 %copy-start.12 = (f32[64]{0:T(128)S(1)}, f32[64]{0:T(128)}, u32[]{:S(2)}) copy-start(f32[64]{0:T(128)} %param.16) | copy-start | bytes 772
  119.3 3.2 %copy-start = (f32[2048,1024]{1,0:T(8,128)}, f32[2048,1024]{1,0:T(8,128)S(1)}, u32[]{:S(2)}) copy-start(f32[2048,1024]{1,0:T(8,128)S(1)} %fusion) | copy-start | bytes 25165828
  131.6 26.8 %all-to-all-start.3 = ((f32[16,1,8256]{2,1,0:T(1,128)}), f32[16,1,8256]{2,1,0:T(1,128)S(1)}, u32[]{:S(2)}, u32[]{:S(2)}) async-start(f32[16,1,8256]{2,1,0:T(1,128)} %all_to_all.24), calls=%async_computation.3 | async-start | bytes 1064960 | tf_op jit(solution)/shard_map/all_to_all | solution.py:289
  158.5 0.8 copy-start.4
  159.3 26.3 %all-to-all-start.2 = ((bf16[16,128,192]{1,2,0:T(8,128)(2,1)}), bf16[16,128,192]{1,2,0:T(8,128)(2,1)S(1)}, u32[]{:S(2)}, u32[]{:S(2)}) async-start(bf16[16,128,192]{1,2,0:T(8,128)(2,1)} %copy_bitcast_fusion), calls=%async_computation.2 | async-start | bytes 1572864 | tf_op jit(solution)/shard_map/all_to_all | solution.py:303
  166.9 6.8 %copy-start.5 = (f32[16,1,8256]{2,1,0:T(1,128)S(1)}, f32[16,1,8256]{2,1,0:T(1,128)}, u32[]{:S(2)}) copy-start(f32[16,1,8256]{2,1,0:T(1,128)} %copy-done.4) | copy-start | bytes 1585156
  173.7 0.8 copy-start.6
  188.4 1.8 copy-start.8
Sparse Core Ops, SparseCore 0:
  10.8 83.1 all-gather.4
  96.2 69.3 all-gather.6

commit v12 on v11

--- a/solution.py
+++ b/solution.py
@@ -286,13 +286,21 @@
         precision=lax.Precision.HIGHEST,
     )
     gain_part = jnp.sum(w_in_cols.astype(jnp.float32) * moments, axis=1) * grad_scale
-    packed = lax.all_to_all(
-        jnp.concatenate(
-            [in_cols.reshape(devices, share * 2 * share), gain_part.reshape(devices, share)],
-            axis=1,
-        ),
+    back = lax.all_to_all(
+        jnp.concatenate([activation, grad_hidden], axis=1).reshape(devices, rows, 3 * share),
         "seq", 0, 0, tiled=True,
     )
+    act_rows = back[:, :, :share].transpose(1, 0, 2).reshape(rows, width)
+    payload, _ = lax.optimization_barrier(
+        (
+            jnp.concatenate(
+                [in_cols.reshape(devices, share * 2 * share), gain_part.reshape(devices, share)],
+                axis=1,
+            ),
+            back,
+        )
+    )
+    packed = lax.all_to_all(payload, "seq", 0, 0, tiled=True)
     grad_w_in = (
         packed[:, : share * 2 * share]
         .reshape(devices, share, 2, share)
@@ -300,11 +308,6 @@
         .reshape(share, 2 * width)
     )
     grad_ln_gain = jnp.sum(packed[:, share * 2 * share :], axis=0)
-    back = lax.all_to_all(
-        jnp.concatenate([activation, grad_hidden], axis=1).reshape(devices, rows, 3 * share),
-        "seq", 0, 0, tiled=True,
-    )
-    act_rows = back[:, :, :share].transpose(1, 0, 2).reshape(rows, width)
     hidden_rows = (
         back[:, :, share:].reshape(devices, rows, 2, share).transpose(1, 2, 0, 3)
         .reshape(rows, 2, width)

time: 202 us -> 206 us (1.020)
  other arithmetic: 29 us -> 35.9 us
  starting transfers between devices: 22.2 us -> 27 us
  matrix products: 19.1 us -> 15.7 us
  waiting for transfers between devices: 94.8 us -> 92 us
    all_to_all x1, waiting for transfers between devices: 20.2 us -> 7.8 us  [channel_local(): packed = lax.all_to_all(payload, 'seq', 0, 0, tiled=True)]
    all_to_all x1, waiting for transfers between devices: 7.26 us -> 18.7 us  [channel_local(): lax.all_to_all(jnp.concatenate([activation, grad_hidden], axis=1).reshape...]
    all_to_all x1, starting transfers between devices: 3.64 us -> 12.1 us  [channel_local(): packed = lax.all_to_all(payload, 'seq', 0, 0, tiled=True)]
    all_to_all x1, starting transfers between devices: 7.6 us -> 3.61 us  [channel_local(): lax.all_to_all(jnp.concatenate([activation, grad_hidden], axis=1).reshape...]
    unnamed x30 -> x134, local copies, waits for them, and re-layouts: 8.18 us -> 4.74 us
    dot_general x1, matrix products: 6.38 us -> 2.98 us  [channel_local(): jnp.einsum('fa,fb->ab', ln_all, grad_hidden.astype(jnp.float32), preferre...]
  transfers between devices with their start and end apart: 6 -> 6, of which waited for: 5 -> 5; matrix products, arithmetic and copies ran while one was open for 25% -> 27% of each run, Pallas kernels for 0% -> 0%
where the time goes in v12:
time: 206 us; the launch traced here: 205 us
  waiting for transfers between devices  92 us (45%)
  other arithmetic  35.9 us (17%)
  starting transfers between devices  27 us (13%)
  local copies, waits for them, and re-layouts  19.5 us (9%)
  matrix products  15.7 us (8%)
  between operations  15.2 us (7%)
    all_gather x1, waiting for transfers between devices, channel_local(): lax.all_gather(jnp.concatenate([frames, out_grad], axis=0), 'seq', axis=0)  49.4 us
    all_to_all x1, waiting for transfers between devices, channel_local(): lax.all_to_all(jnp.concatenate([activation, grad_hidden], axis=1).reshape...  18.7 us
    all_to_all x1, waiting for transfers between devices, channel_local(): lax.all_to_all(w_in.reshape(share, 2, devices, share).transpose(2, 0, 1,...  13.8 us
    all_to_all x1, starting transfers between devices, channel_local(): packed = lax.all_to_all(payload, 'seq', 0, 0, tiled=True)  12.1 us
    all_to_all x1, waiting for transfers between devices, channel_local(): packed = lax.all_to_all(payload, 'seq', 0, 0, tiled=True)  7.8 us
    all_to_all x1, starting transfers between devices, spread(): return lax.all_to_all(copies, 'seq', 0, 0, tiled=True)  7.39 us
    reduce_sum x6, other arithmetic, channel_local(): jnp.sum(grad_conv * padded_glu[tap_index:tap_index + stream].astype(jnp.f...  5.73 us
    another operation x2, other arithmetic  5.53 us
  transfers between devices with their start and end apart: 6, of which 5 were waited for; matrix products, arithmetic and copies ran while one was open for 27% of the time, Pallas kernels for 0%

profile of v12, /device:TPU:0, one launch (start us, length us, event | category | flops | bytes accessed | tf_op | source)
XLA Modules:
  0.0 205.3 jit_solution(9305315491623506365)
XLA Ops:
  7.3 1.9 pad_maximum_fusion.1
  9.2 0.7 convert_element_type.273
  9.9 0.7 pad_maximum_fusion.6
  11.2 7.4 %all-to-all-start = ((f32[16,1,192]{2,1,0:T(1,128)}), f32[16,1,192]{2,1,0:T(1,128)S(1)}, u32[]{:S(2)}, u32[]{:S(2)}) async-start(f32[16,1,192]{2,1,0:T(1,128)} %broadcast_in_dim.2), calls=%async_computation | async-start | bytes 32768 | tf_op jit(solution)/shard_map/all_to_all | solution.py:176
  18.6 1.1 convert_reduce_fusion.1
  19.7 1.5 reshape.184
  21.8 1.1 reshape.199
  22.9 2.2 %all-to-all-done = f32[16,1,192]{2,1,0:T(1,128)S(1)} async-done(((f32[16,1,192]{2,1,0:T(1,128)}), f32[16,1,192]{2,1,0:T(1,128)S(1)}, u32[]{:S(2)}, u32[]{:S(2)}) %all-to-all-start) | async-done | bytes 12320 | tf_op jit(solution)/shard_map/all_to_all | solution.py:176
  25.1 3.8 %all-to-all-start.1 = ((bf16[16,2,4096]{2,1,0:T(2,128)(2,1)}), bf16[16,2,4096]{2,1,0:T(2,128)(2,1)S(1)}, u32[]{:S(2)}, u32[]{:S(2)}) async-start(bf16[16,2,4096]{2,1,0:T(2,128)(2,1)} %reshape.199), calls=%async_computation.1 | async-start | bytes 524288 | tf_op jit(solution)/shard_map/all_to_all | solution.py:186
  29.7 13.8 %all-to-all-done.1 = bf16[16,2,4096]{2,1,0:T(2,128)(2,1)S(1)} async-done(((bf16[16,2,4096]{2,1,0:T(2,128)(2,1)}), bf16[16,2,4096]{2,1,0:T(2,128)(2,1)S(1)}, u32[]{:S(2)}, u32[]{:S(2)}) %all-to-all-start.1) | async-done | bytes 262176 | tf_op jit(solution)/shard_map/all_to_all | solution.py:186
  44.5 49.4 %all-gather.5.cloned.1.call-done = bf16[4096,1024]{1,0:T(8,128)(2,1)} async-done(((bf16[256,1024]{1,0:T(8,128)(2,1)}), bf16[4096,1024]{1,0:T(8,128)(2,1)}) %all-gather.5.cloned.1.call-update) | async-done | bytes 8388624 | tf_op jit(solution)/shard_map/all_gather | solution.py:183
  94.0 0.8 pad_maximum_fusion.3
  95.8 2.8 %slice.622 = bf16[16,128,1024]{2,1,0:T(8,128)(2,1)S(1)} slice(bf16[16,256,1024]{2,1,0:T(8,128)(2,1)} %bitcast.162), slice={[0:16], [128:256], [0:1024]} | slice | bytes 8388608 | tf_op jit(solution)/shard_map/slice | solution.py:185
  98.7 1.8 copy-done
  101.1 1.0 fusion.258
  102.1 1.4 multiply_reduce_fusion
  104.2 1.4 multiply_convert_fusion.1
  105.6 1.5 fusion.267
  107.4 4.2 %fusion.263 = (f32[64]{0:T(128)S(1)}, f32[2048,64]{0,1:T(8,128)S(1)}) fusion(f32[2048]{0:T(1024)S(1)} %get-tuple-element.111, f32[64]{0:T(128)S(1)} %get-tuple-element.87, f32[2048]{0:T(1024)S(1)} %get-tuple-element.94, f32[64]{0:T(128)S(1)} %get-tuple-element.88, f32[2048]{0:T(1024)S(1)} %get-tuple-element.95, f32[64]{0:T(128)S(1)} %get-tuple-element.59, ...), kind=kLoop, calls=%fused_computation.444 | loop fusion | flops 16121792 | bytes 1040384 | tf_op jit(solution)/shard_map/reduce_sum | solution.py:233
  112.0 1.6 fusion.262
  114.1 1.6 fusion.148
  115.8 5.3 %multiply_convert_fusion.6 = (bf16[2048,64]{0,1:T(8,128)(2,1)S(1)}, f32[2048,64]{0,1:T(8,128)S(1)}) fusion(f32[2048,128]{0,1:T(8,128)S(1)} %fusion.267, f32[2048]{0:T(1024)S(1)} %get-tuple-element.122, f32[64]{0:T(128)S(1)} %copy-done.44, f32[2048]{0:T(1024)S(1)} %get-tuple-element.121, f32[64]{0:T(128)S(1)} %copy-done.46, f32[2048]{0:T(1024)S(1)} %get-tuple-element.120, ...), kind=kLoop, calls=%fused_computation.227 | loop fusion | flops 12582912 | bytes 2088704 | tf_op jit(solution)/shard_map/convert.1
  121.4 1.1 copy_bitcast_fusion
  122.5 3.6 %all-to-all-start.2 = ((bf16[16,128,192]{1,2,0:T(8,128)(2,1)}), bf16[16,128,192]{1,2,0:T(8,128)(2,1)S(1)}, u32[]{:S(2)}, u32[]{:S(2)}) async-start(bf16[16,128,192]{1,2,0:T(8,128)(2,1)} %copy_bitcast_fusion), calls=%async_computation.2 | async-start | bytes 1572864 | tf_op jit(solution)/shard_map/all_to_all | solution.py:289
  126.1 1.4 fusion.124
  127.6 2.8 %fusion = f32[2048,1024]{1,0:T(8,128)S(1)} fusion(f32[2048]{0:T(1024)S(1)} %copy-done.23, f32[2048]{0:T(1024)S(1)} %copy-done.22, bf16[16,256,1024]{2,1,0:T(8,128)(2,1)} %bitcast.163), kind=kLoop, calls=%fused_computation.1 | loop fusion | flops 6291456 | bytes 12599296 | tf_op jit(solution)/shard_map/mul | solution.py:208
  130.3 3.0 %fusion.17 = f32[1024]{0:T(1024)S(1)} fusion(f32[2048,1024]{1,0:T(8,128)S(1)} %fusion, bf16[1024,128]{0,1:T(8,128)(2,1)S(1)} %reshape.185, bf16[2048,64]{0,1:T(8,128)(2,1)S(1)} %multiply_convert_fusion.5, bf16[2048,64]{0,1:T(8,128)(2,1)S(1)} %get-tuple-element.49), kind=kOutput, calls=%fused_computation.19 | convolution fusion | flops 3222666240 | bytes 9179136 | tf_op jit(solution)/shard_map/fa,fb->ab/dot_general | solution.py:281
  133.4 1.3 fusion.6
  135.1 0.9 reshape.192
  136.1 0.8 fusion.90
  136.9 0.8 fusion.106
  137.7 1.1 pad_maximum_fusion
  138.8 18.7 %all-to-all-done.2 = bf16[16,128,192]{1,2,0:T(8,128)(2,1)S(1)} async-done(((bf16[16,128,192]{1,2,0:T(8,128)(2,1)}), bf16[16,128,192]{1,2,0:T(8,128)(2,1)S(1)}, u32[]{:S(2)}, u32[]{:S(2)}) %all-to-all-start.2) | async-done | bytes 786464 | tf_op jit(solution)/shard_map/all_to_all | solution.py:289
  157.5 1.2 all_to_all.24
  158.7 12.1 %all-to-all-start.3 = ((f32[16,1,8256]{2,1,0:T(1,128)}), f32[16,1,8256]{2,1,0:T(1,128)S(1)}, u32[]{:S(2)}, u32[]{:S(2)}) async-start(f32[16,1,8256]{2,1,0:T(1,128)} %all_to_all.24), calls=%async_computation.3 | async-start | bytes 1064960 | tf_op jit(solution)/shard_map/all_to_all | solution.py:303
  170.8 0.8 fusion.72
  173.0 3.7 %convolution_multiply_fusion.2 = f32[64,1024]{1,0:T(8,128)} fusion(bf16[2048,64]{0,1:T(8,128)(2,1)S(1)} %get-tuple-element.55, bf16[2048,1024]{1,0:T(8,128)(2,1)} %bitcast.169), kind=kOutput, calls=%fused_computation.20 | convolution fusion | flops 268500992 | bytes 4718592 | tf_op jit(solution)/shard_map/fa,fb->ab/dot_general | solution.py:243
  176.7 0.8 copy.35
  177.6 7.8 %all-to-all-done.3 = f32[16,1,8256]{2,1,0:T(1,128)S(1)} async-done(((f32[16,1,8256]{2,1,0:T(1,128)}), f32[16,1,8256]{2,1,0:T(1,128)S(1)}, u32[]{:S(2)}, u32[]{:S(2)}) %all-to-all-start.3) | async-done | bytes 528416 | tf_op jit(solution)/shard_map/all_to_all | solution.py:303
  185.4 0.8 copy-done.3
  186.3 0.8 reshape.193
  187.6 1.2 reshape.194
  188.8 1.2 slice_reduce_fusion
  190.0 2.8 %fusion.265 = (bf16[16,64,1024]{2,1,0:T(8,128)(2,1)S(1)}, bf16[16,64,1024]{2,1,0:T(8,128)(2,1)S(1)}) fusion(bf16[16,192,1024]{2,1,0:T(8,128)(2,1)} %bitcast.173), kind=kLoop, calls=%fused_computation.445 | loop fusion | bytes 8388608 | tf_op jit(solution)/shard_map/slice | solution.py:199
  192.8 0.8 fusion.193
  193.7 1.0 fusion.261
  194.7 1.0 fusion.26
  195.7 2.8 %fusion.14 = bf16[128,1024]{1,0:T(8,128)(2,1)} fusion(bf16[16,192,1024]{2,1,0:T(8,128)(2,1)} %bitcast.174, bf16[128,1024]{1,0:T(8,128)(2,1)S(1)} %copy-done.2, bf16[16,128,192]{1,2,0:T(8,128)(2,1)S(1)} %all-to-all-done.2), kind=kOutput, calls=%fused_computation.18 | convolution fusion | flops 268828672 | bytes 2883584 | tf_op jit(solution)/shard_map/dot_general | solution.py:315
  (169 shorter events, 8.7 us)
Async XLA Ops:
  7.2 21.8 %copy-start.2 = (bf16[128,1024]{1,0:T(8,128)(2,1)S(1)}, bf16[128,1024]{1,0:T(8,128)(2,1)}, u32[]{:S(2)}) copy-start(bf16[128,1024]{1,0:T(8,128)(2,1)} %param.9) | copy-start | bytes 786436
  7.2 86.8 %copy-start.5 = (bf16[64,2048]{1,0:T(8,128)(2,1)S(1)}, bf16[64,2048]{1,0:T(8,128)(2,1)}, u32[]{:S(2)}) copy-start(bf16[64,2048]{1,0:T(8,128)(2,1)} %param.13) | copy-start | bytes 786436
  7.2 22.4 %copy-start.24 = (f32[31,64]{1,0:T(8,128)S(1)}, f32[31,64]{1,0:T(8,128)}, u32[]{:S(2)}) copy-start(f32[31,64]{1,0:T(8,128)} %param.14) | copy-start | bytes 23812
  7.2 86.8 %copy-start.21 = (bf16[64,1024]{1,0:T(8,128)(2,1)S(1)}, bf16[64,1024]{1,0:T(8,128)(2,1)}, u32[]{:S(2)}) copy-start(bf16[64,1024]{1,0:T(8,128)(2,1)} %param.17) | copy-start | bytes 393220
  7.2 86.8 %all-gather.5.cloned.1.call-start = ((), (), s32[]{:S(2)}) async-start(), calls=%async_computation.4 | async-start | bytes 8912896 | tf_op jit(solution)/shard_map/all_gather | solution.py:183
  11.2 13.9 %all-to-all-start = ((f32[16,1,192]{2,1,0:T(1,128)}), f32[16,1,192]{2,1,0:T(1,128)S(1)}, u32[]{:S(2)}, u32[]{:S(2)}) async-start(f32[16,1,192]{2,1,0:T(1,128)} %broadcast_in_dim.2), calls=%async_computation | async-start | bytes 32768 | tf_op jit(solution)/shard_map/all_to_all | solution.py:176
  25.1 18.4 %all-to-all-start.1 = ((bf16[16,2,4096]{2,1,0:T(2,128)(2,1)}), bf16[16,2,4096]{2,1,0:T(2,128)(2,1)S(1)}, u32[]{:S(2)}, u32[]{:S(2)}) async-start(bf16[16,2,4096]{2,1,0:T(2,128)(2,1)} %reshape.199), calls=%async_computation.1 | async-start | bytes 524288 | tf_op jit(solution)/shard_map/all_to_all | solution.py:186
  28.9 161.1 %all-gather.7.cloned.1.call-start = ((), (), s32[]{:S(2)}) async-start(), calls=%async_computation.5 | async-start | bytes 6684672 | tf_op jit(solution)/shard_map/all_gather | solution.py:192
  29.6 77.7 %copy-start.25 = (f32[64]{0:T(128)}, f32[64]{0:T(128)S(1)}, u32[]{:S(2)}) copy-start(f32[64]{0:T(128)S(1)} %get-tuple-element.78) | copy-start | bytes 772
  29.6 77.7 %copy-start.27 = (f32[64]{0:T(128)}, f32[64]{0:T(128)S(1)}, u32[]{:S(2)}) copy-start(f32[64]{0:T(128)S(1)} %get-tuple-element.79) | copy-start | bytes 772
  29.6 77.7 %copy-start.29 = (f32[64]{0:T(128)}, f32[64]{0:T(128)S(1)}, u32[]{:S(2)}) copy-start(f32[64]{0:T(128)S(1)} %get-tuple-element.80) | copy-start | bytes 772
  29.6 77.7 %copy-start.31 = (f32[64]{0:T(128)}, f32[64]{0:T(128)S(1)}, u32[]{:S(2)}) copy-start(f32[64]{0:T(128)S(1)} %get-tuple-element.81) | copy-start | bytes 772
  29.6 77.7 %copy-start.33 = (f32[64]{0:T(128)}, f32[64]{0:T(128)S(1)}, u32[]{:S(2)}) copy-start(f32[64]{0:T(128)S(1)} %get-tuple-element.82) | copy-start | bytes 772
  29.6 77.7 %copy-start.35 = (f32[64]{0:T(128)}, f32[64]{0:T(128)S(1)}, u32[]{:S(2)}) copy-start(f32[64]{0:T(128)S(1)} %get-tuple-element.83) | copy-start | bytes 772
  29.6 77.7 %copy-start.37 = (f32[64]{0:T(128)}, f32[64]{0:T(128)S(1)}, u32[]{:S(2)}) copy-start(f32[64]{0:T(128)S(1)} %get-tuple-element.84) | copy-start | bytes 772
  29.6 77.7 %copy-start.39 = (f32[64]{0:T(128)}, f32[64]{0:T(128)S(1)}, u32[]{:S(2)}) copy-start(f32[64]{0:T(128)S(1)} %get-tuple-element.85) | copy-start | bytes 772
  29.6 77.7 %copy-start.41 = (f32[64]{0:T(128)}, f32[64]{0:T(128)S(1)}, u32[]{:S(2)}) copy-start(f32[64]{0:T(128)S(1)} %get-tuple-element.86) | copy-start | bytes 772
  29.6 77.7 %copy-start.43 = (f32[64]{0:T(128)}, f32[64]{0:T(128)S(1)}, u32[]{:S(2)}) copy-start(f32[64]{0:T(128)S(1)} %get-tuple-element.87) | copy-start | bytes 772
  29.7 77.7 %copy-start.45 = (f32[64]{0:T(128)}, f32[64]{0:T(128)S(1)}, u32[]{:S(2)}) copy-start(f32[64]{0:T(128)S(1)} %get-tuple-element.88) | copy-start | bytes 772
  95.6 20.0 %copy-start.7 = (f32[2048]{0:T(1024)}, f32[2048]{0:T(1024)S(1)}, u32[]{:S(2)}) copy-start(f32[2048]{0:T(1024)S(1)} %get-tuple-element.120) | copy-start | bytes 24580
  95.7 20.0 %copy-start.9 = (f32[2048]{0:T(1024)}, f32[2048]{0:T(1024)S(1)}, u32[]{:S(2)}) copy-start(f32[2048]{0:T(1024)S(1)} %get-tuple-element.121) | copy-start | bytes 24580
  95.7 20.0 %copy-start.11 = (f32[2048]{0:T(1024)}, f32[2048]{0:T(1024)S(1)}, u32[]{:S(2)}) copy-start(f32[2048]{0:T(1024)S(1)} %get-tuple-element.112) | copy-start | bytes 24580
  95.7 20.0 %copy-start.13 = (f32[2048]{0:T(1024)}, f32[2048]{0:T(1024)S(1)}, u32[]{:S(2)}) copy-start(f32[2048]{0:T(1024)S(1)} %get-tuple-element.113) | copy-start | bytes 24580
  95.7 20.0 %copy-start.15 = (f32[2048]{0:T(1024)}, f32[2048]{0:T(1024)S(1)}, u32[]{:S(2)}) copy-start(f32[2048]{0:T(1024)S(1)} %get-tuple-element.114) | copy-start | bytes 24580
  95.7 20.0 %copy-start.17 = (f32[2048]{0:T(1024)}, f32[2048]{0:T(1024)S(1)}, u32[]{:S(2)}) copy-start(f32[2048]{0:T(1024)S(1)} %get-tuple-element.115) | copy-start | bytes 24580
  95.7 20.0 %copy-start.19 = (f32[2048]{0:T(1024)}, f32[2048]{0:T(1024)S(1)}, u32[]{:S(2)}) copy-start(f32[2048]{0:T(1024)S(1)} %get-tuple-element.122) | copy-start | bytes 24580
  100.5 11.4 %copy-start.1 = (bf16[16,128,1024]{2,1,0:T(8,128)(2,1)}, bf16[16,128,1024]{2,1,0:T(8,128)(2,1)S(1)}, u32[]{:S(2)}) copy-start(bf16[16,128,1024]{2,1,0:T(8,128)(2,1)S(1)} %slice.622) | copy-start | bytes 12582916
  105.6 6.3 %copy-start.61 = (f32[64]{0:T(128)S(1)}, f32[64]{0:T(128)}, u32[]{:S(2)}) copy-start(f32[64]{0:T(128)} %param.15) | copy-start | bytes 772
  105.6 6.3 %copy-start.64 = (f32[64]{0:T(128)S(1)}, f32[64]{0:T(128)}, u32[]{:S(2)}) copy-start(f32[64]{0:T(128)} %param.16) | copy-start | bytes 772
  113.5 9.0 %copy-start.62 = (f32[64]{0:T(128)}, f32[64]{0:T(128)S(1)}, u32[]{:S(2)}) copy-start(f32[64]{0:T(128)S(1)} %get-tuple-element.47) | copy-start | bytes 772
  115.7 11.9 %copy-start.22 = (f32[2048]{0:T(1024)S(1)}, f32[2048]{0:T(1024)}, u32[]{:S(2)}) copy-start(f32[2048]{0:T(1024)} %get-tuple-element.89) | copy-start | bytes 24580
  115.7 11.9 %copy-start.23 = (f32[2048]{0:T(1024)S(1)}, f32[2048]{0:T(1024)}, u32[]{:S(2)}) copy-start(f32[2048]{0:T(1024)} %get-tuple-element.91) | copy-start | bytes 24580
  122.5 35.0 %all-to-all-start.2 = ((bf16[16,128,192]{1,2,0:T(8,128)(2,1)}), bf16[16,128,192]{1,2,0:T(8,128)(2,1)S(1)}, u32[]{:S(2)}, u32[]{:S(2)}) async-start(bf16[16,128,192]{1,2,0:T(8,128)(2,1)} %copy_bitcast_fusion), calls=%async_computation.2 | async-start | bytes 1572864 | tf_op jit(solution)/shard_map/all_to_all | solution.py:289
  134.7 36.0 %copy-start.8 = (f32[2048]{0:T(1024)S(1)}, f32[2048]{0:T(1024)}, u32[]{:S(2)}) copy-start(f32[2048]{0:T(1024)} %copy-done.7) | copy-start | bytes 24580
  134.7 36.0 %copy-start.10 = (f32[2048]{0:T(1024)S(1)}, f32[2048]{0:T(1024)}, u32[]{:S(2)}) copy-start(f32[2048]{0:T(1024)} %copy-done.9) | copy-start | bytes 24580
  134.7 36.9 %copy-start.49 = (f32[64]{0:T(128)S(1)}, f32[64]{0:T(128)}, u32[]{:S(2)}) copy-start(f32[64]{0:T(128)} %get-tuple-element.21) | copy-start | bytes 772
  134.8 36.9 %copy-start.50 = (f32[64]{0:T(128)S(1)}, f32[64]{0:T(128)}, u32[]{:S(2)}) copy-start(f32[64]{0:T(128)} %get-tuple-element.22) | copy-start | bytes 772
  134.8 36.9 %copy-start.51 = (f32[64]{0:T(128)S(1)}, f32[64]{0:T(128)}, u32[]{:S(2)}) copy-start(f32[64]{0:T(128)} %get-tuple-element.23) | copy-start | bytes 772
  134.8 36.9 %copy-start.52 = (f32[64]{0:T(128)S(1)}, f32[64]{0:T(128)}, u32[]{:S(2)}) copy-start(f32[64]{0:T(128)} %get-tuple-element.24) | copy-start | bytes 772
  134.8 36.9 %copy-start.53 = (f32[64]{0:T(128)S(1)}, f32[64]{0:T(128)}, u32[]{:S(2)}) copy-start(f32[64]{0:T(128)} %get-tuple-element.25) | copy-start | bytes 772
  134.8 36.9 %copy-start.54 = (f32[64]{0:T(128)S(1)}, f32[64]{0:T(128)}, u32[]{:S(2)}) copy-start(f32[64]{0:T(128)} %get-tuple-element.14) | copy-start | bytes 772
  134.8 36.9 %copy-start.55 = (f32[64]{0:T(128)S(1)}, f32[64]{0:T(128)}, u32[]{:S(2)}) copy-start(f32[64]{0:T(128)} %get-tuple-element.15) | copy-start | bytes 772
  134.8 36.9 %copy-start.56 = (f32[64]{0:T(128)S(1)}, f32[64]{0:T(128)}, u32[]{:S(2)}) copy-start(f32[64]{0:T(128)} %get-tuple-element.16) | copy-start | bytes 772
  134.8 36.9 %copy-start.57 = (f32[64]{0:T(128)S(1)}, f32[64]{0:T(128)}, u32[]{:S(2)}) copy-start(f32[64]{0:T(128)} %get-tuple-element.17) | copy-start | bytes 772
  134.8 36.9 %copy-start.58 = (f32[64]{0:T(128)S(1)}, f32[64]{0:T(128)}, u32[]{:S(2)}) copy-start(f32[64]{0:T(128)} %get-tuple-element.18) | copy-start | bytes 772
  134.9 36.9 %copy-start.59 = (f32[64]{0:T(128)S(1)}, f32[64]{0:T(128)}, u32[]{:S(2)}) copy-start(f32[64]{0:T(128)} %get-tuple-element.19) | copy-start | bytes 772
  134.9 37.0 %copy-start.63 = (f32[64]{0:T(128)S(1)}, f32[64]{0:T(128)}, u32[]{:S(2)}) copy-start(f32[64]{0:T(128)} %copy-done.62) | copy-start | bytes 772
  158.7 26.7 %all-to-all-start.3 = ((f32[16,1,8256]{2,1,0:T(1,128)}), f32[16,1,8256]{2,1,0:T(1,128)S(1)}, u32[]{:S(2)}, u32[]{:S(2)}) async-start(f32[16,1,8256]{2,1,0:T(1,128)} %all_to_all.24), calls=%async_computation.3 | async-start | bytes 1064960 | tf_op jit(solution)/shard_map/all_to_all | solution.py:303
  (23 other events, 73.1 us)
Sparse Core Ops, SparseCore 0:
  10.8 83.1 all-gather.4
  96.2 74.7 all-gather.6

commit v13 on v11

--- a/solution.py
+++ b/solution.py
@@ -278,12 +278,14 @@
         jnp.einsum("fa,fb->ab", ln_x_all, grad_hidden, preferred_element_type=jnp.float32)
         * grad_scale
     )
+    ln_head = lax.reduce_precision(ln_all, exponent_bits=8, mantissa_bits=7)
     moments = jnp.einsum(
+        "fa,fb->ab", ln_head.astype(jnp.bfloat16), grad_hidden, preferred_element_type=jnp.float32
+    ) + jnp.einsum(
         "fa,fb->ab",
-        ln_all,
-        grad_hidden.astype(jnp.float32),
+        (ln_all - ln_head).astype(jnp.bfloat16),
+        grad_hidden,
         preferred_element_type=jnp.float32,
-        precision=lax.Precision.HIGHEST,
     )
     gain_part = jnp.sum(w_in_cols.astype(jnp.float32) * moments, axis=1) * grad_scale
     packed = lax.all_to_all(

time: 202 us -> 200 us (0.990)
  other arithmetic: 29 us -> 32.3 us
  waiting for transfers between devices: 94.8 us -> 91.5 us
  matrix products: 19.1 us -> 16.7 us
  starting transfers between devices: 22.2 us -> 24.5 us
    convert_element_type x1 -> x2, other arithmetic: 1.42 us -> 6.05 us  [channel_local(): ln_x_all = (ln_all * gains).astype(jnp.bfloat16)]
    unnamed x30 -> x24, local copies, waits for them, and re-layouts: 8.18 us -> 4.62 us
    dot_general x1 -> x2, matrix products: 6.38 us -> 4.01 us  [the longest x1 3.21 us: channel_local(): jnp.einsum('fa,fb->ab', ln_head.astype(jnp.bfloat16), grad_hidden, prefer...]
  transfers between devices with their start and end apart: 6 -> 6, of which waited for: 5 -> 5; matrix products, arithmetic and copies ran while one was open for 25% -> 27% of each run, Pallas kernels for 0% -> 0%
where the time goes in v13:
time: 200 us; the launch traced here: 199 us
  waiting for transfers between devices  91.5 us (46%)
  other arithmetic  32.3 us (16%)
  starting transfers between devices  24.5 us (12%)
  local copies, waits for them, and re-layouts  19.7 us (10%)
  matrix products  16.7 us (8%)
  between operations  14.5 us (7%)
    all_gather x1, waiting for transfers between devices, channel_local(): lax.all_gather(jnp.concatenate([frames, out_grad], axis=0), 'seq', axis=0)  48.5 us
    all_to_all x1, waiting for transfers between devices, channel_local(): lax.all_to_all(jnp.concatenate([in_cols.reshape(devices, share * 2 * shar...  20.2 us
    all_to_all x1, waiting for transfers between devices, channel_local(): lax.all_to_all(w_in.reshape(share, 2, devices, share).transpose(2, 0, 1,...  14.1 us
    all_to_all x1, starting transfers between devices, channel_local(): lax.all_to_all(jnp.concatenate([activation, grad_hidden], axis=1).reshape...  8.76 us
    all_to_all x1, starting transfers between devices, spread(): return lax.all_to_all(copies, 'seq', 0, 0, tiled=True)  7.39 us
    all_to_all x1, waiting for transfers between devices, channel_local(): lax.all_to_all(jnp.concatenate([activation, grad_hidden], axis=1).reshape...  7.28 us
    convert_element_type x2, other arithmetic, channel_local(): ln_x_all = (ln_all * gains).astype(jnp.bfloat16)  6.05 us
    another operation x2, other arithmetic  5.24 us
  transfers between devices with their start and end apart: 6, of which 5 were waited for; matrix products, arithmetic and copies ran while one was open for 27% of the time, Pallas kernels for 0%

profile of v13, /device:TPU:0, one launch (start us, length us, event | category | flops | bytes accessed | tf_op | source)
XLA Modules:
  0.0 199.2 jit_solution(2623336773745442727)
XLA Ops:
  7.2 1.9 pad_maximum_fusion.1
  9.2 0.7 convert_element_type.278
  9.8 0.7 pad_maximum_fusion.7
  10.6 0.6 broadcast_in_dim.2
  11.2 7.4 %all-to-all-start = ((f32[16,1,192]{2,1,0:T(1,128)}), f32[16,1,192]{2,1,0:T(1,128)S(1)}, u32[]{:S(2)}, u32[]{:S(2)}) async-start(f32[16,1,192]{2,1,0:T(1,128)} %broadcast_in_dim.2), calls=%async_computation | async-start | bytes 32768 | tf_op jit(solution)/shard_map/all_to_all | solution.py:176
  18.6 1.0 slice_bitcast_fusion.36
  19.6 1.0 slice_bitcast_fusion.35
  20.6 1.5 reshape.184
  22.7 1.1 reshape.199
  23.8 1.3 all-to-all-done
  25.1 4.7 %all-to-all-start.1 = ((bf16[16,2,4096]{2,1,0:T(2,128)(2,1)}), bf16[16,2,4096]{2,1,0:T(2,128)(2,1)S(1)}, u32[]{:S(2)}, u32[]{:S(2)}) async-start(bf16[16,2,4096]{2,1,0:T(2,128)(2,1)} %reshape.199), calls=%async_computation.1 | async-start | bytes 524288 | tf_op jit(solution)/shard_map/all_to_all | solution.py:186
  30.2 14.1 %all-to-all-done.1 = bf16[16,2,4096]{2,1,0:T(2,128)(2,1)S(1)} async-done(((bf16[16,2,4096]{2,1,0:T(2,128)(2,1)}), bf16[16,2,4096]{2,1,0:T(2,128)(2,1)S(1)}, u32[]{:S(2)}, u32[]{:S(2)}) %all-to-all-start.1) | async-done | bytes 262176 | tf_op jit(solution)/shard_map/all_to_all | solution.py:186
  45.4 48.5 %all-gather.5.cloned.1.call-done = bf16[4096,1024]{1,0:T(8,128)(2,1)} async-done(((bf16[256,1024]{1,0:T(8,128)(2,1)}), bf16[4096,1024]{1,0:T(8,128)(2,1)}) %all-gather.5.cloned.1.call-update) | async-done | bytes 8388624 | tf_op jit(solution)/shard_map/all_gather | solution.py:183
  94.0 0.8 pad_maximum_fusion.3
  94.9 2.8 %slice.622 = bf16[16,128,1024]{2,1,0:T(8,128)(2,1)S(1)} slice(bf16[16,256,1024]{2,1,0:T(8,128)(2,1)} %bitcast.170), slice={[0:16], [128:256], [0:1024]} | slice | bytes 8388608 | tf_op jit(solution)/shard_map/slice | solution.py:185
  97.7 1.8 copy-done
  99.5 0.6 convert_reduce_fusion
  100.2 1.6 multiply_reduce_fusion
  101.8 1.4 multiply_convert_fusion.1
  103.2 1.5 fusion.268
  104.9 4.2 %fusion.264 = (f32[64]{0:T(128)S(1)}, f32[2048,64]{0,1:T(8,128)S(1)}) fusion(f32[2048]{0:T(1024)S(1)} %get-tuple-element.112, f32[64]{0:T(128)S(1)} %get-tuple-element.88, f32[2048]{0:T(1024)S(1)} %get-tuple-element.95, f32[64]{0:T(128)S(1)} %get-tuple-element.89, f32[2048]{0:T(1024)S(1)} %get-tuple-element.96, f32[64]{0:T(128)S(1)} %get-tuple-element.60, ...), kind=kLoop, calls=%fused_computation.448 | loop fusion | flops 16121792 | bytes 1040384 | tf_op jit(solution)/shard_map/reduce_sum | solution.py:233
  109.4 1.6 fusion.263
  111.5 1.0 fusion.147
  112.5 5.1 %multiply_convert_fusion.3 = (bf16[2048,64]{0,1:T(8,128)(2,1)S(1)}, f32[2048,64]{0,1:T(8,128)S(1)}) fusion(f32[2048,128]{0,1:T(8,128)S(1)} %fusion.268, f32[2048]{0:T(1024)S(1)} %get-tuple-element.123, f32[64]{0:T(128)S(1)} %get-tuple-element.88, f32[2048]{0:T(1024)S(1)} %get-tuple-element.122, f32[64]{0:T(128)S(1)} %get-tuple-element.89, ...), kind=kLoop, calls=%fused_computation.229 | loop fusion | flops 12582912 | bytes 2088704 | tf_op jit(solution)/shard_map/convert.1
  117.7 4.6 %multiply_convert_fusion = (bf16[2048,1024]{1,0:T(8,128)(2,1)S(1)}, bf16[2048,1024]{1,0:T(8,128)(2,1)}, bf16[2048,1024]{1,0:T(8,128)(2,1)}) fusion(f32[1024]{0:T(1024)S(1)} %mul.660, f32[2048]{0:T(1024)S(1)} %get-tuple-element.92, f32[2048]{0:T(1024)S(1)} %get-tuple-element.90, bf16[16,256,1024]{2,1,0:T(8,128)(2,1)S(1)} %bitcast.174), kind=kLoop, calls=%fused_computation.5 | loop fusion | flops 18874368 | bytes 16797696 | tf_op jit(solution)/shard_map/convert_element_type | solution.py:211
  122.4 1.3 convolution_multiply_fusion.1
  123.8 3.2 %fusion.193 = f32[1024,128]{0,1:T(8,128)S(1)} fusion(bf16[2048,1024]{1,0:T(8,128)(2,1)} %get-tuple-element.53, bf16[2048,64]{0,1:T(8,128)(2,1)S(1)} %multiply_convert_fusion.2, bf16[2048,64]{0,1:T(8,128)(2,1)S(1)} %get-tuple-element.47), kind=kOutput, calls=%fused_computation.299 | convolution fusion | flops 537919488 | bytes 5242880 | tf_op jit(solution)/shard_map/fa,fb->ab/dot_general | solution.py:282
  127.5 0.8 fusion.16
  128.4 1.2 all_to_all.24
  129.6 3.6 %all-to-all-start.3 = ((f32[16,1,8256]{2,1,0:T(1,128)}), f32[16,1,8256]{2,1,0:T(1,128)S(1)}, u32[]{:S(2)}, u32[]{:S(2)}) async-start(f32[16,1,8256]{2,1,0:T(1,128)} %all_to_all.24), calls=%async_computation.3 | async-start | bytes 1064960 | tf_op jit(solution)/shard_map/all_to_all | solution.py:291
  133.4 1.1 copy_bitcast_fusion
  134.5 0.8 fusion.123
  135.3 0.8 fusion.71
  136.1 20.2 %all-to-all-done.3 = f32[16,1,8256]{2,1,0:T(1,128)S(1)} async-done(((f32[16,1,8256]{2,1,0:T(1,128)}), f32[16,1,8256]{2,1,0:T(1,128)S(1)}, u32[]{:S(2)}, u32[]{:S(2)}) %all-to-all-start.3) | async-done | bytes 528416 | tf_op jit(solution)/shard_map/all_to_all | solution.py:291
  156.4 8.8 %all-to-all-start.2 = ((bf16[16,128,192]{1,2,0:T(8,128)(2,1)}), bf16[16,128,192]{1,2,0:T(8,128)(2,1)S(1)}, u32[]{:S(2)}, u32[]{:S(2)}) async-start(bf16[16,128,192]{1,2,0:T(8,128)(2,1)} %copy_bitcast_fusion), calls=%async_computation.2 | async-start | bytes 1572864 | tf_op jit(solution)/shard_map/all_to_all | solution.py:305
  165.4 0.8 fusion.89
  166.2 0.7 fusion.105
  168.2 3.7 %convolution_multiply_fusion.2 = f32[64,1024]{1,0:T(8,128)} fusion(bf16[2048,64]{0,1:T(8,128)(2,1)S(1)} %get-tuple-element.56, bf16[2048,1024]{1,0:T(8,128)(2,1)} %bitcast.177), kind=kOutput, calls=%fused_computation.22 | convolution fusion | flops 268500992 | bytes 4718592 | tf_op jit(solution)/shard_map/fa,fb->ab/dot_general | solution.py:243
  172.0 0.8 copy-done.4
  172.8 0.8 reshape.193
  174.2 1.2 reshape.194
  175.4 1.2 slice_reduce_fusion
  176.6 7.3 %all-to-all-done.2 = bf16[16,128,192]{1,2,0:T(8,128)(2,1)S(1)} async-done(((bf16[16,128,192]{1,2,0:T(8,128)(2,1)}), bf16[16,128,192]{1,2,0:T(8,128)(2,1)S(1)}, u32[]{:S(2)}, u32[]{:S(2)}) %all-to-all-start.2) | async-done | bytes 786464 | tf_op jit(solution)/shard_map/all_to_all | solution.py:305
  184.0 2.7 %fusion.266 = (bf16[16,64,1024]{2,1,0:T(8,128)(2,1)S(1)}, bf16[16,64,1024]{2,1,0:T(8,128)(2,1)S(1)}) fusion(bf16[16,192,1024]{2,1,0:T(8,128)(2,1)} %bitcast.181), kind=kLoop, calls=%fused_computation.449 | loop fusion | bytes 8388608 | tf_op jit(solution)/shard_map/slice | solution.py:199
  186.7 0.8 fusion.192
  187.6 1.0 fusion.262
  188.6 1.0 fusion.25
  189.5 2.8 %fusion.13 = bf16[128,1024]{1,0:T(8,128)(2,1)} fusion(bf16[16,192,1024]{2,1,0:T(8,128)(2,1)} %bitcast.182, bf16[128,1024]{1,0:T(8,128)(2,1)S(1)} %copy-done.3, bf16[16,128,192]{1,2,0:T(8,128)(2,1)S(1)} %all-to-all-done.2), kind=kOutput, calls=%fused_computation.20 | convolution fusion | flops 268828672 | bytes 2883584 | tf_op jit(solution)/shard_map/dot_general | solution.py:314
  (60 shorter events, 6.5 us)
Async XLA Ops:
  7.2 22.7 %copy-start.3 = (bf16[128,1024]{1,0:T(8,128)(2,1)S(1)}, bf16[128,1024]{1,0:T(8,128)(2,1)}, u32[]{:S(2)}) copy-start(bf16[128,1024]{1,0:T(8,128)(2,1)} %param.9) | copy-start | bytes 786436
  7.2 86.8 %copy-start.5 = (bf16[64,2048]{1,0:T(8,128)(2,1)S(1)}, bf16[64,2048]{1,0:T(8,128)(2,1)}, u32[]{:S(2)}) copy-start(bf16[64,2048]{1,0:T(8,128)(2,1)} %param.13) | copy-start | bytes 786436
  7.2 86.8 %copy-start.7 = (bf16[64,1024]{1,0:T(8,128)(2,1)S(1)}, bf16[64,1024]{1,0:T(8,128)(2,1)}, u32[]{:S(2)}) copy-start(bf16[64,1024]{1,0:T(8,128)(2,1)} %param.17) | copy-start | bytes 393220
  7.2 86.8 %all-gather.5.cloned.1.call-start = ((), (), s32[]{:S(2)}) async-start(), calls=%async_computation.4 | async-start | bytes 8912896 | tf_op jit(solution)/shard_map/all_gather | solution.py:183
  11.2 13.9 %all-to-all-start = ((f32[16,1,192]{2,1,0:T(1,128)}), f32[16,1,192]{2,1,0:T(1,128)S(1)}, u32[]{:S(2)}, u32[]{:S(2)}) async-start(f32[16,1,192]{2,1,0:T(1,128)} %broadcast_in_dim.2), calls=%async_computation | async-start | bytes 32768 | tf_op jit(solution)/shard_map/all_to_all | solution.py:176
  25.1 19.3 %all-to-all-start.1 = ((bf16[16,2,4096]{2,1,0:T(2,128)(2,1)}), bf16[16,2,4096]{2,1,0:T(2,128)(2,1)S(1)}, u32[]{:S(2)}, u32[]{:S(2)}) async-start(bf16[16,2,4096]{2,1,0:T(2,128)(2,1)} %reshape.199), calls=%async_computation.1 | async-start | bytes 524288 | tf_op jit(solution)/shard_map/all_to_all | solution.py:186
  29.8 154.2 %all-gather.7.cloned.1.call-start = ((), (), s32[]{:S(2)}) async-start(), calls=%async_computation.5 | async-start | bytes 6684672 | tf_op jit(solution)/shard_map/all_gather | solution.py:192
  94.9 4.6 %copy-start = (bf16[4096,1024]{1,0:T(8,128)(2,1)S(1)}, bf16[4096,1024]{1,0:T(8,128)(2,1)}, u32[]{:S(2)}) copy-start(bf16[4096,1024]{1,0:T(8,128)(2,1)} %all-gather.5.cloned.1.call-done) | copy-start | bytes 25165828
  99.5 9.8 %copy-start.1 = (bf16[16,128,1024]{2,1,0:T(8,128)(2,1)}, bf16[16,128,1024]{2,1,0:T(8,128)(2,1)S(1)}, u32[]{:S(2)}) copy-start(bf16[16,128,1024]{2,1,0:T(8,128)(2,1)S(1)} %slice.622) | copy-start | bytes 12582916
  103.2 6.1 %copy-start.8 = (f32[64]{0:T(128)S(1)}, f32[64]{0:T(128)}, u32[]{:S(2)}) copy-start(f32[64]{0:T(128)} %param.15) | copy-start | bytes 772
  103.2 6.2 %copy-start.9 = (f32[64]{0:T(128)S(1)}, f32[64]{0:T(128)}, u32[]{:S(2)}) copy-start(f32[64]{0:T(128)} %param.16) | copy-start | bytes 772
  123.8 3.7 %copy-start.2 = (bf16[2048,1024]{1,0:T(8,128)(2,1)S(1)}, bf16[2048,1024]{1,0:T(8,128)(2,1)}, u32[]{:S(2)}) copy-start(bf16[2048,1024]{1,0:T(8,128)(2,1)} %get-tuple-element.52) | copy-start | bytes 12582916
  129.6 26.8 %all-to-all-start.3 = ((f32[16,1,8256]{2,1,0:T(1,128)}), f32[16,1,8256]{2,1,0:T(1,128)S(1)}, u32[]{:S(2)}, u32[]{:S(2)}) async-start(f32[16,1,8256]{2,1,0:T(1,128)} %all_to_all.24), calls=%async_computation.3 | async-start | bytes 1064960 | tf_op jit(solution)/shard_map/all_to_all | solution.py:291
  156.4 27.5 %all-to-all-start.2 = ((bf16[16,128,192]{1,2,0:T(8,128)(2,1)}), bf16[16,128,192]{1,2,0:T(8,128)(2,1)S(1)}, u32[]{:S(2)}, u32[]{:S(2)}) async-start(bf16[16,128,192]{1,2,0:T(8,128)(2,1)} %copy_bitcast_fusion), calls=%async_computation.2 | async-start | bytes 1572864 | tf_op jit(solution)/shard_map/all_to_all | solution.py:305
  172.0 0.8 copy-start.4
  186.7 1.9 copy-start.6
Sparse Core Ops, SparseCore 0:
  10.8 83.1 all-gather.4
  96.2 69.2 all-gather.6

commit v14 on v13

--- a/solution.py
+++ b/solution.py
@@ -207,7 +207,7 @@
         rstd = lax.rsqrt(jnp.mean(centred * centred, axis=1, keepdims=True) + EPSILON)
         return centred * rstd, rstd
 
-    ln_all, _ = norm(frames_all)
+    ln_all, rstd_all = norm(frames_all)
     ln_x_all = (ln_all * gains).astype(jnp.bfloat16)
 
     hidden = jnp.dot(ln_x_all, w_in_cols, preferred_element_type=jnp.float32)
@@ -316,7 +316,9 @@
     grad_ln = jnp.einsum(
         "fe,ne->fn", hidden_rows[:, 0], w_in_left, preferred_element_type=jnp.float32
     ) + jnp.einsum("fe,ne->fn", hidden_rows[:, 1], w_in_right, preferred_element_type=jnp.float32)
-    ln_hat, rstd_ln = norm(frames)
+    first_row = lax.axis_index("seq") * rows
+    ln_hat = lax.dynamic_slice_in_dim(ln_all, first_row, rows, 0)
+    rstd_ln = lax.dynamic_slice_in_dim(rstd_all, first_row, rows, 0)
     grad_hat = grad_ln * gains
     grad_input = rstd_ln * (
         grad_hat

time: 200 us -> 207 us (1.035)
  local copies, waits for them, and re-layouts: 19.7 us -> 23.5 us
  matrix products: 16.7 us -> 19.1 us
    dot_general x1, matrix products: 0.8 us -> 4.48 us  [channel_local(): jnp.einsum('fa,fb->ab', (ln_all - ln_head).astype(jnp.bfloat16), grad_hid...]
    convert_element_type x2 -> x1, other arithmetic: 6.05 us -> 3.1 us  [channel_local(): ln_x_all = (ln_all * gains).astype(jnp.bfloat16)]
    dot_general x1, matrix products: 3.21 us -> 0.81 us  [channel_local(): jnp.einsum('fa,fb->ab', ln_head.astype(jnp.bfloat16), grad_hidden, prefer...]
    reduce_sum x2 -> x1, other arithmetic: 0.73 us -> 2.81 us  [norm(): mean = jnp.mean(block_float, axis=1, keepdims=True)]
    unnamed x24 -> x26, local copies, waits for them, and re-layouts: 4.62 us -> 6.38 us
  transfers between devices with their start and end apart: 6 -> 6, of which waited for: 5 -> 5; matrix products, arithmetic and copies ran while one was open for 27% -> 26% of each run, Pallas kernels for 0% -> 0%
where the time goes in v14:
time: 207 us; the launch traced here: 206 us
  waiting for transfers between devices  91 us (44%)
  other arithmetic  34.3 us (17%)
  starting transfers between devices  24 us (12%)
  local copies, waits for them, and re-layouts  23.5 us (11%)
  matrix products  19.1 us (9%)
  between operations  14.5 us (7%)
    all_gather x1, waiting for transfers between devices, channel_local(): lax.all_gather(jnp.concatenate([frames, out_grad], axis=0), 'seq', axis=0)  48.4 us
    all_to_all x1, waiting for transfers between devices, channel_local(): lax.all_to_all(jnp.concatenate([in_cols.reshape(devices, share * 2 * shar...  18.3 us
    all_to_all x1, waiting for transfers between devices, channel_local(): lax.all_to_all(w_in.reshape(share, 2, devices, share).transpose(2, 0, 1,...  14.2 us
    all_to_all x1, waiting for transfers between devices, channel_local(): lax.all_to_all(jnp.concatenate([activation, grad_hidden], axis=1).reshape...  8.76 us
    all_to_all x1, starting transfers between devices, channel_local(): lax.all_to_all(jnp.concatenate([activation, grad_hidden], axis=1).reshape...  8.11 us
    all_to_all x1, starting transfers between devices, spread(): return lax.all_to_all(copies, 'seq', 0, 0, tiled=True)  7.39 us
    unnamed x26, local copies, waits for them, and re-layouts  6.38 us
    another operation x2, other arithmetic  5.25 us
  transfers between devices with their start and end apart: 6, of which 5 were waited for; matrix products, arithmetic and copies ran while one was open for 26% of the time, Pallas kernels for 0%

profile of v14, /device:TPU:0, one launch (start us, length us, event | category | flops | bytes accessed | tf_op | source)
XLA Modules:
  0.0 206.3 jit_solution(14821119108089014331)
XLA Ops:
  7.2 1.9 pad_maximum_fusion.1
  9.1 0.7 convert_element_type.277
  9.8 0.7 pad_maximum_fusion.7
  10.5 0.6 broadcast_in_dim.2
  11.1 7.4 %all-to-all-start = ((f32[16,1,192]{2,1,0:T(1,128)}), f32[16,1,192]{2,1,0:T(1,128)S(1)}, u32[]{:S(2)}, u32[]{:S(2)}) async-start(f32[16,1,192]{2,1,0:T(1,128)} %broadcast_in_dim.2), calls=%async_computation | async-start | bytes 32768 | tf_op jit(solution)/shard_map/all_to_all | solution.py:176
  18.5 1.0 slice_bitcast_fusion.36
  19.5 1.0 slice_bitcast_fusion.35
  20.5 1.5 reshape.187
  22.6 1.1 reshape.202
  23.7 1.3 all-to-all-done
  25.0 4.8 %all-to-all-start.1 = ((bf16[16,2,4096]{2,1,0:T(2,128)(2,1)}), bf16[16,2,4096]{2,1,0:T(2,128)(2,1)S(1)}, u32[]{:S(2)}, u32[]{:S(2)}) async-start(bf16[16,2,4096]{2,1,0:T(2,128)(2,1)} %reshape.202), calls=%async_computation.1 | async-start | bytes 524288 | tf_op jit(solution)/shard_map/all_to_all | solution.py:186
  30.3 14.2 %all-to-all-done.1 = bf16[16,2,4096]{2,1,0:T(2,128)(2,1)S(1)} async-done(((bf16[16,2,4096]{2,1,0:T(2,128)(2,1)}), bf16[16,2,4096]{2,1,0:T(2,128)(2,1)S(1)}, u32[]{:S(2)}, u32[]{:S(2)}) %all-to-all-start.1) | async-done | bytes 262176 | tf_op jit(solution)/shard_map/all_to_all | solution.py:186
  45.5 48.4 %all-gather.5.cloned.1.call-done = bf16[4096,1024]{1,0:T(8,128)(2,1)} async-done(((bf16[256,1024]{1,0:T(8,128)(2,1)}), bf16[4096,1024]{1,0:T(8,128)(2,1)}) %all-gather.5.cloned.1.call-update) | async-done | bytes 8388624 | tf_op jit(solution)/shard_map/all_gather | solution.py:183
  93.9 4.9 %slice.622 = bf16[16,128,1024]{2,1,0:T(8,128)(2,1)} slice(bf16[16,256,1024]{2,1,0:T(8,128)(2,1)} %bitcast.164), slice={[0:16], [128:256], [0:1024]} | slice | bytes 8388608 | tf_op jit(solution)/shard_map/slice | solution.py:185
  98.8 0.8 pad_maximum_fusion.3
  99.6 2.8 %convert_reduce_fusion = f32[16,128]{1,0:T(8,128)S(1)} fusion(bf16[16,256,1024]{2,1,0:T(8,128)(2,1)} %bitcast.165), kind=kLoop, calls=%fused_computation.8 | loop fusion | flops 4192256 | bytes 4202496 | tf_op jit(solution)/shard_map/reduce_sum | solution.py:205
  102.5 3.2 %multiply_reduce_fusion = f32[16,128]{1,0:T(8,128)S(1)} fusion(f32[16,128]{1,0:T(8,128)S(1)} %get-tuple-element.88, bf16[16,256,1024]{2,1,0:T(8,128)(2,1)} %bitcast.166), kind=kLoop, calls=%fused_computation.7 | loop fusion | flops 8386560 | bytes 4210688 | tf_op jit(solution)/shard_map/reduce_sum | solution.py:207
  105.7 3.1 %multiply_convert_fusion.1 = bf16[16,128,1024]{2,1,0:T(8,128)(2,1)S(1)} fusion(f32[1024]{0:T(1024)S(1)} %mul.660, f32[16,128]{1,0:T(8,128)S(1)} %get-tuple-element.90, f32[16,128]{1,0:T(8,128)S(1)} %get-tuple-element.88, bf16[16,256,1024]{2,1,0:T(8,128)(2,1)} %bitcast.167), kind=kLoop, calls=%fused_computation.6 | loop fusion | flops 10485760 | bytes 8409088 | tf_op jit(solution)/shard_map/convert_element_type | solution.py:211
  108.8 1.5 fusion.264
  110.5 4.2 %fusion.260 = (f32[64]{0:T(128)S(1)}, f32[2048,64]{0,1:T(8,128)S(1)}) fusion(f32[2048]{0:T(1024)S(1)} %get-tuple-element.109, f32[64]{0:T(128)S(1)} %get-tuple-element.85, f32[2048]{0:T(1024)S(1)} %get-tuple-element.92, f32[64]{0:T(128)S(1)} %get-tuple-element.86, f32[2048]{0:T(1024)S(1)} %get-tuple-element.93, f32[64]{0:T(128)S(1)} %get-tuple-element.57, ...), kind=kLoop, calls=%fused_computation.440 | loop fusion | flops 16121792 | bytes 1040384 | tf_op jit(solution)/shard_map/reduce_sum | solution.py:233
  115.0 1.6 fusion.259
  117.1 1.0 fusion.144
  118.1 5.1 %multiply_convert_fusion.6 = (bf16[2048,64]{0,1:T(8,128)(2,1)S(1)}, f32[2048,64]{0,1:T(8,128)S(1)}) fusion(f32[2048,128]{0,1:T(8,128)S(1)} %fusion.264, f32[2048]{0:T(1024)S(1)} %get-tuple-element.120, f32[64]{0:T(128)S(1)} %get-tuple-element.85, f32[2048]{0:T(1024)S(1)} %get-tuple-element.119, f32[64]{0:T(128)S(1)} %get-tuple-element.86, ...), kind=kLoop, calls=%fused_computation.223 | loop fusion | flops 12582912 | bytes 2088704 | tf_op jit(solution)/shard_map/convert.1
  123.4 1.2 fusion.1
  124.6 3.5 %copy-done = f32[2048,1024]{1,0:T(8,128)} copy-done((f32[2048,1024]{1,0:T(8,128)}, f32[2048,1024]{1,0:T(8,128)S(1)}, u32[]{:S(2)}) %copy-start) | copy-done | bytes 8388632
  128.1 1.3 fusion.12
  129.6 4.5 %fusion.3 = f32[1024,128]{0,1:T(8,128)S(1)} fusion(f32[2048,1024]{1,0:T(8,128)} %copy-done, bf16[2048,64]{0,1:T(8,128)(2,1)S(1)} %multiply_convert_fusion.5, bf16[2048,64]{0,1:T(8,128)(2,1)S(1)} %get-tuple-element.47), kind=kOutput, calls=%fused_computation.10 | convolution fusion | flops 544210944 | bytes 9437184 | tf_op jit(solution)/shard_map/fa,fb->ab/dot_general | solution.py:284
  134.1 1.3 copy-done.1
  135.4 0.8 fusion.23
  136.4 1.2 all_to_all.24
  137.6 3.6 %all-to-all-start.3 = ((f32[16,1,8256]{2,1,0:T(1,128)}), f32[16,1,8256]{2,1,0:T(1,128)S(1)}, u32[]{:S(2)}, u32[]{:S(2)}) async-start(f32[16,1,8256]{2,1,0:T(1,128)} %all_to_all.24), calls=%async_computation.3 | async-start | bytes 1064960 | tf_op jit(solution)/shard_map/all_to_all | solution.py:291
  141.1 1.1 copy_bitcast_fusion
  142.2 0.8 fusion.120
  143.1 0.8 fusion.86
  143.9 18.3 %all-to-all-done.3 = f32[16,1,8256]{2,1,0:T(1,128)S(1)} async-done(((f32[16,1,8256]{2,1,0:T(1,128)}), f32[16,1,8256]{2,1,0:T(1,128)S(1)}, u32[]{:S(2)}, u32[]{:S(2)}) %all-to-all-start.3) | async-done | bytes 528416 | tf_op jit(solution)/shard_map/all_to_all | solution.py:291
  162.2 8.1 %all-to-all-start.2 = ((bf16[16,128,192]{1,2,0:T(8,128)(2,1)}), bf16[16,128,192]{1,2,0:T(8,128)(2,1)S(1)}, u32[]{:S(2)}, u32[]{:S(2)}) async-start(bf16[16,128,192]{1,2,0:T(8,128)(2,1)} %copy_bitcast_fusion), calls=%async_computation.2 | async-start | bytes 1572864 | tf_op jit(solution)/shard_map/all_to_all | solution.py:305
  170.5 0.8 fusion.68
  171.4 0.7 fusion.102
  173.3 3.7 %convolution_multiply_fusion.1 = f32[64,1024]{1,0:T(8,128)} fusion(bf16[2048,64]{0,1:T(8,128)(2,1)S(1)} %get-tuple-element.53, bf16[2048,1024]{1,0:T(8,128)(2,1)} %bitcast.172), kind=kOutput, calls=%fused_computation.26 | convolution fusion | flops 268500992 | bytes 4718592 | tf_op jit(solution)/shard_map/fa,fb->ab/dot_general | solution.py:243
  177.2 0.8 reshape.196
  177.9 0.6 copy.38
  178.5 1.2 reshape.197
  180.2 8.8 %all-to-all-done.2 = bf16[16,128,192]{1,2,0:T(8,128)(2,1)S(1)} async-done(((bf16[16,128,192]{1,2,0:T(8,128)(2,1)}), bf16[16,128,192]{1,2,0:T(8,128)(2,1)S(1)}, u32[]{:S(2)}, u32[]{:S(2)}) %all-to-all-start.2) | async-done | bytes 786464 | tf_op jit(solution)/shard_map/all_to_all | solution.py:305
  189.1 2.8 %fusion.262 = (bf16[16,64,1024]{2,1,0:T(8,128)(2,1)S(1)}, bf16[16,64,1024]{2,1,0:T(8,128)(2,1)S(1)}) fusion(bf16[16,192,1024]{2,1,0:T(8,128)(2,1)} %bitcast.177), kind=kLoop, calls=%fused_computation.441 | loop fusion | bytes 8388608 | tf_op jit(solution)/shard_map/slice | solution.py:199
  191.9 0.8 fusion.189
  192.7 2.0 fusion.258
  194.8 1.9 add_convert_fusion
  196.7 2.8 %fusion.20 = bf16[128,1024]{1,0:T(8,128)(2,1)} fusion(bf16[16,192,1024]{2,1,0:T(8,128)(2,1)} %bitcast.178, bf16[128,1024]{1,0:T(8,128)(2,1)S(1)} %copy-done.5, bf16[16,128,192]{1,2,0:T(8,128)(2,1)S(1)} %all-to-all-done.2), kind=kOutput, calls=%fused_computation.24 | convolution fusion | flops 268828672 | bytes 2883584 | tf_op jit(solution)/shard_map/dot_general | solution.py:314
  (60 shorter events, 5.6 us)
Async XLA Ops:
  7.2 86.7 %all-gather.5.cloned.1.call-start = ((), (), s32[]{:S(2)}) async-start(), calls=%async_computation.4 | async-start | bytes 8912896 | tf_op jit(solution)/shard_map/all_gather | solution.py:183
  11.1 13.9 %all-to-all-start = ((f32[16,1,192]{2,1,0:T(1,128)}), f32[16,1,192]{2,1,0:T(1,128)S(1)}, u32[]{:S(2)}, u32[]{:S(2)}) async-start(f32[16,1,192]{2,1,0:T(1,128)} %broadcast_in_dim.2), calls=%async_computation | async-start | bytes 32768 | tf_op jit(solution)/shard_map/all_to_all | solution.py:176
  22.6 76.2 %copy-start.3 = (bf16[64,2048]{1,0:T(8,128)(2,1)S(1)}, bf16[64,2048]{1,0:T(8,128)(2,1)}, u32[]{:S(2)}) copy-start(bf16[64,2048]{1,0:T(8,128)(2,1)} %param.13) | copy-start | bytes 786436
  23.7 75.1 %copy-start.6 = (bf16[64,1024]{1,0:T(8,128)(2,1)S(1)}, bf16[64,1024]{1,0:T(8,128)(2,1)}, u32[]{:S(2)}) copy-start(bf16[64,1024]{1,0:T(8,128)(2,1)} %param.17) | copy-start | bytes 393220
  25.0 19.4 %all-to-all-start.1 = ((bf16[16,2,4096]{2,1,0:T(2,128)(2,1)}), bf16[16,2,4096]{2,1,0:T(2,128)(2,1)S(1)}, u32[]{:S(2)}, u32[]{:S(2)}) async-start(bf16[16,2,4096]{2,1,0:T(2,128)(2,1)} %reshape.202), calls=%async_computation.1 | async-start | bytes 524288 | tf_op jit(solution)/shard_map/all_to_all | solution.py:186
  29.8 159.3 %all-gather.7.cloned.1.call-start = ((), (), s32[]{:S(2)}) async-start(), calls=%async_computation.5 | async-start | bytes 6684672 | tf_op jit(solution)/shard_map/all_gather | solution.py:192
  108.8 6.1 %copy-start.7 = (f32[64]{0:T(128)S(1)}, f32[64]{0:T(128)}, u32[]{:S(2)}) copy-start(f32[64]{0:T(128)} %param.15) | copy-start | bytes 772
  108.8 6.2 %copy-start.2 = (bf16[16,128,1024]{2,1,0:T(8,128)(2,1)S(1)}, bf16[16,128,1024]{2,1,0:T(8,128)(2,1)}, u32[]{:S(2)}) copy-start(bf16[16,128,1024]{2,1,0:T(8,128)(2,1)} %slice.622) | copy-start | bytes 12582916
  108.8 6.2 %copy-start.8 = (f32[64]{0:T(128)S(1)}, f32[64]{0:T(128)}, u32[]{:S(2)}) copy-start(f32[64]{0:T(128)} %param.16) | copy-start | bytes 772
  114.9 8.4 %slice-start = ((s8[8388608]{0:T(1024)(128)(4,1)}), s8[4194304]{0:T(1024)(128)(4,1)S(1)}, s32[]{:S(2)}) async-start(s8[8388608]{0:T(1024)(128)(4,1)} %bitcast.168), calls=%async_computation.6 | async-start | bytes 8388608
  115.0 8.4 %slice-start.1 = ((s8[8388608]{0:T(1024)(128)(4,1)}), s8[4194304]{0:T(1024)(128)(4,1)S(1)}, s32[]{:S(2)}) async-start(s8[8388608]{0:T(1024)(128)(4,1)} %bitcast.168), calls=%async_computation.7 | async-start | bytes 8388608
  124.6 3.5 %copy-start = (f32[2048,1024]{1,0:T(8,128)}, f32[2048,1024]{1,0:T(8,128)S(1)}, u32[]{:S(2)}) copy-start(f32[2048,1024]{1,0:T(8,128)S(1)} %fusion.1) | copy-start | bytes 25165828
  129.6 5.8 %copy-start.1 = (f32[2048,1024]{1,0:T(8,128)S(1)}, f32[2048,1024]{1,0:T(8,128)}, u32[]{:S(2)}) copy-start(f32[2048,1024]{1,0:T(8,128)} %copy-done) | copy-start | bytes 25165828
  137.6 24.6 %all-to-all-start.3 = ((f32[16,1,8256]{2,1,0:T(1,128)}), f32[16,1,8256]{2,1,0:T(1,128)S(1)}, u32[]{:S(2)}, u32[]{:S(2)}) async-start(f32[16,1,8256]{2,1,0:T(1,128)} %all_to_all.24), calls=%async_computation.3 | async-start | bytes 1064960 | tf_op jit(solution)/shard_map/all_to_all | solution.py:291
  162.2 26.8 %all-to-all-start.2 = ((bf16[16,128,192]{1,2,0:T(8,128)(2,1)}), bf16[16,128,192]{1,2,0:T(8,128)(2,1)S(1)}, u32[]{:S(2)}, u32[]{:S(2)}) async-start(bf16[16,128,192]{1,2,0:T(8,128)(2,1)} %copy_bitcast_fusion), calls=%async_computation.2 | async-start | bytes 1572864 | tf_op jit(solution)/shard_map/all_to_all | solution.py:305
  189.1 5.7 %copy-start.4 = (bf16[128,1024]{1,0:T(8,128)(2,1)S(1)}, bf16[128,1024]{1,0:T(8,128)(2,1)}, u32[]{:S(2)}) copy-start(bf16[128,1024]{1,0:T(8,128)(2,1)} %param.11) | copy-start | bytes 786436
  191.9 4.8 %copy-start.5 = (bf16[128,1024]{1,0:T(8,128)(2,1)S(1)}, bf16[128,1024]{1,0:T(8,128)(2,1)}, u32[]{:S(2)}) copy-start(bf16[128,1024]{1,0:T(8,128)(2,1)} %param.9) | copy-start | bytes 786436
Sparse Core Ops, SparseCore 0:
  10.7 83.1 all-gather.4
  99.8 69.2 all-gather.6

commit v15 on v13

--- a/solution.py
+++ b/solution.py
@@ -180,23 +180,19 @@
     all_ids = small[:, share:].reshape(stream).astype(jnp.int32)
 
     out_rows = w_out.shape[0]
-    pieces = lax.all_gather(jnp.concatenate([frames, out_grad], axis=0), "seq", axis=0)
+    pieces = lax.all_gather(jnp.concatenate([frames, out_grad, w_out], axis=0), "seq", axis=0)
     frames_all = pieces[:, :rows].reshape(stream, width)
-    grad_all = pieces[:, rows:].reshape(stream, width)
+    grad_all = pieces[:, rows : 2 * rows].reshape(stream, width)
+    w_out_all = pieces[:, 2 * rows :].reshape(width, width)
     w_in_cols = lax.all_to_all(
         w_in.reshape(share, 2, devices, share).transpose(2, 0, 1, 3), "seq", 0, 0, tiled=True
     ).reshape(width, 2 * share)
-    w_in_late, w_out_late, _, _, _ = lax.optimization_barrier(
-        (w_in, w_out, pieces, w_in_cols, small)
-    )
+    w_in_late, _, _, _ = lax.optimization_barrier((w_in, pieces, w_in_cols, small))
     weights = lax.all_gather(
-        jnp.concatenate([w_out_late, w_in_late[:, :width], w_in_late[:, width:]], axis=0),
-        "seq",
-        axis=0,
-    )
-    w_out_all = weights[:, :out_rows].reshape(width, width)
-    w_in_left = weights[:, out_rows : 2 * out_rows].reshape(width, width)
-    w_in_right = weights[:, 2 * out_rows :].reshape(width, width)
+        jnp.concatenate([w_in_late[:, :width], w_in_late[:, width:]], axis=0), "seq", axis=0
+    )
+    w_in_left = weights[:, :out_rows].reshape(width, width)
+    w_in_right = weights[:, out_rows:].reshape(width, width)
 
     first_channel = lax.axis_index("seq") * share
 

time: 200 us -> 213 us (1.065)
  other arithmetic: 32.3 us -> 40.5 us
  waiting for transfers between devices: 91.5 us -> 99.5 us
  starting transfers between devices: 24.5 us -> 21.5 us
    all_gather x2, waiting for transfers between devices: 48.6 us -> 59.8 us  [the longest x1 59.8 us: channel_local(): lax.all_gather(jnp.concatenate([frames, out_grad, w_out], axis=0), 'seq',...]
    all_to_all x1, starting transfers between devices: 8.76 us -> 4.65 us  [channel_local(): lax.all_to_all(jnp.concatenate([activation, grad_hidden], axis=1).reshape...]
    convert_element_type x2, other arithmetic: 6.05 us -> 9.41 us  [channel_local(): ln_x_all = (ln_all * gains).astype(jnp.bfloat16)]
    reduce_sum x2, other arithmetic: 0.73 us -> 3.9 us  [norm(): mean = jnp.mean(block_float, axis=1, keepdims=True)]
    all_to_all x1, waiting for transfers between devices: 20.2 us -> 18 us  [channel_local(): lax.all_to_all(jnp.concatenate([in_cols.reshape(devices, share * 2 * shar...]
    unnamed x24 -> x22, local copies, waits for them, and re-layouts: 4.62 us -> 2.72 us
  transfers between devices with their start and end apart: 6 -> 6, of which waited for: 5 -> 5; matrix products, arithmetic and copies ran while one was open for 27% -> 26% of each run, Pallas kernels for 0% -> 0%
where the time goes in v15:
time: 213 us; the launch traced here: 212 us
  waiting for transfers between devices  99.5 us (47%)
  other arithmetic  40.5 us (19%)
  starting transfers between devices  21.5 us (10%)
  local copies, waits for them, and re-layouts  19.8 us (9%)
  matrix products  16.6 us (8%)
  between operations  14.4 us (7%)
    all_gather x1, waiting for transfers between devices, channel_local(): lax.all_gather(jnp.concatenate([frames, out_grad, w_out], axis=0), 'seq',...  59.8 us
    all_to_all x1, waiting for transfers between devices, channel_local(): lax.all_to_all(jnp.concatenate([in_cols.reshape(devices, share * 2 * shar...  18 us
    all_to_all x1, waiting for transfers between devices, channel_local(): lax.all_to_all(w_in.reshape(share, 2, devices, share).transpose(2, 0, 1,...  14.2 us
    convert_element_type x2, other arithmetic, channel_local(): ln_x_all = (ln_all * gains).astype(jnp.bfloat16)  9.41 us
    all_to_all x1, starting transfers between devices, spread(): return lax.all_to_all(copies, 'seq', 0, 0, tiled=True)  7.39 us
    all_to_all x1, waiting for transfers between devices, channel_local(): lax.all_to_all(jnp.concatenate([activation, grad_hidden], axis=1).reshape...  7.27 us
    all_to_all x1, starting transfers between devices, channel_local(): lax.all_to_all(w_in.reshape(share, 2, devices, share).transpose(2, 0, 1,...  5.78 us
    another operation x2, other arithmetic  5.24 us
  transfers between devices with their start and end apart: 6, of which 5 were waited for; matrix products, arithmetic and copies ran while one was open for 26% of the time, Pallas kernels for 0%

profile of v15, /device:TPU:0, one launch (start us, length us, event | category | flops | bytes accessed | tf_op | source)
XLA Modules:
  0.0 212.2 jit_solution(4981526573998185713)
XLA Ops:
  7.2 2.0 pad_maximum_fusion
  9.2 0.7 convert_element_type.278
  9.9 0.7 pad_maximum_fusion.7
  10.6 0.6 broadcast_in_dim.2
  11.3 7.4 %all-to-all-start = ((f32[16,1,192]{2,1,0:T(1,128)}), f32[16,1,192]{2,1,0:T(1,128)S(1)}, u32[]{:S(2)}, u32[]{:S(2)}) async-start(f32[16,1,192]{2,1,0:T(1,128)} %broadcast_in_dim.2), calls=%async_computation | async-start | bytes 32768 | tf_op jit(solution)/shard_map/all_to_all | solution.py:176
  18.6 1.0 slice_bitcast_fusion.35
  19.6 1.0 slice_bitcast_fusion.36
  20.6 1.1 convert_reduce_fusion.1
  21.7 1.5 reshape.184
  23.8 1.1 reshape.199
  25.2 5.8 %all-to-all-start.1 = ((bf16[16,2,4096]{2,1,0:T(2,128)(2,1)}), bf16[16,2,4096]{2,1,0:T(2,128)(2,1)S(1)}, u32[]{:S(2)}, u32[]{:S(2)}) async-start(bf16[16,2,4096]{2,1,0:T(2,128)(2,1)} %reshape.199), calls=%async_computation.1 | async-start | bytes 524288 | tf_op jit(solution)/shard_map/all_to_all | solution.py:187
  31.4 14.2 %all-to-all-done.1 = bf16[16,2,4096]{2,1,0:T(2,128)(2,1)S(1)} async-done(((bf16[16,2,4096]{2,1,0:T(2,128)(2,1)}), bf16[16,2,4096]{2,1,0:T(2,128)(2,1)S(1)}, u32[]{:S(2)}, u32[]{:S(2)}) %all-to-all-start.1) | async-done | bytes 262176 | tf_op jit(solution)/shard_map/all_to_all | solution.py:187
  46.6 59.8 %all-gather.5.cloned.1.call-done = bf16[5120,1024]{1,0:T(8,128)(2,1)} async-done(((bf16[320,1024]{1,0:T(8,128)(2,1)}), bf16[5120,1024]{1,0:T(8,128)(2,1)}) %all-gather.5.cloned.1.call-update) | async-done | bytes 10485776 | tf_op jit(solution)/shard_map/all_gather | solution.py:183
  106.4 2.8 %convert_reduce_fusion = f32[16,128]{1,0:T(8,128)S(1)} fusion(bf16[16,320,1024]{2,1,0:T(8,128)(2,1)} %bitcast.170), kind=kLoop, calls=%fused_computation.8 | loop fusion | flops 4192256 | bytes 4202496 | tf_op jit(solution)/shard_map/reduce_sum | solution.py:201
  109.3 4.8 %slice.622 = bf16[16,128,1024]{2,1,0:T(8,128)(2,1)} slice(bf16[16,320,1024]{2,1,0:T(8,128)(2,1)} %bitcast.171), slice={[0:16], [128:256], [0:1024]} | slice | bytes 8388608 | tf_op jit(solution)/shard_map/slice | solution.py:185
  114.0 3.2 %multiply_reduce_fusion = f32[16,128]{1,0:T(8,128)S(1)} fusion(f32[16,128]{1,0:T(8,128)S(1)} %get-tuple-element.89, bf16[16,320,1024]{2,1,0:T(8,128)(2,1)} %bitcast.172), kind=kLoop, calls=%fused_computation.7 | loop fusion | flops 8386560 | bytes 4210688 | tf_op jit(solution)/shard_map/reduce_sum | solution.py:203
  117.3 0.7 pad_maximum_fusion.3
  118.0 3.0 %multiply_convert_fusion.1 = bf16[16,128,1024]{2,1,0:T(8,128)(2,1)S(1)} fusion(f32[1024]{0:T(1024)S(1)} %mul.660, f32[16,128]{1,0:T(8,128)S(1)} %get-tuple-element.91, f32[16,128]{1,0:T(8,128)S(1)} %get-tuple-element.89, bf16[16,320,1024]{2,1,0:T(8,128)(2,1)} %bitcast.173), kind=kLoop, calls=%fused_computation.6 | loop fusion | flops 10485760 | bytes 8409088 | tf_op jit(solution)/shard_map/convert_element_type | solution.py:207
  121.1 1.5 fusion.268
  122.8 4.2 %fusion.264 = (f32[64]{0:T(128)S(1)}, f32[2048,64]{0,1:T(8,128)S(1)}) fusion(f32[2048]{0:T(1024)S(1)} %get-tuple-element.110, f32[64]{0:T(128)S(1)} %get-tuple-element.86, f32[2048]{0:T(1024)S(1)} %get-tuple-element.93, f32[64]{0:T(128)S(1)} %get-tuple-element.87, f32[2048]{0:T(1024)S(1)} %get-tuple-element.94, f32[64]{0:T(128)S(1)} %get-tuple-element.58, ...), kind=kLoop, calls=%fused_computation.448 | loop fusion | flops 16121792 | bytes 1040384 | tf_op jit(solution)/shard_map/reduce_sum | solution.py:229
  127.3 1.6 fusion.263
  129.4 1.0 fusion.147
  130.4 5.1 %multiply_convert_fusion.3 = (bf16[2048,64]{0,1:T(8,128)(2,1)S(1)}, f32[2048,64]{0,1:T(8,128)S(1)}) fusion(f32[2048,128]{0,1:T(8,128)S(1)} %fusion.268, f32[2048]{0:T(1024)S(1)} %get-tuple-element.121, f32[64]{0:T(128)S(1)} %get-tuple-element.86, f32[2048]{0:T(1024)S(1)} %get-tuple-element.120, f32[64]{0:T(128)S(1)} %get-tuple-element.87, ...), kind=kLoop, calls=%fused_computation.229 | loop fusion | flops 12582912 | bytes 2088704 | tf_op jit(solution)/shard_map/convert.1
  135.6 6.4 %multiply_convert_fusion = (bf16[2048,1024]{1,0:T(8,128)(2,1)S(1)}, bf16[2048,1024]{1,0:T(8,128)(2,1)}, bf16[2048,1024]{1,0:T(8,128)(2,1)}) fusion(f32[1024]{0:T(1024)S(1)} %mul.660, f32[2048]{0:T(1024)S(1)} %get-tuple-element.90, f32[2048]{0:T(1024)S(1)} %get-tuple-element.88, bf16[16,320,1024]{2,1,0:T(8,128)(2,1)} %bitcast.174), kind=kLoop, calls=%fused_computation.5 | loop fusion | flops 18874368 | bytes 16797696 | tf_op jit(solution)/shard_map/convert_element_type | solution.py:207
  142.0 1.3 convolution_multiply_fusion.1
  143.4 3.0 %fusion.193 = f32[1024,128]{0,1:T(8,128)S(1)} fusion(bf16[2048,1024]{1,0:T(8,128)(2,1)} %get-tuple-element.51, bf16[2048,64]{0,1:T(8,128)(2,1)S(1)} %multiply_convert_fusion.2, bf16[2048,64]{0,1:T(8,128)(2,1)S(1)} %get-tuple-element.45), kind=kOutput, calls=%fused_computation.299 | convolution fusion | flops 537919488 | bytes 5242880 | tf_op jit(solution)/shard_map/fa,fb->ab/dot_general | solution.py:278
  146.9 0.8 fusion.16
  147.8 1.2 all_to_all.24
  149.0 3.6 %all-to-all-start.3 = ((f32[16,1,8256]{2,1,0:T(1,128)}), f32[16,1,8256]{2,1,0:T(1,128)S(1)}, u32[]{:S(2)}, u32[]{:S(2)}) async-start(f32[16,1,8256]{2,1,0:T(1,128)} %all_to_all.24), calls=%async_computation.3 | async-start | bytes 1064960 | tf_op jit(solution)/shard_map/all_to_all | solution.py:287
  152.8 1.1 copy_bitcast_fusion
  153.9 0.8 fusion.123
  154.8 0.8 fusion.71
  155.6 18.0 %all-to-all-done.3 = f32[16,1,8256]{2,1,0:T(1,128)S(1)} async-done(((f32[16,1,8256]{2,1,0:T(1,128)}), f32[16,1,8256]{2,1,0:T(1,128)S(1)}, u32[]{:S(2)}, u32[]{:S(2)}) %all-to-all-start.3) | async-done | bytes 528416 | tf_op jit(solution)/shard_map/all_to_all | solution.py:287
  173.6 4.7 %all-to-all-start.2 = ((bf16[16,128,192]{1,2,0:T(8,128)(2,1)}), bf16[16,128,192]{1,2,0:T(8,128)(2,1)S(1)}, u32[]{:S(2)}, u32[]{:S(2)}) async-start(bf16[16,128,192]{1,2,0:T(8,128)(2,1)} %copy_bitcast_fusion), calls=%async_computation.2 | async-start | bytes 1572864 | tf_op jit(solution)/shard_map/all_to_all | solution.py:301
  178.5 0.8 fusion.89
  179.3 0.7 fusion.105
  181.3 3.7 %convolution_multiply_fusion.2 = f32[64,1024]{1,0:T(8,128)} fusion(bf16[2048,64]{0,1:T(8,128)(2,1)S(1)} %get-tuple-element.54, bf16[2048,1024]{1,0:T(8,128)(2,1)} %bitcast.177), kind=kOutput, calls=%fused_computation.22 | convolution fusion | flops 268500992 | bytes 4718592 | tf_op jit(solution)/shard_map/fa,fb->ab/dot_general | solution.py:239
  185.0 0.8 copy-done.3
  185.9 0.8 reshape.193
  186.7 0.6 copy.38
  187.3 1.2 reshape.194
  188.4 1.2 slice_reduce_fusion
  189.7 7.3 %all-to-all-done.2 = bf16[16,128,192]{1,2,0:T(8,128)(2,1)S(1)} async-done(((bf16[16,128,192]{1,2,0:T(8,128)(2,1)}), bf16[16,128,192]{1,2,0:T(8,128)(2,1)S(1)}, u32[]{:S(2)}, u32[]{:S(2)}) %all-to-all-start.2) | async-done | bytes 786464 | tf_op jit(solution)/shard_map/all_to_all | solution.py:301
  197.0 2.8 %fusion.13 = bf16[128,1024]{1,0:T(8,128)(2,1)} fusion(bf16[16,320,1024]{2,1,0:T(8,128)(2,1)} %bitcast.175, bf16[128,1024]{1,0:T(8,128)(2,1)S(1)} %copy-done.2, bf16[16,128,192]{1,2,0:T(8,128)(2,1)S(1)} %all-to-all-done.2), kind=kOutput, calls=%fused_computation.20 | convolution fusion | flops 268828672 | bytes 2883584 | tf_op jit(solution)/shard_map/dot_general | solution.py:310
  199.8 2.7 %fusion.266 = (bf16[16,64,1024]{2,1,0:T(8,128)(2,1)S(1)}, bf16[16,64,1024]{2,1,0:T(8,128)(2,1)S(1)}) fusion(bf16[16,128,1024]{2,1,0:T(8,128)(2,1)} %bitcast.181), kind=kLoop, calls=%fused_computation.449 | loop fusion | bytes 8388608 | tf_op jit(solution)/shard_map/slice | solution.py:195
  202.5 0.8 fusion.192
  203.4 1.0 fusion.262
  204.4 1.0 fusion.25
  (58 shorter events, 5.9 us)
Async XLA Ops:
  7.2 99.3 %all-gather.5.cloned.1.call-start = ((), (), s32[]{:S(2)}) async-start(), calls=%async_computation.4 | async-start | bytes 11141120 | tf_op jit(solution)/shard_map/all_gather | solution.py:183
  11.3 13.9 %all-to-all-start = ((f32[16,1,192]{2,1,0:T(1,128)}), f32[16,1,192]{2,1,0:T(1,128)S(1)}, u32[]{:S(2)}, u32[]{:S(2)}) async-start(f32[16,1,192]{2,1,0:T(1,128)} %broadcast_in_dim.2), calls=%async_computation | async-start | bytes 32768 | tf_op jit(solution)/shard_map/all_to_all | solution.py:176
  25.2 20.4 %all-to-all-start.1 = ((bf16[16,2,4096]{2,1,0:T(2,128)(2,1)}), bf16[16,2,4096]{2,1,0:T(2,128)(2,1)S(1)}, u32[]{:S(2)}, u32[]{:S(2)}) async-start(bf16[16,2,4096]{2,1,0:T(2,128)(2,1)} %reshape.199), calls=%async_computation.1 | async-start | bytes 524288 | tf_op jit(solution)/shard_map/all_to_all | solution.py:187
  31.0 168.8 %all-gather.7.cloned.1.call-start = ((), (), s32[]{:S(2)}) async-start(), calls=%async_computation.5 | async-start | bytes 4456448 | tf_op jit(solution)/shard_map/all_gather | solution.py:191
  114.0 3.2 %copy-start.5 = (bf16[64,2048]{1,0:T(8,128)(2,1)S(1)}, bf16[64,2048]{1,0:T(8,128)(2,1)}, u32[]{:S(2)}) copy-start(bf16[64,2048]{1,0:T(8,128)(2,1)} %param.13) | copy-start | bytes 786436
  121.0 6.2 %copy-start.7 = (f32[64]{0:T(128)S(1)}, f32[64]{0:T(128)}, u32[]{:S(2)}) copy-start(f32[64]{0:T(128)} %param.15) | copy-start | bytes 772
  121.1 6.2 %copy-start = (bf16[16,128,1024]{2,1,0:T(8,128)(2,1)S(1)}, bf16[16,128,1024]{2,1,0:T(8,128)(2,1)}, u32[]{:S(2)}) copy-start(bf16[16,128,1024]{2,1,0:T(8,128)(2,1)} %slice.622) | copy-start | bytes 12582916
  121.1 6.2 %copy-start.6 = (bf16[64,1024]{1,0:T(8,128)(2,1)S(1)}, bf16[64,1024]{1,0:T(8,128)(2,1)}, u32[]{:S(2)}) copy-start(bf16[64,1024]{1,0:T(8,128)(2,1)} %param.17) | copy-start | bytes 393220
  121.1 6.2 %copy-start.8 = (f32[64]{0:T(128)S(1)}, f32[64]{0:T(128)}, u32[]{:S(2)}) copy-start(f32[64]{0:T(128)} %param.16) | copy-start | bytes 772
  143.4 3.5 %copy-start.1 = (bf16[2048,1024]{1,0:T(8,128)(2,1)S(1)}, bf16[2048,1024]{1,0:T(8,128)(2,1)}, u32[]{:S(2)}) copy-start(bf16[2048,1024]{1,0:T(8,128)(2,1)} %get-tuple-element.50) | copy-start | bytes 12582916
  146.9 5.7 %copy-start.2 = (bf16[128,1024]{1,0:T(8,128)(2,1)S(1)}, bf16[128,1024]{1,0:T(8,128)(2,1)}, u32[]{:S(2)}) copy-start(bf16[128,1024]{1,0:T(8,128)(2,1)} %param.9) | copy-start | bytes 786436
  149.0 24.6 %all-to-all-start.3 = ((f32[16,1,8256]{2,1,0:T(1,128)}), f32[16,1,8256]{2,1,0:T(1,128)S(1)}, u32[]{:S(2)}, u32[]{:S(2)}) async-start(f32[16,1,8256]{2,1,0:T(1,128)} %all_to_all.24), calls=%async_computation.3 | async-start | bytes 1064960 | tf_op jit(solution)/shard_map/all_to_all | solution.py:287
  173.6 23.4 %all-to-all-start.2 = ((bf16[16,128,192]{1,2,0:T(8,128)(2,1)}), bf16[16,128,192]{1,2,0:T(8,128)(2,1)S(1)}, u32[]{:S(2)}, u32[]{:S(2)}) async-start(bf16[16,128,192]{1,2,0:T(8,128)(2,1)} %copy_bitcast_fusion), calls=%async_computation.2 | async-start | bytes 1572864 | tf_op jit(solution)/shard_map/all_to_all | solution.py:301
  185.0 0.8 copy-start.3
  202.5 1.9 copy-start.4
Sparse Core Ops, SparseCore 0:
  10.3 96.1 all-gather.4
  118.1 56.9 all-gather.6

commit v16 on v11

--- a/solution.py
+++ b/solution.py
@@ -209,6 +209,10 @@
 
     ln_all, _ = norm(frames_all)
     ln_x_all = (ln_all * gains).astype(jnp.bfloat16)
+    ln_head32 = lax.reduce_precision(ln_all, exponent_bits=8, mantissa_bits=7)
+    ln_x_all, ln_head, ln_tail = lax.optimization_barrier(
+        (ln_x_all, ln_head32.astype(jnp.bfloat16), (ln_all - ln_head32).astype(jnp.bfloat16))
+    )
 
     hidden = jnp.dot(ln_x_all, w_in_cols, preferred_element_type=jnp.float32)
     left_half = hidden[:, :share]
@@ -279,12 +283,8 @@
         * grad_scale
     )
     moments = jnp.einsum(
-        "fa,fb->ab",
-        ln_all,
-        grad_hidden.astype(jnp.float32),
-        preferred_element_type=jnp.float32,
-        precision=lax.Precision.HIGHEST,
-    )
+        "fa,fb->ab", ln_head, grad_hidden, preferred_element_type=jnp.float32
+    ) + jnp.einsum("fa,fb->ab", ln_tail, grad_hidden, preferred_element_type=jnp.float32)
     gain_part = jnp.sum(w_in_cols.astype(jnp.float32) * moments, axis=1) * grad_scale
     packed = lax.all_to_all(
         jnp.concatenate(

time: 202 us -> 199 us (0.985)
  local copies, waits for them, and re-layouts: 21.3 us -> 17.6 us
    unnamed x30 -> x26, local copies, waits for them, and re-layouts: 8.18 us -> 4.51 us
    convert_element_type x1, other arithmetic: 1.42 us -> 4.41 us  [channel_local(): (ln_all - ln_head32).astype(jnp.bfloat16)]
    dot_general x1 -> x2, matrix products: 6.38 us -> 4.62 us  [the longest x1 3.82 us: channel_local(): jnp.einsum('fa,fb->ab', ln_head, grad_hidden, preferred_element_type=jnp....]
where the time goes in v16:
time: 199 us
  waiting for transfers between devices  95 us (48%)
  other arithmetic  30.9 us (16%)
  starting transfers between devices  23.4 us (12%)
  local copies, waits for them, and re-layouts  17.6 us (9%)
  matrix products  17.3 us (9%)
  between operations  14.5 us (7%)
    all_gather x1, waiting for transfers between devices, channel_local(): lax.all_gather(jnp.concatenate([frames, out_grad], axis=0), 'seq', axis=0)  49.6 us
    all_to_all x1, waiting for transfers between devices, channel_local(): lax.all_to_all(jnp.concatenate([in_cols.reshape(devices, share * 2 * shar...  20.3 us
    all_to_all x1, waiting for transfers between devices, channel_local(): lax.all_to_all(w_in.reshape(share, 2, devices, share).transpose(2, 0, 1,...  14.5 us
    all_to_all x1, starting transfers between devices, channel_local(): lax.all_to_all(jnp.concatenate([activation, grad_hidden], axis=1).reshape...  8.78 us
    all_to_all x1, starting transfers between devices, spread(): return lax.all_to_all(copies, 'seq', 0, 0, tiled=True)  7.4 us
    all_to_all x1, waiting for transfers between devices, channel_local(): lax.all_to_all(jnp.concatenate([activation, grad_hidden], axis=1).reshape...  7.28 us
    another operation x2, other arithmetic  5.47 us
    unnamed x26, local copies, waits for them, and re-layouts  4.51 us
  transfers between devices with their start and end apart: 6, of which 5 were waited for; matrix products, arithmetic and copies ran while one was open for 25% of the time, Pallas kernels for 0%

profile of v16, /device:TPU:0, one launch (start us, length us, event | category | flops | bytes accessed | tf_op | source)
XLA Modules:
  0.0 198.8 jit_solution(11674970063870928162)
XLA Ops:
  7.2 1.9 pad_maximum_fusion.1
  9.2 0.7 convert_element_type.274
  9.9 0.7 pad_maximum_fusion.7
  10.6 0.6 broadcast_in_dim.2
  11.2 7.4 %all-to-all-start = ((f32[16,1,192]{2,1,0:T(1,128)}), f32[16,1,192]{2,1,0:T(1,128)S(1)}, u32[]{:S(2)}, u32[]{:S(2)}) async-start(f32[16,1,192]{2,1,0:T(1,128)} %broadcast_in_dim.2), calls=%async_computation | async-start | bytes 32768 | tf_op jit(solution)/shard_map/all_to_all | solution.py:176
  18.6 1.5 reshape.168
  20.1 0.6 copy.32
  20.7 1.1 reshape.183
  21.8 3.3 %all-to-all-done = f32[16,1,192]{2,1,0:T(1,128)S(1)} async-done(((f32[16,1,192]{2,1,0:T(1,128)}), f32[16,1,192]{2,1,0:T(1,128)S(1)}, u32[]{:S(2)}, u32[]{:S(2)}) %all-to-all-start) | async-done | bytes 12320 | tf_op jit(solution)/shard_map/all_to_all | solution.py:176
  25.1 3.5 %all-to-all-start.1 = ((bf16[16,2,4096]{2,1,0:T(2,128)(2,1)}), bf16[16,2,4096]{2,1,0:T(2,128)(2,1)S(1)}, u32[]{:S(2)}, u32[]{:S(2)}) async-start(bf16[16,2,4096]{2,1,0:T(2,128)(2,1)} %reshape.183), calls=%async_computation.1 | async-start | bytes 524288 | tf_op jit(solution)/shard_map/all_to_all | solution.py:186
  28.8 14.5 %all-to-all-done.1 = bf16[16,2,4096]{2,1,0:T(2,128)(2,1)S(1)} async-done(((bf16[16,2,4096]{2,1,0:T(2,128)(2,1)}), bf16[16,2,4096]{2,1,0:T(2,128)(2,1)S(1)}, u32[]{:S(2)}, u32[]{:S(2)}) %all-to-all-start.1) | async-done | bytes 262176 | tf_op jit(solution)/shard_map/all_to_all | solution.py:186
  44.3 49.6 %all-gather.5.cloned.1.call-done = bf16[4096,1024]{1,0:T(8,128)(2,1)} async-done(((bf16[256,1024]{1,0:T(8,128)(2,1)}), bf16[4096,1024]{1,0:T(8,128)(2,1)}) %all-gather.5.cloned.1.call-update) | async-done | bytes 8388624 | tf_op jit(solution)/shard_map/all_gather | solution.py:183
  94.0 0.8 pad_maximum_fusion.3
  95.3 2.8 %slice.622 = bf16[16,128,1024]{2,1,0:T(8,128)(2,1)S(1)} slice(bf16[16,256,1024]{2,1,0:T(8,128)(2,1)} %bitcast.169), slice={[0:16], [128:256], [0:1024]} | slice | bytes 8388608 | tf_op jit(solution)/shard_map/slice | solution.py:185
  98.2 1.8 copy-done
  99.9 0.6 convert_reduce_fusion
  100.6 1.6 multiply_reduce_fusion
  102.2 4.4 %fusion = (bf16[2048,1024]{1,0:T(8,128)(2,1)}, bf16[2048,1024]{1,0:T(8,128)(2,1)}, bf16[2048,1024]{1,0:T(8,128)(2,1)S(1)}) fusion(f32[2048]{0:T(1024)S(1)} %rsqrt_bitcast_fusion, f32[2048]{0:T(1024)S(1)} %get-tuple-element.126, bf16[16,256,1024]{2,1,0:T(8,128)(2,1)S(1)} %bitcast.172, f32[1024]{0:T(1024)S(1)} %mul.650), kind=kLoop, calls=%fused_computation.2 | loop fusion | flops 18874368 | bytes 16797696 | tf_op jit(solution)/shard_map/convert_element_type | solution.py:214
  106.6 1.5 fusion.267
  108.3 4.2 %fusion.263 = (f32[64]{0:T(128)S(1)}, f32[2048,64]{0,1:T(8,128)S(1)}) fusion(f32[2048]{0:T(1024)S(1)} %get-tuple-element.114, f32[64]{0:T(128)S(1)} %get-tuple-element.94, f32[2048]{0:T(1024)S(1)} %get-tuple-element.97, f32[64]{0:T(128)S(1)} %get-tuple-element.95, f32[2048]{0:T(1024)S(1)} %get-tuple-element.98, f32[64]{0:T(128)S(1)} %get-tuple-element.66, ...), kind=kLoop, calls=%fused_computation.446 | loop fusion | flops 16121792 | bytes 1040384 | tf_op jit(solution)/shard_map/reduce_sum | solution.py:237
  112.8 1.6 fusion.262
  114.9 1.0 fusion.147
  115.9 5.3 %multiply_convert_fusion.2 = (bf16[2048,64]{0,1:T(8,128)(2,1)S(1)}, f32[2048,64]{0,1:T(8,128)S(1)}) fusion(f32[2048,128]{0,1:T(8,128)S(1)} %fusion.267, f32[2048]{0:T(1024)S(1)} %get-tuple-element.125, f32[64]{0:T(128)S(1)} %get-tuple-element.94, f32[2048]{0:T(1024)S(1)} %get-tuple-element.124, f32[64]{0:T(128)S(1)} %get-tuple-element.95, ...), kind=kLoop, calls=%fused_computation.228 | loop fusion | flops 12582912 | bytes 2088704 | tf_op jit(solution)/shard_map/convert.1
  121.4 1.3 convolution_multiply_fusion.1
  122.8 3.8 %fusion.193 = f32[1024,128]{0,1:T(8,128)S(1)} fusion(bf16[2048,1024]{1,0:T(8,128)(2,1)} %get-tuple-element.16, bf16[2048,64]{0,1:T(8,128)(2,1)S(1)} %multiply_convert_fusion.1, bf16[2048,64]{0,1:T(8,128)(2,1)S(1)} %get-tuple-element.53), kind=kOutput, calls=%fused_computation.298 | convolution fusion | flops 537919488 | bytes 5242880 | tf_op jit(solution)/shard_map/fa,fb->ab/dot_general | solution.py:285
  127.0 0.8 fusion.16
  127.9 1.2 all_to_all.24
  129.1 3.6 %all-to-all-start.3 = ((f32[16,1,8256]{2,1,0:T(1,128)}), f32[16,1,8256]{2,1,0:T(1,128)S(1)}, u32[]{:S(2)}, u32[]{:S(2)}) async-start(f32[16,1,8256]{2,1,0:T(1,128)} %all_to_all.24), calls=%async_computation.3 | async-start | bytes 1064960 | tf_op jit(solution)/shard_map/all_to_all | solution.py:289
  132.9 1.1 copy_bitcast_fusion
  134.0 0.8 fusion.123
  134.8 0.8 fusion.89
  135.7 20.3 %all-to-all-done.3 = f32[16,1,8256]{2,1,0:T(1,128)S(1)} async-done(((f32[16,1,8256]{2,1,0:T(1,128)}), f32[16,1,8256]{2,1,0:T(1,128)S(1)}, u32[]{:S(2)}, u32[]{:S(2)}) %all-to-all-start.3) | async-done | bytes 528416 | tf_op jit(solution)/shard_map/all_to_all | solution.py:289
  156.0 8.8 %all-to-all-start.2 = ((bf16[16,128,192]{1,2,0:T(8,128)(2,1)}), bf16[16,128,192]{1,2,0:T(8,128)(2,1)S(1)}, u32[]{:S(2)}, u32[]{:S(2)}) async-start(bf16[16,128,192]{1,2,0:T(8,128)(2,1)} %copy_bitcast_fusion), calls=%async_computation.2 | async-start | bytes 1572864 | tf_op jit(solution)/shard_map/all_to_all | solution.py:303
  165.0 0.8 fusion.71
  165.8 0.7 fusion.105
  167.2 0.6 broadcast_multiply_fusion
  167.8 3.7 %convolution_multiply_fusion.2 = f32[64,1024]{1,0:T(8,128)} fusion(bf16[2048,64]{0,1:T(8,128)(2,1)S(1)} %get-tuple-element.62, bf16[2048,1024]{1,0:T(8,128)(2,1)} %bitcast.174), kind=kOutput, calls=%fused_computation.21 | convolution fusion | flops 268500992 | bytes 4718592 | tf_op jit(solution)/shard_map/fa,fb->ab/dot_general | solution.py:247
  171.6 0.8 copy-done.4
  172.4 0.8 reshape.177
  173.2 0.6 copy.38
  173.8 1.2 reshape.178
  175.0 1.2 slice_reduce_fusion
  176.2 7.3 %all-to-all-done.2 = bf16[16,128,192]{1,2,0:T(8,128)(2,1)S(1)} async-done(((bf16[16,128,192]{1,2,0:T(8,128)(2,1)}), bf16[16,128,192]{1,2,0:T(8,128)(2,1)S(1)}, u32[]{:S(2)}, u32[]{:S(2)}) %all-to-all-start.2) | async-done | bytes 786464 | tf_op jit(solution)/shard_map/all_to_all | solution.py:303
  183.6 2.7 %fusion.265 = (bf16[16,64,1024]{2,1,0:T(8,128)(2,1)S(1)}, bf16[16,64,1024]{2,1,0:T(8,128)(2,1)S(1)}) fusion(bf16[16,192,1024]{2,1,0:T(8,128)(2,1)} %bitcast.178), kind=kLoop, calls=%fused_computation.447 | loop fusion | bytes 8388608 | tf_op jit(solution)/shard_map/slice | solution.py:199
  186.3 0.8 fusion.192
  187.2 1.0 fusion.261
  188.2 1.0 fusion.25
  189.1 2.8 %fusion.13 = bf16[128,1024]{1,0:T(8,128)(2,1)} fusion(bf16[16,192,1024]{2,1,0:T(8,128)(2,1)} %bitcast.179, bf16[128,1024]{1,0:T(8,128)(2,1)S(1)} %copy-done.3, bf16[16,128,192]{1,2,0:T(8,128)(2,1)S(1)} %all-to-all-done.2), kind=kOutput, calls=%fused_computation.19 | convolution fusion | flops 268828672 | bytes 2883584 | tf_op jit(solution)/shard_map/dot_general | solution.py:312
  (61 shorter events, 4.6 us)
Async XLA Ops:
  7.2 86.8 %copy-start.5 = (bf16[64,2048]{1,0:T(8,128)(2,1)S(1)}, bf16[64,2048]{1,0:T(8,128)(2,1)}, u32[]{:S(2)}) copy-start(bf16[64,2048]{1,0:T(8,128)(2,1)} %param.13) | copy-start | bytes 786436
  7.2 21.6 %copy-start.8 = (f32[31,64]{1,0:T(8,128)S(1)}, f32[31,64]{1,0:T(8,128)}, u32[]{:S(2)}) copy-start(f32[31,64]{1,0:T(8,128)} %param.14) | copy-start | bytes 23812
  7.2 86.8 %copy-start.7 = (bf16[64,1024]{1,0:T(8,128)(2,1)S(1)}, bf16[64,1024]{1,0:T(8,128)(2,1)}, u32[]{:S(2)}) copy-start(bf16[64,1024]{1,0:T(8,128)(2,1)} %param.17) | copy-start | bytes 393220
  7.2 86.8 %all-gather.5.cloned.1.call-start = ((), (), s32[]{:S(2)}) async-start(), calls=%async_computation.4 | async-start | bytes 8912896 | tf_op jit(solution)/shard_map/all_gather | solution.py:183
  9.2 85.6 %copy-start.3 = (bf16[128,1024]{1,0:T(8,128)(2,1)S(1)}, bf16[128,1024]{1,0:T(8,128)(2,1)}, u32[]{:S(2)}) copy-start(bf16[128,1024]{1,0:T(8,128)(2,1)} %param.9) | copy-start | bytes 786436
  11.2 13.9 %all-to-all-start = ((f32[16,1,192]{2,1,0:T(1,128)}), f32[16,1,192]{2,1,0:T(1,128)S(1)}, u32[]{:S(2)}, u32[]{:S(2)}) async-start(f32[16,1,192]{2,1,0:T(1,128)} %broadcast_in_dim.2), calls=%async_computation | async-start | bytes 32768 | tf_op jit(solution)/shard_map/all_to_all | solution.py:176
  25.1 18.1 %all-to-all-start.1 = ((bf16[16,2,4096]{2,1,0:T(2,128)(2,1)}), bf16[16,2,4096]{2,1,0:T(2,128)(2,1)S(1)}, u32[]{:S(2)}, u32[]{:S(2)}) async-start(bf16[16,2,4096]{2,1,0:T(2,128)(2,1)} %reshape.183), calls=%async_computation.1 | async-start | bytes 524288 | tf_op jit(solution)/shard_map/all_to_all | solution.py:186
  28.7 154.9 %all-gather.7.cloned.1.call-start = ((), (), s32[]{:S(2)}) async-start(), calls=%async_computation.5 | async-start | bytes 6684672 | tf_op jit(solution)/shard_map/all_gather | solution.py:192
  95.3 4.6 %copy-start = (bf16[4096,1024]{1,0:T(8,128)(2,1)S(1)}, bf16[4096,1024]{1,0:T(8,128)(2,1)}, u32[]{:S(2)}) copy-start(bf16[4096,1024]{1,0:T(8,128)(2,1)} %all-gather.5.cloned.1.call-done) | copy-start | bytes 25165828
  99.9 12.8 %copy-start.1 = (bf16[16,128,1024]{2,1,0:T(8,128)(2,1)}, bf16[16,128,1024]{2,1,0:T(8,128)(2,1)S(1)}, u32[]{:S(2)}) copy-start(bf16[16,128,1024]{2,1,0:T(8,128)(2,1)S(1)} %slice.622) | copy-start | bytes 12582916
  106.6 6.1 %copy-start.9 = (f32[64]{0:T(128)S(1)}, f32[64]{0:T(128)}, u32[]{:S(2)}) copy-start(f32[64]{0:T(128)} %param.15) | copy-start | bytes 772
  106.6 6.2 %copy-start.10 = (f32[64]{0:T(128)S(1)}, f32[64]{0:T(128)}, u32[]{:S(2)}) copy-start(f32[64]{0:T(128)} %param.16) | copy-start | bytes 772
  122.8 4.2 %copy-start.2 = (bf16[2048,1024]{1,0:T(8,128)(2,1)S(1)}, bf16[2048,1024]{1,0:T(8,128)(2,1)}, u32[]{:S(2)}) copy-start(bf16[2048,1024]{1,0:T(8,128)(2,1)} %get-tuple-element.17) | copy-start | bytes 12582916
  129.1 26.9 %all-to-all-start.3 = ((f32[16,1,8256]{2,1,0:T(1,128)}), f32[16,1,8256]{2,1,0:T(1,128)S(1)}, u32[]{:S(2)}, u32[]{:S(2)}) async-start(f32[16,1,8256]{2,1,0:T(1,128)} %all_to_all.24), calls=%async_computation.3 | async-start | bytes 1064960 | tf_op jit(solution)/shard_map/all_to_all | solution.py:289
  156.0 27.5 %all-to-all-start.2 = ((bf16[16,128,192]{1,2,0:T(8,128)(2,1)}), bf16[16,128,192]{1,2,0:T(8,128)(2,1)S(1)}, u32[]{:S(2)}, u32[]{:S(2)}) async-start(bf16[16,128,192]{1,2,0:T(8,128)(2,1)} %copy_bitcast_fusion), calls=%async_computation.2 | async-start | bytes 1572864 | tf_op jit(solution)/shard_map/all_to_all | solution.py:303
  171.6 0.8 copy-start.4
  186.3 1.9 copy-start.6
Sparse Core Ops, SparseCore 0:
  10.8 83.1 all-gather.4
  96.2 69.2 all-gather.6

commit v17 on v16

--- a/solution.py
+++ b/solution.py
@@ -301,9 +301,9 @@
     )
     grad_ln_gain = jnp.sum(packed[:, share * 2 * share :], axis=0)
     back = lax.all_to_all(
-        jnp.concatenate([activation, grad_hidden], axis=1).reshape(devices, rows, 3 * share),
-        "seq", 0, 0, tiled=True,
-    )
+        jnp.concatenate([activation, grad_hidden], axis=1).T.reshape(3 * share, devices, rows),
+        "seq", 1, 1, tiled=True,
+    ).transpose(1, 2, 0)
     act_rows = back[:, :, :share].transpose(1, 0, 2).reshape(rows, width)
     hidden_rows = (
         back[:, :, share:].reshape(devices, rows, 2, share).transpose(1, 2, 0, 3)

time: 199 us -> 200 us (level)
  no operation moved by 1% of the time
where the time goes in v17:
time: 200 us; the launch traced here: 199 us
  waiting for transfers between devices  95 us (48%)
  other arithmetic  30.9 us (15%)
  starting transfers between devices  23.4 us (12%)
  local copies, waits for them, and re-layouts  17.6 us (9%)
  matrix products  17.4 us (9%)
  between operations  14.5 us (7%)
    all_gather x1, waiting for transfers between devices, channel_local(): lax.all_gather(jnp.concatenate([frames, out_grad], axis=0), 'seq', axis=0)  49.6 us
    all_to_all x1, waiting for transfers between devices, channel_local(): lax.all_to_all(jnp.concatenate([in_cols.reshape(devices, share * 2 * shar...  20.3 us
    all_to_all x1, waiting for transfers between devices, channel_local(): lax.all_to_all(w_in.reshape(share, 2, devices, share).transpose(2, 0, 1,...  14.5 us
    all_to_all x1, starting transfers between devices, channel_local(): lax.all_to_all(jnp.concatenate([activation, grad_hidden], axis=1).T.resha...  8.78 us
    all_to_all x1, starting transfers between devices, spread(): return lax.all_to_all(copies, 'seq', 0, 0, tiled=True)  7.4 us
    all_to_all x1, waiting for transfers between devices, channel_local(): lax.all_to_all(jnp.concatenate([activation, grad_hidden], axis=1).T.resha...  7.28 us
    another operation x2, other arithmetic  5.47 us
    unnamed x26, local copies, waits for them, and re-layouts  4.51 us
  transfers between devices with their start and end apart: 6, of which 5 were waited for; matrix products, arithmetic and copies ran while one was open for 25% of the time, Pallas kernels for 0%

profile of v17, /device:TPU:0, one launch (start us, length us, event | category | flops | bytes accessed | tf_op | source)
XLA Modules:
  0.0 198.8 jit_solution(5224203678007399589)
XLA Ops:
  7.2 1.9 pad_maximum_fusion.1
  9.2 0.7 convert_element_type.274
  9.9 0.7 pad_maximum_fusion.7
  10.6 0.6 broadcast_in_dim.2
  11.2 7.4 %all-to-all-start = ((f32[16,1,192]{2,1,0:T(1,128)}), f32[16,1,192]{2,1,0:T(1,128)S(1)}, u32[]{:S(2)}, u32[]{:S(2)}) async-start(f32[16,1,192]{2,1,0:T(1,128)} %broadcast_in_dim.2), calls=%async_computation | async-start | bytes 32768 | tf_op jit(solution)/shard_map/all_to_all | solution.py:176
  18.6 1.5 reshape.168
  20.1 0.6 copy.32
  20.7 1.1 reshape.183
  21.8 3.3 %all-to-all-done = f32[16,1,192]{2,1,0:T(1,128)S(1)} async-done(((f32[16,1,192]{2,1,0:T(1,128)}), f32[16,1,192]{2,1,0:T(1,128)S(1)}, u32[]{:S(2)}, u32[]{:S(2)}) %all-to-all-start) | async-done | bytes 12320 | tf_op jit(solution)/shard_map/all_to_all | solution.py:176
  25.1 3.5 %all-to-all-start.1 = ((bf16[16,2,4096]{2,1,0:T(2,128)(2,1)}), bf16[16,2,4096]{2,1,0:T(2,128)(2,1)S(1)}, u32[]{:S(2)}, u32[]{:S(2)}) async-start(bf16[16,2,4096]{2,1,0:T(2,128)(2,1)} %reshape.183), calls=%async_computation.1 | async-start | bytes 524288 | tf_op jit(solution)/shard_map/all_to_all | solution.py:186
  28.8 14.5 %all-to-all-done.1 = bf16[16,2,4096]{2,1,0:T(2,128)(2,1)S(1)} async-done(((bf16[16,2,4096]{2,1,0:T(2,128)(2,1)}), bf16[16,2,4096]{2,1,0:T(2,128)(2,1)S(1)}, u32[]{:S(2)}, u32[]{:S(2)}) %all-to-all-start.1) | async-done | bytes 262176 | tf_op jit(solution)/shard_map/all_to_all | solution.py:186
  44.3 49.6 %all-gather.5.cloned.1.call-done = bf16[4096,1024]{1,0:T(8,128)(2,1)} async-done(((bf16[256,1024]{1,0:T(8,128)(2,1)}), bf16[4096,1024]{1,0:T(8,128)(2,1)}) %all-gather.5.cloned.1.call-update) | async-done | bytes 8388624 | tf_op jit(solution)/shard_map/all_gather | solution.py:183
  94.0 0.8 pad_maximum_fusion.3
  95.3 2.8 %slice.622 = bf16[16,128,1024]{2,1,0:T(8,128)(2,1)S(1)} slice(bf16[16,256,1024]{2,1,0:T(8,128)(2,1)} %bitcast.171), slice={[0:16], [128:256], [0:1024]} | slice | bytes 8388608 | tf_op jit(solution)/shard_map/slice | solution.py:185
  98.2 1.8 copy-done
  99.9 0.6 convert_reduce_fusion
  100.6 1.6 multiply_reduce_fusion
  102.2 4.4 %fusion = (bf16[2048,1024]{1,0:T(8,128)(2,1)}, bf16[2048,1024]{1,0:T(8,128)(2,1)}, bf16[2048,1024]{1,0:T(8,128)(2,1)S(1)}) fusion(f32[2048]{0:T(1024)S(1)} %rsqrt_bitcast_fusion, f32[2048]{0:T(1024)S(1)} %get-tuple-element.126, bf16[16,256,1024]{2,1,0:T(8,128)(2,1)S(1)} %bitcast.174, f32[1024]{0:T(1024)S(1)} %mul.650), kind=kLoop, calls=%fused_computation.2 | loop fusion | flops 18874368 | bytes 16797696 | tf_op jit(solution)/shard_map/convert_element_type | solution.py:214
  106.6 1.5 fusion.267
  108.3 4.2 %fusion.263 = (f32[64]{0:T(128)S(1)}, f32[2048,64]{0,1:T(8,128)S(1)}) fusion(f32[2048]{0:T(1024)S(1)} %get-tuple-element.114, f32[64]{0:T(128)S(1)} %get-tuple-element.94, f32[2048]{0:T(1024)S(1)} %get-tuple-element.97, f32[64]{0:T(128)S(1)} %get-tuple-element.95, f32[2048]{0:T(1024)S(1)} %get-tuple-element.98, f32[64]{0:T(128)S(1)} %get-tuple-element.66, ...), kind=kLoop, calls=%fused_computation.446 | loop fusion | flops 16121792 | bytes 1040384 | tf_op jit(solution)/shard_map/reduce_sum | solution.py:237
  112.8 1.6 fusion.262
  114.9 1.0 fusion.147
  115.9 5.3 %multiply_convert_fusion.2 = (bf16[2048,64]{0,1:T(8,128)(2,1)S(1)}, f32[2048,64]{0,1:T(8,128)S(1)}) fusion(f32[2048,128]{0,1:T(8,128)S(1)} %fusion.267, f32[2048]{0:T(1024)S(1)} %get-tuple-element.125, f32[64]{0:T(128)S(1)} %get-tuple-element.94, f32[2048]{0:T(1024)S(1)} %get-tuple-element.124, f32[64]{0:T(128)S(1)} %get-tuple-element.95, ...), kind=kLoop, calls=%fused_computation.228 | loop fusion | flops 12582912 | bytes 2088704 | tf_op jit(solution)/shard_map/convert.1
  121.4 1.3 convolution_multiply_fusion.1
  122.8 3.8 %fusion.193 = f32[1024,128]{0,1:T(8,128)S(1)} fusion(bf16[2048,1024]{1,0:T(8,128)(2,1)} %get-tuple-element.16, bf16[2048,64]{0,1:T(8,128)(2,1)S(1)} %multiply_convert_fusion.1, bf16[2048,64]{0,1:T(8,128)(2,1)S(1)} %get-tuple-element.53), kind=kOutput, calls=%fused_computation.298 | convolution fusion | flops 537919488 | bytes 5242880 | tf_op jit(solution)/shard_map/fa,fb->ab/dot_general | solution.py:285
  127.0 0.8 fusion.16
  127.9 1.2 all_to_all.24
  129.1 3.6 %all-to-all-start.3 = ((f32[16,1,8256]{2,1,0:T(1,128)}), f32[16,1,8256]{2,1,0:T(1,128)S(1)}, u32[]{:S(2)}, u32[]{:S(2)}) async-start(f32[16,1,8256]{2,1,0:T(1,128)} %all_to_all.24), calls=%async_computation.3 | async-start | bytes 1064960 | tf_op jit(solution)/shard_map/all_to_all | solution.py:289
  132.9 1.1 copy_bitcast_fusion
  134.0 0.8 fusion.123
  134.8 0.8 fusion.89
  135.7 20.3 %all-to-all-done.3 = f32[16,1,8256]{2,1,0:T(1,128)S(1)} async-done(((f32[16,1,8256]{2,1,0:T(1,128)}), f32[16,1,8256]{2,1,0:T(1,128)S(1)}, u32[]{:S(2)}, u32[]{:S(2)}) %all-to-all-start.3) | async-done | bytes 528416 | tf_op jit(solution)/shard_map/all_to_all | solution.py:289
  156.0 8.8 %all-to-all-start.2 = ((bf16[192,16,128]{2,0,1:T(8,128)(2,1)}), bf16[192,16,128]{2,0,1:T(8,128)(2,1)S(1)}, u32[]{:S(2)}, u32[]{:S(2)}) async-start(bf16[192,16,128]{2,0,1:T(8,128)(2,1)} %copy_bitcast_fusion), calls=%async_computation.2 | async-start | bytes 1572864 | tf_op jit(solution)/shard_map/all_to_all | solution.py:303
  165.0 0.8 fusion.71
  165.8 0.7 fusion.105
  167.2 0.6 broadcast_multiply_fusion
  167.8 3.7 %convolution_multiply_fusion.2 = f32[64,1024]{1,0:T(8,128)} fusion(bf16[2048,64]{0,1:T(8,128)(2,1)S(1)} %get-tuple-element.62, bf16[2048,1024]{1,0:T(8,128)(2,1)} %bitcast.176), kind=kOutput, calls=%fused_computation.21 | convolution fusion | flops 268500992 | bytes 4718592 | tf_op jit(solution)/shard_map/fa,fb->ab/dot_general | solution.py:247
  171.6 0.8 copy-done.4
  172.4 0.8 reshape.177
  173.2 0.6 copy.38
  173.8 1.2 reshape.178
  175.0 1.2 slice_reduce_fusion
  176.2 7.3 %all-to-all-done.2 = bf16[192,16,128]{2,0,1:T(8,128)(2,1)S(1)} async-done(((bf16[192,16,128]{2,0,1:T(8,128)(2,1)}), bf16[192,16,128]{2,0,1:T(8,128)(2,1)S(1)}, u32[]{:S(2)}, u32[]{:S(2)}) %all-to-all-start.2) | async-done | bytes 786464 | tf_op jit(solution)/shard_map/all_to_all | solution.py:303
  183.6 2.7 %fusion.265 = (bf16[16,64,1024]{2,1,0:T(8,128)(2,1)S(1)}, bf16[16,64,1024]{2,1,0:T(8,128)(2,1)S(1)}) fusion(bf16[16,192,1024]{2,1,0:T(8,128)(2,1)} %bitcast.180), kind=kLoop, calls=%fused_computation.447 | loop fusion | bytes 8388608 | tf_op jit(solution)/shard_map/slice | solution.py:199
  186.3 2.8 %fusion.13 = bf16[128,1024]{1,0:T(8,128)(2,1)} fusion(bf16[16,192,1024]{2,1,0:T(8,128)(2,1)} %bitcast.181, bf16[128,1024]{1,0:T(8,128)(2,1)S(1)} %copy-done.3, bf16[16,128,192]{1,2,0:T(8,128)(2,1)S(1)} %bitcast.183), kind=kOutput, calls=%fused_computation.19 | convolution fusion | flops 268828672 | bytes 2883584 | tf_op jit(solution)/shard_map/dot_general | solution.py:312
  189.1 0.8 fusion.192
  190.0 1.0 fusion.261
  191.0 1.0 fusion.25
  (61 shorter events, 4.6 us)
Async XLA Ops:
  7.2 86.8 %copy-start.5 = (bf16[64,2048]{1,0:T(8,128)(2,1)S(1)}, bf16[64,2048]{1,0:T(8,128)(2,1)}, u32[]{:S(2)}) copy-start(bf16[64,2048]{1,0:T(8,128)(2,1)} %param.13) | copy-start | bytes 786436
  7.2 21.6 %copy-start.8 = (f32[31,64]{1,0:T(8,128)S(1)}, f32[31,64]{1,0:T(8,128)}, u32[]{:S(2)}) copy-start(f32[31,64]{1,0:T(8,128)} %param.14) | copy-start | bytes 23812
  7.2 86.8 %copy-start.7 = (bf16[64,1024]{1,0:T(8,128)(2,1)S(1)}, bf16[64,1024]{1,0:T(8,128)(2,1)}, u32[]{:S(2)}) copy-start(bf16[64,1024]{1,0:T(8,128)(2,1)} %param.17) | copy-start | bytes 393220
  7.2 86.8 %all-gather.5.cloned.1.call-start = ((), (), s32[]{:S(2)}) async-start(), calls=%async_computation.4 | async-start | bytes 8912896 | tf_op jit(solution)/shard_map/all_gather | solution.py:183
  9.2 85.6 %copy-start.3 = (bf16[128,1024]{1,0:T(8,128)(2,1)S(1)}, bf16[128,1024]{1,0:T(8,128)(2,1)}, u32[]{:S(2)}) copy-start(bf16[128,1024]{1,0:T(8,128)(2,1)} %param.9) | copy-start | bytes 786436
  11.2 13.9 %all-to-all-start = ((f32[16,1,192]{2,1,0:T(1,128)}), f32[16,1,192]{2,1,0:T(1,128)S(1)}, u32[]{:S(2)}, u32[]{:S(2)}) async-start(f32[16,1,192]{2,1,0:T(1,128)} %broadcast_in_dim.2), calls=%async_computation | async-start | bytes 32768 | tf_op jit(solution)/shard_map/all_to_all | solution.py:176
  25.1 18.1 %all-to-all-start.1 = ((bf16[16,2,4096]{2,1,0:T(2,128)(2,1)}), bf16[16,2,4096]{2,1,0:T(2,128)(2,1)S(1)}, u32[]{:S(2)}, u32[]{:S(2)}) async-start(bf16[16,2,4096]{2,1,0:T(2,128)(2,1)} %reshape.183), calls=%async_computation.1 | async-start | bytes 524288 | tf_op jit(solution)/shard_map/all_to_all | solution.py:186
  28.7 154.9 %all-gather.7.cloned.1.call-start = ((), (), s32[]{:S(2)}) async-start(), calls=%async_computation.5 | async-start | bytes 6684672 | tf_op jit(solution)/shard_map/all_gather | solution.py:192
  95.3 4.6 %copy-start = (bf16[4096,1024]{1,0:T(8,128)(2,1)S(1)}, bf16[4096,1024]{1,0:T(8,128)(2,1)}, u32[]{:S(2)}) copy-start(bf16[4096,1024]{1,0:T(8,128)(2,1)} %all-gather.5.cloned.1.call-done) | copy-start | bytes 25165828
  99.9 12.8 %copy-start.1 = (bf16[16,128,1024]{2,1,0:T(8,128)(2,1)}, bf16[16,128,1024]{2,1,0:T(8,128)(2,1)S(1)}, u32[]{:S(2)}) copy-start(bf16[16,128,1024]{2,1,0:T(8,128)(2,1)S(1)} %slice.622) | copy-start | bytes 12582916
  106.6 6.1 %copy-start.9 = (f32[64]{0:T(128)S(1)}, f32[64]{0:T(128)}, u32[]{:S(2)}) copy-start(f32[64]{0:T(128)} %param.15) | copy-start | bytes 772
  106.6 6.2 %copy-start.10 = (f32[64]{0:T(128)S(1)}, f32[64]{0:T(128)}, u32[]{:S(2)}) copy-start(f32[64]{0:T(128)} %param.16) | copy-start | bytes 772
  122.8 4.2 %copy-start.2 = (bf16[2048,1024]{1,0:T(8,128)(2,1)S(1)}, bf16[2048,1024]{1,0:T(8,128)(2,1)}, u32[]{:S(2)}) copy-start(bf16[2048,1024]{1,0:T(8,128)(2,1)} %get-tuple-element.17) | copy-start | bytes 12582916
  129.1 26.9 %all-to-all-start.3 = ((f32[16,1,8256]{2,1,0:T(1,128)}), f32[16,1,8256]{2,1,0:T(1,128)S(1)}, u32[]{:S(2)}, u32[]{:S(2)}) async-start(f32[16,1,8256]{2,1,0:T(1,128)} %all_to_all.24), calls=%async_computation.3 | async-start | bytes 1064960 | tf_op jit(solution)/shard_map/all_to_all | solution.py:289
  156.0 27.5 %all-to-all-start.2 = ((bf16[192,16,128]{2,0,1:T(8,128)(2,1)}), bf16[192,16,128]{2,0,1:T(8,128)(2,1)S(1)}, u32[]{:S(2)}, u32[]{:S(2)}) async-start(bf16[192,16,128]{2,0,1:T(8,128)(2,1)} %copy_bitcast_fusion), calls=%async_computation.2 | async-start | bytes 1572864 | tf_op jit(solution)/shard_map/all_to_all | solution.py:303
  171.6 0.8 copy-start.4
  186.3 4.7 %copy-start.6 = (bf16[128,1024]{1,0:T(8,128)(2,1)S(1)}, bf16[128,1024]{1,0:T(8,128)(2,1)}, u32[]{:S(2)}) copy-start(bf16[128,1024]{1,0:T(8,128)(2,1)} %param.11) | copy-start | bytes 786436
Sparse Core Ops, SparseCore 0:
  10.8 83.1 all-gather.4
  96.2 69.2 all-gather.6

commit v18 on v17

--- a/solution.py
+++ b/solution.py
@@ -180,9 +180,9 @@
     all_ids = small[:, share:].reshape(stream).astype(jnp.int32)
 
     out_rows = w_out.shape[0]
-    pieces = lax.all_gather(jnp.concatenate([frames, out_grad], axis=0), "seq", axis=0)
-    frames_all = pieces[:, :rows].reshape(stream, width)
-    grad_all = pieces[:, rows:].reshape(stream, width)
+    pieces = lax.all_gather(jnp.stack([frames, out_grad]), "seq", axis=1, tiled=True)
+    frames_all = pieces[0]
+    grad_all = pieces[1]
     w_in_cols = lax.all_to_all(
         w_in.reshape(share, 2, devices, share).transpose(2, 0, 1, 3), "seq", 0, 0, tiled=True
     ).reshape(width, 2 * share)

time: 200 us -> 200 us (level)
  other arithmetic: 30.9 us -> 35 us
  local copies, waits for them, and re-layouts: 17.6 us -> 14.5 us
    slice x1 -> x0, local copies, waits for them, and re-layouts: 2.84 us -> none  [channel_local(): grad_all = pieces[:, rows:].reshape(stream, width)]
    reduce_sum x2, other arithmetic: 0.73 us -> 3.07 us  [norm(): mean = jnp.mean(block_float, axis=1, keepdims=True)]
    another operation x2 -> x3, other arithmetic: 5.47 us -> 7.36 us
    unnamed x26 -> x22, local copies, waits for them, and re-layouts: 4.51 us -> 3.2 us
  transfers between devices with their start and end apart: 6 -> 6, of which waited for: 5 -> 5; matrix products, arithmetic and copies ran while one was open for 25% -> 27% of each run, Pallas kernels for 0% -> 0%
where the time goes in v18:
time: 200 us; the launch traced here: 199 us
  waiting for transfers between devices  93.9 us (47%)
  other arithmetic  35 us (18%)
  starting transfers between devices  23.7 us (12%)
  matrix products  16.9 us (8%)
  local copies, waits for them, and re-layouts  14.5 us (7%)
  between operations  14.5 us (7%)
    all_gather x1, waiting for transfers between devices, channel_local(): lax.all_gather(jnp.stack([frames, out_grad]), 'seq', axis=1, tiled=True)  49.8 us
    all_to_all x1, waiting for transfers between devices, channel_local(): lax.all_to_all(jnp.concatenate([in_cols.reshape(devices, share * 2 * shar...  20.3 us
    all_to_all x1, waiting for transfers between devices, channel_local(): lax.all_to_all(w_in.reshape(share, 2, devices, share).transpose(2, 0, 1,...  14.2 us
    all_to_all x1, starting transfers between devices, channel_local(): lax.all_to_all(jnp.concatenate([activation, grad_hidden], axis=1).T.resha...  9.15 us
    all_to_all x1, starting transfers between devices, spread(): return lax.all_to_all(copies, 'seq', 0, 0, tiled=True)  7.39 us
    all_to_all x1, waiting for transfers between devices, channel_local(): lax.all_to_all(jnp.concatenate([activation, grad_hidden], axis=1).T.resha...  6.26 us
    another operation x2, other arithmetic  5.43 us
    reduce_sum x6, other arithmetic, channel_local(): jnp.sum(grad_conv * padded_glu[tap_index:tap_index + stream].astype(jnp.f...  4.49 us
  transfers between devices with their start and end apart: 6, of which 5 were waited for; matrix products, arithmetic and copies ran while one was open for 27% of the time, Pallas kernels for 0%

profile of v18, /device:TPU:0, one launch (start us, length us, event | category | flops | bytes accessed | tf_op | source)
XLA Modules:
  0.0 198.6 jit_solution(2900408667304874982)
XLA Ops:
  7.3 1.9 pad_maximum_fusion.1
  9.2 0.7 convert_element_type.269
  9.9 0.7 pad_maximum_fusion.7
  10.6 0.6 broadcast_in_dim.2
  11.2 7.4 %all-to-all-start = ((f32[16,1,192]{2,1,0:T(1,128)}), f32[16,1,192]{2,1,0:T(1,128)S(1)}, u32[]{:S(2)}, u32[]{:S(2)}) async-start(f32[16,1,192]{2,1,0:T(1,128)} %broadcast_in_dim.2), calls=%async_computation | async-start | bytes 32768 | tf_op jit(solution)/shard_map/all_to_all | solution.py:176
  18.6 1.5 reshape.143
  20.1 0.6 copy.32
  20.7 1.1 reshape.155
  21.8 3.3 %all-to-all-done = f32[16,1,192]{2,1,0:T(1,128)S(1)} async-done(((f32[16,1,192]{2,1,0:T(1,128)}), f32[16,1,192]{2,1,0:T(1,128)S(1)}, u32[]{:S(2)}, u32[]{:S(2)}) %all-to-all-start) | async-done | bytes 12320 | tf_op jit(solution)/shard_map/all_to_all | solution.py:176
  25.1 3.5 %all-to-all-start.1 = ((bf16[16,2,4096]{2,1,0:T(2,128)(2,1)}), bf16[16,2,4096]{2,1,0:T(2,128)(2,1)S(1)}, u32[]{:S(2)}, u32[]{:S(2)}) async-start(bf16[16,2,4096]{2,1,0:T(2,128)(2,1)} %reshape.155), calls=%async_computation.1 | async-start | bytes 524288 | tf_op jit(solution)/shard_map/all_to_all | solution.py:186
  29.0 14.2 %all-to-all-done.1 = bf16[16,2,4096]{2,1,0:T(2,128)(2,1)S(1)} async-done(((bf16[16,2,4096]{2,1,0:T(2,128)(2,1)}), bf16[16,2,4096]{2,1,0:T(2,128)(2,1)S(1)}, u32[]{:S(2)}, u32[]{:S(2)}) %all-to-all-start.1) | async-done | bytes 262176 | tf_op jit(solution)/shard_map/all_to_all | solution.py:186
  44.2 49.8 %all-gather.4.cloned.1.call-done = bf16[2,2048,1024]{2,1,0:T(8,128)(2,1)} async-done(((bf16[2,128,1024]{2,1,0:T(8,128)(2,1)}), bf16[2,2048,1024]{2,1,0:T(8,128)(2,1)}) %all-gather.4.cloned.1.call-update) | async-done | bytes 8388624 | tf_op jit(solution)/shard_map/all_gather | solution.py:183
  94.1 0.8 pad_maximum_fusion.3
  95.2 3.0 %convert_reduce_fusion = f32[2048]{0:T(1024)S(1)} fusion(bf16[2,2048,1024]{2,1,0:T(8,128)(2,1)} %all-gather.4.cloned.1.call-done), kind=kLoop, calls=%fused_computation.2 | loop fusion | flops 4192256 | bytes 4202496 | tf_op jit(solution)/shard_map/reduce_sum | solution.py:205
  98.2 3.5 %fusion.5 = f32[2048]{0:T(1024)S(1)} fusion(f32[2048]{0:T(1024)S(1)} %broadcast_multiply_fusion.1, bf16[2,2048,1024]{2,1,0:T(8,128)(2,1)} %all-gather.4.cloned.1.call-done), kind=kLoop, calls=%fused_computation.9 | loop fusion | flops 8386560 | bytes 4210688 | tf_op jit(solution)/shard_map/reduce_sum | solution.py:207
  101.7 4.4 %fusion.6 = (bf16[2048,1024]{1,0:T(8,128)(2,1)}, bf16[2048,1024]{1,0:T(8,128)(2,1)}, bf16[2048,1024]{1,0:T(8,128)(2,1)S(1)}) fusion(f32[2048]{0:T(1024)S(1)} %add_rsqrt_fusion, f32[2048]{0:T(1024)S(1)} %broadcast_multiply_fusion.1, bf16[2,2048,1024]{2,1,0:T(8,128)(2,1)S(1)} %copy-done, f32[1024]{0:T(1024)S(1)} %mul.649), kind=kLoop, calls=%fused_computation.10 | loop fusion | flops 18874368 | bytes 16797696 | tf_op jit(solution)/shard_map/convert_element_type | solution.py:214
  106.0 1.5 fusion.275
  107.7 4.2 %fusion.271 = (f32[64]{0:T(128)S(1)}, f32[2048,64]{0,1:T(8,128)S(1)}) fusion(f32[2048]{0:T(1024)S(1)} %get-tuple-element.114, f32[64]{0:T(128)S(1)} %get-tuple-element.94, f32[2048]{0:T(1024)S(1)} %get-tuple-element.97, f32[64]{0:T(128)S(1)} %get-tuple-element.95, f32[2048]{0:T(1024)S(1)} %get-tuple-element.98, f32[64]{0:T(128)S(1)} %get-tuple-element.66, ...), kind=kLoop, calls=%fused_computation.451 | loop fusion | flops 16121792 | bytes 1040384 | tf_op jit(solution)/shard_map/reduce_sum | solution.py:237
  112.2 1.6 fusion.270
  114.3 1.0 fusion.156
  115.3 5.3 %multiply_convert_fusion.1 = (bf16[2048,64]{0,1:T(8,128)(2,1)S(1)}, f32[2048,64]{0,1:T(8,128)S(1)}) fusion(f32[2048,128]{0,1:T(8,128)S(1)} %fusion.275, f32[2048]{0:T(1024)S(1)} %get-tuple-element.125, f32[64]{0:T(128)S(1)} %get-tuple-element.94, f32[2048]{0:T(1024)S(1)} %get-tuple-element.124, f32[64]{0:T(128)S(1)} %get-tuple-element.95, ...), kind=kLoop, calls=%fused_computation.234 | loop fusion | flops 12582912 | bytes 2088704 | tf_op jit(solution)/shard_map/convert
  120.7 1.3 convolution_multiply_fusion
  122.2 3.3 %fusion.202 = f32[1024,128]{0,1:T(8,128)S(1)} fusion(bf16[2048,1024]{1,0:T(8,128)(2,1)} %get-tuple-element.16, bf16[2048,64]{0,1:T(8,128)(2,1)S(1)} %multiply_convert_fusion, bf16[2048,64]{0,1:T(8,128)(2,1)S(1)} %get-tuple-element.53), kind=kOutput, calls=%fused_computation.304 | convolution fusion | flops 537919488 | bytes 5242880 | tf_op jit(solution)/shard_map/fa,fb->ab/dot_general | solution.py:285
  125.5 0.9 copy-done.1
  126.4 0.8 fusion.24
  127.3 1.2 all_to_all.24
  128.5 3.6 %all-to-all-start.3 = ((f32[16,1,8256]{2,1,0:T(1,128)}), f32[16,1,8256]{2,1,0:T(1,128)S(1)}, u32[]{:S(2)}, u32[]{:S(2)}) async-start(f32[16,1,8256]{2,1,0:T(1,128)} %all_to_all.24), calls=%async_computation.3 | async-start | bytes 1064960 | tf_op jit(solution)/shard_map/all_to_all | solution.py:289
  132.3 1.1 copy_bitcast_fusion
  133.4 0.8 fusion.132
  134.2 0.8 fusion.98
  135.1 20.3 %all-to-all-done.3 = f32[16,1,8256]{2,1,0:T(1,128)S(1)} async-done(((f32[16,1,8256]{2,1,0:T(1,128)}), f32[16,1,8256]{2,1,0:T(1,128)S(1)}, u32[]{:S(2)}, u32[]{:S(2)}) %all-to-all-start.3) | async-done | bytes 528416 | tf_op jit(solution)/shard_map/all_to_all | solution.py:289
  155.4 9.2 %all-to-all-start.2 = ((bf16[192,16,128]{2,0,1:T(8,128)(2,1)}), bf16[192,16,128]{2,0,1:T(8,128)(2,1)S(1)}, u32[]{:S(2)}, u32[]{:S(2)}) async-start(bf16[192,16,128]{2,0,1:T(8,128)(2,1)} %copy_bitcast_fusion), calls=%async_computation.2 | async-start | bytes 1572864 | tf_op jit(solution)/shard_map/all_to_all | solution.py:303
  164.8 0.8 fusion.80
  165.6 0.7 fusion.114
  167.0 0.6 broadcast_multiply_fusion
  167.6 3.7 %fusion.25 = f32[64,1024]{1,0:T(8,128)} fusion(bf16[2048,64]{0,1:T(8,128)(2,1)S(1)} %get-tuple-element.62, bf16[2,2048,1024]{2,1,0:T(8,128)(2,1)} %all-gather.4.cloned.1.call-done), kind=kOutput, calls=%fused_computation.27 | convolution fusion | flops 268500992 | bytes 4718592 | tf_op jit(solution)/shard_map/fa,fb->ab/dot_general | solution.py:247
  171.3 0.8 copy.45
  172.1 1.1 slice.630
  173.2 0.8 reshape.151
  174.0 0.6 copy.38
  174.6 1.2 reshape.152
  175.7 1.2 slice_reduce_fusion
  177.0 6.3 %all-to-all-done.2 = bf16[192,16,128]{2,0,1:T(8,128)(2,1)S(1)} async-done(((bf16[192,16,128]{2,0,1:T(8,128)(2,1)}), bf16[192,16,128]{2,0,1:T(8,128)(2,1)S(1)}, u32[]{:S(2)}, u32[]{:S(2)}) %all-to-all-start.2) | async-done | bytes 786464 | tf_op jit(solution)/shard_map/all_to_all | solution.py:303
  183.3 2.7 %fusion.273 = (bf16[16,64,1024]{2,1,0:T(8,128)(2,1)S(1)}, bf16[16,64,1024]{2,1,0:T(8,128)(2,1)S(1)}) fusion(bf16[16,192,1024]{2,1,0:T(8,128)(2,1)} %bitcast.191), kind=kLoop, calls=%fused_computation.452 | loop fusion | bytes 8388608 | tf_op jit(solution)/shard_map/slice | solution.py:199
  186.1 2.8 %fusion.21 = bf16[128,1024]{1,0:T(8,128)(2,1)} fusion(bf16[16,192,1024]{2,1,0:T(8,128)(2,1)} %bitcast.192, bf16[128,1024]{1,0:T(8,128)(2,1)S(1)} %copy-done.2, bf16[16,128,192]{1,2,0:T(8,128)(2,1)S(1)} %bitcast.194), kind=kOutput, calls=%fused_computation.25 | convolution fusion | flops 268828672 | bytes 2883584 | tf_op jit(solution)/shard_map/dot_general | solution.py:312
  188.9 0.8 fusion.201
  189.7 1.0 fusion.269
  190.7 1.0 fusion.34
  (56 shorter events, 4.2 us)
Async XLA Ops:
  7.2 21.5 %copy-start.2 = (bf16[128,1024]{1,0:T(8,128)(2,1)S(1)}, bf16[128,1024]{1,0:T(8,128)(2,1)}, u32[]{:S(2)}) copy-start(bf16[128,1024]{1,0:T(8,128)(2,1)} %param.9) | copy-start | bytes 786436
  7.2 86.8 %copy-start.3 = (bf16[64,2048]{1,0:T(8,128)(2,1)S(1)}, bf16[64,2048]{1,0:T(8,128)(2,1)}, u32[]{:S(2)}) copy-start(bf16[64,2048]{1,0:T(8,128)(2,1)} %param.13) | copy-start | bytes 786436
  7.2 21.6 %copy-start.6 = (f32[31,64]{1,0:T(8,128)S(1)}, f32[31,64]{1,0:T(8,128)}, u32[]{:S(2)}) copy-start(f32[31,64]{1,0:T(8,128)} %param.14) | copy-start | bytes 23812
  7.2 86.8 %copy-start.5 = (bf16[64,1024]{1,0:T(8,128)(2,1)S(1)}, bf16[64,1024]{1,0:T(8,128)(2,1)}, u32[]{:S(2)}) copy-start(bf16[64,1024]{1,0:T(8,128)(2,1)} %param.17) | copy-start | bytes 393220
  7.2 86.8 %all-gather.4.cloned.1.call-start = ((), (), s32[]{:S(2)}) async-start(), calls=%async_computation.4 | async-start | bytes 8912896 | tf_op jit(solution)/shard_map/all_gather | solution.py:183
  11.2 13.9 %all-to-all-start = ((f32[16,1,192]{2,1,0:T(1,128)}), f32[16,1,192]{2,1,0:T(1,128)S(1)}, u32[]{:S(2)}, u32[]{:S(2)}) async-start(f32[16,1,192]{2,1,0:T(1,128)} %broadcast_in_dim.2), calls=%async_computation | async-start | bytes 32768 | tf_op jit(solution)/shard_map/all_to_all | solution.py:176
  25.1 18.1 %all-to-all-start.1 = ((bf16[16,2,4096]{2,1,0:T(2,128)(2,1)}), bf16[16,2,4096]{2,1,0:T(2,128)(2,1)S(1)}, u32[]{:S(2)}, u32[]{:S(2)}) async-start(bf16[16,2,4096]{2,1,0:T(2,128)(2,1)} %reshape.155), calls=%async_computation.1 | async-start | bytes 524288 | tf_op jit(solution)/shard_map/all_to_all | solution.py:186
  28.6 154.7 %all-gather.6.cloned.1.call-start = ((), (), s32[]{:S(2)}) async-start(), calls=%async_computation.5 | async-start | bytes 6684672 | tf_op jit(solution)/shard_map/all_gather | solution.py:192
  95.2 6.5 %copy-start = (bf16[2,2048,1024]{2,1,0:T(8,128)(2,1)S(1)}, bf16[2,2048,1024]{2,1,0:T(8,128)(2,1)}, u32[]{:S(2)}) copy-start(bf16[2,2048,1024]{2,1,0:T(8,128)(2,1)} %all-gather.4.cloned.1.call-done) | copy-start | bytes 25165828
  106.0 6.1 %copy-start.7 = (f32[64]{0:T(128)S(1)}, f32[64]{0:T(128)}, u32[]{:S(2)}) copy-start(f32[64]{0:T(128)} %param.15) | copy-start | bytes 772
  106.0 6.1 %copy-start.8 = (f32[64]{0:T(128)S(1)}, f32[64]{0:T(128)}, u32[]{:S(2)}) copy-start(f32[64]{0:T(128)} %param.16) | copy-start | bytes 772
  122.1 4.2 %copy-start.1 = (bf16[2048,1024]{1,0:T(8,128)(2,1)S(1)}, bf16[2048,1024]{1,0:T(8,128)(2,1)}, u32[]{:S(2)}) copy-start(bf16[2048,1024]{1,0:T(8,128)(2,1)} %get-tuple-element.17) | copy-start | bytes 12582916
  128.5 26.9 %all-to-all-start.3 = ((f32[16,1,8256]{2,1,0:T(1,128)}), f32[16,1,8256]{2,1,0:T(1,128)S(1)}, u32[]{:S(2)}, u32[]{:S(2)}) async-start(f32[16,1,8256]{2,1,0:T(1,128)} %all_to_all.24), calls=%async_computation.3 | async-start | bytes 1064960 | tf_op jit(solution)/shard_map/all_to_all | solution.py:289
  155.4 27.9 %all-to-all-start.2 = ((bf16[192,16,128]{2,0,1:T(8,128)(2,1)}), bf16[192,16,128]{2,0,1:T(8,128)(2,1)S(1)}, u32[]{:S(2)}, u32[]{:S(2)}) async-start(bf16[192,16,128]{2,0,1:T(8,128)(2,1)} %copy_bitcast_fusion), calls=%async_computation.2 | async-start | bytes 1572864 | tf_op jit(solution)/shard_map/all_to_all | solution.py:303
  186.1 4.7 %copy-start.4 = (bf16[128,1024]{1,0:T(8,128)(2,1)S(1)}, bf16[128,1024]{1,0:T(8,128)(2,1)}, u32[]{:S(2)}) copy-start(bf16[128,1024]{1,0:T(8,128)(2,1)} %param.11) | copy-start | bytes 786436
Sparse Core Ops, SparseCore 0:
  10.8 83.1 all-gather.3
  96.3 69.3 all-gather.5

commit v19 on v18

--- a/solution.py
+++ b/solution.py
@@ -190,13 +190,14 @@
         (w_in, w_out, pieces, w_in_cols, small)
     )
     weights = lax.all_gather(
-        jnp.concatenate([w_out_late, w_in_late[:, :width], w_in_late[:, width:]], axis=0),
+        jnp.stack([w_out_late, w_in_late[:, :width], w_in_late[:, width:]]),
         "seq",
-        axis=0,
-    )
-    w_out_all = weights[:, :out_rows].reshape(width, width)
-    w_in_left = weights[:, out_rows : 2 * out_rows].reshape(width, width)
-    w_in_right = weights[:, 2 * out_rows :].reshape(width, width)
+        axis=1,
+        tiled=True,
+    )
+    w_out_all = weights[0]
+    w_in_left = weights[1]
+    w_in_right = weights[2]
 
     first_channel = lax.axis_index("seq") * share
 

time: 200 us -> 202 us (1.010)
  matrix products: 16.9 us -> 20.3 us
  local copies, waits for them, and re-layouts: 14.5 us -> 11.6 us
  waiting for transfers between devices: 93.9 us -> 96.4 us
    all_to_all x1, waiting for transfers between devices: 6.26 us -> 8.8 us  [channel_local(): lax.all_to_all(jnp.concatenate([activation, grad_hidden], axis=1).T.resha...]
    another operation x2 -> x3, other arithmetic: 5.43 us -> 6.29 us
  transfers between devices with their start and end apart: 6 -> 6, of which waited for: 5 -> 5; matrix products, arithmetic and copies ran while one was open for 27% -> 26% of each run, Pallas kernels for 0% -> 0%
where the time goes in v19:
time: 202 us; the launch traced here: 201 us
  waiting for transfers between devices  96.4 us (48%)
  other arithmetic  34.4 us (17%)
  starting transfers between devices  23.6 us (12%)
  matrix products  20.3 us (10%)
  between operations  14.5 us (7%)
  local copies, waits for them, and re-layouts  11.6 us (6%)
    all_gather x1, waiting for transfers between devices, channel_local(): lax.all_gather(jnp.stack([frames, out_grad]), 'seq', axis=1, tiled=True)  49.8 us
    all_to_all x1, waiting for transfers between devices, channel_local(): lax.all_to_all(jnp.concatenate([in_cols.reshape(devices, share * 2 * shar...  20.2 us
    all_to_all x1, waiting for transfers between devices, channel_local(): lax.all_to_all(w_in.reshape(share, 2, devices, share).transpose(2, 0, 1,...  14.2 us
    all_to_all x1, starting transfers between devices, channel_local(): lax.all_to_all(jnp.concatenate([activation, grad_hidden], axis=1).T.resha...  8.99 us
    all_to_all x1, waiting for transfers between devices, channel_local(): lax.all_to_all(jnp.concatenate([activation, grad_hidden], axis=1).T.resha...  8.8 us
    all_to_all x1, starting transfers between devices, spread(): return lax.all_to_all(copies, 'seq', 0, 0, tiled=True)  7.39 us
    another operation x2, other arithmetic  5.47 us
    reduce_sum x6, other arithmetic, channel_local(): jnp.sum(grad_conv * padded_glu[tap_index:tap_index + stream].astype(jnp.f...  4.53 us
  transfers between devices with their start and end apart: 6, of which 5 were waited for; matrix products, arithmetic and copies ran while one was open for 26% of the time, Pallas kernels for 0%

profile of v19, /device:TPU:0, one launch (start us, length us, event | category | flops | bytes accessed | tf_op | source)
XLA Modules:
  0.0 200.8 jit_solution(7642236849444343833)
XLA Ops:
  7.3 1.9 pad_maximum_fusion.1
  9.2 0.7 convert_element_type.269
  9.9 0.7 pad_maximum_fusion.7
  10.6 0.6 broadcast_in_dim.2
  11.2 7.4 %all-to-all-start = ((f32[16,1,192]{2,1,0:T(1,128)}), f32[16,1,192]{2,1,0:T(1,128)S(1)}, u32[]{:S(2)}, u32[]{:S(2)}) async-start(f32[16,1,192]{2,1,0:T(1,128)} %broadcast_in_dim.2), calls=%async_computation | async-start | bytes 32768 | tf_op jit(solution)/shard_map/all_to_all | solution.py:176
  18.6 1.5 reshape.138
  20.1 0.6 copy.31
  20.7 1.1 reshape.147
  21.8 3.3 %all-to-all-done = f32[16,1,192]{2,1,0:T(1,128)S(1)} async-done(((f32[16,1,192]{2,1,0:T(1,128)}), f32[16,1,192]{2,1,0:T(1,128)S(1)}, u32[]{:S(2)}, u32[]{:S(2)}) %all-to-all-start) | async-done | bytes 12320 | tf_op jit(solution)/shard_map/all_to_all | solution.py:176
  25.1 3.5 %all-to-all-start.1 = ((bf16[16,2,4096]{2,1,0:T(2,128)(2,1)}), bf16[16,2,4096]{2,1,0:T(2,128)(2,1)S(1)}, u32[]{:S(2)}, u32[]{:S(2)}) async-start(bf16[16,2,4096]{2,1,0:T(2,128)(2,1)} %reshape.147), calls=%async_computation.1 | async-start | bytes 524288 | tf_op jit(solution)/shard_map/all_to_all | solution.py:186
  29.0 14.2 %all-to-all-done.1 = bf16[16,2,4096]{2,1,0:T(2,128)(2,1)S(1)} async-done(((bf16[16,2,4096]{2,1,0:T(2,128)(2,1)}), bf16[16,2,4096]{2,1,0:T(2,128)(2,1)S(1)}, u32[]{:S(2)}, u32[]{:S(2)}) %all-to-all-start.1) | async-done | bytes 262176 | tf_op jit(solution)/shard_map/all_to_all | solution.py:186
  44.2 49.8 %all-gather.3.cloned.1.call-done = bf16[2,2048,1024]{2,1,0:T(8,128)(2,1)} async-done(((bf16[2,128,1024]{2,1,0:T(8,128)(2,1)}), bf16[2,2048,1024]{2,1,0:T(8,128)(2,1)}) %all-gather.3.cloned.1.call-update) | async-done | bytes 8388624 | tf_op jit(solution)/shard_map/all_gather | solution.py:183
  94.1 0.8 pad_maximum_fusion.3
  95.2 3.0 %convert_reduce_fusion = f32[2048]{0:T(1024)S(1)} fusion(bf16[2,2048,1024]{2,1,0:T(8,128)(2,1)} %all-gather.3.cloned.1.call-done), kind=kLoop, calls=%fused_computation.2 | loop fusion | flops 4192256 | bytes 4202496 | tf_op jit(solution)/shard_map/reduce_sum | solution.py:206
  98.2 3.5 %fusion.5 = f32[2048]{0:T(1024)S(1)} fusion(f32[2048]{0:T(1024)S(1)} %broadcast_multiply_fusion.1, bf16[2,2048,1024]{2,1,0:T(8,128)(2,1)} %all-gather.3.cloned.1.call-done), kind=kLoop, calls=%fused_computation.9 | loop fusion | flops 8386560 | bytes 4210688 | tf_op jit(solution)/shard_map/reduce_sum | solution.py:208
  101.7 4.4 %fusion.6 = (bf16[2048,1024]{1,0:T(8,128)(2,1)}, bf16[2048,1024]{1,0:T(8,128)(2,1)}, bf16[2048,1024]{1,0:T(8,128)(2,1)S(1)}) fusion(f32[2048]{0:T(1024)S(1)} %add_rsqrt_fusion, f32[2048]{0:T(1024)S(1)} %broadcast_multiply_fusion.1, bf16[2,2048,1024]{2,1,0:T(8,128)(2,1)S(1)} %copy-done, f32[1024]{0:T(1024)S(1)} %mul.649), kind=kLoop, calls=%fused_computation.10 | loop fusion | flops 18874368 | bytes 16797696 | tf_op jit(solution)/shard_map/convert_element_type | solution.py:215
  106.1 1.5 fusion.267
  107.7 4.2 %fusion.265 = (f32[64]{0:T(128)S(1)}, f32[2048,64]{0,1:T(8,128)S(1)}) fusion(f32[2048]{0:T(1024)S(1)} %get-tuple-element.112, f32[64]{0:T(128)S(1)} %get-tuple-element.92, f32[2048]{0:T(1024)S(1)} %get-tuple-element.95, f32[64]{0:T(128)S(1)} %get-tuple-element.93, f32[2048]{0:T(1024)S(1)} %get-tuple-element.96, f32[64]{0:T(128)S(1)} %get-tuple-element.64, ...), kind=kLoop, calls=%fused_computation.454 | loop fusion | flops 16121792 | bytes 1040384 | tf_op jit(solution)/shard_map/reduce_sum | solution.py:238
  112.2 1.6 fusion.264
  114.3 1.0 fusion.151
  115.3 5.3 %multiply_convert_fusion.1 = (bf16[2048,64]{0,1:T(8,128)(2,1)S(1)}, f32[2048,64]{0,1:T(8,128)S(1)}) fusion(f32[2048,128]{0,1:T(8,128)S(1)} %fusion.267, f32[2048]{0:T(1024)S(1)} %get-tuple-element.123, f32[64]{0:T(128)S(1)} %get-tuple-element.92, f32[2048]{0:T(1024)S(1)} %get-tuple-element.122, f32[64]{0:T(128)S(1)} %get-tuple-element.93, ...), kind=kLoop, calls=%fused_computation.237 | loop fusion | flops 12582912 | bytes 2088704 | tf_op jit(solution)/shard_map/convert
  120.8 1.3 convolution_multiply_fusion
  122.2 3.7 %fusion.196 = f32[1024,128]{0,1:T(8,128)S(1)} fusion(bf16[2048,1024]{1,0:T(8,128)(2,1)} %get-tuple-element.16, bf16[2048,64]{0,1:T(8,128)(2,1)S(1)} %multiply_convert_fusion, bf16[2048,64]{0,1:T(8,128)(2,1)S(1)} %get-tuple-element.53), kind=kOutput, calls=%fused_computation.305 | convolution fusion | flops 537919488 | bytes 5242880 | tf_op jit(solution)/shard_map/fa,fb->ab/dot_general | solution.py:286
  125.9 0.5 copy-done.1
  126.4 0.8 fusion.19
  127.4 1.2 all_to_all.24
  128.5 3.6 %all-to-all-start.3 = ((f32[16,1,8256]{2,1,0:T(1,128)}), f32[16,1,8256]{2,1,0:T(1,128)S(1)}, u32[]{:S(2)}, u32[]{:S(2)}) async-start(f32[16,1,8256]{2,1,0:T(1,128)} %all_to_all.24), calls=%async_computation.3 | async-start | bytes 1064960 | tf_op jit(solution)/shard_map/all_to_all | solution.py:290
  132.4 1.1 copy_bitcast_fusion
  133.5 0.8 fusion.127
  134.3 0.8 fusion.93
  135.1 20.2 %all-to-all-done.3 = f32[16,1,8256]{2,1,0:T(1,128)S(1)} async-done(((f32[16,1,8256]{2,1,0:T(1,128)}), f32[16,1,8256]{2,1,0:T(1,128)S(1)}, u32[]{:S(2)}, u32[]{:S(2)}) %all-to-all-start.3) | async-done | bytes 528416 | tf_op jit(solution)/shard_map/all_to_all | solution.py:290
  155.4 9.0 %all-to-all-start.2 = ((bf16[192,16,128]{2,0,1:T(8,128)(2,1)}), bf16[192,16,128]{2,0,1:T(8,128)(2,1)}, u32[]{:S(2)}, u32[]{:S(2)}) async-start(bf16[192,16,128]{2,0,1:T(8,128)(2,1)} %copy_bitcast_fusion), calls=%async_computation.2 | async-start | bytes 1572864 | tf_op jit(solution)/shard_map/all_to_all | solution.py:304
  164.6 0.8 fusion.75
  165.4 0.8 fusion.109
  166.3 0.5 broadcast_multiply_fusion.4
  166.8 0.6 broadcast_multiply_fusion
  167.4 3.7 %fusion.20 = f32[64,1024]{1,0:T(8,128)} fusion(bf16[2048,64]{0,1:T(8,128)(2,1)S(1)} %get-tuple-element.60, bf16[2,2048,1024]{2,1,0:T(8,128)(2,1)} %all-gather.3.cloned.1.call-done), kind=kOutput, calls=%fused_computation.30 | convolution fusion | flops 268500992 | bytes 4718592 | tf_op jit(solution)/shard_map/fa,fb->ab/dot_general | solution.py:248
  171.2 0.8 reshape.145
  172.0 0.6 copy.37
  172.6 1.2 reshape.146
  173.8 0.5 slice_reduce_fusion
  174.3 8.8 %all-to-all-done.2 = bf16[192,16,128]{2,0,1:T(8,128)(2,1)} async-done(((bf16[192,16,128]{2,0,1:T(8,128)(2,1)}), bf16[192,16,128]{2,0,1:T(8,128)(2,1)}, u32[]{:S(2)}, u32[]{:S(2)}) %all-to-all-start.2) | async-done | bytes 786464 | tf_op jit(solution)/shard_map/all_to_all | solution.py:304
  183.1 1.1 slice.625
  184.2 1.0 slice.623
  185.3 2.4 %fusion.11 = f32[128,1024]{1,0:T(8,128)S(1)} fusion(bf16[3,1024,1024]{2,1,0:T(8,128)(2,1)} %all-gather.5.cloned.1.call-done, bf16[128,2,1024]{0,2,1:T(8,128)(2,1)S(1)} %bitcast.211), kind=kOutput, calls=%fused_computation.17 | convolution fusion | flops 268435456 | bytes 2883584 | tf_op jit(solution)/shard_map/fe,ne->fn/dot_general | solution.py:317
  187.7 2.5 %fusion.263 = (f32[128]{0:T(128)S(1)}, f32[128]{0:T(128)S(1)}, f32[128,1024]{1,0:T(8,128)S(1)}) fusion(f32[128]{0:T(128)S(1)} %add_rsqrt_fusion.1, f32[128]{0:T(128)S(1)} %broadcast_multiply_fusion.7, bf16[128,1024]{1,0:T(8,128)(2,1)S(1)} %copy-done.2, f32[1024]{0:T(1024)S(1)} %mul.649, f32[128,1024]{1,0:T(8,128)S(1)} %fusion.11, ...), kind=kOutput, calls=%fused_computation.452 | convolution fusion | flops 269483776 | bytes 3676160 | tf_op jit(solution)/shard_map/fe,ne->fn/dot_general | solution.py:315
  190.3 1.0 fusion.29
  191.2 2.8 %fusion.18 = bf16[128,1024]{1,0:T(8,128)(2,1)} fusion(bf16[128,1024]{0,1:T(8,128)(2,1)S(1)} %bitcast.210, bf16[3,1024,1024]{2,1,0:T(8,128)(2,1)} %all-gather.5.cloned.1.call-done, bf16[128,1024]{1,0:T(8,128)(2,1)S(1)} %copy-done.2), kind=kOutput, calls=%fused_computation.28 | convolution fusion | flops 268828672 | bytes 2883584 | tf_op jit(solution)/shard_map/dot_general | solution.py:313
  (56 shorter events, 3.7 us)
Async XLA Ops:
  7.2 21.5 %copy-start.2 = (bf16[128,1024]{1,0:T(8,128)(2,1)S(1)}, bf16[128,1024]{1,0:T(8,128)(2,1)}, u32[]{:S(2)}) copy-start(bf16[128,1024]{1,0:T(8,128)(2,1)} %param.9) | copy-start | bytes 786436
  7.2 86.8 %copy-start.3 = (bf16[64,2048]{1,0:T(8,128)(2,1)S(1)}, bf16[64,2048]{1,0:T(8,128)(2,1)}, u32[]{:S(2)}) copy-start(bf16[64,2048]{1,0:T(8,128)(2,1)} %param.13) | copy-start | bytes 786436
  7.2 21.6 %copy-start.6 = (f32[31,64]{1,0:T(8,128)S(1)}, f32[31,64]{1,0:T(8,128)}, u32[]{:S(2)}) copy-start(f32[31,64]{1,0:T(8,128)} %param.14) | copy-start | bytes 23812
  7.2 86.8 %copy-start.5 = (bf16[64,1024]{1,0:T(8,128)(2,1)S(1)}, bf16[64,1024]{1,0:T(8,128)(2,1)}, u32[]{:S(2)}) copy-start(bf16[64,1024]{1,0:T(8,128)(2,1)} %param.17) | copy-start | bytes 393220
  7.2 86.8 %all-gather.3.cloned.1.call-start = ((), (), s32[]{:S(2)}) async-start(), calls=%async_computation.4 | async-start | bytes 8912896 | tf_op jit(solution)/shard_map/all_gather | solution.py:183
  11.2 13.9 %all-to-all-start = ((f32[16,1,192]{2,1,0:T(1,128)}), f32[16,1,192]{2,1,0:T(1,128)S(1)}, u32[]{:S(2)}, u32[]{:S(2)}) async-start(f32[16,1,192]{2,1,0:T(1,128)} %broadcast_in_dim.2), calls=%async_computation | async-start | bytes 32768 | tf_op jit(solution)/shard_map/all_to_all | solution.py:176
  25.1 18.1 %all-to-all-start.1 = ((bf16[16,2,4096]{2,1,0:T(2,128)(2,1)}), bf16[16,2,4096]{2,1,0:T(2,128)(2,1)S(1)}, u32[]{:S(2)}, u32[]{:S(2)}) async-start(bf16[16,2,4096]{2,1,0:T(2,128)(2,1)} %reshape.147), calls=%async_computation.1 | async-start | bytes 524288 | tf_op jit(solution)/shard_map/all_to_all | solution.py:186
  28.6 156.6 %all-gather.5.cloned.1.call-start = ((), (), s32[]{:S(2)}) async-start(), calls=%async_computation.5 | async-start | bytes 6684672 | tf_op jit(solution)/shard_map/all_gather | solution.py:192
  95.2 6.5 %copy-start = (bf16[2,2048,1024]{2,1,0:T(8,128)(2,1)S(1)}, bf16[2,2048,1024]{2,1,0:T(8,128)(2,1)}, u32[]{:S(2)}) copy-start(bf16[2,2048,1024]{2,1,0:T(8,128)(2,1)} %all-gather.3.cloned.1.call-done) | copy-start | bytes 25165828
  106.0 6.1 %copy-start.7 = (f32[64]{0:T(128)S(1)}, f32[64]{0:T(128)}, u32[]{:S(2)}) copy-start(f32[64]{0:T(128)} %param.15) | copy-start | bytes 772
  106.1 6.1 %copy-start.8 = (f32[64]{0:T(128)S(1)}, f32[64]{0:T(128)}, u32[]{:S(2)}) copy-start(f32[64]{0:T(128)} %param.16) | copy-start | bytes 772
  122.2 4.2 %copy-start.1 = (bf16[2048,1024]{1,0:T(8,128)(2,1)S(1)}, bf16[2048,1024]{1,0:T(8,128)(2,1)}, u32[]{:S(2)}) copy-start(bf16[2048,1024]{1,0:T(8,128)(2,1)} %get-tuple-element.17) | copy-start | bytes 12582916
  128.5 26.8 %all-to-all-start.3 = ((f32[16,1,8256]{2,1,0:T(1,128)}), f32[16,1,8256]{2,1,0:T(1,128)S(1)}, u32[]{:S(2)}, u32[]{:S(2)}) async-start(f32[16,1,8256]{2,1,0:T(1,128)} %all_to_all.24), calls=%async_computation.3 | async-start | bytes 1064960 | tf_op jit(solution)/shard_map/all_to_all | solution.py:290
  155.4 27.8 %all-to-all-start.2 = ((bf16[192,16,128]{2,0,1:T(8,128)(2,1)}), bf16[192,16,128]{2,0,1:T(8,128)(2,1)}, u32[]{:S(2)}, u32[]{:S(2)}) async-start(bf16[192,16,128]{2,0,1:T(8,128)(2,1)} %copy_bitcast_fusion), calls=%async_computation.2 | async-start | bytes 1572864 | tf_op jit(solution)/shard_map/all_to_all | solution.py:304
  185.2 5.1 %copy-start.4 = (bf16[128,1024]{1,0:T(8,128)(2,1)S(1)}, bf16[128,1024]{1,0:T(8,128)(2,1)}, u32[]{:S(2)}) copy-start(bf16[128,1024]{1,0:T(8,128)(2,1)} %param.11) | copy-start | bytes 786436
Sparse Core Ops, SparseCore 0:
  10.8 83.1 all-gather.2
  96.2 69.0 all-gather.4
